TPU v7x, 256 devices: a whole 4x4x8 slice. The times are simulated.
256 devices in a mesh: row: 8 (over y, core), col: 32 (over x, z).
Axes of the slice: x: 4, y: 4, z: 8, core: 2. Of those that a mesh axis runs over, the one named last changes fastest.
Arguments:
- hidden: bfloat16 [32768, 4608], P('col', 'row'), may hold values from -6 to 6
- w_query: bfloat16 [4608, 4096], P('col', 'row'), may hold values from -0.09375 to 0.09375
- w_key: bfloat16 [4608, 2048], P('col', 'row'), may hold values from -0.09375 to 0.09375
- w_value: bfloat16 [4608, 2048], P('col', 'row'), may hold values from -0.09375 to 0.09375
- adapter_down: bfloat16 [32, 4608, 32], P('col', 'row'), may hold values from -0.09375 to 0.09375
- adapter_up_query: bfloat16 [32, 16, 4096], P('col', None, 'row'), may hold values from -1.5 to 1.5
- adapter_up_value: bfloat16 [32, 16, 2048], P('col', None, 'row'), may hold values from -1.5 to 1.5
- lengths: int32 [32, 10], P('col'), may hold values from 1 to 192, 1024 in all within a row
- request_adapter: int32 [32, 10], P('col'), may hold values from 0 to 31
- adapter_slot: int32 [32], replicated, may hold values from 0 to 31, each once
- page_table: int32 [32, 18], P('col'), may hold values from 0 to 17, each once within a row
Outputs:
- query: bfloat16 [32768, 4096], P('col', 'row')
- key_cache: bfloat16 [576, 128, 2048], P('col', None, 'row')
- value_cache: bfloat16 [576, 128, 2048], P('col', None, 'row')
Inputs may be any that keep to these rules, and one draw needn't show every extreme that they name: Each row of lengths sums to 1024, and its longest request has exactly 192 tokens. `adapter_slot`: a permutation of the slots. `page_table`: each row is a permutation of the 18 local slots.
All inputs are finite; a program needn't handle non-finite values.
Results may differ from a plain program's by a relative error of at most 0.0039.
Values may be sent and summed in bfloat16 or wider, within the bound.
No kernel may reach another device: no remote copies, remote signals or barrier semaphores. Data moves between devices by JAX's collectives and lax.ppermute only.
A program may use at most 128 MiB of HBM per device.

v0:
```python
import math

import jax
import jax.numpy as jnp
from jax import lax
from jax.sharding import PartitionSpec as P

HEAD = 128
PAGE = 128
MOST = 192
TOK_DEV = 1024


def rotate(values, position):
    half_width = HEAD // 2
    frequency = jnp.exp(
        jnp.arange(half_width, dtype=jnp.float32) * (-2.0 * math.log(10000.0) / HEAD)
    )
    angles = position.astype(jnp.float32)[:, None] * frequency[None, :]
    cosine = jnp.cos(angles)[:, None, :]
    sine_value = jnp.sin(angles)[:, None, :]
    shaped = values.reshape(values.shape[0], -1, HEAD)
    leading = shaped[:, :, :half_width]
    second = shaped[:, :, half_width:]
    rotated = jnp.concatenate(
        [leading * cosine - second * sine_value, second * cosine + leading * sine_value], axis=2
    )
    return rotated.reshape(values.shape)


def layout(lengths, page_row):
    token_index = jnp.arange(TOK_DEV, dtype=jnp.int32)
    starts = jnp.cumsum(lengths) - lengths
    request_of = jnp.sum((token_index[:, None] >= starts[None, :]).astype(jnp.int32), axis=1) - 1
    position = token_index - jnp.take(starts, request_of)
    pages_each = (lengths + PAGE - 1) // PAGE
    page_start = jnp.cumsum(pages_each) - pages_each
    page_index = jnp.take(page_start, request_of) + position // PAGE
    target = jnp.take(page_row, page_index) * PAGE + position % PAGE
    return (starts, request_of, position, target)


def expand_up(lowrank, chosen, up_query, up_value):
    adapter_count = up_query.shape[0]
    rank_width = up_query.shape[1]
    onehot = (chosen[:, None] == jnp.arange(adapter_count, dtype=jnp.int32)[None, :]).astype(
        lowrank.dtype
    )
    spread_query = (onehot[:, :, None] * lowrank[:, None, :rank_width]).reshape(
        -1, adapter_count * rank_width
    )
    spread_value = (onehot[:, :, None] * lowrank[:, None, rank_width:]).reshape(
        -1, adapter_count * rank_width
    )
    delta_query = jnp.dot(
        spread_query,
        up_query.reshape(adapter_count * rank_width, -1),
        preferred_element_type=jnp.float32,
    )
    delta_value = jnp.dot(
        spread_value,
        up_value.reshape(adapter_count * rank_width, -1),
        preferred_element_type=jnp.float32,
    )
    return (delta_query, delta_value)


def project_down(source, down_all, starts, lengths, chosen_request):
    tokens = source.shape[0]
    padded = jnp.concatenate([source, jnp.zeros((MOST, source.shape[1]), source.dtype)], axis=0)
    result = jnp.zeros((tokens + MOST, down_all.shape[2]), jnp.float32)
    inner_rows = jnp.arange(MOST, dtype=jnp.int32)

    def one_request(number, result):
        first_row = starts[number]
        window = lax.dynamic_slice_in_dim(padded, first_row, MOST, 0)
        factor = lax.dynamic_index_in_dim(down_all, chosen_request[number], 0, keepdims=False)
        partial_sum = jnp.dot(window, factor, preferred_element_type=jnp.float32)
        inside = (inner_rows < lengths[number]).astype(jnp.float32)[:, None]
        current = lax.dynamic_slice_in_dim(result, first_row, MOST, 0)
        return lax.dynamic_update_slice_in_dim(result, current + partial_sum * inside, first_row, 0)

    result = lax.fori_loop(0, starts.shape[0], one_request, result)
    return result[:tokens]


def shards(
    hidden,
    w_query,
    w_key,
    w_value,
    adapter_down,
    adapter_up_query,
    adapter_up_value,
    lengths,
    request_adapter,
    adapter_slot,
    page_table,
):
    starts, request_of, position, target = layout(lengths[0], page_table[0])
    full_rows = lax.all_gather(hidden, "row", axis=1, tiled=True)
    base_query = jnp.dot(
        full_rows,
        lax.all_gather(w_query, "col", axis=0, tiled=True),
        preferred_element_type=jnp.float32,
    )
    base_key = jnp.dot(
        full_rows,
        lax.all_gather(w_key, "col", axis=0, tiled=True),
        preferred_element_type=jnp.float32,
    )
    base_value = jnp.dot(
        full_rows,
        lax.all_gather(w_value, "col", axis=0, tiled=True),
        preferred_element_type=jnp.float32,
    )
    up_query, up_value = (
        lax.all_gather(adapter_up_query, "col", axis=0, tiled=True),
        lax.all_gather(adapter_up_value, "col", axis=0, tiled=True),
    )
    chosen_request = jnp.take(adapter_slot, request_adapter[0])
    rows_all = lax.all_gather(adapter_down, "row", axis=1, tiled=True)
    down_all = lax.all_gather(rows_all, "col", axis=0, tiled=True)
    lowrank = project_down(full_rows, down_all, starts, lengths[0], chosen_request)
    lowrank = lowrank.astype(jnp.bfloat16)
    chosen = jnp.take(chosen_request, request_of)
    delta_query, delta_value = expand_up(lowrank, chosen, up_query, up_value)
    query = rotate(base_query + delta_query, position).astype(jnp.bfloat16)
    key_rotated = rotate(base_key, position).astype(jnp.bfloat16)
    value_rows = (base_value + delta_value).astype(jnp.bfloat16)
    pages = page_table.shape[1]
    key_width = w_key.shape[1]
    key_cache = (
        jnp.zeros((pages * PAGE, key_width), jnp.bfloat16)
        .at[target]
        .set(key_rotated)
        .reshape(pages, PAGE, key_width)
    )
    value_cache = (
        jnp.zeros((pages * PAGE, key_width), jnp.bfloat16)
        .at[target]
        .set(value_rows)
        .reshape(pages, PAGE, key_width)
    )
    return (query, key_cache, value_cache)


def solution(mesh):
    return jax.shard_map(
        shards,
        mesh=mesh,
        in_specs=(
            P("col", "row"),
            P("col", "row"),
            P("col", "row"),
            P("col", "row"),
            P("col", "row", None),
            P("col", None, "row"),
            P("col", None, "row"),
            P("col", None),
            P("col", None),
            P(),
            P("col", None),
        ),
        out_specs=(P("col", "row"), P("col", None, "row"), P("col", None, "row")),
        check_vma=False,
    )
```

profile of v0, /device:TPU:1, one launch (start us, length us, event | category | flops | bytes accessed | tf_op | source)
XLA Modules:
  0.0 450.9 jit_solution(18159563451350654746)
XLA Ops:
  7.2 0.7 all-gather.12.cloned.1.call-update
  8.0 0.7 all-gather.6.cloned.1.call-update
  8.7 0.7 all-gather.8.cloned.1.call-update
  9.4 1.0 copy.40
  10.4 18.8 %all_gather.26 = bf16[1,4608,32]{2,0,1:T(2,128)(2,1)S(1)} all-gather(bf16[1,576,32]{2,0,1:T(2,128)(2,1)S(1)} %copy.40), channel_id=1, replica_groups=mesh['row'=8,'col'=32] {'row'}, dimensions={1}, use_global_device_ids=true | all-gather | bytes 331776 | tf_op jit(solution)/shard_map/all_gather | solution.py:122
  29.3 3.7 copy.41
  33.6 0.7 fusion.36
  34.8 0.7 gather_fusion
  35.4 0.7 fusion.37
  36.1 0.7 fusion.38
  36.9 0.7 fusion.35
  37.6 24.0 %compare_select_fusion.1 = (s32[1024]{0:T(1024)S(1)}, pred[1024]{0:T(1024)(128)(4,1)S(1)}, pred[1024]{0:T(1024)(128)(4,1)S(1)}, pred[1024]{0:T(1024)(128)(4,1)S(...) fusion(s32[]{:T(128)} %bitcast.41, s32[]{:T(128)} %bitcast.40, ...), kind=kLoop, calls=%fused_computation.41 | loop fusion | flops 105472 | bytes 18584 | tf_op jit(solution)/shard_map/select_n | solution.py:136
  61.6 6.4 %fusion.31 = f32[1024]{0:T(1024)S(1)} fusion(pred[1024]{0:T(1024)(128)(4,1)S(1)} %get-tuple-element.205, pred[1024]{0:T(1024)(128)(4,1)S(1)} %get-tuple-element.204, pred[1024]{0:T(1024)(128)(4,1)S(1)} %get-tuple-element.203, pred[1024]{0:T(1024)(128)(4,1)S(1)} %get-tuple-element.202, pred[1024]{0:T(1024)(128)(4,1)S(1)} %get-tuple-element.201, ...), kind=kLoop, calls=%fused_computation.58 | loop fusion | flops 12288 | bytes 14376 | tf_op jit(solution)/shard_map/convert_element_type | solution.py:19
  68.0 6.3 %select_select_fusion = s32[1024]{0:T(1024)S(1)} fusion(pred[1024]{0:T(1024)(128)(4,1)S(1)} %get-tuple-element.205, pred[1024]{0:T(1024)(128)(4,1)S(1)} %get-tuple-element.204, pred[1024]{0:T(1024)(128)(4,1)S(1)} %get-tuple-element.203, pred[1024]{0:T(1024)(128)(4,1)S(1)} %get-tuple-element.202, pred[1024]{0:T(1024)(128)(4,1)S(1)} %get-tuple-element.201, ...), kind=kLoop, calls=%fused_computation.52 | loop fusion | flops 10240 | bytes 14376 | tf_op jit(solution)/shard_map/jit(_take)/select_n | solution.py:126
  74.3 42.7 %all_gather.28 = bf16[32,16,512]{2,1,0:T(8,128)(2,1)S(1)} all-gather(bf16[1,16,512]{2,1,0:T(8,128)(2,1)S(1)} %copy-done.4), channel_id=1, replica_groups=mesh['row'=8,'col'=32] {'col'}, dimensions={0}, use_global_device_ids=true | all-gather | bytes 540672 | tf_op jit(solution)/shard_map/all_gather | solution.py:118
  117.1 43.2 %all_gather.31 = bf16[32,16,256]{2,1,0:T(8,128)(2,1)} all-gather(bf16[1,16,256]{2,1,0:T(8,128)(2,1)S(1)} %copy-done.5), channel_id=1, replica_groups=mesh['row'=8,'col'=32] {'col'}, dimensions={0}, use_global_device_ids=true | all-gather | bytes 270336 | tf_op jit(solution)/shard_map/all_gather | solution.py:119
  160.3 1.0 multiply_cosine_fusion
  161.3 6.1 %fusion.40 = f32[1024,256]{0,1:T(8,128)S(1)} fusion(bf16[1024,4608]{0,1:T(8,128)(2,1)} %all-gather.6.cloned.1.call-done, bf16[4608,256]{1,0:T(8,128)(2,1)} %all-gather.12.cloned.1.call-done), kind=kOutput, calls=%fused_computation.91 | convolution fusion | flops 2415919104 | bytes 12845056 | tf_op jit(solution)/shard_map/dot_general | solution.py:107
  167.8 12.7 %copy.51 = bf16[1024,4608]{1,0:T(8,128)(2,1)} copy(bf16[1024,4608]{0,1:T(8,128)(2,1)} %all-gather.6.cloned.1.call-done) | data formatting | bytes 18874368
  180.6 9.1 %concatenate.11.clone = bf16[1216,4608]{1,0:T(8,128)(2,1)} pad(bf16[1024,4608]{1,0:T(8,128)(2,1)} %copy.51, bf16[]{:T(256)} %constant.127.clone.1), padding=0_192x0_0 | pad | bytes 20643842 | tf_op jit(solution)/shard_map/concatenate | solution.py:70
  189.6 6.1 %scatter_custom_fusion = bf16[2304,256]{1,0:T(8,128)(2,1)} fusion(s32[1024]{0:T(1024)S(1)} %get-tuple-element.195, bf16[1024,256]{1,0:T(8,128)(2,1)S(1)} %copy.49, bf16[]{:T(256)} %constant.127.clone.1), kind=kCustom, calls=%fused_computation.23 | custom fusion | bytes 1179650 | tf_op jit(solution)/shard_map/scatter | solution.py:136
  195.7 34.8 %all-gather.8.cloned.1.call-done = bf16[4608,512]{1,0:T(8,128)(2,1)} async-done(((bf16[144,512]{1,0:T(8,128)(2,1)}), bf16[4608,512]{1,0:T(8,128)(2,1)}) %all-gather.8.cloned.1.call-update) | async-done | bytes 4718608 | tf_op jit(solution)/shard_map/all_gather | solution.py:104
  230.6 9.1 %fusion.39 = f32[1024,512]{0,1:T(8,128)S(1)} fusion(bf16[1024,4608]{0,1:T(8,128)(2,1)} %all-gather.6.cloned.1.call-done, bf16[4608,512]{1,0:T(8,128)(2,1)} %all-gather.8.cloned.1.call-done), kind=kOutput, calls=%fused_computation.90 | convolution fusion | flops 4831838208 | bytes 16252928 | tf_op jit(solution)/shard_map/dot_general | solution.py:102
  239.7 97.2 %all-gather.10.cloned.1.call-done = bf16[32,4608,32]{1,2,0:T(8,128)(2,1)} async-done(((bf16[1,4608,32]{1,2,0:T(8,128)(2,1)}), bf16[32,4608,32]{1,2,0:T(8,128)(2,1)}) %all-gather.10.cloned.1.call-update) | async-done | bytes 9437200 | tf_op jit(solution)/shard_map/all_gather | solution.py:123
  336.9 91.2 %while.14 = (s32[]{:T(128)}, f32[1216,32]{0,1:T(8,128)S(1)}, s32[10]{0:T(128)S(1)}, bf16[1216,4608]{1,0:T(8,128)(2,1)}, s32[10]{0:T(128)S(1)}, /*index=5*/bf16[3...) while((s32[]{:T(128)}, f32[1216,32]{0,1:T(8,128)S(1)}, ...), condition=%wide.region_3.5_spmd.clone, body=%wide.region_2.4_spmd.clone.sunk | while | flops 56635784 | bytes 2165981 | solution.py:83
  342.6 0.6 compare_convert_fusion.2
  343.2 2.2 fusion.52
  351.6 0.6 compare_convert_fusion.2
  352.2 2.2 fusion.52
  360.7 0.6 compare_convert_fusion.2
  361.3 2.2 fusion.52
  369.8 0.6 compare_convert_fusion.2
  370.5 2.2 fusion.52
  379.0 0.6 compare_convert_fusion.2
  379.6 2.2 fusion.52
  388.1 0.6 compare_convert_fusion.2
  388.7 2.2 fusion.52
  397.2 0.6 compare_convert_fusion.2
  397.9 2.2 fusion.52
  406.4 0.6 compare_convert_fusion.2
  407.0 2.2 fusion.52
  415.5 0.6 compare_convert_fusion.2
  416.2 2.2 fusion.52
  425.3 2.2 fusion.52
  428.1 0.8 bitcast_add_fusion
  429.4 1.3 copy.48
  431.3 7.0 %fusion.13 = bf16[1024,256]{1,0:T(8,128)(2,1)S(1)} fusion(f32[1024,256]{1,0:T(8,128)S(1)} %convolution_bitcast_fusion, bf16[1024,4608]{0,1:T(8,128)(2,1)} %all-gather.6.cloned.1.call-done, bf16[4608,256]{1,0:T(8,128)(2,1)} %all-gather.14.cloned.1.call-done), kind=kOutput, calls=%fused_computation.15 | convolution fusion | flops 2416443392 | bytes 13369344 | tf_op jit(solution)/shard_map/dot_general | solution.py:112
  438.3 6.1 %scatter_custom_fusion.1 = bf16[2304,256]{1,0:T(8,128)(2,1)} fusion(s32[1024]{0:T(1024)S(1)} %get-tuple-element.195, bf16[1024,256]{1,0:T(8,128)(2,1)S(1)} %fusion.13, bf16[]{:T(256)} %constant.127.clone.1), kind=kCustom, calls=%fused_computation.21 | custom fusion | bytes 1179650 | tf_op jit(solution)/shard_map/scatter | solution.py:142
  (86 shorter events, 26.8 us)
Async XLA Ops:
  7.2 27.6 %copy-start = (s32[32]{0:T(128)S(1)}, s32[32]{0:T(128)}, u32[]{:S(2)}) copy-start(s32[32]{0:T(128)} %param.24) | copy-start | bytes 388
  7.2 154.1 %all-gather.12.cloned.1.call-start = ((), (), s32[]{:S(2)}) async-start(), calls=%async_computation.3 | async-start | bytes 2433024 | tf_op jit(solution)/shard_map/all_gather | solution.py:109
  7.9 153.4 %all-gather.6.cloned.1.call-start = ((), (), s32[]{:S(2)}) async-start(), calls=%async_computation | async-start | bytes 10616832 | tf_op jit(solution)/shard_map/all_gather | solution.py:101
  8.7 221.9 %all-gather.8.cloned.1.call-start = ((), (), s32[]{:S(2)}) async-start(), calls=%async_computation.1 | async-start | bytes 4866048 | tf_op jit(solution)/shard_map/all_gather | solution.py:104
  9.4 327.5 %all-gather.10.cloned.1.call-start = ((), (), s32[]{:S(2)}) async-start(), calls=%async_computation.2 | async-start | bytes 9732096 | tf_op jit(solution)/shard_map/all_gather | solution.py:123
  10.4 23.2 %copy-start.3 = (s32[1,18]{1,0:T(1,128)S(1)}, s32[1,18]{1,0:T(1,128)}, u32[]{:S(2)}) copy-start(s32[1,18]{1,0:T(1,128)} %param.25) | copy-start | bytes 220
  10.4 23.9 %copy-start.7 = (s32[1,10]{1,0:T(1,128)S(1)}, s32[1,10]{1,0:T(1,128)}, u32[]{:S(2)}) copy-start(s32[1,10]{1,0:T(1,128)} %param.22) | copy-start | bytes 124
  10.4 24.1 %copy-start.6 = (s32[1,10]{1,0:T(1,128)S(1)}, s32[1,10]{1,0:T(1,128)}, u32[]{:S(2)}) copy-start(s32[1,10]{1,0:T(1,128)} %param.23) | copy-start | bytes 124
  29.3 45.1 %copy-start.4 = (bf16[1,16,512]{2,1,0:T(8,128)(2,1)S(1)}, bf16[1,16,512]{2,1,0:T(8,128)(2,1)}, u32[]{:S(2)}) copy-start(bf16[1,16,512]{2,1,0:T(8,128)(2,1)} %param.20) | copy-start | bytes 49156
  29.3 87.8 %copy-start.5 = (bf16[1,16,256]{2,1,0:T(8,128)(2,1)S(1)}, bf16[1,16,256]{2,1,0:T(8,128)(2,1)}, u32[]{:S(2)}) copy-start(bf16[1,16,256]{2,1,0:T(8,128)(2,1)} %param.21) | copy-start | bytes 24580
  33.0 398.3 %all-gather.14.cloned.1.call-start = ((), (), s32[]{:S(2)}) async-start(), calls=%async_computation.4 | async-start | bytes 2433024 | tf_op jit(solution)/shard_map/all_gather | solution.py:114
  429.3 1.4 copy-start.2
  431.3 13.1 %copy-start.1 = (s32[32]{0:T(128)S(1)}, s32[32]{0:T(128)}, u32[]{:S(2)}) copy-start(s32[32]{0:T(128)} %param.24) | copy-start | bytes 388
Sparse Core Ops, SparseCore 0:
  10.6 77.8 all-gather.11
  90.3 58.5 all-gather.5
  151.5 79.0 all-gather.7
  233.6 103.2 all-gather.9
  339.3 71.4 all-gather.13
where the time goes:
time: 453 us; the launch traced here: 451 us
  waiting for transfers between devices  135 us (30%)
  blocking collectives  105 us (23%)
  local copies, waits for them, and re-layouts  67.1 us (15%)
  matrix products  45.5 us (10%)
  other arithmetic  45.3 us (10%)
  loops' own time  39.3 us (9%)
  between operations  14 us (3%)
    all_gather x1, waiting for transfers between devices, shards(): down_all = lax.all_gather(rows_all, 'col', axis=0, tiled=True)  97.2 us
    all_gather x1, blocking collectives, shards(): lax.all_gather(adapter_up_value, 'col', axis=0, tiled=True)  43.2 us
    all_gather x1, blocking collectives, shards(): lax.all_gather(adapter_up_query, 'col', axis=0, tiled=True)  42.7 us
    another operation x1, loops' own time, project_down(): result = lax.fori_loop(0, starts.shape[0], one_request, result)  39.3 us
    all_gather x1, waiting for transfers between devices, shards(): lax.all_gather(w_query, 'col', axis=0, tiled=True)  34.8 us
    select_n x1, other arithmetic, shards(): key_cache = jnp.zeros((pages * PAGE, key_width), jnp.bfloat16).at[target]...  24 us
    dot_general x10, matrix products, one_request(): partial_sum = jnp.dot(window, factor, preferred_element_type=jnp.float32)  22 us
    all_gather x1, blocking collectives, shards(): rows_all = lax.all_gather(adapter_down, 'row', axis=1, tiled=True)  18.8 us
  transfers between devices with their start and end apart: 5, of which 2 were waited for; matrix products, arithmetic and copies ran while one was open for 32% of the time, Pallas kernels for 0%

commit v1 on v0

v1 whole, which is shorter than its diff:
```python
import math

import jax
import jax.numpy as jnp
from jax import lax
from jax.sharding import PartitionSpec as P

HEAD = 128
PAGE = 128
TOK_DEV = 1024


def rotate(values, cosine, sine_value):
    half_width = HEAD // 2
    shaped = values.reshape(values.shape[0], -1, HEAD)
    leading = shaped[:, :, :half_width]
    second = shaped[:, :, half_width:]
    rotated = jnp.concatenate(
        [leading * cosine - second * sine_value, second * cosine + leading * sine_value], axis=2
    )
    return rotated.reshape(values.shape)


def token_layout(lengths, chosen_request):
    token_index = jnp.arange(TOK_DEV, dtype=jnp.int32)
    starts = jnp.cumsum(lengths) - lengths
    inside = (token_index[:, None] >= starts[None, :]) & (
        token_index[:, None] < (starts + lengths)[None, :]
    )
    inside = inside.astype(jnp.int32)
    position = token_index - jnp.sum(inside * starts[None, :], axis=1)
    chosen = jnp.sum(inside * chosen_request[None, :], axis=1)
    return starts, position, chosen


def cache_rows(lengths, starts, page_row):
    pages = page_row.shape[0]
    pages_each = (lengths + PAGE - 1) // PAGE
    page_start = jnp.cumsum(pages_each) - pages_each
    page_ids = jnp.arange(pages, dtype=jnp.int32)
    owner = (page_row[:, None] == page_ids[None, :]).astype(jnp.int32)
    page_of_slot = jnp.sum(owner * page_ids[:, None], axis=0)
    member = (page_of_slot[:, None] >= page_start[None, :]) & (
        page_of_slot[:, None] < (page_start + pages_each)[None, :]
    )
    member = member.astype(jnp.int32)
    used = jnp.sum(member, axis=1) > 0
    first_page = jnp.sum(member * page_start[None, :], axis=1)
    first_token = jnp.sum(member * starts[None, :], axis=1)
    length = jnp.sum(member * lengths[None, :], axis=1)
    offset = (page_of_slot - first_page) * PAGE
    source = first_token + offset
    valid = jnp.where(used, jnp.minimum(length - offset, PAGE), 0)
    inner = jnp.arange(PAGE, dtype=jnp.int32)
    rows = (source[:, None] + inner[None, :]).reshape(-1)
    keep = (inner[None, :] < valid[:, None]).reshape(-1)
    rows = jnp.clip(rows, 0, TOK_DEV - 1)
    return rows, keep


def shards(
    hidden,
    w_query,
    w_key,
    w_value,
    adapter_down,
    adapter_up_query,
    adapter_up_value,
    lengths,
    request_adapter,
    adapter_slot,
    page_table,
):
    lengths = lengths[0]
    chosen_request = jnp.take(adapter_slot, request_adapter[0])
    starts, position, chosen = token_layout(lengths, chosen_request)
    adapter_count = adapter_slot.shape[0]
    rank_width = adapter_up_query.shape[1]
    query_width = w_query.shape[1]
    key_width = w_key.shape[1]

    weight_width = query_width + 2 * key_width
    feature_rows = w_query.shape[0]
    down_shape = adapter_down.shape[1:]
    row_size = lax.axis_size("row")

    with jax.named_scope("gathers"):
        full_rows = lax.all_gather(hidden, "row", axis=1, tiled=True)
        pieces = [
            jnp.concatenate([w_query, w_key, w_value], axis=1),
            adapter_down.reshape(-1, weight_width),
            adapter_up_query.reshape(-1, weight_width),
            adapter_up_value.reshape(-1, weight_width),
        ]
        bounds = [0]
        for piece in pieces:
            bounds.append(bounds[-1] + piece.shape[0])
        packed = lax.all_gather(jnp.concatenate(pieces, axis=0), "col", axis=0)
        weights = packed[:, : bounds[1]].reshape(-1, weight_width)
        down_local = packed[:, bounds[1] : bounds[2]].reshape((adapter_count,) + down_shape)
        up_query = packed[:, bounds[2] : bounds[3]].reshape(adapter_count, rank_width, -1)
        up_value = packed[:, bounds[3] : bounds[4]].reshape(adapter_count, rank_width, -1)

    with jax.named_scope("lowrank"):
        onehot = (chosen[:, None] == jnp.arange(adapter_count, dtype=jnp.int32)[None, :])
        partial_all = jnp.einsum(
            "tf,sfr->tsr", hidden, down_local, preferred_element_type=jnp.float32
        )
        partial = jnp.sum(jnp.where(onehot[:, :, None], partial_all, 0.0), axis=1)
        distance = 1
        while distance < row_size:
            pairs = [(i, i ^ distance) for i in range(row_size)]
            partial = partial + lax.ppermute(partial, "row", pairs)
            distance *= 2
        lowrank = partial.astype(jnp.bfloat16)
        onehot_b = onehot.astype(jnp.bfloat16)
        spread_query = (onehot_b[:, :, None] * lowrank[:, None, :rank_width]).reshape(
            -1, adapter_count * rank_width
        )
        spread_value = (onehot_b[:, :, None] * lowrank[:, None, rank_width:]).reshape(
            -1, adapter_count * rank_width
        )
        delta_query = jnp.dot(
            spread_query,
            up_query.reshape(adapter_count * rank_width, -1),
            preferred_element_type=jnp.float32,
        )
        delta_value = jnp.dot(
            spread_value,
            up_value.reshape(adapter_count * rank_width, -1),
            preferred_element_type=jnp.float32,
        )

    with jax.named_scope("projection"):
        base = jnp.dot(full_rows, weights, preferred_element_type=jnp.float32)
        base_query = base[:, :query_width]
        base_key = base[:, query_width : query_width + key_width]
        base_value = base[:, query_width + key_width :]

    with jax.named_scope("rotary"):
        half_width = HEAD // 2
        frequency = jnp.exp(
            jnp.arange(half_width, dtype=jnp.float32) * (-2.0 * math.log(10000.0) / HEAD)
        )
        angles = position.astype(jnp.float32)[:, None] * frequency[None, :]
        cosine = jnp.cos(angles)[:, None, :]
        sine_value = jnp.sin(angles)[:, None, :]
        query = rotate(base_query + delta_query, cosine, sine_value).astype(jnp.bfloat16)
        key_rotated = rotate(base_key, cosine, sine_value).astype(jnp.bfloat16)
        value_rows = (base_value + delta_value).astype(jnp.bfloat16)

    with jax.named_scope("cache_write"):
        pages = page_table.shape[1]
        rows, keep = cache_rows(lengths, starts, page_table[0])
        key_cache = jnp.where(keep[:, None], jnp.take(key_rotated, rows, axis=0), 0).reshape(
            pages, PAGE, key_width
        )
        value_cache = jnp.where(keep[:, None], jnp.take(value_rows, rows, axis=0), 0).reshape(
            pages, PAGE, key_width
        )
    return (query, key_cache.astype(jnp.bfloat16), value_cache.astype(jnp.bfloat16))


def solution(mesh):
    return jax.shard_map(
        shards,
        mesh=mesh,
        in_specs=(
            P("col", "row"),
            P("col", "row"),
            P("col", "row"),
            P("col", "row"),
            P("col", "row", None),
            P("col", None, "row"),
            P("col", None, "row"),
            P("col", None),
            P("col", None),
            P(),
            P("col", None),
        ),
        out_specs=(P("col", "row"), P("col", None, "row"), P("col", None, "row")),
        check_vma=False,
    )
```

time: 453 us -> 241 us (0.53)
  blocking collectives: 105 us -> 0 us
  loops' own time: 39.3 us -> 0 us
  other arithmetic: 45.3 us -> 10 us
  local copies, waits for them, and re-layouts: 67.1 us -> 38.3 us
  matrix products: 45.5 us -> 25.3 us
  waiting for transfers between devices: 135 us -> 147 us
  starting transfers between devices: 0.19 us -> 5.83 us
    all_gather x3 -> x0, blocking collectives: 105 us -> none  [the longest x1 43.2 us: shards(): lax.all_gather(adapter_up_value, 'col', axis=0, tiled=True)]
    another operation x1 -> x0, loops' own time: 39.3 us -> none  [project_down(): result = lax.fori_loop(0, starts.shape[0], one_request, result)]
    all_gather x1, waiting for transfers between devices: 0.02 us -> 33.7 us  [shards(): full_rows = lax.all_gather(hidden, 'row', axis=1, tiled=True)]
    select_n x3 -> x4, other arithmetic: 30.3 us -> 2.97 us  [the longest x1 2.87 us: shards(): jnp.where(keep[:, None], jnp.take(value_rows, rows, axis=0), 0)]
    dot_general x15 -> x4, matrix products: 45.5 us -> 25.3 us  [the longest x1 14.7 us: shards(): base = jnp.dot(full_rows, weights, preferred_element_type=jnp.float32)]
    all_gather x4 -> x1, waiting for transfers between devices: 132 us -> 112 us  [shards(): packed = lax.all_gather(jnp.concatenate(pieces, axis=0), 'col', axis=0)]
    dynamic_slice x30 -> x0, local copies, waits for them, and re-layouts: 17.6 us -> none  [the longest x10 5.89 us: one_request(): chosen_request[number]]
    unnamed x18 -> x23, local copies, waits for them, and re-layouts: 13.7 us -> 0.97 us
  transfers between devices with their start and end apart: 5 -> 5, of which waited for: 2 -> 2; matrix products, arithmetic and copies ran while one was open for 32% -> 20% of each run, Pallas kernels for 0% -> 0%
where the time goes in v1:
time: 241 us; the launch traced here: 240 us
  waiting for transfers between devices  147 us (61%)
  local copies, waits for them, and re-layouts  38.3 us (16%)
  matrix products  25.3 us (10%)
  between operations  14.4 us (6%)
  other arithmetic  10 us (4%)
  starting transfers between devices  5.83 us (2%)
    all_gather x1, waiting for transfers between devices, shards(): packed = lax.all_gather(jnp.concatenate(pieces, axis=0), 'col', axis=0)  112 us
    all_gather x1, waiting for transfers between devices, shards(): full_rows = lax.all_gather(hidden, 'row', axis=1, tiled=True)  33.7 us
    dot_general x1, matrix products, shards(): base = jnp.dot(full_rows, weights, preferred_element_type=jnp.float32)  14.7 us
    slice x1, local copies, waits for them, and re-layouts, shards(): weights = packed[:, :bounds[1]].reshape(-1, weight_width)  9.52 us
    gather x1, local copies, waits for them, and re-layouts, shards(): jnp.take(key_rotated, rows, axis=0)  6.86 us
    gather x1, local copies, waits for them, and re-layouts, shards(): jnp.take(value_rows, rows, axis=0)  6.86 us
    ppermute x3, starting transfers between devices, shards(): partial = partial + lax.ppermute(partial, 'row', pairs)  5.75 us
    dot_general x1, matrix products, shards(): jnp.einsum('tf,sfr->tsr', hidden, down_local, preferred_element_type=jnp....  5.55 us
  transfers between devices with their start and end apart: 5, of which 2 were waited for; matrix products, arithmetic and copies ran while one was open for 20% of the time, Pallas kernels for 0%

profile of v1, /device:TPU:1, one launch (start us, length us, event | category | flops | bytes accessed | tf_op | source)
XLA Modules:
  0.0 240.4 jit_solution(12034622873768710716)
XLA Ops:
  7.2 0.0 copy-start
  7.2 0.0 all-gather.7.cloned.1.call-start
  7.3 0.7 reshape.325
  8.0 0.7 reshape.324
  8.7 0.9 copy.31
  9.6 0.2 reshape.323
  9.8 1.8 maximum_bitcast_fusion
  11.6 0.0 all-gather.7.cloned.1.call-update
  11.6 0.0 all-gather.5.cloned.1.call-start
  11.7 0.7 all-gather.5.cloned.1.call-update
  12.4 0.2 reduce-window.6
  12.6 0.2 reduce-window.9
  12.8 0.7 gather_fusion
  13.5 0.1 select_reduce_fusion.2
  13.6 0.1 select_reduce_fusion
  13.7 0.1 select_reduce_fusion.5
  13.8 0.7 compare_and_fusion
  14.4 0.1 compare_select_fusion
  14.5 0.7 fusion.10
  15.2 1.0 multiply_cosine_fusion
  16.2 112.1 %all-gather.7.cloned.1.call-done = bf16[32,174,1024]{2,1,0:T(8,128)(2,1)} async-done(((bf16[1,174,1024]{2,1,0:T(8,128)(2,1)}), bf16[32,174,1024]{2,1,0:T(8,128)(2,1)}) %all-gather.7.cloned.1.call-update) | async-done | bytes 11403280 | tf_op jit(solution)/shard_map/gathers/all_gather | solution.py:98
  128.3 1.4 slice-done.3
  129.7 4.8 %reshape.328 = bf16[32,576,32]{2,1,0:T(8,128)(2,1)} reshape(bf16[32,18,1024]{2,1,0:T(8,128)(2,1)S(1)} %slice-done.3) | data formatting | bytes 2359296 | tf_op jit(solution)/shard_map/gathers/reshape | solution.py:100
  134.6 5.6 %fusion = f32[1024,32]{0,1:T(8,128)S(1)} fusion(bf16[32,576,32]{2,1,0:T(8,128)(2,1)} %reshape.328, pred[1024,32]{0,1:T(8,128)(4,1)S(1)} %get-tuple-element.23, bf16[1024,576]{0,1:T(8,128)(2,1)S(1)} %copy-done.2), kind=kOutput, calls=%fused_computation.4 | convolution fusion | flops 1210023936 | bytes 2523136 | tf_op jit(solution)/shard_map/lowrank/tf,sfr->tsr/dot_general | solution.py:106
  140.1 1.5 collective-permute-start
  141.6 0.6 fusion.4
  142.3 9.5 %slice.58 = bf16[32,144,1024]{2,1,0:T(8,128)(2,1)} slice(bf16[32,174,1024]{2,1,0:T(8,128)(2,1)} %all-gather.7.cloned.1.call-done), slice={[0:32], [0:144], [0:1024]} | slice | bytes 18874368 | tf_op jit(solution)/shard_map/gathers/slice | solution.py:99
  151.8 1.6 collective-permute-start.1
  153.4 33.7 %all-gather.5.cloned.1.call-done = bf16[1024,4608]{0,1:T(8,128)(2,1)} async-done(((bf16[1024,576]{0,1:T(8,128)(2,1)}), bf16[1024,4608]{0,1:T(8,128)(2,1)}) %all-gather.5.cloned.1.call-update) | async-done | bytes 9437200 | tf_op jit(solution)/shard_map/gathers/all_gather | solution.py:88
  187.1 14.7 %convolution_bitcast_fusion = f32[1024,1024]{0,1:T(8,128)S(1)} fusion(bf16[4608,1024]{1,0:T(8,128)(2,1)} %bitcast.63, bf16[1024,4608]{0,1:T(8,128)(2,1)} %all-gather.5.cloned.1.call-done), kind=kOutput, calls=%fused_computation.5 | convolution fusion | flops 9663676416 | bytes 23068672 | tf_op jit(solution)/shard_map/projection/dot_general | solution.py:135
  201.8 0.1 slice.65
  201.9 2.7 %collective-permute-start.2 = (f32[1024,32]{0,1:T(8,128)S(1)}, f32[1024,32]{0,1:T(8,128)S(1)}, u32[]{:S(2)}, u32[]{:S(2)}) collective-permute-start(f32[1024,32]{0,1:T(8,128)S(1)} %add.98), channel_id=1, source_target_pairs={{0,128},{32,160},{64,192},{96,224},{128,0},{160,32},{192,64},{224,... | collective-permute-start | bytes 393224 | tf_op jit(solution)/shard_map/lowrank/ppermute | solution.py:113
  204.6 0.2 subtract_convert_fusion.1
  204.8 0.1 slice.70
  205.0 0.2 reshape.333
  205.2 1.4 slice.62
  206.6 1.0 reshape.329
  207.6 0.2 copy.40
  207.8 6.9 %gather_fusion.1 = bf16[2304,256]{1,0:T(8,128)(2,1)S(1)} fusion(bf16[1024,256]{1,0:T(8,128)(2,1)S(1)} %copy.40, s32[3072]{0:T(1024)S(1)} %pad_clamp_fusion), kind=kCustom, calls=%fused_computation.clone | custom fusion | bytes 2368512 | tf_op jit(solution)/shard_map/cache_write/jit(_take)/gather | solution.py:155
  214.7 1.0 broadcast_multiply_fusion
  215.7 2.5 %fusion.1 = bf16[1024,256]{0,1:T(8,128)(2,1)} fusion(bf16[1024,512]{0,1:T(8,128)(2,1)S(1)} %bitcast.68, bf16[512,256]{1,0:T(8,128)(2,1)S(1)} %reshape.333, f32[1024,1024]{0,1:T(8,128)} %copy-done.1), kind=kOutput, calls=%fused_computation.8 | convolution fusion | flops 268959744 | bytes 2883584 | tf_op jit(solution)/shard_map/lowrank/dot_general | solution.py:128
  218.2 1.2 copy.36
  219.5 2.5 %slice_add_fusion = f32[1024,512]{0,1:T(8,128)S(1)} fusion(f32[1024,1024]{0,1:T(8,128)} %copy-done.1, bf16[1024,512]{0,1:T(8,128)(2,1)S(1)} %bitcast.67, bf16[512,512]{1,0:T(8,128)(2,1)} %reshape.329), kind=kOutput, calls=%fused_computation.6 | convolution fusion | flops 537395200 | bytes 5767168 | tf_op jit(solution)/shard_map/lowrank/dot_general | solution.py:123
  222.0 0.3 subtract_convert_fusion
  222.4 0.1 pad_maximum_fusion
  222.5 1.3 copy.39
  223.8 6.9 %gather_fusion.2 = bf16[2304,256]{1,0:T(8,128)(2,1)S(1)} fusion(bf16[1024,256]{1,0:T(8,128)(2,1)S(1)} %copy.36, s32[3072]{0:T(1024)S(1)} %pad_clamp_fusion), kind=kCustom, calls=%fused_computation.1.clone | custom fusion | bytes 2368512 | tf_op jit(solution)/shard_map/cache_write/jit(_take)/gather | solution.py:158
  230.7 2.9 %select_select_fusion = (bf16[2304,256]{1,0:T(8,128)(2,1)}, bf16[2304,256]{1,0:T(8,128)(2,1)}) fusion(bf16[2304,256]{1,0:T(8,128)(2,1)S(1)} %gather_fusion.2, pred[2304]{0:T(1024)(128)(4,1)S(1)} %copy-done.3, pred[2304]{0:T(1024)(128)(4,1)S(1)} %copy-done.4, bf16[2304,256]{1,0:T(8,128)(2,1)S(1)} %gather_fusion.1), kind=kLoop, calls=%fused_computation.10 | loop fusion | flops 2359296 | bytes 4723200 | tf_op jit(solution)/shard_map/cache_write/jit(_where)/select_n | solution.py:158
  (39 shorter events, 0.2 us)
Async XLA Ops:
  7.2 5.6 %copy-start = (s32[32]{0:T(128)S(1)}, s32[32]{0:T(128)}, u32[]{:S(2)}) copy-start(s32[32]{0:T(128)} %param.22) | copy-start | bytes 388
  7.2 5.2 %copy-start.5 = (s32[1,10]{1,0:T(1,128)S(1)}, s32[1,10]{1,0:T(1,128)}, u32[]{:S(2)}) copy-start(s32[1,10]{1,0:T(1,128)} %param.20) | copy-start | bytes 124
  7.2 5.6 %copy-start.6 = (s32[1,10]{1,0:T(1,128)S(1)}, s32[1,10]{1,0:T(1,128)}, u32[]{:S(2)}) copy-start(s32[1,10]{1,0:T(1,128)} %param.21) | copy-start | bytes 124
  7.2 6.2 %copy-start.7 = (s32[1,18]{1,0:T(1,128)S(1)}, s32[1,18]{1,0:T(1,128)}, u32[]{:S(2)}) copy-start(s32[1,18]{1,0:T(1,128)} %param.23) | copy-start | bytes 220
  7.2 121.1 %all-gather.7.cloned.1.call-start = ((), (), s32[]{:S(2)}) async-start(), calls=%async_computation.1 | async-start | bytes 11894784 | tf_op jit(solution)/shard_map/gathers/all_gather | solution.py:98
  11.6 175.5 %all-gather.5.cloned.1.call-start = ((), (), s32[]{:S(2)}) async-start(), calls=%async_computation | async-start | bytes 10616832 | tf_op jit(solution)/shard_map/gathers/all_gather | solution.py:88
  128.3 1.4 slice-start.3
  129.7 4.9 %copy-start.2 = (bf16[1024,576]{0,1:T(8,128)(2,1)S(1)}, bf16[1024,576]{0,1:T(8,128)(2,1)}, u32[]{:S(2)}) copy-start(bf16[1024,576]{0,1:T(8,128)(2,1)} %param.13) | copy-start | bytes 3538948
  140.1 11.7 %collective-permute-start = (f32[1024,32]{0,1:T(8,128)S(1)}, f32[1024,32]{0,1:T(8,128)S(1)}, u32[]{:S(2)}, u32[]{:S(2)}) collective-permute-start(f32[1024,32]{0,1:T(8,128)S(1)} %fusion), channel_id=1, source_target_pairs={{0,32},{32,0},{64,96},{96,64},{128,160},{160,128},{192,224},{224,1... | collective-permute-start | bytes 393224 | tf_op jit(solution)/shard_map/lowrank/ppermute | solution.py:113
  151.8 50.1 %collective-permute-start.1 = (f32[1024,32]{0,1:T(8,128)S(1)}, f32[1024,32]{0,1:T(8,128)S(1)}, u32[]{:S(2)}, u32[]{:S(2)}) collective-permute-start(f32[1024,32]{0,1:T(8,128)S(1)} %add.97), channel_id=1, source_target_pairs={{0,64},{32,96},{64,0},{96,32},{128,192},{160,224},{192,128},{224,1... | collective-permute-start | bytes 393224 | tf_op jit(solution)/shard_map/lowrank/ppermute | solution.py:113
  187.1 17.7 %slice-start = ((s8[11534336]{0:T(1024)(128)(4,1)}), s8[4194304]{0:T(1024)(128)(4,1)S(1)}, s32[]{:S(2)}) async-start(s8[11534336]{0:T(1024)(128)(4,1)} %bitcast.61), calls=%async_computation.2 | async-start | bytes 8388608
  187.1 17.7 %slice-start.1 = ((s8[11534336]{0:T(1024)(128)(4,1)}), s8[4194304]{0:T(1024)(128)(4,1)S(1)}, s32[]{:S(2)}) async-start(s8[11534336]{0:T(1024)(128)(4,1)} %bitcast.61), calls=%async_computation.3 | async-start | bytes 8388608
  187.1 17.8 %slice-start.2 = ((s8[11534336]{0:T(1024)(128)(4,1)}), s8[3145728]{0:T(1024)(128)(4,1)S(1)}, s32[]{:S(2)}) async-start(s8[11534336]{0:T(1024)(128)(4,1)} %bitcast.61), calls=%async_computation.4 | async-start | bytes 6291456
  201.8 3.0 %copy-start.1 = (f32[1024,1024]{0,1:T(8,128)}, f32[1024,1024]{0,1:T(8,128)S(1)}, u32[]{:S(2)}) copy-start(f32[1024,1024]{0,1:T(8,128)S(1)} %convolution_bitcast_fusion) | copy-start | bytes 12582916
  201.9 12.8 %collective-permute-start.2 = (f32[1024,32]{0,1:T(8,128)S(1)}, f32[1024,32]{0,1:T(8,128)S(1)}, u32[]{:S(2)}, u32[]{:S(2)}) collective-permute-start(f32[1024,32]{0,1:T(8,128)S(1)} %add.98), channel_id=1, source_target_pairs={{0,128},{32,160},{64,192},{96,224},{128,0},{160,32},{192,64},{224,... | collective-permute-start | bytes 393224 | tf_op jit(solution)/shard_map/lowrank/ppermute | solution.py:113
  223.8 6.9 %copy-start.3 = (pred[2304]{0:T(1024)(128)(4,1)S(1)}, pred[2304]{0:T(1024)(128)(4,1)}, u32[]{:S(2)}) copy-start(pred[2304]{0:T(1024)(128)(4,1)} %compare_and_fusion) | copy-start | bytes 6916
  223.8 6.9 %copy-start.4 = (pred[2304]{0:T(1024)(128)(4,1)S(1)}, pred[2304]{0:T(1024)(128)(4,1)}, u32[]{:S(2)}) copy-start(pred[2304]{0:T(1024)(128)(4,1)} %fusion.4) | copy-start | bytes 6916
Sparse Core Ops, SparseCore 0:
  11.7 116.5 all-gather.6
  130.1 56.9 all-gather.4

commit v2 on v1

--- a/solution.py
+++ b/solution.py
@@ -56,6 +56,41 @@
     keep = (inner[None, :] < valid[:, None]).reshape(-1)
     rows = jnp.clip(rows, 0, TOK_DEV - 1)
     return rows, keep
+
+
+def gather_rows(hidden, row_size):
+    chips = row_size // 2
+    assert chips == 4
+    tokens, width = hidden.shape
+    index = lax.axis_index("row")
+    core = index % 2
+    chip = index // 2
+    step = 2 * core - 1
+    swap = [(i, i ^ 1) for i in range(row_size)]
+    ring = [
+        (i, ((i // 2 + 1) % chips) * 2 if i % 2 == 0 else ((i // 2 - 1) % chips) * 2 + 1)
+        for i in range(row_size)
+    ]
+    partner = lax.ppermute(hidden, "row", swap)
+    own_block = jnp.where(
+        core == 0,
+        jnp.concatenate([hidden, partner], axis=1),
+        jnp.concatenate([partner, hidden], axis=1),
+    )
+    near = lax.ppermute(own_block, "row", ring)
+    half = tokens // 2
+    forwarded = lax.dynamic_slice_in_dim(near, core * half, half, 0)
+    far_half = lax.ppermute(forwarded, "row", ring)
+    from_partner, far_other = lax.ppermute((near, far_half), "row", swap)
+    block = 2 * width
+    full = jnp.zeros((tokens, chips * block), hidden.dtype)
+    full = lax.dynamic_update_slice(full, own_block, (0, chip * block))
+    full = lax.dynamic_update_slice(full, near, (0, ((chip + step) % chips) * block))
+    full = lax.dynamic_update_slice(full, from_partner, (0, ((chip - step) % chips) * block))
+    far = ((chip + 2) % chips) * block
+    full = lax.dynamic_update_slice(full, far_half, (core * half, far))
+    full = lax.dynamic_update_slice(full, far_other, ((1 - core) * half, far))
+    return full
 
 
 def shards(
@@ -85,7 +120,7 @@
     row_size = lax.axis_size("row")
 
     with jax.named_scope("gathers"):
-        full_rows = lax.all_gather(hidden, "row", axis=1, tiled=True)
+        full_rows = gather_rows(hidden, row_size)
         pieces = [
             jnp.concatenate([w_query, w_key, w_value], axis=1),
             adapter_down.reshape(-1, weight_width),
@@ -152,12 +187,16 @@
     with jax.named_scope("cache_write"):
         pages = page_table.shape[1]
         rows, keep = cache_rows(lengths, starts, page_table[0])
-        key_cache = jnp.where(keep[:, None], jnp.take(key_rotated, rows, axis=0), 0).reshape(
-            pages, PAGE, key_width
-        )
-        value_cache = jnp.where(keep[:, None], jnp.take(value_rows, rows, axis=0), 0).reshape(
-            pages, PAGE, key_width
-        )
+        select = (
+            (rows[:, None] == jnp.arange(TOK_DEV, dtype=jnp.int32)[None, :]) & keep[:, None]
+        ).astype(jnp.bfloat16)
+        both = jnp.dot(
+            select,
+            jnp.concatenate([key_rotated, value_rows], axis=1),
+            preferred_element_type=jnp.float32,
+        ).astype(jnp.bfloat16)
+        key_cache = both[:, :key_width].reshape(pages, PAGE, key_width)
+        value_cache = both[:, key_width:].reshape(pages, PAGE, key_width)
     return (query, key_cache.astype(jnp.bfloat16), value_cache.astype(jnp.bfloat16))
 
 

time: 241 us -> 227 us (0.942)
  waiting for transfers between devices: 147 us -> 95.4 us
  local copies, waits for them, and re-layouts: 38.3 us -> 63.8 us
  starting transfers between devices: 5.83 us -> 14.1 us
    all_gather x1, waiting for transfers between devices: 112 us -> 54 us  [shards(): packed = lax.all_gather(jnp.concatenate(pieces, axis=0), 'col', axis=0)]
    ppermute x0 -> x5, waiting for transfers between devices: none -> 41.3 us  [the longest x1 25.7 us: gather_rows(): near = lax.ppermute(own_block, 'row', ring)]
    all_gather x1 -> x0, waiting for transfers between devices: 33.7 us -> none  [shards(): full_rows = lax.all_gather(hidden, 'row', axis=1, tiled=True)]
    dynamic_update_slice x0 -> x4, local copies, waits for them, and re-layouts: none -> 31.1 us  [the longest x1 12.9 us: gather_rows(): full = lax.dynamic_update_slice(full, far_other, ((1 - core) * half, far))]
    gather x2 -> x0, local copies, waits for them, and re-layouts: 13.7 us -> none  [the longest x1 6.86 us: shards(): jnp.take(key_rotated, rows, axis=0)]
    ppermute x0 -> x5, starting transfers between devices: none -> 8.78 us  [the longest x2 4.41 us: gather_rows(): from_partner, far_other = lax.ppermute((near, far_half), 'row', swap)]
    broadcast_in_dim x0 -> x1, local copies, waits for them, and re-layouts: none -> 4.86 us  [gather_rows(): full = jnp.zeros((tokens, chips * block), hidden.dtype)]
    dot_general x0 -> x1, matrix products: none -> 3.55 us  [shards(): jnp.dot(select, jnp.concatenate([key_rotated, value_rows], axis=1), prefe...]
  transfers between devices with their start and end apart: 5 -> 9, of which waited for: 2 -> 4; matrix products, arithmetic and copies ran while one was open for 20% -> 36% of each run, Pallas kernels for 0% -> 0%
where the time goes in v2:
time: 227 us; the launch traced here: 226 us
  waiting for transfers between devices  95.4 us (42%)
  local copies, waits for them, and re-layouts  63.8 us (28%)
  matrix products  27.3 us (12%)
  between operations  14.3 us (6%)
  starting transfers between devices  14.1 us (6%)
  other arithmetic  10.8 us (5%)
    all_gather x1, waiting for transfers between devices, shards(): packed = lax.all_gather(jnp.concatenate(pieces, axis=0), 'col', axis=0)  54 us
    ppermute x1, waiting for transfers between devices, gather_rows(): near = lax.ppermute(own_block, 'row', ring)  25.7 us
    dot_general x1, matrix products, shards(): base = jnp.dot(full_rows, weights, preferred_element_type=jnp.float32)  16 us
    ppermute x1, waiting for transfers between devices, gather_rows(): far_half = lax.ppermute(forwarded, 'row', ring)  12.9 us
    dynamic_update_slice x1, local copies, waits for them, and re-layouts, gather_rows(): full = lax.dynamic_update_slice(full, far_other, ((1 - core) * half, far))  12.9 us
    dynamic_update_slice x1, local copies, waits for them, and re-layouts, gather_rows(): full = lax.dynamic_update_slice(full, far_half, (core * half, far))  11.5 us
    slice x1, local copies, waits for them, and re-layouts, shards(): weights = packed[:, :bounds[1]].reshape(-1, weight_width)  9.15 us
    ppermute x3, starting transfers between devices, shards(): partial = partial + lax.ppermute(partial, 'row', pairs)  5.31 us
  transfers between devices with their start and end apart: 9, of which 4 were waited for; matrix products, arithmetic and copies ran while one was open for 36% of the time, Pallas kernels for 0%

profile of v2, /device:TPU:1, one launch (start us, length us, event | category | flops | bytes accessed | tf_op | source)
XLA Modules:
  0.0 225.7 jit_solution(17107422098513248465)
XLA Ops:
  7.2 0.9 copy.22
  8.1 0.2 reshape.327
  8.3 0.7 reshape.328
  9.1 0.7 reshape.329
  9.8 1.8 maximum_bitcast_fusion
  11.6 3.3 %collective-permute-start = (bf16[1024,576]{0,1:T(8,128)(2,1)}, bf16[1024,576]{0,1:T(8,128)(2,1)S(1)}, u32[]{:S(2)}, u32[]{:S(2)}) collective-permute-start(bf16[1024,576]{0,1:T(8,128)(2,1)} %param.11), channel_id=1, source_target_pairs={{0,32},{32,0},{64,96},{96,64},{128,160},{160,128},{192,224},{224,1... | collective-permute-start | bytes 3538952 | tf_op jit(solution)/shard_map/gathers/ppermute | solution.py:74
  14.9 2.7 %collective-permute-done = bf16[1024,576]{0,1:T(8,128)(2,1)S(1)} collective-permute-done((bf16[1024,576]{0,1:T(8,128)(2,1)}, bf16[1024,576]{0,1:T(8,128)(2,1)S(1)}, u32[]{:S(2)}, u32[]{:S(2)}) %collective-permute-start) | collective-permute-done | bytes 1179680 | tf_op jit(solution)/shard_map/gathers/ppermute | solution.py:74
  17.5 4.9 %broadcast_in_dim.13 = bf16[1024,4608]{0,1:T(8,128)(2,1)} broadcast(bf16[]{:T(256)} %constant.91.clone.1), dimensions={} | broadcast | bytes 9437186 | tf_op jit(solution)/shard_map/gathers/broadcast_in_dim | solution.py:86
  22.4 2.4 %constant_dynamic-update-slice_fusion.2 = (bf16[1024,4608]{0,1:T(8,128)(2,1)}, bf16[1024,1152]{0,1:T(8,128)(2,1)S(1)}) fusion(bf16[1024,4608]{0,1:T(8,128)(2,1)} %broadcast_in_dim.13, s32[]{:T(128)S(6)} %select_n.103, bf16[1024,576]{0,1:T(8,128)(2,1)S(1)} %copy-done.4, bf16[1024,576]{0,1:T(8,128)(2,1)S(1)} %collective-permute-done, pred[]{:T(512)S(6)} %eq.56), kind=kLoop, calls=%fused_computation.62 | loop fusion | flops 10616832 | bytes 7077893 | tf_op jit(solution)/shard_map/gathers/dynamic_update_slice | solution.py:87
  24.8 1.0 collective-permute-start.1
  25.9 0.2 reduce-window.9
  26.0 0.2 reduce-window.6
  26.3 0.7 gather_fusion
  27.2 25.7 %collective-permute-done.1 = bf16[1024,1152]{0,1:T(8,128)(2,1)} collective-permute-done((bf16[1024,1152]{0,1:T(8,128)(2,1)S(1)}, bf16[1024,1152]{0,1:T(8,128)(2,1)}, u32[]{:S(2)}, u32[]{:S(2)}) %collective-permute-start.1) | collective-permute-done | bytes 2359328 | tf_op jit(solution)/shard_map/gathers/ppermute | solution.py:80
  52.9 2.4 %collective-permute-start.2 = (bf16[1024,1152]{0,1:T(8,128)(2,1)}, bf16[1024,1152]{0,1:T(8,128)(2,1)}, u32[]{:S(2)}, u32[]{:S(2)}) collective-permute-start(bf16[1024,1152]{0,1:T(8,128)(2,1)} %collective-permute-done.1), channel_id=1, source_target_pairs={{0,32},{32,0},{64,96},{96,64},{128,160},{160,128},{192,224},{224,1... | collective-permute-start | bytes 7077896 | tf_op jit(solution)/shard_map/gathers/ppermute | solution.py:84
  55.4 1.3 constant_dynamic-slice_fusion
  56.9 0.6 fusion.22
  57.6 1.7 multiply_cosine_fusion
  59.3 12.9 %collective-permute-done.3 = bf16[512,1152]{0,1:T(8,128)(2,1)S(1)} collective-permute-done((bf16[512,1152]{0,1:T(8,128)(2,1)S(1)}, bf16[512,1152]{0,1:T(8,128)(2,1)S(1)}, u32[]{:S(2)}, u32[]{:S(2)}) %collective-permute-start.3) | collective-permute-done | bytes 1179680 | tf_op jit(solution)/shard_map/gathers/ppermute | solution.py:83
  72.3 2.0 collective-permute-start.4
  74.3 54.0 %all-gather.4.cloned.1.call-done = bf16[32,174,1024]{2,1,0:T(8,128)(2,1)} async-done(((bf16[1,174,1024]{2,1,0:T(8,128)(2,1)}), bf16[32,174,1024]{2,1,0:T(8,128)(2,1)}) %all-gather.4.cloned.1.call-update) | async-done | bytes 11403280 | tf_op jit(solution)/shard_map/gathers/all_gather | solution.py:133
  128.3 1.4 slice-done.3
  129.7 4.8 %reshape.332 = bf16[32,576,32]{2,1,0:T(8,128)(2,1)} reshape(bf16[32,18,1024]{2,1,0:T(8,128)(2,1)S(1)} %slice-done.3) | data formatting | bytes 2359296 | tf_op jit(solution)/shard_map/gathers/reshape | solution.py:135
  134.5 4.8 %fusion.8 = f32[1024,32]{0,1:T(8,128)S(1)} fusion(bf16[32,576,32]{2,1,0:T(8,128)(2,1)} %reshape.332, pred[1024,32]{0,1:T(8,128)(4,1)S(1)} %get-tuple-element.26, bf16[1024,576]{0,1:T(8,128)(2,1)} %param.11), kind=kOutput, calls=%fused_computation.8 | convolution fusion | flops 1210023936 | bytes 2523136 | tf_op jit(solution)/shard_map/lowrank/tf,sfr->tsr/dot_general | solution.py:141
  139.4 1.5 collective-permute-start.5
  140.8 3.4 %constant_dynamic-update-slice_fusion.1 = bf16[1024,4608]{0,1:T(8,128)(2,1)} fusion(bf16[1024,4608]{0,1:T(8,128)(2,1)} %get-tuple-element.9, bf16[1024,1152]{0,1:T(8,128)(2,1)} %collective-permute-done.1, s32[]{:T(128)S(6)} %select_n.105), kind=kLoop, calls=%fused_computation.61 | loop fusion | bytes 4718596 | tf_op jit(solution)/shard_map/gathers/dynamic_update_slice | solution.py:88
  144.2 1.4 collective-permute-start.6
  145.7 3.4 %constant_dynamic-update-slice_fusion = bf16[1024,4608]{0,1:T(8,128)(2,1)} fusion(bf16[1024,4608]{0,1:T(8,128)(2,1)} %constant_dynamic-update-slice_fusion.1, bf16[1024,1152]{0,1:T(8,128)(2,1)} %collective-permute-done.2, s32[]{:T(128)S(6)} %select_n.107), kind=kLoop, calls=%fused_computation.60 | loop fusion | bytes 4718596 | tf_op jit(solution)/shard_map/gathers/dynamic_update_slice | solution.py:89
  149.0 11.5 %dynamic_update_slice.18 = bf16[1024,4608]{0,1:T(8,128)(2,1)} dynamic-update-slice(bf16[1024,4608]{0,1:T(8,128)(2,1)} %constant_dynamic-update-slice_fusion, bf16[512,1152]{0,1:T(8,128)(2,1)S(1)} %collective-permute-done.3, s32[]{:T(128)S(6)} %select_n.108, s32[]{:T(128)S(6)} %select_n.110) | dynamic-update-slice | bytes 2359300 | tf_op jit(solution)/shard_map/gathers/dynamic_update_slice | solution.py:91
  160.5 12.9 %dynamic_update_slice.19 = bf16[1024,4608]{0,1:T(8,128)(2,1)} dynamic-update-slice(bf16[1024,4608]{0,1:T(8,128)(2,1)} %dynamic_update_slice.18, bf16[512,1152]{0,1:T(8,128)(2,1)} %collective-permute-done.4, s32[]{:T(128)S(6)} %select_n.111, s32[]{:T(128)S(6)} %select_n.110) | dynamic-update-slice | bytes 2359300 | tf_op jit(solution)/shard_map/gathers/dynamic_update_slice | solution.py:92
  173.4 9.2 %slice.62 = bf16[32,144,1024]{2,1,0:T(8,128)(2,1)} slice(bf16[32,174,1024]{2,1,0:T(8,128)(2,1)} %all-gather.4.cloned.1.call-done), slice={[0:32], [0:144], [0:1024]} | slice | bytes 18874368 | tf_op jit(solution)/shard_map/gathers/slice | solution.py:134
  182.5 1.6 add.153
  184.1 2.4 %collective-permute-start.7 = (f32[1024,32]{0,1:T(8,128)}, f32[1024,32]{0,1:T(8,128)}, u32[]{:S(2)}, u32[]{:S(2)}) collective-permute-start(f32[1024,32]{0,1:T(8,128)} %add.153), channel_id=1, source_target_pairs={{0,128},{32,160},{64,192},{96,224},{128,0},{160,32},{192,64},{224,... | collective-permute-start | bytes 393224 | tf_op jit(solution)/shard_map/lowrank/ppermute | solution.py:148
  186.5 16.0 %fusion.26 = f32[1024,1024]{0,1:T(8,128)} fusion(bf16[1024,4608]{0,1:T(8,128)(2,1)} %dynamic_update_slice.19, bf16[4608,1024]{1,0:T(8,128)(2,1)} %bitcast.59), kind=kOutput, calls=%fused_computation.77 | convolution fusion | flops 9663676416 | bytes 23068672 | tf_op jit(solution)/shard_map/projection/dot_general | solution.py:170
  202.6 0.8 slice.74
  203.4 1.1 reshape.336
  204.6 1.4 slice.66
  206.0 0.2 reshape.333
  206.2 1.0 add_convert_fusion.2
  207.2 0.1 broadcast_multiply_fusion
  207.3 2.1 fusion.23
  209.5 0.2 subtract_convert_fusion.1
  209.7 3.6 %fusion.5 = bf16[2304,512]{1,0:T(8,128)(2,1)S(1)} fusion(s32[2304]{0:T(1024)S(1)} %clamp_bitcast_fusion, pred[2304]{0:T(1024)(128)(4,1)S(1)} %fusion.15, bf16[1024,256]{0,1:T(8,128)(2,1)S(1)} %get-tuple-element.12, bf16[1024,256]{0,1:T(8,128)(2,1)S(1)} %bitcast.67), kind=kOutput, calls=%fused_computation.6 | convolution fusion | flops 2423914496 | bytes 3419392 | tf_op jit(solution)/shard_map/cache_write/dot_general | solution.py:193
  213.3 1.6 fusion.24
  214.9 1.5 copy-done.3
  216.3 0.8 slice_add_fusion
  217.1 0.3 subtract_convert_fusion
  217.6 1.3 copy.26
  (50 shorter events, 0.8 us)
Async XLA Ops:
  7.2 19.1 %copy-start = (s32[32]{0:T(128)S(1)}, s32[32]{0:T(128)}, u32[]{:S(2)}) copy-start(s32[32]{0:T(128)} %param.20) | copy-start | bytes 388
  7.2 121.1 %all-gather.4.cloned.1.call-start = ((), (), s32[]{:S(2)}) async-start(), calls=%async_computation | async-start | bytes 11894784 | tf_op jit(solution)/shard_map/gathers/all_gather | solution.py:133
  11.6 6.0 %collective-permute-start = (bf16[1024,576]{0,1:T(8,128)(2,1)}, bf16[1024,576]{0,1:T(8,128)(2,1)S(1)}, u32[]{:S(2)}, u32[]{:S(2)}) collective-permute-start(bf16[1024,576]{0,1:T(8,128)(2,1)} %param.11), channel_id=1, source_target_pairs={{0,32},{32,0},{64,96},{96,64},{128,160},{160,128},{192,224},{224,1... | collective-permute-start | bytes 3538952 | tf_op jit(solution)/shard_map/gathers/ppermute | solution.py:74
  14.9 7.5 %copy-start.4 = (bf16[1024,576]{0,1:T(8,128)(2,1)S(1)}, bf16[1024,576]{0,1:T(8,128)(2,1)}, u32[]{:S(2)}) copy-start(bf16[1024,576]{0,1:T(8,128)(2,1)} %param.11) | copy-start | bytes 3538948
  22.4 3.4 %copy-start.6 = (s32[1,10]{1,0:T(1,128)S(1)}, s32[1,10]{1,0:T(1,128)}, u32[]{:S(2)}) copy-start(s32[1,10]{1,0:T(1,128)} %param.18) | copy-start | bytes 124
  22.4 3.8 %copy-start.8 = (s32[1,10]{1,0:T(1,128)S(1)}, s32[1,10]{1,0:T(1,128)}, u32[]{:S(2)}) copy-start(s32[1,10]{1,0:T(1,128)} %param.19) | copy-start | bytes 124
  22.4 4.5 %copy-start.7 = (s32[1,18]{1,0:T(1,128)S(1)}, s32[1,18]{1,0:T(1,128)}, u32[]{:S(2)}) copy-start(s32[1,18]{1,0:T(1,128)} %param.21) | copy-start | bytes 220
  24.8 28.1 %collective-permute-start.1 = (bf16[1024,1152]{0,1:T(8,128)(2,1)S(1)}, bf16[1024,1152]{0,1:T(8,128)(2,1)}, u32[]{:S(2)}, u32[]{:S(2)}) collective-permute-start(bf16[1024,1152]{0,1:T(8,128)(2,1)S(1)} %get-tuple-element.10), channel_id=1, source_target_pairs={{0,64},{32,224},{64,128},{96,32},{128,192},{160,96},{192,0},{224,1... | collective-permute-start | bytes 7077896 | tf_op jit(solution)/shard_map/gathers/ppermute | solution.py:80
  52.9 92.7 %collective-permute-start.2 = (bf16[1024,1152]{0,1:T(8,128)(2,1)}, bf16[1024,1152]{0,1:T(8,128)(2,1)}, u32[]{:S(2)}, u32[]{:S(2)}) collective-permute-start(bf16[1024,1152]{0,1:T(8,128)(2,1)} %collective-permute-done.1), channel_id=1, source_target_pairs={{0,32},{32,0},{64,96},{96,64},{128,160},{160,128},{192,224},{224,1... | collective-permute-start | bytes 7077896 | tf_op jit(solution)/shard_map/gathers/ppermute | solution.py:84
  56.7 15.5 %collective-permute-start.3 = (bf16[512,1152]{0,1:T(8,128)(2,1)S(1)}, bf16[512,1152]{0,1:T(8,128)(2,1)S(1)}, u32[]{:S(2)}, u32[]{:S(2)}) collective-permute-start(bf16[512,1152]{0,1:T(8,128)(2,1)S(1)} %constant_dynamic-slice_fusion), channel_id=1, source_target_pairs={{0,64},{32,224},{64,128},{96,32},{128,192},{160,96},{192,0},{224,1... | collective-permute-start | bytes 3538952 | tf_op jit(solution)/shard_map/gathers/ppermute | solution.py:83
  72.3 88.3 %collective-permute-start.4 = (bf16[512,1152]{0,1:T(8,128)(2,1)S(1)}, bf16[512,1152]{0,1:T(8,128)(2,1)}, u32[]{:S(2)}, u32[]{:S(2)}) collective-permute-start(bf16[512,1152]{0,1:T(8,128)(2,1)S(1)} %collective-permute-done.3), channel_id=1, source_target_pairs={{0,32},{32,0},{64,96},{96,64},{128,160},{160,128},{192,224},{224,1... | collective-permute-start | bytes 3538952 | tf_op jit(solution)/shard_map/gathers/ppermute | solution.py:84
  128.3 1.4 slice-start.3
  139.4 4.8 %collective-permute-start.5 = (f32[1024,32]{0,1:T(8,128)S(1)}, f32[1024,32]{0,1:T(8,128)S(1)}, u32[]{:S(2)}, u32[]{:S(2)}) collective-permute-start(f32[1024,32]{0,1:T(8,128)S(1)} %fusion.8), channel_id=1, source_target_pairs={{0,32},{32,0},{64,96},{96,64},{128,160},{160,128},{192,224},{224,1... | collective-permute-start | bytes 393224 | tf_op jit(solution)/shard_map/lowrank/ppermute | solution.py:148
  144.2 38.3 %collective-permute-start.6 = (f32[1024,32]{0,1:T(8,128)S(1)}, f32[1024,32]{0,1:T(8,128)}, u32[]{:S(2)}, u32[]{:S(2)}) collective-permute-start(f32[1024,32]{0,1:T(8,128)S(1)} %add.152), channel_id=1, source_target_pairs={{0,64},{32,96},{64,0},{96,32},{128,192},{160,224},{192,128},{224,1... | collective-permute-start | bytes 393224 | tf_op jit(solution)/shard_map/lowrank/ppermute | solution.py:148
  173.4 29.2 %slice-start = ((s8[11534336]{0:T(1024)(128)(4,1)}), s8[3145728]{0:T(1024)(128)(4,1)S(1)}, s32[]{:S(2)}) async-start(s8[11534336]{0:T(1024)(128)(4,1)} %bitcast.57), calls=%async_computation.1 | async-start | bytes 6291456
  184.1 22.0 %collective-permute-start.7 = (f32[1024,32]{0,1:T(8,128)}, f32[1024,32]{0,1:T(8,128)}, u32[]{:S(2)}, u32[]{:S(2)}) collective-permute-start(f32[1024,32]{0,1:T(8,128)} %add.153), channel_id=1, source_target_pairs={{0,128},{32,160},{64,192},{96,224},{128,0},{160,32},{192,64},{224,... | collective-permute-start | bytes 393224 | tf_op jit(solution)/shard_map/lowrank/ppermute | solution.py:148
  186.5 16.1 %slice-start.1 = ((s8[11534336]{0:T(1024)(128)(4,1)}), s8[4194304]{0:T(1024)(128)(4,1)S(1)}, s32[]{:S(2)}) async-start(s8[11534336]{0:T(1024)(128)(4,1)} %bitcast.57), calls=%async_computation.2 | async-start | bytes 8388608
  186.5 16.1 %slice-start.2 = ((s8[11534336]{0:T(1024)(128)(4,1)}), s8[4194304]{0:T(1024)(128)(4,1)S(1)}, s32[]{:S(2)}) async-start(s8[11534336]{0:T(1024)(128)(4,1)} %bitcast.57), calls=%async_computation.3 | async-start | bytes 8388608
  202.6 4.6 %copy-start.5 = (bf16[1024,32]{0,1:T(8,128)(2,1)S(1)}, bf16[1024,32]{0,1:T(8,128)(2,1)}, u32[]{:S(2)}) copy-start(bf16[1024,32]{0,1:T(8,128)(2,1)} %get-tuple-element.25) | copy-start | bytes 196612
  207.3 2.2 copy-start.2
  213.3 3.0 %copy-start.3 = (f32[1024,1024]{0,1:T(8,128)S(1)}, f32[1024,1024]{0,1:T(8,128)}, u32[]{:S(2)}) copy-start(f32[1024,1024]{0,1:T(8,128)} %fusion.26) | copy-start | bytes 12582916
  217.1 1.8 copy-start.1
Sparse Core Ops, SparseCore 0:
  11.7 116.5 all-gather.3

commit v3 on v2

--- a/solution.py
+++ b/solution.py
@@ -82,14 +82,25 @@
     forwarded = lax.dynamic_slice_in_dim(near, core * half, half, 0)
     far_half = lax.ppermute(forwarded, "row", ring)
     from_partner, far_other = lax.ppermute((near, far_half), "row", swap)
-    block = 2 * width
-    full = jnp.zeros((tokens, chips * block), hidden.dtype)
-    full = lax.dynamic_update_slice(full, own_block, (0, chip * block))
-    full = lax.dynamic_update_slice(full, near, (0, ((chip + step) % chips) * block))
-    full = lax.dynamic_update_slice(full, from_partner, (0, ((chip - step) % chips) * block))
-    far = ((chip + 2) % chips) * block
-    full = lax.dynamic_update_slice(full, far_half, (core * half, far))
-    full = lax.dynamic_update_slice(full, far_other, ((1 - core) * half, far))
+    first = core == 0
+    after = jnp.where(first, from_partner, near)
+    before = jnp.where(first, near, from_partner)
+    far = jnp.where(
+        first,
+        jnp.concatenate([far_half, far_other], axis=0),
+        jnp.concatenate([far_other, far_half], axis=0),
+    )
+    blocks = []
+    for k in range(chips):
+        relative = (k - chip) % chips
+        blocks.append(
+            jnp.where(
+                relative == 0,
+                own_block,
+                jnp.where(relative == 1, after, jnp.where(relative == 2, far, before)),
+            )
+        )
+    full = jnp.concatenate(blocks, axis=1)
     return full
 
 
@@ -121,26 +132,37 @@
 
     with jax.named_scope("gathers"):
         full_rows = gather_rows(hidden, row_size)
+        features = down_shape[0]
+        down_rows = jnp.pad(
+            jnp.transpose(adapter_down[0]), ((0, 0), (0, weight_width - features))
+        )
         pieces = [
             jnp.concatenate([w_query, w_key, w_value], axis=1),
-            adapter_down.reshape(-1, weight_width),
+            down_rows,
             adapter_up_query.reshape(-1, weight_width),
             adapter_up_value.reshape(-1, weight_width),
         ]
+        pieces = [jnp.pad(p, ((0, -p.shape[0] % 8), (0, 0))) for p in pieces]
         bounds = [0]
         for piece in pieces:
             bounds.append(bounds[-1] + piece.shape[0])
         packed = lax.all_gather(jnp.concatenate(pieces, axis=0), "col", axis=0)
-        weights = packed[:, : bounds[1]].reshape(-1, weight_width)
-        down_local = packed[:, bounds[1] : bounds[2]].reshape((adapter_count,) + down_shape)
-        up_query = packed[:, bounds[2] : bounds[3]].reshape(adapter_count, rank_width, -1)
-        up_value = packed[:, bounds[3] : bounds[4]].reshape(adapter_count, rank_width, -1)
+        weights = packed[:, :feature_rows]
+        down_local = packed[:, bounds[1] : bounds[2]].reshape(-1, weight_width)
+        up_query = packed[:, bounds[2] : bounds[3]].reshape(adapter_count, -1)
+        up_query = up_query[:, : rank_width * query_width].reshape(adapter_count, rank_width, -1)
+        up_value = packed[:, bounds[3] : bounds[4]].reshape(adapter_count, -1)
+        up_value = up_value[:, : rank_width * key_width].reshape(adapter_count, rank_width, -1)
 
     with jax.named_scope("lowrank"):
         onehot = (chosen[:, None] == jnp.arange(adapter_count, dtype=jnp.int32)[None, :])
-        partial_all = jnp.einsum(
-            "tf,sfr->tsr", hidden, down_local, preferred_element_type=jnp.float32
-        )
+        padded_hidden = jnp.pad(hidden, ((0, 0), (0, weight_width - features)))
+        partial_all = lax.dot_general(
+            padded_hidden,
+            down_local,
+            (((1,), (1,)), ((), ())),
+            preferred_element_type=jnp.float32,
+        ).reshape(hidden.shape[0], adapter_count, -1)
         partial = jnp.sum(jnp.where(onehot[:, :, None], partial_all, 0.0), axis=1)
         distance = 1
         while distance < row_size:
@@ -167,7 +189,12 @@
         )
 
     with jax.named_scope("projection"):
-        base = jnp.dot(full_rows, weights, preferred_element_type=jnp.float32)
+        base = jnp.einsum(
+            "tci,cin->tn",
+            full_rows.reshape(full_rows.shape[0], packed.shape[0], feature_rows),
+            weights,
+            preferred_element_type=jnp.float32,
+        )
         base_query = base[:, :query_width]
         base_key = base[:, query_width : query_width + key_width]
         base_value = base[:, query_width + key_width :]

time: 227 us -> 181 us (0.80)
  local copies, waits for them, and re-layouts: 63.8 us -> 14.4 us
  other arithmetic: 10.8 us -> 35.2 us
  waiting for transfers between devices: 95.4 us -> 76.5 us
  matrix products: 27.3 us -> 22.7 us
  starting transfers between devices: 14.1 us -> 17 us
    dynamic_update_slice x4 -> x0, local copies, waits for them, and re-layouts: 31.1 us -> none  [the longest x1 12.9 us: gather_rows(): full = lax.dynamic_update_slice(full, far_other, ((1 - core) * half, far))]
    all_gather x1, waiting for transfers between devices: 54 us -> 38.7 us  [shards(): packed = lax.all_gather(jnp.concatenate(pieces, axis=0), 'col', axis=0)]
    select_n x0 -> x4, other arithmetic: none -> 15.2 us  [the longest x3 12.9 us: gather_rows(): jnp.where(relative == 0, own_block, jnp.where(relative == 1, after, jnp.w...]
    slice x5 -> x3, local copies, waits for them, and re-layouts: 12.8 us -> 1.66 us  [the longest x1 1.54 us: shards(): up_value = packed[:, bounds[3]:bounds[4]].reshape(adapter_count, -1)]
    ppermute x1, waiting for transfers between devices: 12.9 us -> 5.34 us  [gather_rows(): far_half = lax.ppermute(forwarded, 'row', ring)]
    concatenate x0 -> x2, other arithmetic: none -> 6.15 us  [the longest x1 4.35 us: gather_rows(): full = jnp.concatenate(blocks, axis=1)]
    reshape x2 -> x0, local copies, waits for them, and re-layouts: 5 us -> none  [the longest x1 4.8 us: shards(): packed[:, bounds[1]:bounds[2]].reshape((adapter_count,) + down_shape)]
    broadcast_in_dim x1 -> x0, local copies, waits for them, and re-layouts: 4.86 us -> none  [gather_rows(): full = jnp.zeros((tokens, chips * block), hidden.dtype)]
  transfers between devices with their start and end apart: 9 -> 9, of which waited for: 4 -> 6; matrix products, arithmetic and copies ran while one was open for 36% -> 30% of each run, Pallas kernels for 0% -> 0%
where the time goes in v3:
time: 181 us; the launch traced here: 180 us
  waiting for transfers between devices  76.5 us (42%)
  other arithmetic  35.2 us (19%)
  matrix products  22.7 us (13%)
  starting transfers between devices  17 us (9%)
  local copies, waits for them, and re-layouts  14.4 us (8%)
  between operations  14.3 us (8%)
    all_gather x1, waiting for transfers between devices, shards(): packed = lax.all_gather(jnp.concatenate(pieces, axis=0), 'col', axis=0)  38.7 us
    ppermute x1, waiting for transfers between devices, gather_rows(): near = lax.ppermute(own_block, 'row', ring)  26.5 us
    select_n x3, other arithmetic, gather_rows(): jnp.where(relative == 0, own_block, jnp.where(relative == 1, after, jnp.w...  12.9 us
    dot_general x1, matrix products, shards(): jnp.einsum('tci,cin->tn', full_rows.reshape(full_rows.shape[0], packed.sh...  12.5 us
    ppermute x3, starting transfers between devices, shards(): partial = partial + lax.ppermute(partial, 'row', pairs)  5.75 us
    ppermute x1, waiting for transfers between devices, gather_rows(): far_half = lax.ppermute(forwarded, 'row', ring)  5.34 us
    unnamed x32, local copies, waits for them, and re-layouts  4.56 us
    ppermute x2, starting transfers between devices, gather_rows(): from_partner, far_other = lax.ppermute((near, far_half), 'row', swap)  4.54 us
  transfers between devices with their start and end apart: 9, of which 6 were waited for; matrix products, arithmetic and copies ran while one was open for 30% of the time, Pallas kernels for 0%

profile of v3, /device:TPU:1, one launch (start us, length us, event | category | flops | bytes accessed | tf_op | source)
XLA Modules:
  0.0 180.2 jit_solution(2612669899181100176)
XLA Ops:
  7.2 0.7 reshape.329
  8.0 0.7 reshape.330
  8.7 1.8 fusion.25
  10.5 3.3 %collective-permute-start = (bf16[1024,576]{0,1:T(8,128)(2,1)}, bf16[1024,576]{0,1:T(8,128)(2,1)S(1)}, u32[]{:S(2)}, u32[]{:S(2)}) collective-permute-start(bf16[1024,576]{0,1:T(8,128)(2,1)} %param.11), channel_id=1, source_target_pairs={{0,32},{32,0},{64,96},{96,64},{128,160},{160,128},{192,224},{224,1... | collective-permute-start | bytes 3538952 | tf_op jit(solution)/shard_map/gathers/ppermute | solution.py:74
  13.8 2.7 %collective-permute-done = bf16[1024,576]{0,1:T(8,128)(2,1)S(1)} collective-permute-done((bf16[1024,576]{0,1:T(8,128)(2,1)}, bf16[1024,576]{0,1:T(8,128)(2,1)S(1)}, u32[]{:S(2)}, u32[]{:S(2)}) %collective-permute-start) | collective-permute-done | bytes 1179680 | tf_op jit(solution)/shard_map/gathers/ppermute | solution.py:74
  16.5 2.3 %maximum_select_fusion = bf16[1024,1152]{0,1:T(8,128)(2,1)S(1)} fusion(bf16[1024,576]{0,1:T(8,128)(2,1)S(1)} %collective-permute-done, bf16[1024,576]{0,1:T(8,128)(2,1)} %param.11, pred[]{:T(512)S(6)} %eq.95), kind=kLoop, calls=%fused_computation.11 | loop fusion | flops 10616832 | bytes 4718593 | tf_op jit(solution)/shard_map/gathers/jit(_where)/select_n | solution.py:75
  18.8 1.1 collective-permute-start.1
  19.9 0.5 and_select_fusion.1
  20.4 26.5 %collective-permute-done.1 = bf16[1024,1152]{0,1:T(8,128)(2,1)} collective-permute-done((bf16[1024,1152]{0,1:T(8,128)(2,1)S(1)}, bf16[1024,1152]{0,1:T(8,128)(2,1)}, u32[]{:S(2)}, u32[]{:S(2)}) %collective-permute-start.1) | collective-permute-done | bytes 2359328 | tf_op jit(solution)/shard_map/gathers/ppermute | solution.py:80
  47.0 2.4 %constant_dynamic-slice_fusion = bf16[512,1152]{0,1:T(8,128)(2,1)} fusion(bf16[1024,1152]{0,1:T(8,128)(2,1)} %collective-permute-done.1, s32[]{:T(128)S(6)} %select_n.179), kind=kLoop, calls=%fused_computation.87 | loop fusion | bytes 2359300 | tf_op jit(solution)/shard_map/gathers/dynamic_slice | solution.py:82
  49.4 2.2 %collective-permute-start.3 = (bf16[512,1152]{0,1:T(8,128)(2,1)}, bf16[512,1152]{0,1:T(8,128)(2,1)S(1)}, u32[]{:S(2)}, u32[]{:S(2)}) collective-permute-start(bf16[512,1152]{0,1:T(8,128)(2,1)} %constant_dynamic-slice_fusion), channel_id=1, source_target_pairs={{0,64},{32,224},{64,128},{96,32},{128,192},{160,96},{192,0},{224,1... | collective-permute-start | bytes 3538952 | tf_op jit(solution)/shard_map/gathers/ppermute | solution.py:83
  51.6 0.5 fusion.28
  52.1 0.8 reduce-window.9
  53.0 0.7 reduce-window.6
  53.8 0.6 pad_clamp_fusion
  54.4 1.2 gather_fusion
  55.6 0.7 select_reduce_fusion.3
  56.4 0.7 fusion.31
  57.0 0.7 fusion.29
  57.7 0.8 select_reduce_fusion.1
  58.5 0.7 select_reduce_fusion.4
  59.7 5.3 %collective-permute-done.3 = bf16[512,1152]{0,1:T(8,128)(2,1)S(1)} collective-permute-done((bf16[512,1152]{0,1:T(8,128)(2,1)}, bf16[512,1152]{0,1:T(8,128)(2,1)S(1)}, u32[]{:S(2)}, u32[]{:S(2)}) %collective-permute-start.3) | collective-permute-done | bytes 1179680 | tf_op jit(solution)/shard_map/gathers/ppermute | solution.py:83
  65.1 4.3 %collective-permute-start.4 = (bf16[512,1152]{0,1:T(8,128)(2,1)S(1)}, bf16[512,1152]{0,1:T(8,128)(2,1)}, u32[]{:S(2)}, u32[]{:S(2)}) collective-permute-start(bf16[512,1152]{0,1:T(8,128)(2,1)S(1)} %collective-permute-done.3), channel_id=1, source_target_pairs={{0,32},{32,0},{64,96},{96,64},{128,160},{160,128},{192,224},{224,1... | collective-permute-start | bytes 3538952 | tf_op jit(solution)/shard_map/gathers/ppermute | solution.py:84
  69.4 0.6 multiply_exponential_fusion
  70.0 2.4 %copy.19 = bf16[1024,576]{1,0:T(8,128)(2,1)} copy(bf16[1024,576]{0,1:T(8,128)(2,1)} %param.11) | data formatting | bytes 2359296 | tf_op args[0]
  72.5 1.3 clamp_bitcast_fusion
  73.8 0.7 fusion.35
  74.5 2.5 %multiply_cosine_fusion = (f32[1024,64]{0,1:T(8,128)}, f32[1024,64]{0,1:T(8,128)}) fusion(f32[64]{0:T(128)} %multiply_exponential_fusion, f32[1024]{0:T(1024)S(1)} %subtract_convert_fusion.2), kind=kLoop, calls=%fused_computation.47 | loop fusion | flops 65536 | bytes 528640 | tf_op jit(solution)/shard_map/rotary/cos | solution.py:208
  77.0 4.8 %select_select_fusion.3 = (bf16[1024,1152]{0,1:T(8,128)(2,1)S(1)}, bf16[1024,1152]{0,1:T(8,128)(2,1)S(1)}, bf16[1024,1152]{0,1:T(8,128)(2,1)S(1)}) fusion(bf16[1024,1152]{0,1:T(8,128)(2,1)S(1)} %maximum_select_fusion, pred[]{:T(512)S(6)} %eq.97, pred[]{:T(512)S(6)} %eq.96, pred[]{:T(512)S(6)} %eq.94, bf16[512,1152]{0,1:T(8,128)(2,1)S(1)} %collective-permute-done.3, ...), kind=kLoop, calls=%fused_computation.16 | loop fusion | flops 16515072 | bytes 16515076 | tf_op jit(solution)/shard_map/gathers/jit(_where)/select_n | solution.py:97
  81.7 3.9 %select_select_fusion.1 = bf16[1024,1152]{0,1:T(8,128)(2,1)S(1)} fusion(bf16[1024,1152]{0,1:T(8,128)(2,1)S(1)} %maximum_select_fusion, bf16[1024,1152]{0,1:T(8,128)(2,1)S(1)} %get-tuple-element.11, bf16[1024,1152]{0,1:T(8,128)(2,1)S(1)} %get-tuple-element.10, pred[]{:T(512)S(6)} %eq.103, pred[]{:T(512)S(6)} %eq.102, pred[]{:T(512)S(6)} %eq.101, ...), kind=kLoop, calls=%fused_computation.14 | loop fusion | flops 14155776 | bytes 11796484 | tf_op jit(solution)/shard_map/gathers/jit(_where)/select_n | solution.py:97
  85.7 4.2 %select_select_fusion.2 = (bf16[1024,1152]{0,1:T(8,128)(2,1)S(1)}, bf16[1024,1152]{0,1:T(8,128)(2,1)S(1)}) fusion(bf16[1024,1152]{0,1:T(8,128)(2,1)S(1)} %maximum_select_fusion, bf16[1024,1152]{0,1:T(8,128)(2,1)S(1)} %get-tuple-element.11, bf16[1024,1152]{0,1:T(8,128)(2,1)S(1)} %get-tuple-element.10, pred[]{:T(512)S(6)} %eq.100, pred[]{:T(512)S(6)} %eq.99, ...), kind=kLoop, calls=%fused_computation.15 | loop fusion | flops 17694720 | bytes 14155783 | tf_op jit(solution)/shard_map/gathers/jit(_where)/select_n | solution.py:97
  89.9 4.3 %pad_maximum_fusion = bf16[1024,4608]{0,1:T(8,128)(2,1)} fusion(bf16[1024,1152]{0,1:T(8,128)(2,1)S(1)} %get-tuple-element.15, bf16[1024,1152]{0,1:T(8,128)(2,1)S(1)} %select_select_fusion.1, bf16[1024,1152]{0,1:T(8,128)(2,1)S(1)} %get-tuple-element.14, bf16[1024,1152]{0,1:T(8,128)(2,1)S(1)} %get-tuple-element.9), kind=kLoop, calls=%fused_computation.3 | loop fusion | flops 37748736 | bytes 18874368 | tf_op jit(solution)/shard_map/gathers/concatenate | solution.py:103
  94.2 38.7 %all-gather.3.cloned.1.call-done = bf16[6144,1024]{1,0:T(8,128)(2,1)} async-done(((bf16[192,1024]{1,0:T(8,128)(2,1)}), bf16[6144,1024]{1,0:T(8,128)(2,1)}) %all-gather.3.cloned.1.call-update) | async-done | bytes 12582928 | tf_op jit(solution)/shard_map/gathers/all_gather | solution.py:149
  132.9 4.1 %select_reduce_fusion = f32[1024,32]{0,1:T(8,128)S(1)} fusion(bf16[32,192,1024]{2,1,0:T(8,128)(2,1)} %bitcast.68, bf16[1024,576]{1,0:T(8,128)(2,1)S(1)} %copy-done.7, pred[1024,32]{0,1:T(8,128)(4,1)S(1)} %copy-done.10), kind=kOutput, calls=%fused_computation.10 | convolution fusion | flops 2149548032 | bytes 3440640 | tf_op jit(solution)/shard_map/lowrank/dot_general | solution.py:160
  137.0 1.7 collective-permute-start.5
  138.7 12.5 %fusion.10 = f32[1024,1024]{0,1:T(8,128)S(1)} fusion(bf16[1024,32,144]{0,2,1:T(8,128)(2,1)S(1)} %bitcast.57, bf16[32,192,1024]{2,1,0:T(8,128)(2,1)} %bitcast.69), kind=kOutput, calls=%fused_computation.19 | convolution fusion | flops 9663676416 | bytes 23068672 | tf_op jit(solution)/shard_map/projection/tci,cin->tn/dot_general | solution.py:192
  151.3 1.3 collective-permute-start.6
  152.6 1.5 fusion.36
  154.3 2.2 %collective-permute-done.6 = f32[1024,32]{0,1:T(8,128)S(1)} collective-permute-done((f32[1024,32]{0,1:T(8,128)S(1)}, f32[1024,32]{0,1:T(8,128)S(1)}, u32[]{:S(2)}, u32[]{:S(2)}) %collective-permute-start.6) | collective-permute-done | bytes 131104 | tf_op jit(solution)/shard_map/lowrank/ppermute | solution.py:170
  156.5 2.8 %collective-permute-start.7 = (f32[1024,32]{0,1:T(8,128)S(1)}, f32[1024,32]{0,1:T(8,128)S(1)}, u32[]{:S(2)}, u32[]{:S(2)}) collective-permute-start(f32[1024,32]{0,1:T(8,128)S(1)} %add.132), channel_id=1, source_target_pairs={{0,128},{32,160},{64,192},{96,224},{128,0},{160,32},{192,64},{224,... | collective-permute-start | bytes 393224 | tf_op jit(solution)/shard_map/lowrank/ppermute | solution.py:170
  159.3 0.9 subtract_convert_fusion.1
  161.2 1.1 collective-permute-done.7
  162.4 1.7 fusion.16
  164.2 3.6 %fusion.7 = bf16[2304,512]{1,0:T(8,128)(2,1)S(1)} fusion(s32[2304]{0:T(1024)S(1)} %copy-done.11, pred[2304]{0:T(1024)(128)(4,1)S(1)} %fusion.27, bf16[1024,256]{0,1:T(8,128)(2,1)S(1)} %fusion.16, bf16[1024,256]{0,1:T(8,128)(2,1)S(1)} %bitcast.67), kind=kOutput, calls=%fused_computation.9 | convolution fusion | flops 2423914496 | bytes 3419392 | tf_op jit(solution)/shard_map/cache_write/dot_general | solution.py:220
  167.7 1.6 fusion.37
  169.3 1.5 copy-done.4
  170.8 0.8 slice_add_fusion
  172.0 1.3 copy.21
  (51 shorter events, 2.6 us)
Async XLA Ops:
  7.2 47.3 %copy-start = (s32[32]{0:T(128)S(1)}, s32[32]{0:T(128)}, u32[]{:S(2)}) copy-start(s32[32]{0:T(128)} %param.20) | copy-start | bytes 388
  7.2 125.7 %all-gather.3.cloned.1.call-start = ((), (), s32[]{:S(2)}) async-start(), calls=%async_computation | async-start | bytes 12976128 | tf_op jit(solution)/shard_map/gathers/all_gather | solution.py:149
  10.5 6.0 %collective-permute-start = (bf16[1024,576]{0,1:T(8,128)(2,1)}, bf16[1024,576]{0,1:T(8,128)(2,1)S(1)}, u32[]{:S(2)}, u32[]{:S(2)}) collective-permute-start(bf16[1024,576]{0,1:T(8,128)(2,1)} %param.11), channel_id=1, source_target_pairs={{0,32},{32,0},{64,96},{96,64},{128,160},{160,128},{192,224},{224,1... | collective-permute-start | bytes 3538952 | tf_op jit(solution)/shard_map/gathers/ppermute | solution.py:74
  13.8 6.1 %copy-start.12 = (s32[1,10]{1,0:T(1,128)S(1)}, s32[1,10]{1,0:T(1,128)}, u32[]{:S(2)}) copy-start(s32[1,10]{1,0:T(1,128)} %param.18) | copy-start | bytes 124
  18.8 32.8 %copy-start.14 = (s32[1,10]{1,0:T(1,128)S(1)}, s32[1,10]{1,0:T(1,128)}, u32[]{:S(2)}) copy-start(s32[1,10]{1,0:T(1,128)} %param.19) | copy-start | bytes 124
  18.8 28.2 %collective-permute-start.1 = (bf16[1024,1152]{0,1:T(8,128)(2,1)S(1)}, bf16[1024,1152]{0,1:T(8,128)(2,1)}, u32[]{:S(2)}, u32[]{:S(2)}) collective-permute-start(bf16[1024,1152]{0,1:T(8,128)(2,1)S(1)} %maximum_select_fusion), channel_id=1, source_target_pairs={{0,64},{32,224},{64,128},{96,32},{128,192},{160,96},{192,0},{224,1... | collective-permute-start | bytes 7077896 | tf_op jit(solution)/shard_map/gathers/ppermute | solution.py:80
  49.4 15.7 %collective-permute-start.3 = (bf16[512,1152]{0,1:T(8,128)(2,1)}, bf16[512,1152]{0,1:T(8,128)(2,1)S(1)}, u32[]{:S(2)}, u32[]{:S(2)}) collective-permute-start(bf16[512,1152]{0,1:T(8,128)(2,1)} %constant_dynamic-slice_fusion), channel_id=1, source_target_pairs={{0,64},{32,224},{64,128},{96,32},{128,192},{160,96},{192,0},{224,1... | collective-permute-start | bytes 3538952 | tf_op jit(solution)/shard_map/gathers/ppermute | solution.py:83
  53.0 4.8 %copy-start.13 = (s32[10,1]{0,1:T(1,128)}, s32[10,1]{0,1:T(1,128)S(1)}, u32[]{:S(2)}) copy-start(s32[10,1]{0,1:T(1,128)S(1)} %reduce-window.9) | copy-start | bytes 124
  53.6 23.3 %collective-permute-start.2 = (bf16[1024,1152]{0,1:T(8,128)(2,1)}, bf16[1024,1152]{0,1:T(8,128)(2,1)}, u32[]{:S(2)}, u32[]{:S(2)}) collective-permute-start(bf16[1024,1152]{0,1:T(8,128)(2,1)} %collective-permute-done.1), channel_id=1, source_target_pairs={{0,32},{32,0},{64,96},{96,64},{128,160},{160,128},{192,224},{224,1... | collective-permute-start | bytes 7077896 | tf_op jit(solution)/shard_map/gathers/ppermute | solution.py:84
  65.1 11.9 %collective-permute-start.4 = (bf16[512,1152]{0,1:T(8,128)(2,1)S(1)}, bf16[512,1152]{0,1:T(8,128)(2,1)}, u32[]{:S(2)}, u32[]{:S(2)}) collective-permute-start(bf16[512,1152]{0,1:T(8,128)(2,1)S(1)} %collective-permute-done.3), channel_id=1, source_target_pairs={{0,32},{32,0},{64,96},{96,64},{128,160},{160,128},{192,224},{224,1... | collective-permute-start | bytes 3538952 | tf_op jit(solution)/shard_map/gathers/ppermute | solution.py:84
  89.9 43.1 %copy-start.7 = (bf16[1024,576]{1,0:T(8,128)(2,1)S(1)}, bf16[1024,576]{1,0:T(8,128)(2,1)}, u32[]{:S(2)}) copy-start(bf16[1024,576]{1,0:T(8,128)(2,1)} %copy.19) | copy-start | bytes 3538948
  89.9 43.1 %copy-start.10 = (pred[1024,32]{0,1:T(8,128)(4,1)S(1)}, pred[1024,32]{0,1:T(8,128)(4,1)}, u32[]{:S(2)}) copy-start(pred[1024,32]{0,1:T(8,128)(4,1)} %get-tuple-element.29) | copy-start | bytes 98308
  132.9 5.8 %copy-start.2 = (bf16[1024,4608]{0,1:T(8,128)(2,1)S(1)}, bf16[1024,4608]{0,1:T(8,128)(2,1)}, u32[]{:S(2)}) copy-start(bf16[1024,4608]{0,1:T(8,128)(2,1)} %pad_maximum_fusion) | copy-start | bytes 28311556
  137.0 14.2 %collective-permute-start.5 = (f32[1024,32]{0,1:T(8,128)S(1)}, f32[1024,32]{0,1:T(8,128)S(1)}, u32[]{:S(2)}, u32[]{:S(2)}) collective-permute-start(f32[1024,32]{0,1:T(8,128)S(1)} %select_reduce_fusion), channel_id=1, source_target_pairs={{0,32},{32,0},{64,96},{96,64},{128,160},{160,128},{192,224},{224,1... | collective-permute-start | bytes 393224 | tf_op jit(solution)/shard_map/lowrank/ppermute | solution.py:170
  151.3 5.2 %copy-start.3 = (f32[1024,1024]{0,1:T(8,128)}, f32[1024,1024]{0,1:T(8,128)S(1)}, u32[]{:S(2)}) copy-start(f32[1024,1024]{0,1:T(8,128)S(1)} %fusion.10) | copy-start | bytes 12582916
  151.3 8.0 %copy-start.5 = (f32[1024,64]{0,1:T(8,128)S(1)}, f32[1024,64]{0,1:T(8,128)}, u32[]{:S(2)}) copy-start(f32[1024,64]{0,1:T(8,128)} %get-tuple-element.26) | copy-start | bytes 786436
  151.3 7.9 %copy-start.6 = (f32[1024,64]{0,1:T(8,128)S(1)}, f32[1024,64]{0,1:T(8,128)}, u32[]{:S(2)}) copy-start(f32[1024,64]{0,1:T(8,128)} %get-tuple-element.27) | copy-start | bytes 786436
  151.3 5.1 %collective-permute-start.6 = (f32[1024,32]{0,1:T(8,128)S(1)}, f32[1024,32]{0,1:T(8,128)S(1)}, u32[]{:S(2)}, u32[]{:S(2)}) collective-permute-start(f32[1024,32]{0,1:T(8,128)S(1)} %add.131), channel_id=1, source_target_pairs={{0,64},{32,96},{64,0},{96,32},{128,192},{160,224},{192,128},{224,1... | collective-permute-start | bytes 393224 | tf_op jit(solution)/shard_map/lowrank/ppermute | solution.py:170
  156.5 5.8 %collective-permute-start.7 = (f32[1024,32]{0,1:T(8,128)S(1)}, f32[1024,32]{0,1:T(8,128)S(1)}, u32[]{:S(2)}, u32[]{:S(2)}) collective-permute-start(f32[1024,32]{0,1:T(8,128)S(1)} %add.132), channel_id=1, source_target_pairs={{0,128},{32,160},{64,192},{96,224},{128,0},{160,32},{192,64},{224,... | collective-permute-start | bytes 393224 | tf_op jit(solution)/shard_map/lowrank/ppermute | solution.py:170
  160.2 0.9 copy-start.8
  160.2 2.1 %copy-start.9 = (bf16[1024,32]{0,1:T(8,128)(2,1)S(1)}, bf16[1024,32]{0,1:T(8,128)(2,1)}, u32[]{:S(2)}) copy-start(bf16[1024,32]{0,1:T(8,128)(2,1)} %get-tuple-element.28) | copy-start | bytes 196612
  162.3 1.9 %copy-start.11 = (s32[2304]{0:T(1024)S(1)}, s32[2304]{0:T(1024)}, u32[]{:S(2)}) copy-start(s32[2304]{0:T(1024)} %clamp_bitcast_fusion) | copy-start | bytes 27652
  167.7 3.0 %copy-start.4 = (f32[1024,1024]{0,1:T(8,128)S(1)}, f32[1024,1024]{0,1:T(8,128)}, u32[]{:S(2)}) copy-start(f32[1024,1024]{0,1:T(8,128)} %copy-done.3) | copy-start | bytes 12582916
  171.6 1.8 copy-start.1
Sparse Core Ops, SparseCore 0:
  11.1 121.7 all-gather.2

commit v4 on v3

--- a/solution.py
+++ b/solution.py
@@ -130,39 +130,31 @@
     down_shape = adapter_down.shape[1:]
     row_size = lax.axis_size("row")
 
+    col_size = lax.axis_size("col")
+    col_index = lax.axis_index("col")
+
     with jax.named_scope("gathers"):
         full_rows = gather_rows(hidden, row_size)
-        features = down_shape[0]
-        down_rows = jnp.pad(
-            jnp.transpose(adapter_down[0]), ((0, 0), (0, weight_width - features))
-        )
-        pieces = [
-            jnp.concatenate([w_query, w_key, w_value], axis=1),
-            down_rows,
-            adapter_up_query.reshape(-1, weight_width),
-            adapter_up_value.reshape(-1, weight_width),
-        ]
-        pieces = [jnp.pad(p, ((0, -p.shape[0] % 8), (0, 0))) for p in pieces]
-        bounds = [0]
-        for piece in pieces:
-            bounds.append(bounds[-1] + piece.shape[0])
-        packed = lax.all_gather(jnp.concatenate(pieces, axis=0), "col", axis=0)
-        weights = packed[:, :feature_rows]
-        down_local = packed[:, bounds[1] : bounds[2]].reshape(-1, weight_width)
-        up_query = packed[:, bounds[2] : bounds[3]].reshape(adapter_count, -1)
-        up_query = up_query[:, : rank_width * query_width].reshape(adapter_count, rank_width, -1)
-        up_value = packed[:, bounds[3] : bounds[4]].reshape(adapter_count, -1)
-        up_value = up_value[:, : rank_width * key_width].reshape(adapter_count, rank_width, -1)
+        weights = lax.all_gather(
+            jnp.concatenate([w_query, w_key, w_value], axis=1), "col", axis=0, tiled=True
+        )
+        factors = (adapter_down, adapter_up_query, adapter_up_value)
+        distance = 1
+        while distance < col_size:
+            pairs = [(i, i ^ distance) for i in range(col_size)]
+            received = lax.ppermute(factors, "col", pairs)
+            factors = tuple(
+                jnp.concatenate([mine, theirs], axis=0) for mine, theirs in zip(factors, received)
+            )
+            distance *= 2
+        down_local, up_query, up_value = factors
 
     with jax.named_scope("lowrank"):
-        onehot = (chosen[:, None] == jnp.arange(adapter_count, dtype=jnp.int32)[None, :])
-        padded_hidden = jnp.pad(hidden, ((0, 0), (0, weight_width - features)))
-        partial_all = lax.dot_general(
-            padded_hidden,
-            down_local,
-            (((1,), (1,)), ((), ())),
-            preferred_element_type=jnp.float32,
-        ).reshape(hidden.shape[0], adapter_count, -1)
+        relative_slot = jnp.bitwise_xor(chosen, col_index)
+        onehot = relative_slot[:, None] == jnp.arange(adapter_count, dtype=jnp.int32)[None, :]
+        partial_all = jnp.einsum(
+            "tf,sfr->tsr", hidden, down_local, preferred_element_type=jnp.float32
+        )
         partial = jnp.sum(jnp.where(onehot[:, :, None], partial_all, 0.0), axis=1)
         distance = 1
         while distance < row_size:
@@ -189,12 +181,7 @@
         )
 
     with jax.named_scope("projection"):
-        base = jnp.einsum(
-            "tci,cin->tn",
-            full_rows.reshape(full_rows.shape[0], packed.shape[0], feature_rows),
-            weights,
-            preferred_element_type=jnp.float32,
-        )
+        base = jnp.dot(full_rows, weights, preferred_element_type=jnp.float32)
         base_query = base[:, :query_width]
         base_key = base[:, query_width : query_width + key_width]
         base_value = base[:, query_width + key_width :]

time: 181 us -> 187 us (1.033)
  waiting for transfers between devices: 76.5 us -> 35.2 us
  starting transfers between devices: 17 us -> 40 us
  local copies, waits for them, and re-layouts: 14.4 us -> 28.7 us
  other arithmetic: 35.2 us -> 42.5 us
    all_gather x1, waiting for transfers between devices: 38.7 us -> 0.01 us  [shards(): lax.all_gather(jnp.concatenate([w_query, w_key, w_value], axis=1), 'col',...]
    ppermute x0 -> x15, waiting for transfers between devices: none -> 34.5 us  [shards(): received = lax.ppermute(factors, 'col', pairs)]
    ppermute x1, waiting for transfers between devices: 26.5 us -> 0.01 us  [gather_rows(): near = lax.ppermute(own_block, 'row', ring)]
    ppermute x0 -> x15, starting transfers between devices: none -> 22.1 us  [shards(): received = lax.ppermute(factors, 'col', pairs)]
    concatenate x0 -> x6, local copies, waits for them, and re-layouts: none -> 16 us  [shards(): jnp.concatenate([mine, theirs], axis=0)]
    ppermute x1, waiting for transfers between devices: 5.34 us -> 0.01 us  [gather_rows(): far_half = lax.ppermute(forwarded, 'row', ring)]
    concatenate x2 -> x10, other arithmetic: 6.15 us -> 9.99 us  [the longest x9 8.26 us: shards(): jnp.concatenate([mine, theirs], axis=0)]
    add x2, other arithmetic: 0.03 us -> 3.27 us  [shards(): partial = partial + lax.ppermute(partial, 'row', pairs)]
  transfers between devices with their start and end apart: 9 -> 24, of which waited for: 6 -> 7; matrix products, arithmetic and copies ran while one was open for 30% -> 35% of each run, Pallas kernels for 0% -> 0%
where the time goes in v4:
time: 187 us; the launch traced here: 185 us
  other arithmetic  42.5 us (23%)
  starting transfers between devices  40 us (21%)
  waiting for transfers between devices  35.2 us (19%)
  local copies, waits for them, and re-layouts  28.7 us (15%)
  matrix products  24 us (13%)
  between operations  14.4 us (8%)
    ppermute x15, waiting for transfers between devices, shards(): received = lax.ppermute(factors, 'col', pairs)  34.5 us
    ppermute x15, starting transfers between devices, shards(): received = lax.ppermute(factors, 'col', pairs)  22.1 us
    dot_general x1, matrix products, shards(): base = jnp.dot(full_rows, weights, preferred_element_type=jnp.float32)  16.7 us
    concatenate x6, local copies, waits for them, and re-layouts, shards(): jnp.concatenate([mine, theirs], axis=0)  16 us
    select_n x3, other arithmetic, gather_rows(): jnp.where(relative == 0, own_block, jnp.where(relative == 1, after, jnp.w...  15.9 us
    ppermute x3, starting transfers between devices, shards(): partial = partial + lax.ppermute(partial, 'row', pairs)  8.39 us
    concatenate x9, other arithmetic, shards(): jnp.concatenate([mine, theirs], axis=0)  8.26 us
    unnamed x48, local copies, waits for them, and re-layouts  6.02 us
  transfers between devices with their start and end apart: 24, of which 7 were waited for; matrix products, arithmetic and copies ran while one was open for 35% of the time, Pallas kernels for 0%

profile of v4, /device:TPU:1, one launch (start us, length us, event | category | flops | bytes accessed | tf_op | source)
XLA Modules:
  0.0 184.8 jit_solution(2222157201283257832)
XLA Ops:
  7.2 1.7 pad_maximum_fusion.3
  9.0 3.3 %collective-permute-start = (bf16[1024,576]{0,1:T(8,128)(2,1)}, bf16[1024,576]{0,1:T(8,128)(2,1)S(1)}, u32[]{:S(2)}, u32[]{:S(2)}) collective-permute-start(bf16[1024,576]{0,1:T(8,128)(2,1)} %param.11), channel_id=1, source_target_pairs={{0,32},{32,0},{64,96},{96,64},{128,160},{160,128},{192,224},{224,1... | collective-permute-start | bytes 3538952 | tf_op jit(solution)/shard_map/gathers/ppermute | solution.py:74
  12.3 1.3 copy.40
  13.6 1.5 collective-permute-start.18
  15.0 1.3 copy.33
  17.1 1.2 and_select_fusion.1
  18.2 2.3 %maximum_select_fusion = bf16[1024,1152]{0,1:T(8,128)(2,1)S(1)} fusion(bf16[1024,576]{0,1:T(8,128)(2,1)S(1)} %collective-permute-done, bf16[1024,576]{0,1:T(8,128)(2,1)} %param.11, pred[]{:T(512)S(6)} %eq.95), kind=kLoop, calls=%fused_computation.17 | loop fusion | flops 10616832 | bytes 4718593 | tf_op jit(solution)/shard_map/gathers/jit(_where)/select_n | solution.py:75
  20.6 2.7 %collective-permute-start.1 = (bf16[1024,1152]{0,1:T(8,128)(2,1)S(1)}, bf16[1024,1152]{0,1:T(8,128)(2,1)}, u32[]{:S(2)}, u32[]{:S(2)}) collective-permute-start(bf16[1024,1152]{0,1:T(8,128)(2,1)S(1)} %maximum_select_fusion), channel_id=1, source_target_pairs={{0,64},{32,224},{64,128},{96,32},{128,192},{160,96},{192,0},{224,1... | collective-permute-start | bytes 7077896 | tf_op jit(solution)/shard_map/gathers/ppermute | solution.py:80
  25.7 1.8 multiply_cosine_fusion
  28.3 3.1 %collective-permute-start.6 = (bf16[2,576,32]{1,2,0:T(8,128)(2,1)S(1)}, bf16[2,576,32]{1,2,0:T(8,128)(2,1)S(1)}, u32[]{:S(2)}, u32[]{:S(2)}) collective-permute-start(bf16[2,576,32]{1,2,0:T(8,128)(2,1)S(1)} %pad_maximum_fusion.6), channel_id=1, source_target_pairs={{0,2},{1,3},{2,0},{3,1},{4,6},{5,7},{6,4},{7,5},{8,10},{9,11},{10,... | collective-permute-start | bytes 221192 | tf_op jit(solution)/shard_map/gathers/ppermute | solution.py:145
  32.1 5.4 %collective-permute-done.6 = bf16[2,576,32]{1,2,0:T(8,128)(2,1)S(1)} collective-permute-done((bf16[2,576,32]{1,2,0:T(8,128)(2,1)S(1)}, bf16[2,576,32]{1,2,0:T(8,128)(2,1)S(1)}, u32[]{:S(2)}, u32[]{:S(2)}) %collective-permute-start.6) | collective-permute-done | bytes 73760 | tf_op jit(solution)/shard_map/gathers/ppermute | solution.py:145
  38.3 4.9 %collective-permute-start.7 = (bf16[4,576,32]{1,2,0:T(8,128)(2,1)S(1)}, bf16[4,576,32]{1,2,0:T(8,128)(2,1)S(1)}, u32[]{:S(2)}, u32[]{:S(2)}) collective-permute-start(bf16[4,576,32]{1,2,0:T(8,128)(2,1)S(1)} %pad_maximum_fusion.4), channel_id=1, source_target_pairs={{0,4},{1,5},{2,6},{3,7},{4,0},{5,1},{6,2},{7,3},{8,12},{9,13},{10,... | collective-permute-start | bytes 442376 | tf_op jit(solution)/shard_map/gathers/ppermute | solution.py:145
  44.7 9.2 %collective-permute-done.7 = bf16[4,576,32]{1,2,0:T(8,128)(2,1)S(1)} collective-permute-done((bf16[4,576,32]{1,2,0:T(8,128)(2,1)S(1)}, bf16[4,576,32]{1,2,0:T(8,128)(2,1)S(1)}, u32[]{:S(2)}, u32[]{:S(2)}) %collective-permute-start.7) | collective-permute-done | bytes 147488 | tf_op jit(solution)/shard_map/gathers/ppermute | solution.py:145
  55.7 6.9 %collective-permute-done.8 = bf16[8,576,32]{1,2,0:T(8,128)(2,1)S(1)} collective-permute-done((bf16[8,576,32]{1,2,0:T(8,128)(2,1)S(1)}, bf16[8,576,32]{1,2,0:T(8,128)(2,1)S(1)}, u32[]{:S(2)}, u32[]{:S(2)}) %collective-permute-start.8) | collective-permute-done | bytes 294944 | tf_op jit(solution)/shard_map/gathers/ppermute | solution.py:145
  62.7 1.2 collective-permute-start.9
  63.9 1.3 constant_dynamic-slice_fusion
  65.7 3.0 %collective-permute-start.2 = (bf16[1024,1152]{0,1:T(8,128)(2,1)}, bf16[1024,1152]{0,1:T(8,128)(2,1)}, u32[]{:S(2)}, u32[]{:S(2)}) collective-permute-start(bf16[1024,1152]{0,1:T(8,128)(2,1)} %collective-permute-done.1), channel_id=1, source_target_pairs={{0,32},{32,0},{64,96},{96,64},{128,160},{160,128},{192,224},{224,1... | collective-permute-start | bytes 7077896 | tf_op jit(solution)/shard_map/gathers/ppermute | solution.py:84
  69.7 1.5 collective-permute-start.14
  72.0 1.1 collective-permute-start.19
  73.0 2.3 %collective-permute-done.14 = bf16[2,16,512]{2,0,1:T(2,128)(2,1)S(1)} collective-permute-done((bf16[2,16,512]{2,0,1:T(2,128)(2,1)S(1)}, bf16[2,16,512]{2,0,1:T(2,128)(2,1)S(1)}, u32[]{:S(2)}, u32[]{:S(2)}) %collective-permute-start.14) | collective-permute-done | bytes 32800 | tf_op jit(solution)/shard_map/gathers/ppermute | solution.py:145
  75.3 0.9 pad_maximum_fusion.7
  76.2 3.9 %collective-permute-start.15 = (bf16[4,16,512]{2,0,1:T(4,128)(2,1)S(1)}, bf16[4,16,512]{2,0,1:T(4,128)(2,1)S(1)}, u32[]{:S(2)}, u32[]{:S(2)}) collective-permute-start(bf16[4,16,512]{2,0,1:T(4,128)(2,1)S(1)} %pad_maximum_fusion.7), channel_id=1, source_target_pairs={{0,4},{1,5},{2,6},{3,7},{4,0},{5,1},{6,2},{7,3},{8,12},{9,13},{10,... | collective-permute-start | bytes 196616 | tf_op jit(solution)/shard_map/gathers/ppermute | solution.py:145
  81.0 1.6 collective-permute-start.20
  82.6 3.0 %collective-permute-done.15 = bf16[4,16,512]{2,0,1:T(4,128)(2,1)S(1)} collective-permute-done((bf16[4,16,512]{2,0,1:T(4,128)(2,1)S(1)}, bf16[4,16,512]{2,0,1:T(4,128)(2,1)S(1)}, u32[]{:S(2)}, u32[]{:S(2)}) %collective-permute-start.15) | collective-permute-done | bytes 65568 | tf_op jit(solution)/shard_map/gathers/ppermute | solution.py:145
  85.6 1.0 pad_maximum_fusion.5
  87.0 2.4 %fusion.16 = f32[1024,32]{0,1:T(8,128)} fusion(bf16[32,576,32]{1,2,0:T(8,128)(2,1)S(1)} %constant_dynamic-update-slice_fusion.5, pred[1024,32]{0,1:T(8,128)(4,1)S(1)} %copy-done.13, bf16[1024,576]{0,1:T(8,128)(2,1)S(1)} %copy-done.5), kind=kOutput, calls=%fused_computation.16 | convolution fusion | flops 1210023936 | bytes 2523136 | tf_op jit(solution)/shard_map/lowrank/tf,sfr->tsr/dot_general | solution.py:155
  89.4 7.0 %collective-permute-start.10 = (f32[1024,32]{0,1:T(8,128)}, f32[1024,32]{0,1:T(8,128)}, u32[]{:S(2)}, u32[]{:S(2)}) collective-permute-start(f32[1024,32]{0,1:T(8,128)} %fusion.16), channel_id=1, source_target_pairs={{0,32},{32,0},{64,96},{96,64},{128,160},{160,128},{192,224},{224,1... | collective-permute-start | bytes 393224 | tf_op jit(solution)/shard_map/lowrank/ppermute | solution.py:162
  97.6 1.4 pad_maximum_fusion.8
  99.1 3.3 %concatenate.100 = bf16[16,16,512]{2,0,1:T(8,128)(2,1)} concatenate(bf16[1,16,512]{2,0,1:T(2,128)(2,1)} %copy.33, bf16[1,16,512]{2,0,1:T(2,128)(2,1)} %collective-permute-done.13, bf16[2,16,512]{2,0,1:T(2,128)(2,1)} %copy-done.7, bf16[4,16,512]{2,0,1:T(4,128)(2,1)} %copy-done.6, bf16[8,16,512]{2,0,1:T(8,128)(2,1)} %collective-permute-done.16), dimensions={0} | concatenate | bytes 524288 | tf_op jit(solution)/shard_map/gathers/concatenate | solution.py:147
  102.4 3.0 %collective-permute-start.17 = (bf16[16,16,512]{2,0,1:T(8,128)(2,1)}, bf16[16,16,512]{2,0,1:T(8,128)(2,1)}, u32[]{:S(2)}, u32[]{:S(2)}) collective-permute-start(bf16[16,16,512]{2,0,1:T(8,128)(2,1)} %concatenate.100), channel_id=1, source_target_pairs={{0,16},{1,17},{2,18},{3,19},{4,20},{5,21},{6,22},{7,23},{8,24},{9,... | collective-permute-start | bytes 786440 | tf_op jit(solution)/shard_map/gathers/ppermute | solution.py:145
  105.3 1.6 add.125
  107.7 3.0 %concatenate.107 = bf16[16,16,256]{2,0,1:T(8,128)(2,1)} concatenate(bf16[1,16,256]{2,0,1:T(2,128)(2,1)} %copy.40, bf16[1,16,256]{2,0,1:T(2,128)(2,1)} %collective-permute-done.18, bf16[2,16,256]{2,0,1:T(2,128)(2,1)} %copy-done.10, bf16[4,16,256]{2,0,1:T(4,128)(2,1)} %copy-done.8, bf16[8,16,256]{2,0,1:T(8,128)(2,1)} %collective-permute-done.21), dimensions={0} | concatenate | bytes 262144 | tf_op jit(solution)/shard_map/gathers/concatenate | solution.py:147
  111.4 1.6 add.126
  113.0 1.4 collective-permute-start.12
  114.4 1.3 fusion.31
  115.7 7.8 %collective-permute-done.22 = bf16[16,16,256]{2,0,1:T(8,128)(2,1)} collective-permute-done((bf16[16,16,256]{2,0,1:T(8,128)(2,1)}, bf16[16,16,256]{2,0,1:T(8,128)(2,1)}, u32[]{:S(2)}, u32[]{:S(2)}) %collective-permute-start.22) | collective-permute-done | bytes 131104 | tf_op jit(solution)/shard_map/gathers/ppermute | solution.py:145
  123.5 4.6 %concatenate.108 = bf16[32,16,256]{2,0,1:T(8,128)(2,1)} concatenate(bf16[1,16,256]{2,0,1:T(2,128)(2,1)} %copy.40, bf16[1,16,256]{2,0,1:T(2,128)(2,1)} %collective-permute-done.18, bf16[2,16,256]{2,0,1:T(2,128)(2,1)} %copy-done.10, bf16[4,16,256]{2,0,1:T(4,128)(2,1)} %copy-done.8, bf16[8,16,256]{2,0,1:T(8,128)(2,1)} %collective-permute-done.21, ...), dimensions={0} | concatenate | bytes 524288 | tf_op jit(solution)/shard_map/gathers/concatenate | solution.py:147
  128.0 5.0 %concatenate.101 = bf16[32,16,512]{2,0,1:T(8,128)(2,1)} concatenate(bf16[1,16,512]{2,0,1:T(2,128)(2,1)} %copy.33, bf16[1,16,512]{2,0,1:T(2,128)(2,1)} %collective-permute-done.13, bf16[2,16,512]{2,0,1:T(2,128)(2,1)} %copy-done.7, bf16[4,16,512]{2,0,1:T(4,128)(2,1)} %copy-done.6, bf16[8,16,512]{2,0,1:T(8,128)(2,1)} %collective-permute-done.16, ...), dimensions={0} | concatenate | bytes 1048576 | tf_op jit(solution)/shard_map/gathers/concatenate | solution.py:147
  133.0 1.0 add_convert_fusion.2
  134.6 5.8 %select_select_fusion.3 = (bf16[1024,1152]{0,1:T(8,128)(2,1)}, bf16[1024,1152]{0,1:T(8,128)(2,1)S(1)}, bf16[1024,1152]{0,1:T(8,128)(2,1)S(1)}) fusion(bf16[1024,1152]{0,1:T(8,128)(2,1)S(1)} %maximum_select_fusion, pred[]{:T(512)S(6)} %eq.97, pred[]{:T(512)S(6)} %eq.96, pred[]{:T(512)S(6)} %eq.94, bf16[512,1152]{0,1:T(8,128)(2,1)S(1)} %collective-permute-done.3, ...), kind=kLoop, calls=%fused_computation.22 | loop fusion | flops 16515072 | bytes 16515076 | tf_op jit(solution)/shard_map/gathers/jit(_where)/select_n | solution.py:97
  140.4 4.7 %select_select_fusion.1 = bf16[1024,1152]{0,1:T(8,128)(2,1)} fusion(bf16[1024,1152]{0,1:T(8,128)(2,1)S(1)} %maximum_select_fusion, bf16[1024,1152]{0,1:T(8,128)(2,1)S(1)} %get-tuple-element.11, bf16[1024,1152]{0,1:T(8,128)(2,1)S(1)} %get-tuple-element.10, pred[]{:T(512)S(6)} %eq.103, pred[]{:T(512)S(6)} %eq.102, pred[]{:T(512)S(6)} %eq.101, ...), kind=kLoop, calls=%fused_computation.20 | loop fusion | flops 14155776 | bytes 11796484 | tf_op jit(solution)/shard_map/gathers/jit(_where)/select_n | solution.py:97
  145.1 5.4 %select_select_fusion.2 = (bf16[1024,1152]{0,1:T(8,128)(2,1)}, bf16[1024,1152]{0,1:T(8,128)(2,1)}) fusion(bf16[1024,1152]{0,1:T(8,128)(2,1)S(1)} %maximum_select_fusion, bf16[1024,1152]{0,1:T(8,128)(2,1)S(1)} %get-tuple-element.11, bf16[1024,1152]{0,1:T(8,128)(2,1)S(1)} %get-tuple-element.10, pred[]{:T(512)S(6)} %eq.100, pred[]{:T(512)S(6)} %eq.99, ...), kind=kLoop, calls=%fused_computation.21 | loop fusion | flops 17694720 | bytes 14155783 | tf_op jit(solution)/shard_map/gathers/jit(_where)/select_n | solution.py:97
  150.6 16.7 %fusion = f32[1024,1024]{0,1:T(8,128)} fusion(bf16[4608,1024]{1,0:T(8,128)(2,1)} %all-gather.2.cloned.1.call-done, bf16[1024,1152]{0,1:T(8,128)(2,1)} %get-tuple-element.13, bf16[1024,1152]{0,1:T(8,128)(2,1)} %select_select_fusion.1, bf16[1024,1152]{0,1:T(8,128)(2,1)} %get-tuple-element.12, bf16[1024,1152]{0,1:T(8,128)(2,1)} %get-tuple-element.9), kind=kOutput, calls=%fused_computation.1 | convolution fusion | flops 9701425152 | bytes 23068672 | tf_op jit(solution)/shard_map/projection/dot_general | solution.py:184
  167.3 1.2 slice-done
  168.8 1.0 copy-done.1
  170.3 3.6 %fusion.13 = bf16[2304,512]{1,0:T(8,128)(2,1)S(1)} fusion(s32[2304]{0:T(1024)S(1)} %clamp_bitcast_fusion, pred[2304]{0:T(1024)(128)(4,1)S(1)} %copy-done.15, bf16[1024,256]{0,1:T(8,128)(2,1)S(1)} %fusion.18, bf16[1024,256]{0,1:T(8,128)(2,1)S(1)} %bitcast.60), kind=kOutput, calls=%fused_computation.14 | convolution fusion | flops 2423914496 | bytes 3419392 | tf_op jit(solution)/shard_map/cache_write/dot_general | solution.py:207
  173.9 1.6 fusion.40
  176.7 1.3 copy.41
  (105 shorter events, 17.4 us)
Async XLA Ops:
  7.2 17.2 %copy-start = (s32[32]{0:T(128)S(1)}, s32[32]{0:T(128)}, u32[]{:S(2)}) copy-start(s32[32]{0:T(128)} %param.20) | copy-start | bytes 388
  7.2 143.3 %all-gather.2.cloned.1.call-start = ((), (), s32[]{:S(2)}) async-start(), calls=%async_computation | async-start | bytes 9732096 | tf_op jit(solution)/shard_map/gathers/all_gather | solution.py:138
  9.0 9.3 %collective-permute-start = (bf16[1024,576]{0,1:T(8,128)(2,1)}, bf16[1024,576]{0,1:T(8,128)(2,1)S(1)}, u32[]{:S(2)}, u32[]{:S(2)}) collective-permute-start(bf16[1024,576]{0,1:T(8,128)(2,1)} %param.11), channel_id=1, source_target_pairs={{0,32},{32,0},{64,96},{96,64},{128,160},{160,128},{192,224},{224,1... | collective-permute-start | bytes 3538952 | tf_op jit(solution)/shard_map/gathers/ppermute | solution.py:74
  12.3 15.2 %collective-permute-start.5 = (bf16[1,576,32]{1,2,0:T(8,128)(2,1)}, bf16[1,576,32]{1,2,0:T(8,128)(2,1)}, u32[]{:S(2)}, u32[]{:S(2)}) collective-permute-start(bf16[1,576,32]{1,2,0:T(8,128)(2,1)} %param.15), channel_id=1, source_target_pairs={{0,1},{1,0},{2,3},{3,2},{4,5},{5,4},{6,7},{7,6},{8,9},{9,8},{10,11... | collective-permute-start | bytes 110600 | tf_op jit(solution)/shard_map/gathers/ppermute | solution.py:145
  13.6 57.6 %collective-permute-start.18 = (bf16[1,16,256]{2,0,1:T(2,128)(2,1)}, bf16[1,16,256]{2,0,1:T(2,128)(2,1)}, u32[]{:S(2)}, u32[]{:S(2)}) collective-permute-start(bf16[1,16,256]{2,0,1:T(2,128)(2,1)} %copy.40), channel_id=1, source_target_pairs={{0,1},{1,0},{2,3},{3,2},{4,5},{5,4},{6,7},{7,6},{8,9},{9,8},{10,11... | collective-permute-start | bytes 24584 | tf_op jit(solution)/shard_map/gathers/ppermute | solution.py:145
  16.4 52.4 %collective-permute-start.13 = (bf16[1,16,512]{2,0,1:T(2,128)(2,1)}, bf16[1,16,512]{2,0,1:T(2,128)(2,1)}, u32[]{:S(2)}, u32[]{:S(2)}) collective-permute-start(bf16[1,16,512]{2,0,1:T(2,128)(2,1)} %copy.33), channel_id=1, source_target_pairs={{0,1},{1,0},{2,3},{3,2},{4,5},{5,4},{6,7},{7,6},{8,9},{9,8},{10,11... | collective-permute-start | bytes 49160 | tf_op jit(solution)/shard_map/gathers/ppermute | solution.py:145
  18.2 5.9 %copy-start.16 = (s32[1,10]{1,0:T(1,128)S(1)}, s32[1,10]{1,0:T(1,128)}, u32[]{:S(2)}) copy-start(s32[1,10]{1,0:T(1,128)} %param.18) | copy-start | bytes 124
  18.2 6.8 %copy-start.20 = (s32[1,10]{1,0:T(1,128)S(1)}, s32[1,10]{1,0:T(1,128)}, u32[]{:S(2)}) copy-start(s32[1,10]{1,0:T(1,128)} %param.19) | copy-start | bytes 124
  20.6 43.3 %collective-permute-start.1 = (bf16[1024,1152]{0,1:T(8,128)(2,1)S(1)}, bf16[1024,1152]{0,1:T(8,128)(2,1)}, u32[]{:S(2)}, u32[]{:S(2)}) collective-permute-start(bf16[1024,1152]{0,1:T(8,128)(2,1)S(1)} %maximum_select_fusion), channel_id=1, source_target_pairs={{0,64},{32,224},{64,128},{96,32},{128,192},{160,96},{192,0},{224,1... | collective-permute-start | bytes 7077896 | tf_op jit(solution)/shard_map/gathers/ppermute | solution.py:80
  24.2 3.3 %copy-start.17 = (s32[10,1]{0,1:T(1,128)}, s32[10,1]{0,1:T(1,128)S(1)}, u32[]{:S(2)}) copy-start(s32[10,1]{0,1:T(1,128)S(1)} %reduce-window.9) | copy-start | bytes 124
  28.3 9.1 %collective-permute-start.6 = (bf16[2,576,32]{1,2,0:T(8,128)(2,1)S(1)}, bf16[2,576,32]{1,2,0:T(8,128)(2,1)S(1)}, u32[]{:S(2)}, u32[]{:S(2)}) collective-permute-start(bf16[2,576,32]{1,2,0:T(8,128)(2,1)S(1)} %pad_maximum_fusion.6), channel_id=1, source_target_pairs={{0,2},{1,3},{2,0},{3,1},{4,6},{5,7},{6,4},{7,5},{8,10},{9,11},{10,... | collective-permute-start | bytes 221192 | tf_op jit(solution)/shard_map/gathers/ppermute | solution.py:145
  38.3 15.6 %collective-permute-start.7 = (bf16[4,576,32]{1,2,0:T(8,128)(2,1)S(1)}, bf16[4,576,32]{1,2,0:T(8,128)(2,1)S(1)}, u32[]{:S(2)}, u32[]{:S(2)}) collective-permute-start(bf16[4,576,32]{1,2,0:T(8,128)(2,1)S(1)} %pad_maximum_fusion.4), channel_id=1, source_target_pairs={{0,4},{1,5},{2,6},{3,7},{4,0},{5,1},{6,2},{7,3},{8,12},{9,13},{10,... | collective-permute-start | bytes 442376 | tf_op jit(solution)/shard_map/gathers/ppermute | solution.py:145
  44.7 24.0 %copy-start.18 = (s32[10,1]{0,1:T(1,128)S(1)}, s32[10,1]{0,1:T(1,128)}, u32[]{:S(2)}) copy-start(s32[10,1]{0,1:T(1,128)} %copy-done.17) | copy-start | bytes 124
  44.7 24.0 %copy-start.19 = (s32[10]{0:T(128)S(1)}, s32[10]{0:T(128)}, u32[]{:S(2)}) copy-start(s32[10]{0:T(128)} %get-tuple-element.38) | copy-start | bytes 124
  54.8 7.8 %collective-permute-start.8 = (bf16[8,576,32]{1,2,0:T(8,128)(2,1)S(1)}, bf16[8,576,32]{1,2,0:T(8,128)(2,1)S(1)}, u32[]{:S(2)}, u32[]{:S(2)}) collective-permute-start(bf16[8,576,32]{1,2,0:T(8,128)(2,1)S(1)} %pad_maximum_fusion.2), channel_id=1, source_target_pairs={{0,8},{1,9},{2,10},{3,11},{4,12},{5,13},{6,14},{7,15},{8,0},{9,1},... | collective-permute-start | bytes 884744 | tf_op jit(solution)/shard_map/gathers/ppermute | solution.py:145
  62.7 24.3 %copy-start.5 = (bf16[1024,576]{0,1:T(8,128)(2,1)S(1)}, bf16[1024,576]{0,1:T(8,128)(2,1)}, u32[]{:S(2)}) copy-start(bf16[1024,576]{0,1:T(8,128)(2,1)} %param.11) | copy-start | bytes 3538948
  62.7 24.3 %copy-start.13 = (pred[1024,32]{0,1:T(8,128)(4,1)S(1)}, pred[1024,32]{0,1:T(8,128)(4,1)}, u32[]{:S(2)}) copy-start(pred[1024,32]{0,1:T(8,128)(4,1)} %get-tuple-element.35) | copy-start | bytes 98308
  62.7 24.1 %collective-permute-start.9 = (bf16[16,576,32]{1,2,0:T(8,128)(2,1)S(1)}, bf16[16,576,32]{1,2,0:T(8,128)(2,1)S(1)}, u32[]{:S(2)}, u32[]{:S(2)}) collective-permute-start(bf16[16,576,32]{1,2,0:T(8,128)(2,1)S(1)} %get-tuple-element.20), channel_id=1, source_target_pairs={{0,16},{1,17},{2,18},{3,19},{4,20},{5,21},{6,22},{7,23},{8,24},{9,... | collective-permute-start | bytes 1769480 | tf_op jit(solution)/shard_map/gathers/ppermute | solution.py:145
  65.3 31.2 %collective-permute-start.3 = (bf16[512,1152]{0,1:T(8,128)(2,1)S(1)}, bf16[512,1152]{0,1:T(8,128)(2,1)S(1)}, u32[]{:S(2)}, u32[]{:S(2)}) collective-permute-start(bf16[512,1152]{0,1:T(8,128)(2,1)S(1)} %constant_dynamic-slice_fusion), channel_id=1, source_target_pairs={{0,64},{32,224},{64,128},{96,32},{128,192},{160,96},{192,0},{224,1... | collective-permute-start | bytes 3538952 | tf_op jit(solution)/shard_map/gathers/ppermute | solution.py:83
  65.7 68.9 %collective-permute-start.2 = (bf16[1024,1152]{0,1:T(8,128)(2,1)}, bf16[1024,1152]{0,1:T(8,128)(2,1)}, u32[]{:S(2)}, u32[]{:S(2)}) collective-permute-start(bf16[1024,1152]{0,1:T(8,128)(2,1)} %collective-permute-done.1), channel_id=1, source_target_pairs={{0,32},{32,0},{64,96},{96,64},{128,160},{160,128},{192,224},{224,1... | collective-permute-start | bytes 7077896 | tf_op jit(solution)/shard_map/gathers/ppermute | solution.py:84
  69.7 5.6 %collective-permute-start.14 = (bf16[2,16,512]{2,0,1:T(2,128)(2,1)S(1)}, bf16[2,16,512]{2,0,1:T(2,128)(2,1)S(1)}, u32[]{:S(2)}, u32[]{:S(2)}) collective-permute-start(bf16[2,16,512]{2,0,1:T(2,128)(2,1)S(1)} %pad_maximum_fusion.9), channel_id=1, source_target_pairs={{0,2},{1,3},{2,0},{3,1},{4,6},{5,7},{6,4},{7,5},{8,10},{9,11},{10,... | collective-permute-start | bytes 98312 | tf_op jit(solution)/shard_map/gathers/ppermute | solution.py:145
  72.0 8.2 %collective-permute-start.19 = (bf16[2,16,256]{2,0,1:T(2,128)(2,1)S(1)}, bf16[2,16,256]{2,0,1:T(2,128)(2,1)S(1)}, u32[]{:S(2)}, u32[]{:S(2)}) collective-permute-start(bf16[2,16,256]{2,0,1:T(2,128)(2,1)S(1)} %pad_maximum_fusion.11), channel_id=1, source_target_pairs={{0,2},{1,3},{2,0},{3,1},{4,6},{5,7},{6,4},{7,5},{8,10},{9,11},{10,... | collective-permute-start | bytes 49160 | tf_op jit(solution)/shard_map/gathers/ppermute | solution.py:145
  75.3 11.6 %copy-start.7 = (bf16[2,16,512]{2,0,1:T(2,128)(2,1)}, bf16[2,16,512]{2,0,1:T(2,128)(2,1)S(1)}, u32[]{:S(2)}) copy-start(bf16[2,16,512]{2,0,1:T(2,128)(2,1)S(1)} %collective-permute-done.14) | copy-start | bytes 98308
  76.2 9.4 %collective-permute-start.15 = (bf16[4,16,512]{2,0,1:T(4,128)(2,1)S(1)}, bf16[4,16,512]{2,0,1:T(4,128)(2,1)S(1)}, u32[]{:S(2)}, u32[]{:S(2)}) collective-permute-start(bf16[4,16,512]{2,0,1:T(4,128)(2,1)S(1)} %pad_maximum_fusion.7), channel_id=1, source_target_pairs={{0,4},{1,5},{2,6},{3,7},{4,0},{5,1},{6,2},{7,3},{8,12},{9,13},{10,... | collective-permute-start | bytes 196616 | tf_op jit(solution)/shard_map/gathers/ppermute | solution.py:145
  80.2 16.8 %copy-start.10 = (bf16[2,16,256]{2,0,1:T(2,128)(2,1)}, bf16[2,16,256]{2,0,1:T(2,128)(2,1)S(1)}, u32[]{:S(2)}) copy-start(bf16[2,16,256]{2,0,1:T(2,128)(2,1)S(1)} %collective-permute-done.19) | copy-start | bytes 49156
  81.0 16.0 %collective-permute-start.20 = (bf16[4,16,256]{2,0,1:T(4,128)(2,1)S(1)}, bf16[4,16,256]{2,0,1:T(4,128)(2,1)S(1)}, u32[]{:S(2)}, u32[]{:S(2)}) collective-permute-start(bf16[4,16,256]{2,0,1:T(4,128)(2,1)S(1)} %pad_maximum_fusion.10), channel_id=1, source_target_pairs={{0,4},{1,5},{2,6},{3,7},{4,0},{5,1},{6,2},{7,3},{8,12},{9,13},{10,... | collective-permute-start | bytes 98312 | tf_op jit(solution)/shard_map/gathers/ppermute | solution.py:145
  85.6 1.4 copy-start.6
  86.6 12.5 %collective-permute-start.16 = (bf16[8,16,512]{2,0,1:T(8,128)(2,1)S(1)}, bf16[8,16,512]{2,0,1:T(8,128)(2,1)}, u32[]{:S(2)}, u32[]{:S(2)}) collective-permute-start(bf16[8,16,512]{2,0,1:T(8,128)(2,1)S(1)} %pad_maximum_fusion.5), channel_id=1, source_target_pairs={{0,8},{1,9},{2,10},{3,11},{4,12},{5,13},{6,14},{7,15},{8,0},{9,1},... | collective-permute-start | bytes 393224 | tf_op jit(solution)/shard_map/gathers/ppermute | solution.py:145
  89.4 15.9 %collective-permute-start.10 = (f32[1024,32]{0,1:T(8,128)}, f32[1024,32]{0,1:T(8,128)}, u32[]{:S(2)}, u32[]{:S(2)}) collective-permute-start(f32[1024,32]{0,1:T(8,128)} %fusion.16), channel_id=1, source_target_pairs={{0,32},{32,0},{64,96},{96,64},{128,160},{160,128},{192,224},{224,1... | collective-permute-start | bytes 393224 | tf_op jit(solution)/shard_map/lowrank/ppermute | solution.py:162
  96.5 38.2 %collective-permute-start.4 = (bf16[512,1152]{0,1:T(8,128)(2,1)S(1)}, bf16[512,1152]{0,1:T(8,128)(2,1)}, u32[]{:S(2)}, u32[]{:S(2)}) collective-permute-start(bf16[512,1152]{0,1:T(8,128)(2,1)S(1)} %collective-permute-done.3), channel_id=1, source_target_pairs={{0,32},{32,0},{64,96},{96,64},{128,160},{160,128},{192,224},{224,1... | collective-permute-start | bytes 3538952 | tf_op jit(solution)/shard_map/gathers/ppermute | solution.py:84
  97.0 0.6 copy-start.8
  99.1 8.6 %collective-permute-start.21 = (bf16[8,16,256]{2,0,1:T(8,128)(2,1)}, bf16[8,16,256]{2,0,1:T(8,128)(2,1)}, u32[]{:S(2)}, u32[]{:S(2)}) collective-permute-start(bf16[8,16,256]{2,0,1:T(8,128)(2,1)} %pad_maximum_fusion.8), channel_id=1, source_target_pairs={{0,8},{1,9},{2,10},{3,11},{4,12},{5,13},{6,14},{7,15},{8,0},{9,1},... | collective-permute-start | bytes 196616 | tf_op jit(solution)/shard_map/gathers/ppermute | solution.py:145
  102.4 25.7 %collective-permute-start.17 = (bf16[16,16,512]{2,0,1:T(8,128)(2,1)}, bf16[16,16,512]{2,0,1:T(8,128)(2,1)}, u32[]{:S(2)}, u32[]{:S(2)}) collective-permute-start(bf16[16,16,512]{2,0,1:T(8,128)(2,1)} %concatenate.100), channel_id=1, source_target_pairs={{0,16},{1,17},{2,18},{3,19},{4,20},{5,21},{6,22},{7,23},{8,24},{9,... | collective-permute-start | bytes 786440 | tf_op jit(solution)/shard_map/gathers/ppermute | solution.py:145
  107.0 4.4 %collective-permute-start.11 = (f32[1024,32]{0,1:T(8,128)}, f32[1024,32]{0,1:T(8,128)}, u32[]{:S(2)}, u32[]{:S(2)}) collective-permute-start(f32[1024,32]{0,1:T(8,128)} %add.125), channel_id=1, source_target_pairs={{0,64},{32,96},{64,0},{96,32},{128,192},{160,224},{192,128},{224,1... | collective-permute-start | bytes 393224 | tf_op jit(solution)/shard_map/lowrank/ppermute | solution.py:162
  110.7 12.7 %collective-permute-start.22 = (bf16[16,16,256]{2,0,1:T(8,128)(2,1)}, bf16[16,16,256]{2,0,1:T(8,128)(2,1)}, u32[]{:S(2)}, u32[]{:S(2)}) collective-permute-start(bf16[16,16,256]{2,0,1:T(8,128)(2,1)} %concatenate.107), channel_id=1, source_target_pairs={{0,16},{1,17},{2,18},{3,19},{4,20},{5,21},{6,22},{7,23},{8,24},{9,... | collective-permute-start | bytes 393224 | tf_op jit(solution)/shard_map/gathers/ppermute | solution.py:145
  113.0 20.0 %collective-permute-start.12 = (f32[1024,32]{0,1:T(8,128)}, f32[1024,32]{0,1:T(8,128)}, u32[]{:S(2)}, u32[]{:S(2)}) collective-permute-start(f32[1024,32]{0,1:T(8,128)} %add.126), channel_id=1, source_target_pairs={{0,128},{32,160},{64,192},{96,224},{128,0},{160,32},{192,64},{224,... | collective-permute-start | bytes 393224 | tf_op jit(solution)/shard_map/lowrank/ppermute | solution.py:162
  150.5 16.8 %copy-start.2 = (f32[1024,64]{0,1:T(8,128)S(1)}, f32[1024,64]{0,1:T(8,128)}, u32[]{:S(2)}) copy-start(f32[1024,64]{0,1:T(8,128)} %get-tuple-element.32) | copy-start | bytes 786436
  150.5 16.8 %copy-start.3 = (f32[1024,64]{0,1:T(8,128)S(1)}, f32[1024,64]{0,1:T(8,128)}, u32[]{:S(2)}) copy-start(f32[1024,64]{0,1:T(8,128)} %get-tuple-element.33) | copy-start | bytes 786436
  150.5 18.2 %copy-start.9 = (bf16[1024,32]{0,1:T(8,128)(2,1)S(1)}, bf16[1024,32]{0,1:T(8,128)(2,1)}, u32[]{:S(2)}) copy-start(bf16[1024,32]{0,1:T(8,128)(2,1)} %get-tuple-element.34) | copy-start | bytes 196612
  150.5 18.2 %copy-start.11 = (bf16[32,16,256]{2,0,1:T(8,128)(2,1)S(1)}, bf16[32,16,256]{2,0,1:T(8,128)(2,1)}, u32[]{:S(2)}) copy-start(bf16[32,16,256]{2,0,1:T(8,128)(2,1)} %concatenate.108) | copy-start | bytes 786436
  150.6 18.2 %copy-start.14 = (bf16[1024,16]{0,1:T(8,128)(2,1)S(1)}, bf16[1024,16]{0,1:T(8,128)(2,1)}, u32[]{:S(2)}) copy-start(bf16[1024,16]{0,1:T(8,128)(2,1)} %get-tuple-element.26) | copy-start | bytes 98308
  167.3 1.2 slice-start
  167.3 2.5 %copy-start.1 = (f32[1024,1024]{0,1:T(8,128)S(1)}, f32[1024,1024]{0,1:T(8,128)}, u32[]{:S(2)}) copy-start(f32[1024,1024]{0,1:T(8,128)} %fusion) | copy-start | bytes 12582916
  168.5 1.8 copy-start.15
  173.9 1.6 copy-start.4
  173.9 1.6 copy-start.12
Sparse Core Ops, SparseCore 0:
  11.1 128.1 all-gather.1

commit v5 on v3

--- a/solution.py
+++ b/solution.py
@@ -164,6 +164,7 @@
             preferred_element_type=jnp.float32,
         ).reshape(hidden.shape[0], adapter_count, -1)
         partial = jnp.sum(jnp.where(onehot[:, :, None], partial_all, 0.0), axis=1)
+        partial, full_rows, packed = lax.optimization_barrier((partial, full_rows, packed))
         distance = 1
         while distance < row_size:
             pairs = [(i, i ^ distance) for i in range(row_size)]
@@ -189,15 +190,22 @@
         )
 
     with jax.named_scope("projection"):
-        base = jnp.einsum(
-            "tci,cin->tn",
-            full_rows.reshape(full_rows.shape[0], packed.shape[0], feature_rows),
-            weights,
-            preferred_element_type=jnp.float32,
-        )
-        base_query = base[:, :query_width]
-        base_key = base[:, query_width : query_width + key_width]
-        base_value = base[:, query_width + key_width :]
+        stacked_rows = full_rows.reshape(full_rows.shape[0], packed.shape[0], feature_rows)
+        bases = []
+        for first, last in (
+            (0, query_width),
+            (query_width, query_width + key_width),
+            (query_width + key_width, weight_width),
+        ):
+            bases.append(
+                jnp.einsum(
+                    "tci,cin->tn",
+                    stacked_rows,
+                    packed[:, :feature_rows, first:last],
+                    preferred_element_type=jnp.float32,
+                )
+            )
+        base_query, base_key, base_value = lax.optimization_barrier(tuple(bases))
 
     with jax.named_scope("rotary"):
         half_width = HEAD // 2

time: 181 us -> 193 us (1.066)
  other arithmetic: 35.2 us -> 43.4 us
  matrix products: 22.7 us -> 25.9 us
  local copies, waits for them, and re-layouts: 14.4 us -> 17.3 us
  waiting for transfers between devices: 76.5 us -> 74 us
    concatenate x2, other arithmetic: 0.11 us -> 2.84 us  [rotate(): jnp.concatenate([leading * cosine - second * sine_value, second * cosine...]
    reshape x0 -> x2, local copies, waits for them, and re-layouts: none -> 2.47 us  [rotate(): shaped = values.reshape(values.shape[0], -1, HEAD)]
    another operation x4, other arithmetic: 2.73 us -> 4.99 us
    dot_general x1 -> x3, matrix products: 12.5 us -> 14.5 us  [shards(): jnp.einsum('tci,cin->tn', stacked_rows, packed[:, :feature_rows, first:la...]
    unnamed x32 -> x34, local copies, waits for them, and re-layouts: 4.56 us -> 5.94 us
  transfers between devices with their start and end apart: 9 -> 9, of which waited for: 6 -> 5; matrix products, arithmetic and copies ran while one was open for 30% -> 26% of each run, Pallas kernels for 0% -> 0%
where the time goes in v5:
time: 193 us; the launch traced here: 192 us
  waiting for transfers between devices  74 us (38%)
  other arithmetic  43.4 us (22%)
  matrix products  25.9 us (13%)
  local copies, waits for them, and re-layouts  17.3 us (9%)
  starting transfers between devices  17 us (9%)
  between operations  14.3 us (7%)
    all_gather x1, waiting for transfers between devices, shards(): packed = lax.all_gather(jnp.concatenate(pieces, axis=0), 'col', axis=0)  37.3 us
    ppermute x1, waiting for transfers between devices, gather_rows(): near = lax.ppermute(own_block, 'row', ring)  26.5 us
    dot_general x3, matrix products, shards(): jnp.einsum('tci,cin->tn', stacked_rows, packed[:, :feature_rows, first:la...  14.5 us
    select_n x3, other arithmetic, gather_rows(): jnp.where(relative == 0, own_block, jnp.where(relative == 1, after, jnp.w...  13 us
    unnamed x34, local copies, waits for them, and re-layouts  5.94 us
    ppermute x3, starting transfers between devices, shards(): partial = partial + lax.ppermute(partial, 'row', pairs)  5.75 us
    ppermute x1, waiting for transfers between devices, gather_rows(): far_half = lax.ppermute(forwarded, 'row', ring)  5.34 us
    another operation x4, other arithmetic  4.99 us
  transfers between devices with their start and end apart: 9, of which 5 were waited for; matrix products, arithmetic and copies ran while one was open for 26% of the time, Pallas kernels for 0%

profile of v5, /device:TPU:1, one launch (start us, length us, event | category | flops | bytes accessed | tf_op | source)
XLA Modules:
  0.0 192.0 jit_solution(8324283230484853370)
XLA Ops:
  7.2 0.7 reshape.329
  8.7 1.8 fusion.35
  10.5 3.3 %collective-permute-start = (bf16[1024,576]{0,1:T(8,128)(2,1)}, bf16[1024,576]{0,1:T(8,128)(2,1)S(1)}, u32[]{:S(2)}, u32[]{:S(2)}) collective-permute-start(bf16[1024,576]{0,1:T(8,128)(2,1)} %param.11), channel_id=1, source_target_pairs={{0,32},{32,0},{64,96},{96,64},{128,160},{160,128},{192,224},{224,1... | collective-permute-start | bytes 3538952 | tf_op jit(solution)/shard_map/gathers/ppermute | solution.py:74
  13.8 2.7 %collective-permute-done = bf16[1024,576]{0,1:T(8,128)(2,1)S(1)} collective-permute-done((bf16[1024,576]{0,1:T(8,128)(2,1)}, bf16[1024,576]{0,1:T(8,128)(2,1)S(1)}, u32[]{:S(2)}, u32[]{:S(2)}) %collective-permute-start) | collective-permute-done | bytes 1179680 | tf_op jit(solution)/shard_map/gathers/ppermute | solution.py:74
  16.5 2.3 %maximum_select_fusion = bf16[1024,1152]{0,1:T(8,128)(2,1)S(1)} fusion(bf16[1024,576]{0,1:T(8,128)(2,1)S(1)} %collective-permute-done, bf16[1024,576]{0,1:T(8,128)(2,1)} %param.11, pred[]{:T(512)S(6)} %eq.98), kind=kLoop, calls=%fused_computation.11 | loop fusion | flops 10616832 | bytes 4718593 | tf_op jit(solution)/shard_map/gathers/jit(_where)/select_n | solution.py:75
  18.8 1.1 collective-permute-start.1
  20.4 26.5 %collective-permute-done.1 = bf16[1024,1152]{0,1:T(8,128)(2,1)} collective-permute-done((bf16[1024,1152]{0,1:T(8,128)(2,1)S(1)}, bf16[1024,1152]{0,1:T(8,128)(2,1)}, u32[]{:S(2)}, u32[]{:S(2)}) %collective-permute-start.1) | collective-permute-done | bytes 2359328 | tf_op jit(solution)/shard_map/gathers/ppermute | solution.py:80
  47.0 2.4 %constant_dynamic-slice_fusion = bf16[512,1152]{0,1:T(8,128)(2,1)} fusion(bf16[1024,1152]{0,1:T(8,128)(2,1)} %collective-permute-done.1, s32[]{:T(128)S(6)} %select_n.183), kind=kLoop, calls=%fused_computation.95 | loop fusion | bytes 2359300 | tf_op jit(solution)/shard_map/gathers/dynamic_slice | solution.py:82
  49.4 2.2 %collective-permute-start.3 = (bf16[512,1152]{0,1:T(8,128)(2,1)}, bf16[512,1152]{0,1:T(8,128)(2,1)S(1)}, u32[]{:S(2)}, u32[]{:S(2)}) collective-permute-start(bf16[512,1152]{0,1:T(8,128)(2,1)} %constant_dynamic-slice_fusion), channel_id=1, source_target_pairs={{0,64},{32,224},{64,128},{96,32},{128,192},{160,96},{192,0},{224,1... | collective-permute-start | bytes 3538952 | tf_op jit(solution)/shard_map/gathers/ppermute | solution.py:83
  52.1 0.8 reduce-window.9
  54.4 1.2 gather_fusion
  55.6 0.7 select_reduce_fusion.3
  57.7 0.8 select_reduce_fusion.1
  58.5 0.7 select_reduce_fusion.4
  59.7 5.3 %collective-permute-done.3 = bf16[512,1152]{0,1:T(8,128)(2,1)S(1)} collective-permute-done((bf16[512,1152]{0,1:T(8,128)(2,1)}, bf16[512,1152]{0,1:T(8,128)(2,1)S(1)}, u32[]{:S(2)}, u32[]{:S(2)}) %collective-permute-start.3) | collective-permute-done | bytes 1179680 | tf_op jit(solution)/shard_map/gathers/ppermute | solution.py:83
  65.1 4.3 %collective-permute-start.4 = (bf16[512,1152]{0,1:T(8,128)(2,1)S(1)}, bf16[512,1152]{0,1:T(8,128)(2,1)}, u32[]{:S(2)}, u32[]{:S(2)}) collective-permute-start(bf16[512,1152]{0,1:T(8,128)(2,1)S(1)} %collective-permute-done.3), channel_id=1, source_target_pairs={{0,32},{32,0},{64,96},{96,64},{128,160},{160,128},{192,224},{224,1... | collective-permute-start | bytes 3538952 | tf_op jit(solution)/shard_map/gathers/ppermute | solution.py:84
  70.0 2.4 %copy.19 = bf16[1024,576]{1,0:T(8,128)(2,1)} copy(bf16[1024,576]{0,1:T(8,128)(2,1)} %param.11) | data formatting | bytes 2359296 | tf_op args[0]
  72.5 1.3 clamp_bitcast_fusion
  74.5 3.7 %multiply_cosine_fusion = (f32[1024,64]{1,0:T(8,128)}, f32[1024,64]{1,0:T(8,128)}) fusion(f32[64]{0:T(128)} %multiply_exponential_fusion, f32[1024]{0:T(1024)S(1)} %subtract_convert_fusion.2), kind=kLoop, calls=%fused_computation.48 | loop fusion | flops 65536 | bytes 528640 | tf_op jit(solution)/shard_map/rotary/cos | solution.py:216
  78.2 4.9 %select_select_fusion.3 = (bf16[1024,1152]{0,1:T(8,128)(2,1)S(1)}, bf16[1024,1152]{0,1:T(8,128)(2,1)S(1)}, bf16[1024,1152]{0,1:T(8,128)(2,1)S(1)}) fusion(bf16[1024,1152]{0,1:T(8,128)(2,1)S(1)} %maximum_select_fusion, pred[]{:T(512)S(6)} %eq.100, pred[]{:T(512)S(6)} %eq.99, pred[]{:T(512)S(6)} %eq.97, bf16[512,1152]{0,1:T(8,128)(2,1)S(1)} %collective-permute-done.3, ...), kind=kLoop, calls=%fused_computation.20 | loop fusion | flops 16515072 | bytes 16515076 | tf_op jit(solution)/shard_map/gathers/jit(_where)/select_n | solution.py:97
  83.1 3.9 %select_select_fusion.1 = bf16[1024,1152]{0,1:T(8,128)(2,1)S(1)} fusion(bf16[1024,1152]{0,1:T(8,128)(2,1)S(1)} %maximum_select_fusion, bf16[1024,1152]{0,1:T(8,128)(2,1)S(1)} %get-tuple-element.23, bf16[1024,1152]{0,1:T(8,128)(2,1)S(1)} %get-tuple-element.22, pred[]{:T(512)S(6)} %eq.106, pred[]{:T(512)S(6)} %eq.105, pred[]{:T(512)S(6)} %eq.104, ...), kind=kLoop, calls=%fused_computation.18 | loop fusion | flops 14155776 | bytes 11796484 | tf_op jit(solution)/shard_map/gathers/jit(_where)/select_n | solution.py:97
  87.0 4.2 %select_select_fusion.2 = (bf16[1024,1152]{0,1:T(8,128)(2,1)S(1)}, bf16[1024,1152]{0,1:T(8,128)(2,1)S(1)}) fusion(bf16[1024,1152]{0,1:T(8,128)(2,1)S(1)} %maximum_select_fusion, bf16[1024,1152]{0,1:T(8,128)(2,1)S(1)} %get-tuple-element.23, bf16[1024,1152]{0,1:T(8,128)(2,1)S(1)} %get-tuple-element.22, pred[]{:T(512)S(6)} %eq.103, pred[]{:T(512)S(6)} %eq.102, ...), kind=kLoop, calls=%fused_computation.19 | loop fusion | flops 17694720 | bytes 14155783 | tf_op jit(solution)/shard_map/gathers/jit(_where)/select_n | solution.py:97
  91.2 4.4 %pad_maximum_fusion = bf16[1024,4608]{0,1:T(8,128)(2,1)} fusion(bf16[1024,1152]{0,1:T(8,128)(2,1)S(1)} %get-tuple-element.27, bf16[1024,1152]{0,1:T(8,128)(2,1)S(1)} %select_select_fusion.1, bf16[1024,1152]{0,1:T(8,128)(2,1)S(1)} %get-tuple-element.26, bf16[1024,1152]{0,1:T(8,128)(2,1)S(1)} %get-tuple-element.21), kind=kLoop, calls=%fused_computation.1 | loop fusion | flops 37748736 | bytes 18874368 | tf_op jit(solution)/shard_map/gathers/concatenate | solution.py:103
  95.6 37.3 %all-gather.3.cloned.1.call-done = bf16[6144,1024]{1,0:T(8,128)(2,1)} async-done(((bf16[192,1024]{1,0:T(8,128)(2,1)}), bf16[6144,1024]{1,0:T(8,128)(2,1)}) %all-gather.3.cloned.1.call-update) | async-done | bytes 12582928 | tf_op jit(solution)/shard_map/gathers/all_gather | solution.py:149
  132.9 4.1 %select_reduce_fusion = f32[1024,32]{0,1:T(8,128)S(1)} fusion(bf16[32,192,1024]{2,1,0:T(8,128)(2,1)} %bitcast.80, bf16[1024,576]{1,0:T(8,128)(2,1)S(1)} %copy-done.7, pred[1024,32]{0,1:T(8,128)(4,1)S(1)} %copy-done.10), kind=kOutput, calls=%fused_computation.10 | convolution fusion | flops 2149548032 | bytes 3440640 | tf_op jit(solution)/shard_map/lowrank/dot_general | solution.py:160
  137.2 5.4 %fusion.23 = f32[1024,256]{1,0:T(8,128)} fusion(bf16[1024,32,144]{0,2,1:T(8,128)(2,1)S(1)} %bitcast.67, bf16[32,192,1024]{2,1,0:T(8,128)(2,1)} %bitcast.81), kind=kOutput, calls=%fused_computation.31 | convolution fusion | flops 2415919104 | bytes 12845056 | tf_op jit(solution)/shard_map/projection/tci,cin->tn/dot_general | solution.py:201
  142.7 6.4 %fusion.17 = f32[1024,512]{1,0:T(8,128)} fusion(bf16[1024,32,144]{0,2,1:T(8,128)(2,1)S(1)} %bitcast.68, bf16[32,192,1024]{2,1,0:T(8,128)(2,1)S(1)} %bitcast.83), kind=kOutput, calls=%fused_computation.28 | convolution fusion | flops 4831838208 | bytes 16252928 | tf_op jit(solution)/shard_map/projection/tci,cin->tn/dot_general | solution.py:201
  149.1 1.4 collective-permute-start.5
  150.5 2.6 %fusion.20 = f32[1024,256]{1,0:T(8,128)S(1)} fusion(bf16[1024,32,144]{0,2,1:T(8,128)(2,1)S(1)} %bitcast.69, bf16[32,192,1024]{2,1,0:T(8,128)(2,1)S(1)} %bitcast.84), kind=kOutput, calls=%fused_computation.30 | convolution fusion | flops 2415919104 | bytes 12845056 | tf_op jit(solution)/shard_map/projection/tci,cin->tn/dot_general | solution.py:201
  153.7 1.5 collective-permute-start.6
  155.2 1.7 subtract_convert_fusion.1
  157.0 2.1 %collective-permute-done.6 = f32[1024,32]{0,1:T(8,128)S(1)} collective-permute-done((f32[1024,32]{0,1:T(8,128)S(1)}, f32[1024,32]{0,1:T(8,128)S(1)}, u32[]{:S(2)}, u32[]{:S(2)}) %collective-permute-start.6) | collective-permute-done | bytes 131104 | tf_op jit(solution)/shard_map/lowrank/ppermute | solution.py:171
  159.1 2.8 %collective-permute-start.7 = (f32[1024,32]{0,1:T(8,128)S(1)}, f32[1024,32]{0,1:T(8,128)}, u32[]{:S(2)}, u32[]{:S(2)}) collective-permute-start(f32[1024,32]{0,1:T(8,128)S(1)} %add.132), channel_id=1, source_target_pairs={{0,128},{32,160},{64,192},{96,224},{128,0},{160,32},{192,64},{224,... | collective-permute-start | bytes 393224 | tf_op jit(solution)/shard_map/lowrank/ppermute | solution.py:171
  161.9 1.3 fusion.46
  163.2 1.4 pad_maximum_fusion.2
  164.6 0.9 copy.30
  166.0 1.0 reshape.332
  166.9 0.9 add_convert_fusion.2
  167.9 1.0 broadcast_multiply_fusion
  168.9 1.7 fusion.26
  170.7 3.5 %fusion.7 = bf16[2304,512]{1,0:T(8,128)(2,1)S(1)} fusion(s32[2304]{0:T(1024)S(1)} %copy-done.11, pred[2304]{0:T(1024)(128)(4,1)S(1)} %fusion.37, bf16[1024,256]{1,0:T(8,128)(2,1)S(1)} %fusion.26, bf16[1024,256]{1,0:T(8,128)(2,1)S(1)} %bitcast.79), kind=kOutput, calls=%fused_computation.9 | convolution fusion | flops 2423914496 | bytes 3419392 | tf_op jit(solution)/shard_map/cache_write/dot_general | solution.py:228
  174.3 1.6 fusion.47
  175.8 0.9 copy-done.5
  176.8 2.1 %convolution_add_fusion = f32[1024,512]{1,0:T(8,128)} fusion(f32[1024,512]{1,0:T(8,128)S(1)} %copy-done.5, bf16[1024,512]{0,1:T(8,128)(2,1)S(1)} %bitcast.71, bf16[512,512]{1,0:T(8,128)(2,1)S(1)} %copy-done.6), kind=kOutput, calls=%fused_computation.29 | convolution fusion | flops 537395200 | bytes 5767168 | tf_op jit(solution)/shard_map/lowrank/dot_general | solution.py:181
  178.8 1.9 %reshape.333 = f32[1024,4,128]{2,1,0:T(4,128)S(1)} reshape(f32[1024,512]{1,0:T(8,128)} %convolution_add_fusion) | data formatting | bytes 4194304 | tf_op jit(solution)/shard_map/rotary/reshape | solution.py:15
  180.8 1.8 subtract_convert_fusion
  182.6 1.4 pad_maximum_fusion.1
  184.0 1.2 copy.29
  (55 shorter events, 7.9 us)
Async XLA Ops:
  7.2 47.3 %copy-start = (s32[32]{0:T(128)S(1)}, s32[32]{0:T(128)}, u32[]{:S(2)}) copy-start(s32[32]{0:T(128)} %param.20) | copy-start | bytes 388
  7.2 125.7 %all-gather.3.cloned.1.call-start = ((), (), s32[]{:S(2)}) async-start(), calls=%async_computation | async-start | bytes 12976128 | tf_op jit(solution)/shard_map/gathers/all_gather | solution.py:149
  10.5 6.0 %collective-permute-start = (bf16[1024,576]{0,1:T(8,128)(2,1)}, bf16[1024,576]{0,1:T(8,128)(2,1)S(1)}, u32[]{:S(2)}, u32[]{:S(2)}) collective-permute-start(bf16[1024,576]{0,1:T(8,128)(2,1)} %param.11), channel_id=1, source_target_pairs={{0,32},{32,0},{64,96},{96,64},{128,160},{160,128},{192,224},{224,1... | collective-permute-start | bytes 3538952 | tf_op jit(solution)/shard_map/gathers/ppermute | solution.py:74
  13.8 6.1 %copy-start.12 = (s32[1,10]{1,0:T(1,128)S(1)}, s32[1,10]{1,0:T(1,128)}, u32[]{:S(2)}) copy-start(s32[1,10]{1,0:T(1,128)} %param.18) | copy-start | bytes 124
  18.8 32.8 %copy-start.14 = (s32[1,10]{1,0:T(1,128)S(1)}, s32[1,10]{1,0:T(1,128)}, u32[]{:S(2)}) copy-start(s32[1,10]{1,0:T(1,128)} %param.19) | copy-start | bytes 124
  18.8 28.2 %collective-permute-start.1 = (bf16[1024,1152]{0,1:T(8,128)(2,1)S(1)}, bf16[1024,1152]{0,1:T(8,128)(2,1)}, u32[]{:S(2)}, u32[]{:S(2)}) collective-permute-start(bf16[1024,1152]{0,1:T(8,128)(2,1)S(1)} %maximum_select_fusion), channel_id=1, source_target_pairs={{0,64},{32,224},{64,128},{96,32},{128,192},{160,96},{192,0},{224,1... | collective-permute-start | bytes 7077896 | tf_op jit(solution)/shard_map/gathers/ppermute | solution.py:80
  49.4 15.7 %collective-permute-start.3 = (bf16[512,1152]{0,1:T(8,128)(2,1)}, bf16[512,1152]{0,1:T(8,128)(2,1)S(1)}, u32[]{:S(2)}, u32[]{:S(2)}) collective-permute-start(bf16[512,1152]{0,1:T(8,128)(2,1)} %constant_dynamic-slice_fusion), channel_id=1, source_target_pairs={{0,64},{32,224},{64,128},{96,32},{128,192},{160,96},{192,0},{224,1... | collective-permute-start | bytes 3538952 | tf_op jit(solution)/shard_map/gathers/ppermute | solution.py:83
  53.0 4.8 %copy-start.13 = (s32[10,1]{0,1:T(1,128)}, s32[10,1]{0,1:T(1,128)S(1)}, u32[]{:S(2)}) copy-start(s32[10,1]{0,1:T(1,128)S(1)} %reduce-window.9) | copy-start | bytes 124
  53.6 24.6 %collective-permute-start.2 = (bf16[1024,1152]{0,1:T(8,128)(2,1)}, bf16[1024,1152]{0,1:T(8,128)(2,1)}, u32[]{:S(2)}, u32[]{:S(2)}) collective-permute-start(bf16[1024,1152]{0,1:T(8,128)(2,1)} %collective-permute-done.1), channel_id=1, source_target_pairs={{0,32},{32,0},{64,96},{96,64},{128,160},{160,128},{192,224},{224,1... | collective-permute-start | bytes 7077896 | tf_op jit(solution)/shard_map/gathers/ppermute | solution.py:84
  65.1 13.1 %collective-permute-start.4 = (bf16[512,1152]{0,1:T(8,128)(2,1)S(1)}, bf16[512,1152]{0,1:T(8,128)(2,1)}, u32[]{:S(2)}, u32[]{:S(2)}) collective-permute-start(bf16[512,1152]{0,1:T(8,128)(2,1)S(1)} %collective-permute-done.3), channel_id=1, source_target_pairs={{0,32},{32,0},{64,96},{96,64},{128,160},{160,128},{192,224},{224,1... | collective-permute-start | bytes 3538952 | tf_op jit(solution)/shard_map/gathers/ppermute | solution.py:84
  91.2 41.7 %copy-start.7 = (bf16[1024,576]{1,0:T(8,128)(2,1)S(1)}, bf16[1024,576]{1,0:T(8,128)(2,1)}, u32[]{:S(2)}) copy-start(bf16[1024,576]{1,0:T(8,128)(2,1)} %copy.19) | copy-start | bytes 3538948
  91.2 41.7 %copy-start.10 = (pred[1024,32]{0,1:T(8,128)(4,1)S(1)}, pred[1024,32]{0,1:T(8,128)(4,1)}, u32[]{:S(2)}) copy-start(pred[1024,32]{0,1:T(8,128)(4,1)} %get-tuple-element.41) | copy-start | bytes 98308
  132.9 4.3 %copy-start.2 = (bf16[1024,4608]{0,1:T(8,128)(2,1)S(1)}, bf16[1024,4608]{0,1:T(8,128)(2,1)}, u32[]{:S(2)}) copy-start(bf16[1024,4608]{0,1:T(8,128)(2,1)} %pad_maximum_fusion) | copy-start | bytes 28311556
  137.2 5.5 %copy-start.9 = (bf16[6144,1024]{1,0:T(8,128)(2,1)S(1)}, bf16[6144,1024]{1,0:T(8,128)(2,1)}, u32[]{:S(2)}) copy-start(bf16[6144,1024]{1,0:T(8,128)(2,1)} %all-gather.3.cloned.1.call-done) | copy-start | bytes 37748740
  149.1 4.6 %collective-permute-start.5 = (f32[1024,32]{0,1:T(8,128)S(1)}, f32[1024,32]{0,1:T(8,128)S(1)}, u32[]{:S(2)}, u32[]{:S(2)}) collective-permute-start(f32[1024,32]{0,1:T(8,128)S(1)} %select_reduce_fusion), channel_id=1, source_target_pairs={{0,32},{32,0},{64,96},{96,64},{128,160},{160,128},{192,224},{224,1... | collective-permute-start | bytes 393224 | tf_op jit(solution)/shard_map/lowrank/ppermute | solution.py:171
  153.1 2.1 %copy-start.3 = (f32[1024,64]{1,0:T(8,128)S(1)}, f32[1024,64]{1,0:T(8,128)}, u32[]{:S(2)}) copy-start(f32[1024,64]{1,0:T(8,128)} %get-tuple-element.38) | copy-start | bytes 786436
  153.1 2.1 %copy-start.4 = (f32[1024,64]{1,0:T(8,128)S(1)}, f32[1024,64]{1,0:T(8,128)}, u32[]{:S(2)}) copy-start(f32[1024,64]{1,0:T(8,128)} %get-tuple-element.39) | copy-start | bytes 786436
  153.7 5.4 %collective-permute-start.6 = (f32[1024,32]{0,1:T(8,128)S(1)}, f32[1024,32]{0,1:T(8,128)S(1)}, u32[]{:S(2)}, u32[]{:S(2)}) collective-permute-start(f32[1024,32]{0,1:T(8,128)S(1)} %add.131), channel_id=1, source_target_pairs={{0,64},{32,96},{64,0},{96,32},{128,192},{160,224},{192,128},{224,1... | collective-permute-start | bytes 393224 | tf_op jit(solution)/shard_map/lowrank/ppermute | solution.py:171
  159.1 7.8 %collective-permute-start.7 = (f32[1024,32]{0,1:T(8,128)S(1)}, f32[1024,32]{0,1:T(8,128)}, u32[]{:S(2)}, u32[]{:S(2)}) collective-permute-start(f32[1024,32]{0,1:T(8,128)S(1)} %add.132), channel_id=1, source_target_pairs={{0,128},{32,160},{64,192},{96,224},{128,0},{160,32},{192,64},{224,... | collective-permute-start | bytes 393224 | tf_op jit(solution)/shard_map/lowrank/ppermute | solution.py:171
  167.9 2.8 %copy-start.8 = (bf16[128,8,2,128]{3,1,2,0:T(8,128)(2,1)S(1)}, bf16[128,8,2,128]{3,1,2,0:T(8,128)(2,1)}, u32[]{:S(2)}) copy-start(bf16[128,8,2,128]{3,1,2,0:T(8,128)(2,1)} %copy.30) | copy-start | bytes 1572868
  167.9 2.8 %copy-start.11 = (s32[2304]{0:T(1024)S(1)}, s32[2304]{0:T(1024)}, u32[]{:S(2)}) copy-start(s32[2304]{0:T(1024)} %clamp_bitcast_fusion) | copy-start | bytes 27652
  174.2 2.4 %copy-start.5 = (f32[1024,512]{1,0:T(8,128)S(1)}, f32[1024,512]{1,0:T(8,128)}, u32[]{:S(2)}) copy-start(f32[1024,512]{1,0:T(8,128)} %fusion.17) | copy-start | bytes 6291460
  174.2 2.5 %copy-start.6 = (bf16[512,512]{1,0:T(8,128)(2,1)S(1)}, bf16[512,512]{1,0:T(8,128)(2,1)}, u32[]{:S(2)}) copy-start(bf16[512,512]{1,0:T(8,128)(2,1)} %reshape.332) | copy-start | bytes 1572868
  182.6 2.6 %copy-start.1 = (s32[32]{0:T(128)S(1)}, s32[32]{0:T(128)}, u32[]{:S(2)}) copy-start(s32[32]{0:T(128)} %param.20) | copy-start | bytes 388
Sparse Core Ops, SparseCore 0:
  11.1 121.7 all-gather.2

commit v6 on v3

--- a/solution.py
+++ b/solution.py
@@ -164,6 +164,7 @@
             preferred_element_type=jnp.float32,
         ).reshape(hidden.shape[0], adapter_count, -1)
         partial = jnp.sum(jnp.where(onehot[:, :, None], partial_all, 0.0), axis=1)
+        partial, full_rows = lax.optimization_barrier((partial, full_rows))
         distance = 1
         while distance < row_size:
             pairs = [(i, i ^ distance) for i in range(row_size)]
@@ -217,13 +218,10 @@
         select = (
             (rows[:, None] == jnp.arange(TOK_DEV, dtype=jnp.int32)[None, :]) & keep[:, None]
         ).astype(jnp.bfloat16)
-        both = jnp.dot(
-            select,
-            jnp.concatenate([key_rotated, value_rows], axis=1),
-            preferred_element_type=jnp.float32,
-        ).astype(jnp.bfloat16)
-        key_cache = both[:, :key_width].reshape(pages, PAGE, key_width)
-        value_cache = both[:, key_width:].reshape(pages, PAGE, key_width)
+        key_cache = jnp.dot(select, key_rotated, preferred_element_type=jnp.float32)
+        key_cache = key_cache.astype(jnp.bfloat16).reshape(pages, PAGE, key_width)
+        value_cache = jnp.dot(select, value_rows, preferred_element_type=jnp.float32)
+        value_cache = value_cache.astype(jnp.bfloat16).reshape(pages, PAGE, key_width)
     return (query, key_cache.astype(jnp.bfloat16), value_cache.astype(jnp.bfloat16))
 
 

time: 181 us -> 181 us (level)
  matrix products: 22.7 us -> 27.5 us
  waiting for transfers between devices: 76.5 us -> 73.9 us
    dot_general x2, matrix products: 5.27 us -> 8.4 us  [the longest x1 4.78 us: shards(): jnp.dot(select, value_rows, preferred_element_type=jnp.float32)]
    ppermute x3, waiting for transfers between devices: 3.26 us -> 0.52 us  [shards(): partial = partial + lax.ppermute(partial, 'row', pairs)]
    unnamed x32 -> x30, local copies, waits for them, and re-layouts: 4.56 us -> 4.38 us
  transfers between devices with their start and end apart: 9 -> 9, of which waited for: 6 -> 6; matrix products, arithmetic and copies ran while one was open for 30% -> 32% of each run, Pallas kernels for 0% -> 0%
where the time goes in v6:
time: 181 us; the launch traced here: 180 us
  waiting for transfers between devices  73.9 us (41%)
  other arithmetic  34.4 us (19%)
  matrix products  27.5 us (15%)
  starting transfers between devices  17 us (9%)
  between operations  14.3 us (8%)
  local copies, waits for them, and re-layouts  13 us (7%)
    all_gather x1, waiting for transfers between devices, shards(): packed = lax.all_gather(jnp.concatenate(pieces, axis=0), 'col', axis=0)  38.8 us
    ppermute x1, waiting for transfers between devices, gather_rows(): near = lax.ppermute(own_block, 'row', ring)  26.5 us
    select_n x3, other arithmetic, gather_rows(): jnp.where(relative == 0, own_block, jnp.where(relative == 1, after, jnp.w...  12.9 us
    dot_general x1, matrix products, shards(): jnp.einsum('tci,cin->tn', full_rows.reshape(full_rows.shape[0], packed.sh...  12.6 us
    ppermute x3, starting transfers between devices, shards(): partial = partial + lax.ppermute(partial, 'row', pairs)  5.77 us
    ppermute x1, waiting for transfers between devices, gather_rows(): far_half = lax.ppermute(forwarded, 'row', ring)  5.37 us
    dot_general x1, matrix products, shards(): jnp.dot(select, value_rows, preferred_element_type=jnp.float32)  4.78 us
    ppermute x2, starting transfers between devices, gather_rows(): from_partner, far_other = lax.ppermute((near, far_half), 'row', swap)  4.54 us
  transfers between devices with their start and end apart: 9, of which 6 were waited for; matrix products, arithmetic and copies ran while one was open for 32% of the time, Pallas kernels for 0%

profile of v6, /device:TPU:1, one launch (start us, length us, event | category | flops | bytes accessed | tf_op | source)
XLA Modules:
  0.0 180.1 jit_solution(6287580772959670780)
XLA Ops:
  7.2 0.7 reshape.329
  8.0 0.7 reshape.330
  8.7 1.8 fusion.30
  10.5 3.3 %collective-permute-start = (bf16[1024,576]{0,1:T(8,128)(2,1)}, bf16[1024,576]{0,1:T(8,128)(2,1)S(1)}, u32[]{:S(2)}, u32[]{:S(2)}) collective-permute-start(bf16[1024,576]{0,1:T(8,128)(2,1)} %param.11), channel_id=1, source_target_pairs={{0,32},{32,0},{64,96},{96,64},{128,160},{160,128},{192,224},{224,1... | collective-permute-start | bytes 3538952 | tf_op jit(solution)/shard_map/gathers/ppermute | solution.py:74
  13.8 2.7 %collective-permute-done = bf16[1024,576]{0,1:T(8,128)(2,1)S(1)} collective-permute-done((bf16[1024,576]{0,1:T(8,128)(2,1)}, bf16[1024,576]{0,1:T(8,128)(2,1)S(1)}, u32[]{:S(2)}, u32[]{:S(2)}) %collective-permute-start) | collective-permute-done | bytes 1179680 | tf_op jit(solution)/shard_map/gathers/ppermute | solution.py:74
  16.5 2.3 %maximum_select_fusion = bf16[1024,1152]{0,1:T(8,128)(2,1)S(1)} fusion(bf16[1024,576]{0,1:T(8,128)(2,1)S(1)} %collective-permute-done, bf16[1024,576]{0,1:T(8,128)(2,1)} %param.11, pred[]{:T(512)S(6)} %eq.98), kind=kLoop, calls=%fused_computation.15 | loop fusion | flops 10616832 | bytes 4718593 | tf_op jit(solution)/shard_map/gathers/jit(_where)/select_n | solution.py:75
  18.8 1.1 collective-permute-start.1
  19.9 0.5 and_select_fusion.1
  20.4 26.5 %collective-permute-done.1 = bf16[1024,1152]{0,1:T(8,128)(2,1)} collective-permute-done((bf16[1024,1152]{0,1:T(8,128)(2,1)S(1)}, bf16[1024,1152]{0,1:T(8,128)(2,1)}, u32[]{:S(2)}, u32[]{:S(2)}) %collective-permute-start.1) | collective-permute-done | bytes 2359328 | tf_op jit(solution)/shard_map/gathers/ppermute | solution.py:80
  47.0 2.4 %constant_dynamic-slice_fusion = bf16[512,1152]{0,1:T(8,128)(2,1)} fusion(bf16[1024,1152]{0,1:T(8,128)(2,1)} %collective-permute-done.1, s32[]{:T(128)S(6)} %select_n.183), kind=kLoop, calls=%fused_computation.89 | loop fusion | bytes 2359300 | tf_op jit(solution)/shard_map/gathers/dynamic_slice | solution.py:82
  49.4 2.2 %collective-permute-start.3 = (bf16[512,1152]{0,1:T(8,128)(2,1)}, bf16[512,1152]{0,1:T(8,128)(2,1)S(1)}, u32[]{:S(2)}, u32[]{:S(2)}) collective-permute-start(bf16[512,1152]{0,1:T(8,128)(2,1)} %constant_dynamic-slice_fusion), channel_id=1, source_target_pairs={{0,64},{32,224},{64,128},{96,32},{128,192},{160,96},{192,0},{224,1... | collective-permute-start | bytes 3538952 | tf_op jit(solution)/shard_map/gathers/ppermute | solution.py:83
  51.6 0.5 fusion.33
  52.1 0.8 reduce-window.9
  52.9 0.7 reduce-window.6
  53.8 0.6 pad_clamp_fusion
  54.4 1.2 gather_fusion
  55.6 0.7 select_reduce_fusion.3
  56.4 0.7 fusion.36
  57.0 0.7 fusion.34
  57.7 0.8 select_reduce_fusion.1
  58.5 0.7 select_reduce_fusion.4
  59.2 0.5 compare_select_fusion.2
  59.7 5.4 %collective-permute-done.3 = bf16[512,1152]{0,1:T(8,128)(2,1)S(1)} collective-permute-done((bf16[512,1152]{0,1:T(8,128)(2,1)}, bf16[512,1152]{0,1:T(8,128)(2,1)S(1)}, u32[]{:S(2)}, u32[]{:S(2)}) %collective-permute-start.3) | collective-permute-done | bytes 1179680 | tf_op jit(solution)/shard_map/gathers/ppermute | solution.py:83
  65.1 4.3 %collective-permute-start.4 = (bf16[512,1152]{0,1:T(8,128)(2,1)S(1)}, bf16[512,1152]{0,1:T(8,128)(2,1)}, u32[]{:S(2)}, u32[]{:S(2)}) collective-permute-start(bf16[512,1152]{0,1:T(8,128)(2,1)S(1)} %collective-permute-done.3), channel_id=1, source_target_pairs={{0,32},{32,0},{64,96},{96,64},{128,160},{160,128},{192,224},{224,1... | collective-permute-start | bytes 3538952 | tf_op jit(solution)/shard_map/gathers/ppermute | solution.py:84
  69.4 0.5 multiply_exponential_fusion
  69.9 2.4 %copy.19 = bf16[1024,576]{1,0:T(8,128)(2,1)} copy(bf16[1024,576]{0,1:T(8,128)(2,1)} %param.11) | data formatting | bytes 2359296 | tf_op args[0]
  72.4 1.3 clamp_bitcast_fusion
  73.8 0.7 fusion.39
  74.4 2.4 %multiply_cosine_fusion = (f32[1024,64]{0,1:T(8,128)}, f32[1024,64]{0,1:T(8,128)}) fusion(f32[64]{0:T(128)} %multiply_exponential_fusion, f32[1024]{0:T(1024)S(1)} %subtract_convert_fusion.2), kind=kLoop, calls=%fused_computation.49 | loop fusion | flops 65536 | bytes 528640 | tf_op jit(solution)/shard_map/rotary/cos | solution.py:209
  76.9 4.8 %select_select_fusion.3 = (bf16[1024,1152]{0,1:T(8,128)(2,1)S(1)}, bf16[1024,1152]{0,1:T(8,128)(2,1)S(1)}, bf16[1024,1152]{0,1:T(8,128)(2,1)S(1)}) fusion(bf16[1024,1152]{0,1:T(8,128)(2,1)S(1)} %maximum_select_fusion, pred[]{:T(512)S(6)} %eq.100, pred[]{:T(512)S(6)} %eq.99, pred[]{:T(512)S(6)} %eq.97, bf16[512,1152]{0,1:T(8,128)(2,1)S(1)} %collective-permute-done.3, ...), kind=kLoop, calls=%fused_computation.20 | loop fusion | flops 16515072 | bytes 16515076 | tf_op jit(solution)/shard_map/gathers/jit(_where)/select_n | solution.py:97
  81.6 3.9 %select_select_fusion.1 = bf16[1024,1152]{0,1:T(8,128)(2,1)S(1)} fusion(bf16[1024,1152]{0,1:T(8,128)(2,1)S(1)} %maximum_select_fusion, bf16[1024,1152]{0,1:T(8,128)(2,1)S(1)} %get-tuple-element.15, bf16[1024,1152]{0,1:T(8,128)(2,1)S(1)} %get-tuple-element.14, pred[]{:T(512)S(6)} %eq.106, pred[]{:T(512)S(6)} %eq.105, pred[]{:T(512)S(6)} %eq.104, ...), kind=kLoop, calls=%fused_computation.18 | loop fusion | flops 14155776 | bytes 11796484 | tf_op jit(solution)/shard_map/gathers/jit(_where)/select_n | solution.py:97
  85.5 4.2 %select_select_fusion.2 = (bf16[1024,1152]{0,1:T(8,128)(2,1)S(1)}, bf16[1024,1152]{0,1:T(8,128)(2,1)S(1)}) fusion(bf16[1024,1152]{0,1:T(8,128)(2,1)S(1)} %maximum_select_fusion, bf16[1024,1152]{0,1:T(8,128)(2,1)S(1)} %get-tuple-element.15, bf16[1024,1152]{0,1:T(8,128)(2,1)S(1)} %get-tuple-element.14, pred[]{:T(512)S(6)} %eq.103, pred[]{:T(512)S(6)} %eq.102, ...), kind=kLoop, calls=%fused_computation.19 | loop fusion | flops 17694720 | bytes 14155783 | tf_op jit(solution)/shard_map/gathers/jit(_where)/select_n | solution.py:97
  89.8 4.4 %pad_maximum_fusion = bf16[1024,4608]{0,1:T(8,128)(2,1)} fusion(bf16[1024,1152]{0,1:T(8,128)(2,1)S(1)} %get-tuple-element.19, bf16[1024,1152]{0,1:T(8,128)(2,1)S(1)} %select_select_fusion.1, bf16[1024,1152]{0,1:T(8,128)(2,1)S(1)} %get-tuple-element.18, bf16[1024,1152]{0,1:T(8,128)(2,1)S(1)} %get-tuple-element.13), kind=kLoop, calls=%fused_computation.3 | loop fusion | flops 37748736 | bytes 18874368 | tf_op jit(solution)/shard_map/gathers/concatenate | solution.py:103
  94.1 38.8 %all-gather.3.cloned.1.call-done = bf16[6144,1024]{1,0:T(8,128)(2,1)} async-done(((bf16[192,1024]{1,0:T(8,128)(2,1)}), bf16[6144,1024]{1,0:T(8,128)(2,1)}) %all-gather.3.cloned.1.call-update) | async-done | bytes 12582928 | tf_op jit(solution)/shard_map/gathers/all_gather | solution.py:149
  132.9 4.1 %select_reduce_fusion = f32[1024,32]{0,1:T(8,128)S(1)} fusion(bf16[32,192,1024]{2,1,0:T(8,128)(2,1)} %bitcast.67, bf16[1024,576]{1,0:T(8,128)(2,1)S(1)} %copy-done.6, pred[1024,32]{0,1:T(8,128)(4,1)S(1)} %copy-done.9), kind=kOutput, calls=%fused_computation.12 | convolution fusion | flops 2149548032 | bytes 3440640 | tf_op jit(solution)/shard_map/lowrank/dot_general | solution.py:160
  137.0 1.7 collective-permute-start.5
  138.7 12.6 %fusion.17 = f32[1024,1024]{0,1:T(8,128)S(1)} fusion(bf16[1024,32,144]{0,2,1:T(8,128)(2,1)S(1)} %bitcast.58, bf16[32,192,1024]{2,1,0:T(8,128)(2,1)} %bitcast.68), kind=kOutput, calls=%fused_computation.23 | convolution fusion | flops 9663676416 | bytes 23068672 | tf_op jit(solution)/shard_map/projection/tci,cin->tn/dot_general | solution.py:193
  151.7 1.6 copy-done.5
  153.3 1.3 collective-permute-start.6
  154.6 3.6 %fusion.11 = bf16[2304,256]{1,0:T(8,128)(2,1)} fusion(bf16[1024,256]{0,1:T(8,128)(2,1)S(1)} %bitcast.66, s32[2304]{0:T(1024)S(1)} %copy-done.10, pred[2304]{0:T(1024)(128)(4,1)S(1)} %fusion.32), kind=kOutput, calls=%fused_computation.13 | convolution fusion | flops 1213267968 | bytes 1715456 | tf_op jit(solution)/shard_map/cache_write/dot_general | solution.py:221
  158.4 2.8 %collective-permute-start.7 = (f32[1024,32]{0,1:T(8,128)S(1)}, f32[1024,32]{0,1:T(8,128)S(1)}, u32[]{:S(2)}, u32[]{:S(2)}) collective-permute-start(f32[1024,32]{0,1:T(8,128)S(1)} %add.132), channel_id=1, source_target_pairs={{0,128},{32,160},{64,192},{96,224},{128,0},{160,32},{192,64},{224,... | collective-permute-start | bytes 393224 | tf_op jit(solution)/shard_map/lowrank/ppermute | solution.py:171
  161.2 1.3 fusion.40
  162.8 0.8 reshape.337
  163.8 0.3 collective-permute-done.7
  164.4 2.3 %slice_add_fusion = f32[1024,512]{0,1:T(8,128)S(1)} fusion(f32[1024,1024]{0,1:T(8,128)} %copy-done.5, bf16[1024,512]{0,1:T(8,128)(2,1)S(1)} %bitcast.62, bf16[512,512]{1,0:T(8,128)(2,1)S(1)} %reshape.332), kind=kOutput, calls=%fused_computation.24 | convolution fusion | flops 537395200 | bytes 5767168 | tf_op jit(solution)/shard_map/lowrank/dot_general | solution.py:181
  166.7 0.3 subtract_convert_fusion
  167.2 1.3 copy.23
  168.5 4.8 %fusion.14 = bf16[2304,256]{1,0:T(8,128)(2,1)} fusion(s32[2304]{0:T(1024)S(1)} %copy-done.10, pred[2304]{0:T(1024)(128)(4,1)S(1)} %fusion.32, bf16[1024,512]{0,1:T(8,128)(2,1)S(1)} %bitcast.65, bf16[512,256]{1,0:T(8,128)(2,1)S(1)} %copy-done.8, f32[1024,1024]{0,1:T(8,128)} %copy-done.5), kind=kOutput, calls=%fused_computation.14 | convolution fusion | flops 1482227712 | bytes 3550464 | tf_op jit(solution)/shard_map/cache_write/dot_general | solution.py:223
  (48 shorter events, 1.6 us)
Async XLA Ops:
  7.2 47.3 %copy-start = (s32[32]{0:T(128)S(1)}, s32[32]{0:T(128)}, u32[]{:S(2)}) copy-start(s32[32]{0:T(128)} %param.20) | copy-start | bytes 388
  7.2 125.7 %all-gather.3.cloned.1.call-start = ((), (), s32[]{:S(2)}) async-start(), calls=%async_computation | async-start | bytes 12976128 | tf_op jit(solution)/shard_map/gathers/all_gather | solution.py:149
  10.5 6.0 %collective-permute-start = (bf16[1024,576]{0,1:T(8,128)(2,1)}, bf16[1024,576]{0,1:T(8,128)(2,1)S(1)}, u32[]{:S(2)}, u32[]{:S(2)}) collective-permute-start(bf16[1024,576]{0,1:T(8,128)(2,1)} %param.11), channel_id=1, source_target_pairs={{0,32},{32,0},{64,96},{96,64},{128,160},{160,128},{192,224},{224,1... | collective-permute-start | bytes 3538952 | tf_op jit(solution)/shard_map/gathers/ppermute | solution.py:74
  13.8 6.1 %copy-start.11 = (s32[1,10]{1,0:T(1,128)S(1)}, s32[1,10]{1,0:T(1,128)}, u32[]{:S(2)}) copy-start(s32[1,10]{1,0:T(1,128)} %param.18) | copy-start | bytes 124
  18.8 32.8 %copy-start.13 = (s32[1,10]{1,0:T(1,128)S(1)}, s32[1,10]{1,0:T(1,128)}, u32[]{:S(2)}) copy-start(s32[1,10]{1,0:T(1,128)} %param.19) | copy-start | bytes 124
  18.8 28.2 %collective-permute-start.1 = (bf16[1024,1152]{0,1:T(8,128)(2,1)S(1)}, bf16[1024,1152]{0,1:T(8,128)(2,1)}, u32[]{:S(2)}, u32[]{:S(2)}) collective-permute-start(bf16[1024,1152]{0,1:T(8,128)(2,1)S(1)} %maximum_select_fusion), channel_id=1, source_target_pairs={{0,64},{32,224},{64,128},{96,32},{128,192},{160,96},{192,0},{224,1... | collective-permute-start | bytes 7077896 | tf_op jit(solution)/shard_map/gathers/ppermute | solution.py:80
  49.4 15.7 %collective-permute-start.3 = (bf16[512,1152]{0,1:T(8,128)(2,1)}, bf16[512,1152]{0,1:T(8,128)(2,1)S(1)}, u32[]{:S(2)}, u32[]{:S(2)}) collective-permute-start(bf16[512,1152]{0,1:T(8,128)(2,1)} %constant_dynamic-slice_fusion), channel_id=1, source_target_pairs={{0,64},{32,224},{64,128},{96,32},{128,192},{160,96},{192,0},{224,1... | collective-permute-start | bytes 3538952 | tf_op jit(solution)/shard_map/gathers/ppermute | solution.py:83
  52.9 4.7 %copy-start.12 = (s32[10,1]{0,1:T(1,128)}, s32[10,1]{0,1:T(1,128)S(1)}, u32[]{:S(2)}) copy-start(s32[10,1]{0,1:T(1,128)S(1)} %reduce-window.9) | copy-start | bytes 124
  53.6 23.2 %collective-permute-start.2 = (bf16[1024,1152]{0,1:T(8,128)(2,1)}, bf16[1024,1152]{0,1:T(8,128)(2,1)}, u32[]{:S(2)}, u32[]{:S(2)}) collective-permute-start(bf16[1024,1152]{0,1:T(8,128)(2,1)} %collective-permute-done.1), channel_id=1, source_target_pairs={{0,32},{32,0},{64,96},{96,64},{128,160},{160,128},{192,224},{224,1... | collective-permute-start | bytes 7077896 | tf_op jit(solution)/shard_map/gathers/ppermute | solution.py:84
  65.1 11.8 %collective-permute-start.4 = (bf16[512,1152]{0,1:T(8,128)(2,1)S(1)}, bf16[512,1152]{0,1:T(8,128)(2,1)}, u32[]{:S(2)}, u32[]{:S(2)}) collective-permute-start(bf16[512,1152]{0,1:T(8,128)(2,1)S(1)} %collective-permute-done.3), channel_id=1, source_target_pairs={{0,32},{32,0},{64,96},{96,64},{128,160},{160,128},{192,224},{224,1... | collective-permute-start | bytes 3538952 | tf_op jit(solution)/shard_map/gathers/ppermute | solution.py:84
  89.7 43.2 %copy-start.6 = (bf16[1024,576]{1,0:T(8,128)(2,1)S(1)}, bf16[1024,576]{1,0:T(8,128)(2,1)}, u32[]{:S(2)}) copy-start(bf16[1024,576]{1,0:T(8,128)(2,1)} %copy.19) | copy-start | bytes 3538948
  89.8 43.2 %copy-start.9 = (pred[1024,32]{0,1:T(8,128)(4,1)S(1)}, pred[1024,32]{0,1:T(8,128)(4,1)}, u32[]{:S(2)}) copy-start(pred[1024,32]{0,1:T(8,128)(4,1)} %get-tuple-element.31) | copy-start | bytes 98308
  132.9 5.8 %copy-start.2 = (bf16[1024,4608]{0,1:T(8,128)(2,1)S(1)}, bf16[1024,4608]{0,1:T(8,128)(2,1)}, u32[]{:S(2)}) copy-start(bf16[1024,4608]{0,1:T(8,128)(2,1)} %pad_maximum_fusion) | copy-start | bytes 28311556
  137.0 16.2 %collective-permute-start.5 = (f32[1024,32]{0,1:T(8,128)S(1)}, f32[1024,32]{0,1:T(8,128)S(1)}, u32[]{:S(2)}, u32[]{:S(2)}) collective-permute-start(f32[1024,32]{0,1:T(8,128)S(1)} %select_reduce_fusion), channel_id=1, source_target_pairs={{0,32},{32,0},{64,96},{96,64},{128,160},{160,128},{192,224},{224,1... | collective-permute-start | bytes 393224 | tf_op jit(solution)/shard_map/lowrank/ppermute | solution.py:171
  138.7 12.7 %copy-start.3 = (f32[1024,64]{0,1:T(8,128)S(1)}, f32[1024,64]{0,1:T(8,128)}, u32[]{:S(2)}) copy-start(f32[1024,64]{0,1:T(8,128)} %get-tuple-element.28) | copy-start | bytes 786436
  138.7 12.7 %copy-start.4 = (f32[1024,64]{0,1:T(8,128)S(1)}, f32[1024,64]{0,1:T(8,128)}, u32[]{:S(2)}) copy-start(f32[1024,64]{0,1:T(8,128)} %get-tuple-element.29) | copy-start | bytes 786436
  151.3 1.9 %copy-start.5 = (f32[1024,1024]{0,1:T(8,128)}, f32[1024,1024]{0,1:T(8,128)S(1)}, u32[]{:S(2)}) copy-start(f32[1024,1024]{0,1:T(8,128)S(1)} %fusion.17) | copy-start | bytes 12582916
  151.4 3.2 %copy-start.10 = (s32[2304]{0:T(1024)S(1)}, s32[2304]{0:T(1024)}, u32[]{:S(2)}) copy-start(s32[2304]{0:T(1024)} %clamp_bitcast_fusion) | copy-start | bytes 27652
  153.3 5.1 %collective-permute-start.6 = (f32[1024,32]{0,1:T(8,128)S(1)}, f32[1024,32]{0,1:T(8,128)S(1)}, u32[]{:S(2)}, u32[]{:S(2)}) collective-permute-start(f32[1024,32]{0,1:T(8,128)S(1)} %add.131), channel_id=1, source_target_pairs={{0,64},{32,96},{64,0},{96,32},{128,192},{160,224},{192,128},{224,1... | collective-permute-start | bytes 393224 | tf_op jit(solution)/shard_map/lowrank/ppermute | solution.py:171
  158.4 5.8 %copy-start.7 = (bf16[1024,32]{0,1:T(8,128)(2,1)S(1)}, bf16[1024,32]{0,1:T(8,128)(2,1)}, u32[]{:S(2)}) copy-start(bf16[1024,32]{0,1:T(8,128)(2,1)} %get-tuple-element.30) | copy-start | bytes 196612
  158.4 5.7 %collective-permute-start.7 = (f32[1024,32]{0,1:T(8,128)S(1)}, f32[1024,32]{0,1:T(8,128)S(1)}, u32[]{:S(2)}, u32[]{:S(2)}) collective-permute-start(f32[1024,32]{0,1:T(8,128)S(1)} %add.132), channel_id=1, source_target_pairs={{0,128},{32,160},{64,192},{96,224},{128,0},{160,32},{192,64},{224,... | collective-permute-start | bytes 393224 | tf_op jit(solution)/shard_map/lowrank/ppermute | solution.py:171
  167.1 1.4 copy-start.8
  168.5 4.8 %copy-start.1 = (s32[32]{0:T(128)S(1)}, s32[32]{0:T(128)}, u32[]{:S(2)}) copy-start(s32[32]{0:T(128)} %param.20) | copy-start | bytes 388
Sparse Core Ops, SparseCore 0:
  11.1 121.7 all-gather.2

commit v7 on v6

--- a/solution.py
+++ b/solution.py
@@ -133,14 +133,16 @@
     with jax.named_scope("gathers"):
         full_rows = gather_rows(hidden, row_size)
         features = down_shape[0]
-        down_rows = jnp.pad(
-            jnp.transpose(adapter_down[0]), ((0, 0), (0, weight_width - features))
-        )
+        spare = weight_width - features
+        down_t = jnp.transpose(adapter_down[0])
+        up_flat = jnp.concatenate(
+            [adapter_up_query.reshape(-1), adapter_up_value.reshape(-1)]
+        )
+        up_flat = jnp.pad(up_flat, (0, down_t.shape[0] * spare - up_flat.shape[0]))
+        down_rows = jnp.concatenate([down_t, up_flat.reshape(down_t.shape[0], spare)], axis=1)
         pieces = [
             jnp.concatenate([w_query, w_key, w_value], axis=1),
             down_rows,
-            adapter_up_query.reshape(-1, weight_width),
-            adapter_up_value.reshape(-1, weight_width),
         ]
         pieces = [jnp.pad(p, ((0, -p.shape[0] % 8), (0, 0))) for p in pieces]
         bounds = [0]
@@ -149,10 +151,11 @@
         packed = lax.all_gather(jnp.concatenate(pieces, axis=0), "col", axis=0)
         weights = packed[:, :feature_rows]
         down_local = packed[:, bounds[1] : bounds[2]].reshape(-1, weight_width)
-        up_query = packed[:, bounds[2] : bounds[3]].reshape(adapter_count, -1)
-        up_query = up_query[:, : rank_width * query_width].reshape(adapter_count, rank_width, -1)
-        up_value = packed[:, bounds[3] : bounds[4]].reshape(adapter_count, -1)
-        up_value = up_value[:, : rank_width * key_width].reshape(adapter_count, rank_width, -1)
+        up_all = packed[:, bounds[1] : bounds[2], features:].reshape(adapter_count, -1)
+        query_size = rank_width * query_width
+        up_query = up_all[:, :query_size].reshape(adapter_count, rank_width, -1)
+        up_value = up_all[:, query_size : query_size + rank_width * key_width]
+        up_value = up_value.reshape(adapter_count, rank_width, -1)
 
     with jax.named_scope("lowrank"):
         onehot = (chosen[:, None] == jnp.arange(adapter_count, dtype=jnp.int32)[None, :])

time: 181 us -> 180 us (level)
  waiting for transfers between devices: 73.9 us -> 72 us
    all_gather x1, waiting for transfers between devices: 38.8 us -> 33.7 us  [shards(): packed = lax.all_gather(jnp.concatenate(pieces, axis=0), 'col', axis=0)]
    ppermute x3, waiting for transfers between devices: 0.52 us -> 3.23 us  [shards(): partial = partial + lax.ppermute(partial, 'row', pairs)]
    unnamed x30 -> x31, local copies, waits for them, and re-layouts: 4.38 us -> 4.27 us
  transfers between devices with their start and end apart: 9 -> 9, of which waited for: 6 -> 5; matrix products, arithmetic and copies ran while one was open for 32% -> 32% of each run, Pallas kernels for 0% -> 0%
where the time goes in v7:
time: 180 us
  waiting for transfers between devices  72 us (40%)
  other arithmetic  35.6 us (20%)
  matrix products  27.4 us (15%)
  starting transfers between devices  17.2 us (10%)
  between operations  14.3 us (8%)
  local copies, waits for them, and re-layouts  13.4 us (7%)
    all_gather x1, waiting for transfers between devices, shards(): packed = lax.all_gather(jnp.concatenate(pieces, axis=0), 'col', axis=0)  33.7 us
    ppermute x1, waiting for transfers between devices, gather_rows(): near = lax.ppermute(own_block, 'row', ring)  26.5 us
    select_n x3, other arithmetic, gather_rows(): jnp.where(relative == 0, own_block, jnp.where(relative == 1, after, jnp.w...  12.7 us
    dot_general x1, matrix products, shards(): jnp.einsum('tci,cin->tn', full_rows.reshape(full_rows.shape[0], packed.sh...  12.5 us
    ppermute x3, starting transfers between devices, shards(): partial = partial + lax.ppermute(partial, 'row', pairs)  6 us
    ppermute x1, waiting for transfers between devices, gather_rows(): far_half = lax.ppermute(forwarded, 'row', ring)  5.81 us
    dot_general x1, matrix products, shards(): jnp.dot(select, value_rows, preferred_element_type=jnp.float32)  4.77 us
    ppermute x2, starting transfers between devices, gather_rows(): from_partner, far_other = lax.ppermute((near, far_half), 'row', swap)  4.55 us
  transfers between devices with their start and end apart: 9, of which 5 were waited for; matrix products, arithmetic and copies ran while one was open for 32% of the time, Pallas kernels for 0%

profile of v7, /device:TPU:1, one launch (start us, length us, event | category | flops | bytes accessed | tf_op | source)
XLA Modules:
  0.0 179.9 jit_solution(2070708024169722740)
XLA Ops:
  7.2 0.7 copy.24
  8.0 0.7 copy.25
  8.8 1.8 %maximum_maximum_fusion = bf16[176,1024]{1,0:T(8,128)(2,1)} fusion(bf16[32,448]{1,0:T(8,128)(2,1)S(1)} %reshape.334, bf16[32,576]{1,0:T(8,128)(2,1)} %bitcast.71, bf16[144,256]{1,0:T(8,128)(2,1)} %param.14, bf16[144,256]{1,0:T(8,128)(2,1)} %param.13, bf16[144,512]{1,0:T(8,128)(2,1)} %param.12), kind=kLoop, calls=%fused_computation.41 | loop fusion | flops 1802240 | bytes 720896 | tf_op jit(solution)/shard_map/gathers/concatenate | solution.py:151
  10.6 3.3 %collective-permute-start = (bf16[1024,576]{0,1:T(8,128)(2,1)}, bf16[1024,576]{0,1:T(8,128)(2,1)S(1)}, u32[]{:S(2)}, u32[]{:S(2)}) collective-permute-start(bf16[1024,576]{0,1:T(8,128)(2,1)} %param.11), channel_id=1, source_target_pairs={{0,32},{32,0},{64,96},{96,64},{128,160},{160,128},{192,224},{224,1... | collective-permute-start | bytes 3538952 | tf_op jit(solution)/shard_map/gathers/ppermute | solution.py:74
  13.9 2.7 %collective-permute-done = bf16[1024,576]{0,1:T(8,128)(2,1)S(1)} collective-permute-done((bf16[1024,576]{0,1:T(8,128)(2,1)}, bf16[1024,576]{0,1:T(8,128)(2,1)S(1)}, u32[]{:S(2)}, u32[]{:S(2)}) %collective-permute-start) | collective-permute-done | bytes 1179680 | tf_op jit(solution)/shard_map/gathers/ppermute | solution.py:74
  16.6 2.3 %maximum_select_fusion = bf16[1024,1152]{0,1:T(8,128)(2,1)S(1)} fusion(bf16[1024,576]{0,1:T(8,128)(2,1)S(1)} %collective-permute-done, bf16[1024,576]{0,1:T(8,128)(2,1)} %param.11, pred[]{:T(512)S(6)} %eq.98), kind=kLoop, calls=%fused_computation.15 | loop fusion | flops 10616832 | bytes 4718593 | tf_op jit(solution)/shard_map/gathers/jit(_where)/select_n | solution.py:75
  18.9 1.1 collective-permute-start.1
  20.0 0.5 and_select_fusion.1
  20.5 26.5 %collective-permute-done.1 = bf16[1024,1152]{0,1:T(8,128)(2,1)} collective-permute-done((bf16[1024,1152]{0,1:T(8,128)(2,1)S(1)}, bf16[1024,1152]{0,1:T(8,128)(2,1)}, u32[]{:S(2)}, u32[]{:S(2)}) %collective-permute-start.1) | collective-permute-done | bytes 2359328 | tf_op jit(solution)/shard_map/gathers/ppermute | solution.py:80
  47.1 2.4 %constant_dynamic-slice_fusion = bf16[512,1152]{0,1:T(8,128)(2,1)} fusion(bf16[1024,1152]{0,1:T(8,128)(2,1)} %collective-permute-done.1, s32[]{:T(128)S(6)} %select_n.183), kind=kLoop, calls=%fused_computation.85 | loop fusion | bytes 2359300 | tf_op jit(solution)/shard_map/gathers/dynamic_slice | solution.py:82
  49.4 2.2 %collective-permute-start.3 = (bf16[512,1152]{0,1:T(8,128)(2,1)}, bf16[512,1152]{0,1:T(8,128)(2,1)S(1)}, u32[]{:S(2)}, u32[]{:S(2)}) collective-permute-start(bf16[512,1152]{0,1:T(8,128)(2,1)} %constant_dynamic-slice_fusion), channel_id=1, source_target_pairs={{0,64},{32,224},{64,128},{96,32},{128,192},{160,96},{192,0},{224,1... | collective-permute-start | bytes 3538952 | tf_op jit(solution)/shard_map/gathers/ppermute | solution.py:83
  51.7 0.6 fusion.30
  52.3 0.8 reduce-window.9
  53.1 0.7 reduce-window.6
  54.0 0.7 pad_clamp_fusion
  54.6 1.2 gather_fusion
  55.9 0.7 select_reduce_fusion.3
  56.6 0.7 fusion.33
  57.3 0.7 fusion.31
  58.0 0.8 select_reduce_fusion.1
  58.8 0.5 compare_select_fusion.2
  59.3 5.8 %collective-permute-done.3 = bf16[512,1152]{0,1:T(8,128)(2,1)S(1)} collective-permute-done((bf16[512,1152]{0,1:T(8,128)(2,1)}, bf16[512,1152]{0,1:T(8,128)(2,1)S(1)}, u32[]{:S(2)}, u32[]{:S(2)}) %collective-permute-start.3) | collective-permute-done | bytes 1179680 | tf_op jit(solution)/shard_map/gathers/ppermute | solution.py:83
  65.1 4.4 %collective-permute-start.4 = (bf16[512,1152]{0,1:T(8,128)(2,1)S(1)}, bf16[512,1152]{0,1:T(8,128)(2,1)}, u32[]{:S(2)}, u32[]{:S(2)}) collective-permute-start(bf16[512,1152]{0,1:T(8,128)(2,1)S(1)} %collective-permute-done.3), channel_id=1, source_target_pairs={{0,32},{32,0},{64,96},{96,64},{128,160},{160,128},{192,224},{224,1... | collective-permute-start | bytes 3538952 | tf_op jit(solution)/shard_map/gathers/ppermute | solution.py:84
  70.0 2.4 %copy.19 = bf16[1024,576]{1,0:T(8,128)(2,1)} copy(bf16[1024,576]{0,1:T(8,128)(2,1)} %param.11) | data formatting | bytes 2359296 | tf_op args[0]
  72.4 0.7 fusion.29
  73.1 0.7 clamp_bitcast_fusion
  73.8 0.7 fusion.36
  74.5 2.4 %multiply_cosine_fusion = (f32[1024,64]{0,1:T(8,128)}, f32[1024,64]{0,1:T(8,128)}) fusion(f32[64]{0:T(128)} %multiply_exponential_fusion, f32[1024]{0:T(1024)S(1)} %subtract_convert_fusion.2), kind=kLoop, calls=%fused_computation.40 | loop fusion | flops 65536 | bytes 528640 | tf_op jit(solution)/shard_map/rotary/cos | solution.py:212
  76.8 4.8 %select_select_fusion.3 = (bf16[1024,1152]{0,1:T(8,128)(2,1)S(1)}, bf16[1024,1152]{0,1:T(8,128)(2,1)S(1)}, bf16[1024,1152]{0,1:T(8,128)(2,1)S(1)}) fusion(bf16[1024,1152]{0,1:T(8,128)(2,1)S(1)} %maximum_select_fusion, pred[]{:T(512)S(6)} %eq.100, pred[]{:T(512)S(6)} %eq.99, pred[]{:T(512)S(6)} %eq.97, bf16[512,1152]{0,1:T(8,128)(2,1)S(1)} %collective-permute-done.3, ...), kind=kLoop, calls=%fused_computation.20 | loop fusion | flops 16515072 | bytes 16515076 | tf_op jit(solution)/shard_map/gathers/jit(_where)/select_n | solution.py:97
  81.7 3.8 %select_select_fusion.1 = bf16[1024,1152]{0,1:T(8,128)(2,1)S(1)} fusion(bf16[1024,1152]{0,1:T(8,128)(2,1)S(1)} %maximum_select_fusion, bf16[1024,1152]{0,1:T(8,128)(2,1)S(1)} %get-tuple-element.15, bf16[1024,1152]{0,1:T(8,128)(2,1)S(1)} %get-tuple-element.14, pred[]{:T(512)S(6)} %eq.106, pred[]{:T(512)S(6)} %eq.105, pred[]{:T(512)S(6)} %eq.104, ...), kind=kLoop, calls=%fused_computation.18 | loop fusion | flops 14155776 | bytes 11796484 | tf_op jit(solution)/shard_map/gathers/jit(_where)/select_n | solution.py:97
  85.5 4.1 %select_select_fusion.2 = (bf16[1024,1152]{0,1:T(8,128)(2,1)S(1)}, bf16[1024,1152]{0,1:T(8,128)(2,1)S(1)}) fusion(bf16[1024,1152]{0,1:T(8,128)(2,1)S(1)} %maximum_select_fusion, bf16[1024,1152]{0,1:T(8,128)(2,1)S(1)} %get-tuple-element.15, bf16[1024,1152]{0,1:T(8,128)(2,1)S(1)} %get-tuple-element.14, pred[]{:T(512)S(6)} %eq.103, pred[]{:T(512)S(6)} %eq.102, ...), kind=kLoop, calls=%fused_computation.19 | loop fusion | flops 17694720 | bytes 14155783 | tf_op jit(solution)/shard_map/gathers/jit(_where)/select_n | solution.py:97
  89.6 4.4 %pad_maximum_fusion = bf16[1024,4608]{0,1:T(8,128)(2,1)} fusion(bf16[1024,1152]{0,1:T(8,128)(2,1)S(1)} %get-tuple-element.17, bf16[1024,1152]{0,1:T(8,128)(2,1)S(1)} %select_select_fusion.1, bf16[1024,1152]{0,1:T(8,128)(2,1)S(1)} %get-tuple-element.16, bf16[1024,1152]{0,1:T(8,128)(2,1)S(1)} %get-tuple-element.13), kind=kLoop, calls=%fused_computation.3 | loop fusion | flops 37748736 | bytes 18874368 | tf_op jit(solution)/shard_map/gathers/concatenate | solution.py:103
  94.0 33.7 %all-gather.3.cloned.1.call-done = bf16[5632,1024]{1,0:T(8,128)(2,1)} async-done(((bf16[176,1024]{1,0:T(8,128)(2,1)}), bf16[5632,1024]{1,0:T(8,128)(2,1)}) %all-gather.3.cloned.1.call-update) | async-done | bytes 11534352 | tf_op jit(solution)/shard_map/gathers/all_gather | solution.py:151
  127.7 4.1 %select_reduce_fusion = f32[1024,32]{0,1:T(8,128)S(1)} fusion(bf16[32,176,1024]{2,1,0:T(8,128)(2,1)} %bitcast.67, bf16[1024,576]{1,0:T(8,128)(2,1)S(1)} %copy-done.6, pred[1024,32]{0,1:T(8,128)(4,1)S(1)} %copy-done.10), kind=kOutput, calls=%fused_computation.12 | convolution fusion | flops 2149548032 | bytes 3440640 | tf_op jit(solution)/shard_map/lowrank/dot_general | solution.py:163
  131.8 1.7 collective-permute-start.5
  133.5 12.5 %fusion.17 = f32[1024,1024]{0,1:T(8,128)S(1)} fusion(bf16[1024,32,144]{0,2,1:T(8,128)(2,1)S(1)} %bitcast.60, bf16[32,176,1024]{2,1,0:T(8,128)(2,1)} %bitcast.68), kind=kOutput, calls=%fused_computation.23 | convolution fusion | flops 9663676416 | bytes 23068672 | tf_op jit(solution)/shard_map/projection/tci,cin->tn/dot_general | solution.py:196
  146.2 1.3 collective-permute-start.6
  148.1 3.2 %collective-permute-done.6 = f32[1024,32]{0,1:T(8,128)S(1)} collective-permute-done((f32[1024,32]{0,1:T(8,128)S(1)}, f32[1024,32]{0,1:T(8,128)S(1)}, u32[]{:S(2)}, u32[]{:S(2)}) %collective-permute-start.6) | collective-permute-done | bytes 131104 | tf_op jit(solution)/shard_map/lowrank/ppermute | solution.py:174
  151.3 3.1 %collective-permute-start.7 = (f32[1024,32]{0,1:T(8,128)S(1)}, f32[1024,32]{0,1:T(8,128)}, u32[]{:S(2)}, u32[]{:S(2)}) collective-permute-start(f32[1024,32]{0,1:T(8,128)S(1)} %add.130), channel_id=1, source_target_pairs={{0,128},{32,160},{64,192},{96,224},{128,0},{160,32},{192,64},{224,... | collective-permute-start | bytes 393224 | tf_op jit(solution)/shard_map/lowrank/ppermute | solution.py:174
  154.4 3.6 %fusion.11 = bf16[2304,256]{1,0:T(8,128)(2,1)} fusion(bf16[1024,256]{0,1:T(8,128)(2,1)S(1)} %bitcast.66, s32[2304]{0:T(1024)S(1)} %copy-done.11, pred[2304]{0:T(1024)(128)(4,1)S(1)} %fusion.29), kind=kOutput, calls=%fused_computation.13 | convolution fusion | flops 1213267968 | bytes 1715456 | tf_op jit(solution)/shard_map/cache_write/dot_general | solution.py:224
  158.0 1.7 slice.62
  159.8 1.2 reshape.336
  161.0 0.8 reshape.341
  162.1 0.9 add_convert_fusion.2
  163.0 1.1 broadcast_multiply_fusion
  164.2 2.3 %slice_add_fusion = f32[1024,512]{0,1:T(8,128)S(1)} fusion(f32[1024,1024]{0,1:T(8,128)} %copy-done.5, bf16[1024,512]{0,1:T(8,128)(2,1)S(1)} %bitcast.64, bf16[512,512]{1,0:T(8,128)(2,1)S(1)} %reshape.337), kind=kOutput, calls=%fused_computation.24 | convolution fusion | flops 537395200 | bytes 5767168 | tf_op jit(solution)/shard_map/lowrank/dot_general | solution.py:184
  166.9 1.3 copy.23
  168.3 4.8 %fusion.14 = bf16[2304,256]{1,0:T(8,128)(2,1)} fusion(s32[2304]{0:T(1024)S(1)} %copy-done.11, pred[2304]{0:T(1024)(128)(4,1)S(1)} %fusion.29, bf16[1024,512]{0,1:T(8,128)(2,1)S(1)} %bitcast.65, bf16[512,256]{1,0:T(8,128)(2,1)S(1)} %copy-done.9, f32[1024,1024]{0,1:T(8,128)} %copy-done.5), kind=kOutput, calls=%fused_computation.14 | convolution fusion | flops 1482227712 | bytes 3550464 | tf_op jit(solution)/shard_map/cache_write/dot_general | solution.py:226
  (51 shorter events, 2.4 us)
Async XLA Ops:
  7.2 47.5 %copy-start = (s32[32]{0:T(128)S(1)}, s32[32]{0:T(128)}, u32[]{:S(2)}) copy-start(s32[32]{0:T(128)} %param.20) | copy-start | bytes 388
  7.2 120.5 %all-gather.3.cloned.1.call-start = ((), (), s32[]{:S(2)}) async-start(), calls=%async_computation | async-start | bytes 11894784 | tf_op jit(solution)/shard_map/gathers/all_gather | solution.py:151
  10.6 6.0 %collective-permute-start = (bf16[1024,576]{0,1:T(8,128)(2,1)}, bf16[1024,576]{0,1:T(8,128)(2,1)S(1)}, u32[]{:S(2)}, u32[]{:S(2)}) collective-permute-start(bf16[1024,576]{0,1:T(8,128)(2,1)} %param.11), channel_id=1, source_target_pairs={{0,32},{32,0},{64,96},{96,64},{128,160},{160,128},{192,224},{224,1... | collective-permute-start | bytes 3538952 | tf_op jit(solution)/shard_map/gathers/ppermute | solution.py:74
  13.9 6.1 %copy-start.12 = (s32[1,10]{1,0:T(1,128)S(1)}, s32[1,10]{1,0:T(1,128)}, u32[]{:S(2)}) copy-start(s32[1,10]{1,0:T(1,128)} %param.18) | copy-start | bytes 124
  18.9 32.8 %copy-start.13 = (s32[1,10]{1,0:T(1,128)S(1)}, s32[1,10]{1,0:T(1,128)}, u32[]{:S(2)}) copy-start(s32[1,10]{1,0:T(1,128)} %param.19) | copy-start | bytes 124
  18.9 28.2 %collective-permute-start.1 = (bf16[1024,1152]{0,1:T(8,128)(2,1)S(1)}, bf16[1024,1152]{0,1:T(8,128)(2,1)}, u32[]{:S(2)}, u32[]{:S(2)}) collective-permute-start(bf16[1024,1152]{0,1:T(8,128)(2,1)S(1)} %maximum_select_fusion), channel_id=1, source_target_pairs={{0,64},{32,224},{64,128},{96,32},{128,192},{160,96},{192,0},{224,1... | collective-permute-start | bytes 7077896 | tf_op jit(solution)/shard_map/gathers/ppermute | solution.py:80
  49.4 15.7 %collective-permute-start.3 = (bf16[512,1152]{0,1:T(8,128)(2,1)}, bf16[512,1152]{0,1:T(8,128)(2,1)S(1)}, u32[]{:S(2)}, u32[]{:S(2)}) collective-permute-start(bf16[512,1152]{0,1:T(8,128)(2,1)} %constant_dynamic-slice_fusion), channel_id=1, source_target_pairs={{0,64},{32,224},{64,128},{96,32},{128,192},{160,96},{192,0},{224,1... | collective-permute-start | bytes 3538952 | tf_op jit(solution)/shard_map/gathers/ppermute | solution.py:83
  53.8 23.1 %collective-permute-start.2 = (bf16[1024,1152]{0,1:T(8,128)(2,1)}, bf16[1024,1152]{0,1:T(8,128)(2,1)}, u32[]{:S(2)}, u32[]{:S(2)}) collective-permute-start(bf16[1024,1152]{0,1:T(8,128)(2,1)} %collective-permute-done.1), channel_id=1, source_target_pairs={{0,32},{32,0},{64,96},{96,64},{128,160},{160,128},{192,224},{224,1... | collective-permute-start | bytes 7077896 | tf_op jit(solution)/shard_map/gathers/ppermute | solution.py:84
  65.1 11.7 %collective-permute-start.4 = (bf16[512,1152]{0,1:T(8,128)(2,1)S(1)}, bf16[512,1152]{0,1:T(8,128)(2,1)}, u32[]{:S(2)}, u32[]{:S(2)}) collective-permute-start(bf16[512,1152]{0,1:T(8,128)(2,1)S(1)} %collective-permute-done.3), channel_id=1, source_target_pairs={{0,32},{32,0},{64,96},{96,64},{128,160},{160,128},{192,224},{224,1... | collective-permute-start | bytes 3538952 | tf_op jit(solution)/shard_map/gathers/ppermute | solution.py:84
  89.6 38.1 %copy-start.6 = (bf16[1024,576]{1,0:T(8,128)(2,1)S(1)}, bf16[1024,576]{1,0:T(8,128)(2,1)}, u32[]{:S(2)}) copy-start(bf16[1024,576]{1,0:T(8,128)(2,1)} %copy.19) | copy-start | bytes 3538948
  89.6 38.1 %copy-start.10 = (pred[1024,32]{0,1:T(8,128)(4,1)S(1)}, pred[1024,32]{0,1:T(8,128)(4,1)}, u32[]{:S(2)}) copy-start(pred[1024,32]{0,1:T(8,128)(4,1)} %get-tuple-element.29) | copy-start | bytes 98308
  127.7 5.8 %copy-start.2 = (bf16[1024,4608]{0,1:T(8,128)(2,1)S(1)}, bf16[1024,4608]{0,1:T(8,128)(2,1)}, u32[]{:S(2)}) copy-start(bf16[1024,4608]{0,1:T(8,128)(2,1)} %pad_maximum_fusion) | copy-start | bytes 28311556
  131.8 14.3 %collective-permute-start.5 = (f32[1024,32]{0,1:T(8,128)S(1)}, f32[1024,32]{0,1:T(8,128)S(1)}, u32[]{:S(2)}, u32[]{:S(2)}) collective-permute-start(f32[1024,32]{0,1:T(8,128)S(1)} %select_reduce_fusion), channel_id=1, source_target_pairs={{0,32},{32,0},{64,96},{96,64},{128,160},{160,128},{192,224},{224,1... | collective-permute-start | bytes 393224 | tf_op jit(solution)/shard_map/lowrank/ppermute | solution.py:174
  146.1 2.0 %copy-start.5 = (f32[1024,1024]{0,1:T(8,128)}, f32[1024,1024]{0,1:T(8,128)S(1)}, u32[]{:S(2)}) copy-start(f32[1024,1024]{0,1:T(8,128)S(1)} %fusion.17) | copy-start | bytes 12582916
  146.1 1.4 copy-start.3
  146.1 1.4 copy-start.4
  146.2 8.2 %copy-start.11 = (s32[2304]{0:T(1024)S(1)}, s32[2304]{0:T(1024)}, u32[]{:S(2)}) copy-start(s32[2304]{0:T(1024)} %clamp_bitcast_fusion) | copy-start | bytes 27652
  146.2 5.1 %collective-permute-start.6 = (f32[1024,32]{0,1:T(8,128)S(1)}, f32[1024,32]{0,1:T(8,128)S(1)}, u32[]{:S(2)}, u32[]{:S(2)}) collective-permute-start(f32[1024,32]{0,1:T(8,128)S(1)} %add.129), channel_id=1, source_target_pairs={{0,64},{32,96},{64,0},{96,32},{128,192},{160,224},{192,128},{224,1... | collective-permute-start | bytes 393224 | tf_op jit(solution)/shard_map/lowrank/ppermute | solution.py:174
  151.3 10.7 %collective-permute-start.7 = (f32[1024,32]{0,1:T(8,128)S(1)}, f32[1024,32]{0,1:T(8,128)}, u32[]{:S(2)}, u32[]{:S(2)}) collective-permute-start(f32[1024,32]{0,1:T(8,128)S(1)} %add.130), channel_id=1, source_target_pairs={{0,128},{32,160},{64,192},{96,224},{128,0},{160,32},{192,64},{224,... | collective-permute-start | bytes 393224 | tf_op jit(solution)/shard_map/lowrank/ppermute | solution.py:174
  159.8 3.3 %copy-start.8 = (bf16[1024,32]{0,1:T(8,128)(2,1)S(1)}, bf16[1024,32]{0,1:T(8,128)(2,1)}, u32[]{:S(2)}) copy-start(bf16[1024,32]{0,1:T(8,128)(2,1)} %get-tuple-element.28) | copy-start | bytes 196612
  166.8 1.4 copy-start.7
  166.9 1.4 copy-start.9
  168.3 4.8 %copy-start.1 = (s32[32]{0:T(128)S(1)}, s32[32]{0:T(128)}, u32[]{:S(2)}) copy-start(s32[32]{0:T(128)} %param.20) | copy-start | bytes 388
Sparse Core Ops, SparseCore 0:
  11.1 116.5 all-gather.2

commit v8 on v7

--- a/solution.py
+++ b/solution.py
@@ -168,11 +168,11 @@
         ).reshape(hidden.shape[0], adapter_count, -1)
         partial = jnp.sum(jnp.where(onehot[:, :, None], partial_all, 0.0), axis=1)
         partial, full_rows = lax.optimization_barrier((partial, full_rows))
-        distance = 1
-        while distance < row_size:
+        distance = row_size // 2
+        while distance >= 1:
             pairs = [(i, i ^ distance) for i in range(row_size)]
             partial = partial + lax.ppermute(partial, "row", pairs)
-            distance *= 2
+            distance //= 2
         lowrank = partial.astype(jnp.bfloat16)
         onehot_b = onehot.astype(jnp.bfloat16)
         spread_query = (onehot_b[:, :, None] * lowrank[:, None, :rank_width]).reshape(

time: 180 us -> 181 us (level)
  no operation moved by 1% of the time
where the time goes in v8:
time: 181 us; the launch traced here: 180 us
  waiting for transfers between devices  70.8 us (39%)
  other arithmetic  35.6 us (20%)
  matrix products  27.4 us (15%)
  starting transfers between devices  17.8 us (10%)
  local copies, waits for them, and re-layouts  14.3 us (8%)
  between operations  14.3 us (8%)
    all_gather x1, waiting for transfers between devices, shards(): packed = lax.all_gather(jnp.concatenate(pieces, axis=0), 'col', axis=0)  33.7 us
    ppermute x1, waiting for transfers between devices, gather_rows(): near = lax.ppermute(own_block, 'row', ring)  26.5 us
    select_n x3, other arithmetic, gather_rows(): jnp.where(relative == 0, own_block, jnp.where(relative == 1, after, jnp.w...  12.7 us
    dot_general x1, matrix products, shards(): jnp.einsum('tci,cin->tn', full_rows.reshape(full_rows.shape[0], packed.sh...  12.5 us
    ppermute x3, starting transfers between devices, shards(): partial = partial + lax.ppermute(partial, 'row', pairs)  6.54 us
    ppermute x1, waiting for transfers between devices, gather_rows(): far_half = lax.ppermute(forwarded, 'row', ring)  5.81 us
    unnamed x31, local copies, waits for them, and re-layouts  5.16 us
    dot_general x1, matrix products, shards(): jnp.dot(select, value_rows, preferred_element_type=jnp.float32)  4.78 us
  transfers between devices with their start and end apart: 9, of which 5 were waited for; matrix products, arithmetic and copies ran while one was open for 32% of the time, Pallas kernels for 0%

profile of v8, /device:TPU:1, one launch (start us, length us, event | category | flops | bytes accessed | tf_op | source)
XLA Modules:
  0.0 180.1 jit_solution(16828652220218933441)
XLA Ops:
  7.2 0.7 copy.24
  8.0 0.7 copy.25
  8.8 1.8 %maximum_maximum_fusion = bf16[176,1024]{1,0:T(8,128)(2,1)} fusion(bf16[32,448]{1,0:T(8,128)(2,1)S(1)} %reshape.334, bf16[32,576]{1,0:T(8,128)(2,1)} %bitcast.71, bf16[144,256]{1,0:T(8,128)(2,1)} %param.14, bf16[144,256]{1,0:T(8,128)(2,1)} %param.13, bf16[144,512]{1,0:T(8,128)(2,1)} %param.12), kind=kLoop, calls=%fused_computation.41 | loop fusion | flops 1802240 | bytes 720896 | tf_op jit(solution)/shard_map/gathers/concatenate | solution.py:151
  10.6 3.3 %collective-permute-start = (bf16[1024,576]{0,1:T(8,128)(2,1)}, bf16[1024,576]{0,1:T(8,128)(2,1)S(1)}, u32[]{:S(2)}, u32[]{:S(2)}) collective-permute-start(bf16[1024,576]{0,1:T(8,128)(2,1)} %param.11), channel_id=1, source_target_pairs={{0,32},{32,0},{64,96},{96,64},{128,160},{160,128},{192,224},{224,1... | collective-permute-start | bytes 3538952 | tf_op jit(solution)/shard_map/gathers/ppermute | solution.py:74
  13.9 2.7 %collective-permute-done = bf16[1024,576]{0,1:T(8,128)(2,1)S(1)} collective-permute-done((bf16[1024,576]{0,1:T(8,128)(2,1)}, bf16[1024,576]{0,1:T(8,128)(2,1)S(1)}, u32[]{:S(2)}, u32[]{:S(2)}) %collective-permute-start) | collective-permute-done | bytes 1179680 | tf_op jit(solution)/shard_map/gathers/ppermute | solution.py:74
  16.6 2.3 %maximum_select_fusion = bf16[1024,1152]{0,1:T(8,128)(2,1)S(1)} fusion(bf16[1024,576]{0,1:T(8,128)(2,1)S(1)} %collective-permute-done, bf16[1024,576]{0,1:T(8,128)(2,1)} %param.11, pred[]{:T(512)S(6)} %eq.98), kind=kLoop, calls=%fused_computation.15 | loop fusion | flops 10616832 | bytes 4718593 | tf_op jit(solution)/shard_map/gathers/jit(_where)/select_n | solution.py:75
  18.9 1.1 collective-permute-start.1
  20.0 0.5 and_select_fusion.1
  20.5 26.5 %collective-permute-done.1 = bf16[1024,1152]{0,1:T(8,128)(2,1)} collective-permute-done((bf16[1024,1152]{0,1:T(8,128)(2,1)S(1)}, bf16[1024,1152]{0,1:T(8,128)(2,1)}, u32[]{:S(2)}, u32[]{:S(2)}) %collective-permute-start.1) | collective-permute-done | bytes 2359328 | tf_op jit(solution)/shard_map/gathers/ppermute | solution.py:80
  47.1 2.4 %constant_dynamic-slice_fusion = bf16[512,1152]{0,1:T(8,128)(2,1)} fusion(bf16[1024,1152]{0,1:T(8,128)(2,1)} %collective-permute-done.1, s32[]{:T(128)S(6)} %select_n.183), kind=kLoop, calls=%fused_computation.85 | loop fusion | bytes 2359300 | tf_op jit(solution)/shard_map/gathers/dynamic_slice | solution.py:82
  49.4 2.2 %collective-permute-start.3 = (bf16[512,1152]{0,1:T(8,128)(2,1)}, bf16[512,1152]{0,1:T(8,128)(2,1)S(1)}, u32[]{:S(2)}, u32[]{:S(2)}) collective-permute-start(bf16[512,1152]{0,1:T(8,128)(2,1)} %constant_dynamic-slice_fusion), channel_id=1, source_target_pairs={{0,64},{32,224},{64,128},{96,32},{128,192},{160,96},{192,0},{224,1... | collective-permute-start | bytes 3538952 | tf_op jit(solution)/shard_map/gathers/ppermute | solution.py:83
  51.7 0.6 fusion.30
  52.3 0.8 reduce-window.9
  53.1 0.7 reduce-window.6
  54.0 0.7 pad_clamp_fusion
  54.6 1.2 gather_fusion
  55.9 0.7 select_reduce_fusion.3
  56.6 0.7 fusion.33
  57.3 0.7 fusion.31
  58.0 0.8 select_reduce_fusion.1
  58.8 0.5 compare_select_fusion.2
  59.3 5.8 %collective-permute-done.3 = bf16[512,1152]{0,1:T(8,128)(2,1)S(1)} collective-permute-done((bf16[512,1152]{0,1:T(8,128)(2,1)}, bf16[512,1152]{0,1:T(8,128)(2,1)S(1)}, u32[]{:S(2)}, u32[]{:S(2)}) %collective-permute-start.3) | collective-permute-done | bytes 1179680 | tf_op jit(solution)/shard_map/gathers/ppermute | solution.py:83
  65.1 4.4 %collective-permute-start.4 = (bf16[512,1152]{0,1:T(8,128)(2,1)S(1)}, bf16[512,1152]{0,1:T(8,128)(2,1)}, u32[]{:S(2)}, u32[]{:S(2)}) collective-permute-start(bf16[512,1152]{0,1:T(8,128)(2,1)S(1)} %collective-permute-done.3), channel_id=1, source_target_pairs={{0,32},{32,0},{64,96},{96,64},{128,160},{160,128},{192,224},{224,1... | collective-permute-start | bytes 3538952 | tf_op jit(solution)/shard_map/gathers/ppermute | solution.py:84
  70.0 2.4 %copy.19 = bf16[1024,576]{1,0:T(8,128)(2,1)} copy(bf16[1024,576]{0,1:T(8,128)(2,1)} %param.11) | data formatting | bytes 2359296 | tf_op args[0]
  72.4 0.7 fusion.29
  73.1 0.7 clamp_bitcast_fusion
  73.8 0.7 fusion.36
  74.5 2.4 %multiply_cosine_fusion = (f32[1024,64]{0,1:T(8,128)}, f32[1024,64]{0,1:T(8,128)}) fusion(f32[64]{0:T(128)} %multiply_exponential_fusion, f32[1024]{0:T(1024)S(1)} %subtract_convert_fusion.2), kind=kLoop, calls=%fused_computation.40 | loop fusion | flops 65536 | bytes 528640 | tf_op jit(solution)/shard_map/rotary/cos | solution.py:212
  76.8 4.8 %select_select_fusion.3 = (bf16[1024,1152]{0,1:T(8,128)(2,1)S(1)}, bf16[1024,1152]{0,1:T(8,128)(2,1)S(1)}, bf16[1024,1152]{0,1:T(8,128)(2,1)S(1)}) fusion(bf16[1024,1152]{0,1:T(8,128)(2,1)S(1)} %maximum_select_fusion, pred[]{:T(512)S(6)} %eq.100, pred[]{:T(512)S(6)} %eq.99, pred[]{:T(512)S(6)} %eq.97, bf16[512,1152]{0,1:T(8,128)(2,1)S(1)} %collective-permute-done.3, ...), kind=kLoop, calls=%fused_computation.20 | loop fusion | flops 16515072 | bytes 16515076 | tf_op jit(solution)/shard_map/gathers/jit(_where)/select_n | solution.py:97
  81.7 3.8 %select_select_fusion.1 = bf16[1024,1152]{0,1:T(8,128)(2,1)S(1)} fusion(bf16[1024,1152]{0,1:T(8,128)(2,1)S(1)} %maximum_select_fusion, bf16[1024,1152]{0,1:T(8,128)(2,1)S(1)} %get-tuple-element.15, bf16[1024,1152]{0,1:T(8,128)(2,1)S(1)} %get-tuple-element.14, pred[]{:T(512)S(6)} %eq.106, pred[]{:T(512)S(6)} %eq.105, pred[]{:T(512)S(6)} %eq.104, ...), kind=kLoop, calls=%fused_computation.18 | loop fusion | flops 14155776 | bytes 11796484 | tf_op jit(solution)/shard_map/gathers/jit(_where)/select_n | solution.py:97
  85.5 4.1 %select_select_fusion.2 = (bf16[1024,1152]{0,1:T(8,128)(2,1)S(1)}, bf16[1024,1152]{0,1:T(8,128)(2,1)S(1)}) fusion(bf16[1024,1152]{0,1:T(8,128)(2,1)S(1)} %maximum_select_fusion, bf16[1024,1152]{0,1:T(8,128)(2,1)S(1)} %get-tuple-element.15, bf16[1024,1152]{0,1:T(8,128)(2,1)S(1)} %get-tuple-element.14, pred[]{:T(512)S(6)} %eq.103, pred[]{:T(512)S(6)} %eq.102, ...), kind=kLoop, calls=%fused_computation.19 | loop fusion | flops 17694720 | bytes 14155783 | tf_op jit(solution)/shard_map/gathers/jit(_where)/select_n | solution.py:97
  89.6 4.4 %pad_maximum_fusion = bf16[1024,4608]{0,1:T(8,128)(2,1)} fusion(bf16[1024,1152]{0,1:T(8,128)(2,1)S(1)} %get-tuple-element.17, bf16[1024,1152]{0,1:T(8,128)(2,1)S(1)} %select_select_fusion.1, bf16[1024,1152]{0,1:T(8,128)(2,1)S(1)} %get-tuple-element.16, bf16[1024,1152]{0,1:T(8,128)(2,1)S(1)} %get-tuple-element.13), kind=kLoop, calls=%fused_computation.3 | loop fusion | flops 37748736 | bytes 18874368 | tf_op jit(solution)/shard_map/gathers/concatenate | solution.py:103
  94.0 33.7 %all-gather.3.cloned.1.call-done = bf16[5632,1024]{1,0:T(8,128)(2,1)} async-done(((bf16[176,1024]{1,0:T(8,128)(2,1)}), bf16[5632,1024]{1,0:T(8,128)(2,1)}) %all-gather.3.cloned.1.call-update) | async-done | bytes 11534352 | tf_op jit(solution)/shard_map/gathers/all_gather | solution.py:151
  127.7 4.1 %select_reduce_fusion = f32[1024,32]{0,1:T(8,128)S(1)} fusion(bf16[32,176,1024]{2,1,0:T(8,128)(2,1)} %bitcast.67, bf16[1024,576]{1,0:T(8,128)(2,1)S(1)} %copy-done.6, pred[1024,32]{0,1:T(8,128)(4,1)S(1)} %copy-done.10), kind=kOutput, calls=%fused_computation.12 | convolution fusion | flops 2149548032 | bytes 3440640 | tf_op jit(solution)/shard_map/lowrank/dot_general | solution.py:163
  131.8 3.0 %collective-permute-start.5 = (f32[1024,32]{0,1:T(8,128)S(1)}, f32[1024,32]{0,1:T(8,128)S(1)}, u32[]{:S(2)}, u32[]{:S(2)}) collective-permute-start(f32[1024,32]{0,1:T(8,128)S(1)} %select_reduce_fusion), channel_id=1, source_target_pairs={{0,128},{32,160},{64,192},{96,224},{128,0},{160,32},{192,64},{224,... | collective-permute-start | bytes 393224 | tf_op jit(solution)/shard_map/lowrank/ppermute | solution.py:174
  134.8 12.5 %fusion.17 = f32[1024,1024]{0,1:T(8,128)S(1)} fusion(bf16[1024,32,144]{0,2,1:T(8,128)(2,1)S(1)} %bitcast.60, bf16[32,176,1024]{2,1,0:T(8,128)(2,1)} %bitcast.68), kind=kOutput, calls=%fused_computation.23 | convolution fusion | flops 9663676416 | bytes 23068672 | tf_op jit(solution)/shard_map/projection/tci,cin->tn/dot_general | solution.py:196
  148.0 0.6 copy-done.3
  149.4 2.0 %collective-permute-done.6 = f32[1024,32]{0,1:T(8,128)S(1)} collective-permute-done((f32[1024,32]{0,1:T(8,128)S(1)}, f32[1024,32]{0,1:T(8,128)S(1)}, u32[]{:S(2)}, u32[]{:S(2)}) %collective-permute-start.6) | collective-permute-done | bytes 131104 | tf_op jit(solution)/shard_map/lowrank/ppermute | solution.py:174
  151.5 3.1 %collective-permute-start.7 = (f32[1024,32]{0,1:T(8,128)S(1)}, f32[1024,32]{0,1:T(8,128)}, u32[]{:S(2)}, u32[]{:S(2)}) collective-permute-start(f32[1024,32]{0,1:T(8,128)S(1)} %add.130), channel_id=1, source_target_pairs={{0,32},{32,0},{64,96},{96,64},{128,160},{160,128},{192,224},{224,1... | collective-permute-start | bytes 393224 | tf_op jit(solution)/shard_map/lowrank/ppermute | solution.py:174
  154.6 3.6 %fusion.11 = bf16[2304,256]{1,0:T(8,128)(2,1)} fusion(bf16[1024,256]{0,1:T(8,128)(2,1)S(1)} %bitcast.66, s32[2304]{0:T(1024)S(1)} %copy-done.11, pred[2304]{0:T(1024)(128)(4,1)S(1)} %fusion.29), kind=kOutput, calls=%fused_computation.13 | convolution fusion | flops 1213267968 | bytes 1715456 | tf_op jit(solution)/shard_map/cache_write/dot_general | solution.py:224
  158.2 1.7 slice.62
  160.0 1.2 reshape.336
  161.2 0.8 reshape.341
  162.3 0.9 add_convert_fusion.2
  163.3 1.1 broadcast_multiply_fusion
  164.4 2.3 %slice_add_fusion = f32[1024,512]{0,1:T(8,128)S(1)} fusion(f32[1024,1024]{0,1:T(8,128)} %copy-done.5, bf16[1024,512]{0,1:T(8,128)(2,1)S(1)} %bitcast.64, bf16[512,512]{1,0:T(8,128)(2,1)S(1)} %reshape.337), kind=kOutput, calls=%fused_computation.24 | convolution fusion | flops 537395200 | bytes 5767168 | tf_op jit(solution)/shard_map/lowrank/dot_general | solution.py:184
  167.2 1.3 copy.23
  168.5 4.8 %fusion.14 = bf16[2304,256]{1,0:T(8,128)(2,1)} fusion(s32[2304]{0:T(1024)S(1)} %copy-done.11, pred[2304]{0:T(1024)(128)(4,1)S(1)} %fusion.29, bf16[1024,512]{0,1:T(8,128)(2,1)S(1)} %bitcast.65, bf16[512,256]{1,0:T(8,128)(2,1)S(1)} %copy-done.9, f32[1024,1024]{0,1:T(8,128)} %copy-done.5), kind=kOutput, calls=%fused_computation.14 | convolution fusion | flops 1482227712 | bytes 3550464 | tf_op jit(solution)/shard_map/cache_write/dot_general | solution.py:226
  (51 shorter events, 3.1 us)
Async XLA Ops:
  7.2 47.5 %copy-start = (s32[32]{0:T(128)S(1)}, s32[32]{0:T(128)}, u32[]{:S(2)}) copy-start(s32[32]{0:T(128)} %param.20) | copy-start | bytes 388
  7.2 120.5 %all-gather.3.cloned.1.call-start = ((), (), s32[]{:S(2)}) async-start(), calls=%async_computation | async-start | bytes 11894784 | tf_op jit(solution)/shard_map/gathers/all_gather | solution.py:151
  10.6 6.0 %collective-permute-start = (bf16[1024,576]{0,1:T(8,128)(2,1)}, bf16[1024,576]{0,1:T(8,128)(2,1)S(1)}, u32[]{:S(2)}, u32[]{:S(2)}) collective-permute-start(bf16[1024,576]{0,1:T(8,128)(2,1)} %param.11), channel_id=1, source_target_pairs={{0,32},{32,0},{64,96},{96,64},{128,160},{160,128},{192,224},{224,1... | collective-permute-start | bytes 3538952 | tf_op jit(solution)/shard_map/gathers/ppermute | solution.py:74
  13.9 6.1 %copy-start.12 = (s32[1,10]{1,0:T(1,128)S(1)}, s32[1,10]{1,0:T(1,128)}, u32[]{:S(2)}) copy-start(s32[1,10]{1,0:T(1,128)} %param.18) | copy-start | bytes 124
  18.9 32.8 %copy-start.13 = (s32[1,10]{1,0:T(1,128)S(1)}, s32[1,10]{1,0:T(1,128)}, u32[]{:S(2)}) copy-start(s32[1,10]{1,0:T(1,128)} %param.19) | copy-start | bytes 124
  18.9 28.2 %collective-permute-start.1 = (bf16[1024,1152]{0,1:T(8,128)(2,1)S(1)}, bf16[1024,1152]{0,1:T(8,128)(2,1)}, u32[]{:S(2)}, u32[]{:S(2)}) collective-permute-start(bf16[1024,1152]{0,1:T(8,128)(2,1)S(1)} %maximum_select_fusion), channel_id=1, source_target_pairs={{0,64},{32,224},{64,128},{96,32},{128,192},{160,96},{192,0},{224,1... | collective-permute-start | bytes 7077896 | tf_op jit(solution)/shard_map/gathers/ppermute | solution.py:80
  49.4 15.7 %collective-permute-start.3 = (bf16[512,1152]{0,1:T(8,128)(2,1)}, bf16[512,1152]{0,1:T(8,128)(2,1)S(1)}, u32[]{:S(2)}, u32[]{:S(2)}) collective-permute-start(bf16[512,1152]{0,1:T(8,128)(2,1)} %constant_dynamic-slice_fusion), channel_id=1, source_target_pairs={{0,64},{32,224},{64,128},{96,32},{128,192},{160,96},{192,0},{224,1... | collective-permute-start | bytes 3538952 | tf_op jit(solution)/shard_map/gathers/ppermute | solution.py:83
  53.8 23.1 %collective-permute-start.2 = (bf16[1024,1152]{0,1:T(8,128)(2,1)}, bf16[1024,1152]{0,1:T(8,128)(2,1)}, u32[]{:S(2)}, u32[]{:S(2)}) collective-permute-start(bf16[1024,1152]{0,1:T(8,128)(2,1)} %collective-permute-done.1), channel_id=1, source_target_pairs={{0,32},{32,0},{64,96},{96,64},{128,160},{160,128},{192,224},{224,1... | collective-permute-start | bytes 7077896 | tf_op jit(solution)/shard_map/gathers/ppermute | solution.py:84
  65.1 11.7 %collective-permute-start.4 = (bf16[512,1152]{0,1:T(8,128)(2,1)S(1)}, bf16[512,1152]{0,1:T(8,128)(2,1)}, u32[]{:S(2)}, u32[]{:S(2)}) collective-permute-start(bf16[512,1152]{0,1:T(8,128)(2,1)S(1)} %collective-permute-done.3), channel_id=1, source_target_pairs={{0,32},{32,0},{64,96},{96,64},{128,160},{160,128},{192,224},{224,1... | collective-permute-start | bytes 3538952 | tf_op jit(solution)/shard_map/gathers/ppermute | solution.py:84
  89.6 38.1 %copy-start.6 = (bf16[1024,576]{1,0:T(8,128)(2,1)S(1)}, bf16[1024,576]{1,0:T(8,128)(2,1)}, u32[]{:S(2)}) copy-start(bf16[1024,576]{1,0:T(8,128)(2,1)} %copy.19) | copy-start | bytes 3538948
  89.6 38.1 %copy-start.10 = (pred[1024,32]{0,1:T(8,128)(4,1)S(1)}, pred[1024,32]{0,1:T(8,128)(4,1)}, u32[]{:S(2)}) copy-start(pred[1024,32]{0,1:T(8,128)(4,1)} %get-tuple-element.29) | copy-start | bytes 98308
  127.7 7.1 %copy-start.2 = (bf16[1024,4608]{0,1:T(8,128)(2,1)S(1)}, bf16[1024,4608]{0,1:T(8,128)(2,1)}, u32[]{:S(2)}) copy-start(bf16[1024,4608]{0,1:T(8,128)(2,1)} %pad_maximum_fusion) | copy-start | bytes 28311556
  131.8 15.7 %collective-permute-start.5 = (f32[1024,32]{0,1:T(8,128)S(1)}, f32[1024,32]{0,1:T(8,128)S(1)}, u32[]{:S(2)}, u32[]{:S(2)}) collective-permute-start(f32[1024,32]{0,1:T(8,128)S(1)} %select_reduce_fusion), channel_id=1, source_target_pairs={{0,128},{32,160},{64,192},{96,224},{128,0},{160,32},{192,64},{224,... | collective-permute-start | bytes 393224 | tf_op jit(solution)/shard_map/lowrank/ppermute | solution.py:174
  147.4 2.0 %copy-start.5 = (f32[1024,1024]{0,1:T(8,128)}, f32[1024,1024]{0,1:T(8,128)S(1)}, u32[]{:S(2)}) copy-start(f32[1024,1024]{0,1:T(8,128)S(1)} %fusion.17) | copy-start | bytes 12582916
  147.4 1.1 copy-start.3
  147.4 1.4 copy-start.4
  147.5 7.1 %copy-start.11 = (s32[2304]{0:T(1024)S(1)}, s32[2304]{0:T(1024)}, u32[]{:S(2)}) copy-start(s32[2304]{0:T(1024)} %clamp_bitcast_fusion) | copy-start | bytes 27652
  147.5 3.9 %collective-permute-start.6 = (f32[1024,32]{0,1:T(8,128)S(1)}, f32[1024,32]{0,1:T(8,128)S(1)}, u32[]{:S(2)}, u32[]{:S(2)}) collective-permute-start(f32[1024,32]{0,1:T(8,128)S(1)} %add.129), channel_id=1, source_target_pairs={{0,64},{32,96},{64,0},{96,32},{128,192},{160,224},{192,128},{224,1... | collective-permute-start | bytes 393224 | tf_op jit(solution)/shard_map/lowrank/ppermute | solution.py:174
  151.5 10.8 %collective-permute-start.7 = (f32[1024,32]{0,1:T(8,128)S(1)}, f32[1024,32]{0,1:T(8,128)}, u32[]{:S(2)}, u32[]{:S(2)}) collective-permute-start(f32[1024,32]{0,1:T(8,128)S(1)} %add.130), channel_id=1, source_target_pairs={{0,32},{32,0},{64,96},{96,64},{128,160},{160,128},{192,224},{224,1... | collective-permute-start | bytes 393224 | tf_op jit(solution)/shard_map/lowrank/ppermute | solution.py:174
  160.0 3.3 %copy-start.8 = (bf16[1024,32]{0,1:T(8,128)(2,1)S(1)}, bf16[1024,32]{0,1:T(8,128)(2,1)}, u32[]{:S(2)}) copy-start(bf16[1024,32]{0,1:T(8,128)(2,1)} %get-tuple-element.28) | copy-start | bytes 196612
  167.1 1.4 copy-start.7
  167.1 1.4 copy-start.9
  168.5 4.8 %copy-start.1 = (s32[32]{0:T(128)S(1)}, s32[32]{0:T(128)}, u32[]{:S(2)}) copy-start(s32[32]{0:T(128)} %param.20) | copy-start | bytes 388
Sparse Core Ops, SparseCore 0:
  11.1 116.5 all-gather.2

commit v9 on v7

--- a/solution.py
+++ b/solution.py
@@ -171,7 +171,12 @@
         distance = 1
         while distance < row_size:
             pairs = [(i, i ^ distance) for i in range(row_size)]
-            partial = partial + lax.ppermute(partial, "row", pairs)
+            received = lax.ppermute(partial, "row", pairs)
+            if distance == 2:
+                received, up_query, up_value = lax.optimization_barrier(
+                    (received, up_query, up_value)
+                )
+            partial = partial + received
             distance *= 2
         lowrank = partial.astype(jnp.bfloat16)
         onehot_b = onehot.astype(jnp.bfloat16)

time: 180 us -> 174 us (0.967)
  waiting for transfers between devices: 72 us -> 68.1 us
    ppermute x3, waiting for transfers between devices: 3.23 us -> 0.01 us  [shards(): received = lax.ppermute(partial, 'row', pairs)]
    unnamed x31 -> x37, local copies, waits for them, and re-layouts: 4.27 us -> 4.85 us
  transfers between devices with their start and end apart: 9 -> 9, of which waited for: 5 -> 4; matrix products, arithmetic and copies ran while one was open for 32% -> 34% of each run, Pallas kernels for 0% -> 0%
where the time goes in v9:
time: 174 us; the launch traced here: 173 us
  waiting for transfers between devices  68.1 us (39%)
  other arithmetic  35.1 us (20%)
  matrix products  25.9 us (15%)
  starting transfers between devices  17.2 us (10%)
  between operations  14.3 us (8%)
  local copies, waits for them, and re-layouts  12.8 us (7%)
    all_gather x1, waiting for transfers between devices, shards(): packed = lax.all_gather(jnp.concatenate(pieces, axis=0), 'col', axis=0)  33.4 us
    ppermute x1, waiting for transfers between devices, gather_rows(): near = lax.ppermute(own_block, 'row', ring)  26.5 us
    select_n x3, other arithmetic, gather_rows(): jnp.where(relative == 0, own_block, jnp.where(relative == 1, after, jnp.w...  12.8 us
    dot_general x1, matrix products, shards(): jnp.einsum('tci,cin->tn', full_rows.reshape(full_rows.shape[0], packed.sh...  12.5 us
    ppermute x3, starting transfers between devices, shards(): received = lax.ppermute(partial, 'row', pairs)  5.98 us
    ppermute x1, waiting for transfers between devices, gather_rows(): far_half = lax.ppermute(forwarded, 'row', ring)  5.38 us
    unnamed x37, local copies, waits for them, and re-layouts  4.85 us
    dot_general x1, matrix products, shards(): jnp.dot(select, value_rows, preferred_element_type=jnp.float32)  4.78 us
  transfers between devices with their start and end apart: 9, of which 4 were waited for; matrix products, arithmetic and copies ran while one was open for 34% of the time, Pallas kernels for 0%

profile of v9, /device:TPU:1, one launch (start us, length us, event | category | flops | bytes accessed | tf_op | source)
XLA Modules:
  0.0 173.4 jit_solution(11439551209812392678)
XLA Ops:
  7.2 0.7 copy.27
  8.0 0.7 copy.28
  8.8 1.8 %maximum_maximum_fusion = bf16[176,1024]{1,0:T(8,128)(2,1)} fusion(bf16[32,448]{1,0:T(8,128)(2,1)S(1)} %reshape.312, bf16[32,576]{1,0:T(8,128)(2,1)} %bitcast.81, bf16[144,256]{1,0:T(8,128)(2,1)} %param.14, bf16[144,256]{1,0:T(8,128)(2,1)} %param.13, bf16[144,512]{1,0:T(8,128)(2,1)} %param.12), kind=kLoop, calls=%fused_computation.47 | loop fusion | flops 1802240 | bytes 720896 | tf_op jit(solution)/shard_map/gathers/concatenate | solution.py:151
  10.6 3.3 %collective-permute-start = (bf16[1024,576]{0,1:T(8,128)(2,1)}, bf16[1024,576]{0,1:T(8,128)(2,1)S(1)}, u32[]{:S(2)}, u32[]{:S(2)}) collective-permute-start(bf16[1024,576]{0,1:T(8,128)(2,1)} %param.11), channel_id=1, source_target_pairs={{0,32},{32,0},{64,96},{96,64},{128,160},{160,128},{192,224},{224,1... | collective-permute-start | bytes 3538952 | tf_op jit(solution)/shard_map/gathers/ppermute | solution.py:74
  13.9 2.7 %collective-permute-done = bf16[1024,576]{0,1:T(8,128)(2,1)S(1)} collective-permute-done((bf16[1024,576]{0,1:T(8,128)(2,1)}, bf16[1024,576]{0,1:T(8,128)(2,1)S(1)}, u32[]{:S(2)}, u32[]{:S(2)}) %collective-permute-start) | collective-permute-done | bytes 1179680 | tf_op jit(solution)/shard_map/gathers/ppermute | solution.py:74
  16.6 2.3 %maximum_select_fusion = bf16[1024,1152]{0,1:T(8,128)(2,1)S(1)} fusion(bf16[1024,576]{0,1:T(8,128)(2,1)S(1)} %collective-permute-done, bf16[1024,576]{0,1:T(8,128)(2,1)} %param.11, pred[]{:T(512)S(6)} %eq.98), kind=kLoop, calls=%fused_computation.15 | loop fusion | flops 10616832 | bytes 4718593 | tf_op jit(solution)/shard_map/gathers/jit(_where)/select_n | solution.py:75
  18.9 1.1 collective-permute-start.1
  20.0 0.5 and_select_fusion.1
  20.5 26.5 %collective-permute-done.1 = bf16[1024,1152]{0,1:T(8,128)(2,1)} collective-permute-done((bf16[1024,1152]{0,1:T(8,128)(2,1)S(1)}, bf16[1024,1152]{0,1:T(8,128)(2,1)}, u32[]{:S(2)}, u32[]{:S(2)}) %collective-permute-start.1) | collective-permute-done | bytes 2359328 | tf_op jit(solution)/shard_map/gathers/ppermute | solution.py:80
  47.1 2.4 %constant_dynamic-slice_fusion = bf16[512,1152]{0,1:T(8,128)(2,1)} fusion(bf16[1024,1152]{0,1:T(8,128)(2,1)} %collective-permute-done.1, s32[]{:T(128)S(6)} %select_n.183), kind=kLoop, calls=%fused_computation.92 | loop fusion | bytes 2359300 | tf_op jit(solution)/shard_map/gathers/dynamic_slice | solution.py:82
  49.4 2.2 %collective-permute-start.3 = (bf16[512,1152]{0,1:T(8,128)(2,1)}, bf16[512,1152]{0,1:T(8,128)(2,1)S(1)}, u32[]{:S(2)}, u32[]{:S(2)}) collective-permute-start(bf16[512,1152]{0,1:T(8,128)(2,1)} %constant_dynamic-slice_fusion), channel_id=1, source_target_pairs={{0,64},{32,224},{64,128},{96,32},{128,192},{160,96},{192,0},{224,1... | collective-permute-start | bytes 3538952 | tf_op jit(solution)/shard_map/gathers/ppermute | solution.py:83
  51.7 0.5 fusion.43
  52.2 0.8 reduce-window.9
  53.0 0.7 reduce-window.6
  53.9 0.6 pad_clamp_fusion
  54.5 1.2 gather_fusion
  55.7 0.7 select_reduce_fusion.3
  56.4 0.7 fusion.46
  57.1 0.7 fusion.44
  57.7 0.8 select_reduce_fusion.1
  58.5 0.7 select_reduce_fusion.4
  59.2 0.5 compare_select_fusion.2
  59.8 5.4 %collective-permute-done.3 = bf16[512,1152]{0,1:T(8,128)(2,1)S(1)} collective-permute-done((bf16[512,1152]{0,1:T(8,128)(2,1)}, bf16[512,1152]{0,1:T(8,128)(2,1)S(1)}, u32[]{:S(2)}, u32[]{:S(2)}) %collective-permute-start.3) | collective-permute-done | bytes 1179680 | tf_op jit(solution)/shard_map/gathers/ppermute | solution.py:83
  65.1 4.4 %collective-permute-start.4 = (bf16[512,1152]{0,1:T(8,128)(2,1)S(1)}, bf16[512,1152]{0,1:T(8,128)(2,1)}, u32[]{:S(2)}, u32[]{:S(2)}) collective-permute-start(bf16[512,1152]{0,1:T(8,128)(2,1)S(1)} %collective-permute-done.3), channel_id=1, source_target_pairs={{0,32},{32,0},{64,96},{96,64},{128,160},{160,128},{192,224},{224,1... | collective-permute-start | bytes 3538952 | tf_op jit(solution)/shard_map/gathers/ppermute | solution.py:84
  69.5 0.6 multiply_exponential_fusion
  70.1 2.4 %copy.19 = bf16[1024,576]{1,0:T(8,128)(2,1)} copy(bf16[1024,576]{0,1:T(8,128)(2,1)} %param.11) | data formatting | bytes 2359296 | tf_op args[0]
  72.6 1.3 clamp_bitcast_fusion
  73.9 0.7 fusion.49
  74.6 2.5 %multiply_cosine_fusion = (f32[1024,64]{0,1:T(8,128)}, f32[1024,64]{0,1:T(8,128)}) fusion(f32[64]{0:T(128)} %multiply_exponential_fusion, f32[1024]{0:T(1024)S(1)} %subtract_convert_fusion.2), kind=kLoop, calls=%fused_computation.46 | loop fusion | flops 65536 | bytes 528640 | tf_op jit(solution)/shard_map/rotary/cos | solution.py:217
  77.1 4.9 %select_select_fusion.3 = (bf16[1024,1152]{0,1:T(8,128)(2,1)S(1)}, bf16[1024,1152]{0,1:T(8,128)(2,1)S(1)}, bf16[1024,1152]{0,1:T(8,128)(2,1)S(1)}) fusion(bf16[1024,1152]{0,1:T(8,128)(2,1)S(1)} %maximum_select_fusion, pred[]{:T(512)S(6)} %eq.100, pred[]{:T(512)S(6)} %eq.99, pred[]{:T(512)S(6)} %eq.97, bf16[512,1152]{0,1:T(8,128)(2,1)S(1)} %collective-permute-done.3, ...), kind=kLoop, calls=%fused_computation.20 | loop fusion | flops 16515072 | bytes 16515076 | tf_op jit(solution)/shard_map/gathers/jit(_where)/select_n | solution.py:97
  82.0 3.8 %select_select_fusion.1 = bf16[1024,1152]{0,1:T(8,128)(2,1)S(1)} fusion(bf16[1024,1152]{0,1:T(8,128)(2,1)S(1)} %maximum_select_fusion, bf16[1024,1152]{0,1:T(8,128)(2,1)S(1)} %get-tuple-element.21, bf16[1024,1152]{0,1:T(8,128)(2,1)S(1)} %get-tuple-element.20, pred[]{:T(512)S(6)} %eq.106, pred[]{:T(512)S(6)} %eq.105, pred[]{:T(512)S(6)} %eq.104, ...), kind=kLoop, calls=%fused_computation.18 | loop fusion | flops 14155776 | bytes 11796484 | tf_op jit(solution)/shard_map/gathers/jit(_where)/select_n | solution.py:97
  85.8 4.1 %select_select_fusion.2 = (bf16[1024,1152]{0,1:T(8,128)(2,1)S(1)}, bf16[1024,1152]{0,1:T(8,128)(2,1)S(1)}) fusion(bf16[1024,1152]{0,1:T(8,128)(2,1)S(1)} %maximum_select_fusion, bf16[1024,1152]{0,1:T(8,128)(2,1)S(1)} %get-tuple-element.21, bf16[1024,1152]{0,1:T(8,128)(2,1)S(1)} %get-tuple-element.20, pred[]{:T(512)S(6)} %eq.103, pred[]{:T(512)S(6)} %eq.102, ...), kind=kLoop, calls=%fused_computation.19 | loop fusion | flops 17694720 | bytes 14155783 | tf_op jit(solution)/shard_map/gathers/jit(_where)/select_n | solution.py:97
  89.9 4.4 %pad_maximum_fusion = bf16[1024,4608]{0,1:T(8,128)(2,1)} fusion(bf16[1024,1152]{0,1:T(8,128)(2,1)S(1)} %get-tuple-element.23, bf16[1024,1152]{0,1:T(8,128)(2,1)S(1)} %select_select_fusion.1, bf16[1024,1152]{0,1:T(8,128)(2,1)S(1)} %get-tuple-element.22, bf16[1024,1152]{0,1:T(8,128)(2,1)S(1)} %get-tuple-element.19), kind=kLoop, calls=%fused_computation.3 | loop fusion | flops 37748736 | bytes 18874368 | tf_op jit(solution)/shard_map/gathers/concatenate | solution.py:103
  94.3 33.4 %all-gather.3.cloned.1.call-done = bf16[5632,1024]{1,0:T(8,128)(2,1)} async-done(((bf16[176,1024]{1,0:T(8,128)(2,1)}), bf16[5632,1024]{1,0:T(8,128)(2,1)}) %all-gather.3.cloned.1.call-update) | async-done | bytes 11534352 | tf_op jit(solution)/shard_map/gathers/all_gather | solution.py:151
  127.7 4.1 %select_reduce_fusion = f32[1024,32]{0,1:T(8,128)S(1)} fusion(bf16[32,176,1024]{2,1,0:T(8,128)(2,1)} %bitcast.77, bf16[1024,576]{1,0:T(8,128)(2,1)S(1)} %copy-done.7, pred[1024,32]{0,1:T(8,128)(4,1)S(1)} %copy-done.11), kind=kOutput, calls=%fused_computation.12 | convolution fusion | flops 2149548032 | bytes 3440640 | tf_op jit(solution)/shard_map/lowrank/dot_general | solution.py:163
  131.8 1.7 collective-permute-start.5
  133.5 12.5 %fusion.17 = f32[1024,1024]{0,1:T(8,128)S(1)} fusion(bf16[1024,32,144]{0,2,1:T(8,128)(2,1)S(1)} %bitcast.68, bf16[32,176,1024]{2,1,0:T(8,128)(2,1)} %bitcast.78), kind=kOutput, calls=%fused_computation.23 | convolution fusion | flops 9663676416 | bytes 23068672 | tf_op jit(solution)/shard_map/projection/tci,cin->tn/dot_general | solution.py:201
  146.2 1.3 collective-permute-start.6
  147.5 1.0 subtract_convert_fusion.1
  148.5 1.7 slice.61
  150.2 1.2 reshape.314
  151.7 0.6 copy-done.8
  152.5 3.0 %collective-permute-start.7 = (f32[1024,32]{0,1:T(8,128)S(1)}, f32[1024,32]{0,1:T(8,128)S(1)}, u32[]{:S(2)}, u32[]{:S(2)}) collective-permute-start(f32[1024,32]{0,1:T(8,128)S(1)} %add.130), channel_id=1, source_target_pairs={{0,128},{32,160},{64,192},{96,224},{128,0},{160,32},{192,64},{224,... | collective-permute-start | bytes 393224 | tf_op jit(solution)/shard_map/lowrank/ppermute | solution.py:174
  155.5 3.6 %fusion.11 = bf16[2304,256]{1,0:T(8,128)(2,1)} fusion(bf16[1024,256]{0,1:T(8,128)(2,1)S(1)} %bitcast.75, s32[2304]{0:T(1024)S(1)} %copy-done.12, pred[2304]{0:T(1024)(128)(4,1)S(1)} %fusion.42), kind=kOutput, calls=%fused_computation.13 | convolution fusion | flops 1213267968 | bytes 1715456 | tf_op jit(solution)/shard_map/cache_write/dot_general | solution.py:229
  159.2 0.8 slice_add_fusion
  160.0 0.3 subtract_convert_fusion
  160.5 1.3 copy.25
  161.8 4.8 %fusion.14 = bf16[2304,256]{1,0:T(8,128)(2,1)} fusion(s32[2304]{0:T(1024)S(1)} %copy-done.12, pred[2304]{0:T(1024)(128)(4,1)S(1)} %fusion.42, f32[1024,1024]{0,1:T(8,128)} %copy-done.5, bf16[1024,16]{0,1:T(8,128)(2,1)S(1)} %get-tuple-element.28, bf16[1024,32]{0,1:T(8,128)(2,1)S(1)} %copy-done.10, bf16[32,16,256]{2,1,0:T(8,128)(2,1)S(1)} %bitcast.76), kind=kOutput, calls=%fused_computation.14 | convolution fusion | flops 1482752000 | bytes 2600192 | tf_op jit(solution)/shard_map/cache_write/dot_general | solution.py:231
  (54 shorter events, 1.1 us)
Async XLA Ops:
  7.2 47.3 %copy-start = (s32[32]{0:T(128)S(1)}, s32[32]{0:T(128)}, u32[]{:S(2)}) copy-start(s32[32]{0:T(128)} %param.20) | copy-start | bytes 388
  7.2 120.5 %all-gather.3.cloned.1.call-start = ((), (), s32[]{:S(2)}) async-start(), calls=%async_computation | async-start | bytes 11894784 | tf_op jit(solution)/shard_map/gathers/all_gather | solution.py:151
  10.6 6.0 %collective-permute-start = (bf16[1024,576]{0,1:T(8,128)(2,1)}, bf16[1024,576]{0,1:T(8,128)(2,1)S(1)}, u32[]{:S(2)}, u32[]{:S(2)}) collective-permute-start(bf16[1024,576]{0,1:T(8,128)(2,1)} %param.11), channel_id=1, source_target_pairs={{0,32},{32,0},{64,96},{96,64},{128,160},{160,128},{192,224},{224,1... | collective-permute-start | bytes 3538952 | tf_op jit(solution)/shard_map/gathers/ppermute | solution.py:74
  13.9 6.1 %copy-start.13 = (s32[1,10]{1,0:T(1,128)S(1)}, s32[1,10]{1,0:T(1,128)}, u32[]{:S(2)}) copy-start(s32[1,10]{1,0:T(1,128)} %param.18) | copy-start | bytes 124
  18.9 32.8 %copy-start.15 = (s32[1,10]{1,0:T(1,128)S(1)}, s32[1,10]{1,0:T(1,128)}, u32[]{:S(2)}) copy-start(s32[1,10]{1,0:T(1,128)} %param.19) | copy-start | bytes 124
  18.9 28.2 %collective-permute-start.1 = (bf16[1024,1152]{0,1:T(8,128)(2,1)S(1)}, bf16[1024,1152]{0,1:T(8,128)(2,1)}, u32[]{:S(2)}, u32[]{:S(2)}) collective-permute-start(bf16[1024,1152]{0,1:T(8,128)(2,1)S(1)} %maximum_select_fusion), channel_id=1, source_target_pairs={{0,64},{32,224},{64,128},{96,32},{128,192},{160,96},{192,0},{224,1... | collective-permute-start | bytes 7077896 | tf_op jit(solution)/shard_map/gathers/ppermute | solution.py:80
  49.4 15.7 %collective-permute-start.3 = (bf16[512,1152]{0,1:T(8,128)(2,1)}, bf16[512,1152]{0,1:T(8,128)(2,1)S(1)}, u32[]{:S(2)}, u32[]{:S(2)}) collective-permute-start(bf16[512,1152]{0,1:T(8,128)(2,1)} %constant_dynamic-slice_fusion), channel_id=1, source_target_pairs={{0,64},{32,224},{64,128},{96,32},{128,192},{160,96},{192,0},{224,1... | collective-permute-start | bytes 3538952 | tf_op jit(solution)/shard_map/gathers/ppermute | solution.py:83
  53.0 4.7 %copy-start.14 = (s32[10,1]{0,1:T(1,128)}, s32[10,1]{0,1:T(1,128)S(1)}, u32[]{:S(2)}) copy-start(s32[10,1]{0,1:T(1,128)S(1)} %reduce-window.9) | copy-start | bytes 124
  53.7 23.4 %collective-permute-start.2 = (bf16[1024,1152]{0,1:T(8,128)(2,1)}, bf16[1024,1152]{0,1:T(8,128)(2,1)}, u32[]{:S(2)}, u32[]{:S(2)}) collective-permute-start(bf16[1024,1152]{0,1:T(8,128)(2,1)} %collective-permute-done.1), channel_id=1, source_target_pairs={{0,32},{32,0},{64,96},{96,64},{128,160},{160,128},{192,224},{224,1... | collective-permute-start | bytes 7077896 | tf_op jit(solution)/shard_map/gathers/ppermute | solution.py:84
  65.1 11.9 %collective-permute-start.4 = (bf16[512,1152]{0,1:T(8,128)(2,1)S(1)}, bf16[512,1152]{0,1:T(8,128)(2,1)}, u32[]{:S(2)}, u32[]{:S(2)}) collective-permute-start(bf16[512,1152]{0,1:T(8,128)(2,1)S(1)} %collective-permute-done.3), channel_id=1, source_target_pairs={{0,32},{32,0},{64,96},{96,64},{128,160},{160,128},{192,224},{224,1... | collective-permute-start | bytes 3538952 | tf_op jit(solution)/shard_map/gathers/ppermute | solution.py:84
  89.9 37.9 %copy-start.7 = (bf16[1024,576]{1,0:T(8,128)(2,1)S(1)}, bf16[1024,576]{1,0:T(8,128)(2,1)}, u32[]{:S(2)}) copy-start(bf16[1024,576]{1,0:T(8,128)(2,1)} %copy.19) | copy-start | bytes 3538948
  89.9 37.9 %copy-start.11 = (pred[1024,32]{0,1:T(8,128)(4,1)S(1)}, pred[1024,32]{0,1:T(8,128)(4,1)}, u32[]{:S(2)}) copy-start(pred[1024,32]{0,1:T(8,128)(4,1)} %get-tuple-element.33) | copy-start | bytes 98308
  127.7 5.8 %copy-start.2 = (bf16[1024,4608]{0,1:T(8,128)(2,1)S(1)}, bf16[1024,4608]{0,1:T(8,128)(2,1)}, u32[]{:S(2)}) copy-start(bf16[1024,4608]{0,1:T(8,128)(2,1)} %pad_maximum_fusion) | copy-start | bytes 28311556
  131.8 14.3 %collective-permute-start.5 = (f32[1024,32]{0,1:T(8,128)S(1)}, f32[1024,32]{0,1:T(8,128)S(1)}, u32[]{:S(2)}, u32[]{:S(2)}) collective-permute-start(f32[1024,32]{0,1:T(8,128)S(1)} %select_reduce_fusion), channel_id=1, source_target_pairs={{0,32},{32,0},{64,96},{96,64},{128,160},{160,128},{192,224},{224,1... | collective-permute-start | bytes 393224 | tf_op jit(solution)/shard_map/lowrank/ppermute | solution.py:174
  146.1 2.4 %copy-start.5 = (f32[1024,1024]{0,1:T(8,128)}, f32[1024,1024]{0,1:T(8,128)S(1)}, u32[]{:S(2)}) copy-start(f32[1024,1024]{0,1:T(8,128)S(1)} %fusion.17) | copy-start | bytes 12582916
  146.1 1.4 copy-start.3
  146.1 1.4 copy-start.4
  146.2 6.3 %collective-permute-start.6 = (f32[1024,32]{0,1:T(8,128)S(1)}, f32[1024,32]{0,1:T(8,128)S(1)}, u32[]{:S(2)}, u32[]{:S(2)}) collective-permute-start(f32[1024,32]{0,1:T(8,128)S(1)} %add.129), channel_id=1, source_target_pairs={{0,64},{32,96},{64,0},{96,32},{128,192},{160,224},{192,128},{224,1... | collective-permute-start | bytes 393224 | tf_op jit(solution)/shard_map/lowrank/ppermute | solution.py:174
  151.4 1.0 copy-start.8
  151.4 1.0 copy-start.9
  151.4 4.1 %copy-start.12 = (s32[2304]{0:T(1024)S(1)}, s32[2304]{0:T(1024)}, u32[]{:S(2)}) copy-start(s32[2304]{0:T(1024)} %clamp_bitcast_fusion) | copy-start | bytes 27652
  152.5 6.7 %collective-permute-start.7 = (f32[1024,32]{0,1:T(8,128)S(1)}, f32[1024,32]{0,1:T(8,128)S(1)}, u32[]{:S(2)}, u32[]{:S(2)}) collective-permute-start(f32[1024,32]{0,1:T(8,128)S(1)} %add.130), channel_id=1, source_target_pairs={{0,128},{32,160},{64,192},{96,224},{128,0},{160,32},{192,64},{224,... | collective-permute-start | bytes 393224 | tf_op jit(solution)/shard_map/lowrank/ppermute | solution.py:174
  155.5 3.7 %copy-start.6 = (f32[1024,1024]{0,1:T(8,128)S(1)}, f32[1024,1024]{0,1:T(8,128)}, u32[]{:S(2)}) copy-start(f32[1024,1024]{0,1:T(8,128)} %copy-done.5) | copy-start | bytes 12582916
  155.5 3.7 %copy-start.10 = (bf16[1024,32]{0,1:T(8,128)(2,1)S(1)}, bf16[1024,32]{0,1:T(8,128)(2,1)}, u32[]{:S(2)}) copy-start(bf16[1024,32]{0,1:T(8,128)(2,1)} %get-tuple-element.32) | copy-start | bytes 196612
  161.8 4.8 %copy-start.1 = (s32[32]{0:T(128)S(1)}, s32[32]{0:T(128)}, u32[]{:S(2)}) copy-start(s32[32]{0:T(128)} %param.20) | copy-start | bytes 388
Sparse Core Ops, SparseCore 0:
  11.1 116.5 all-gather.2

commit v10 on v9

--- a/solution.py
+++ b/solution.py
@@ -159,10 +159,11 @@
 
     with jax.named_scope("lowrank"):
         onehot = (chosen[:, None] == jnp.arange(adapter_count, dtype=jnp.int32)[None, :])
-        padded_hidden = jnp.pad(hidden, ((0, 0), (0, weight_width - features)))
+        lane_width = -(-features // 128) * 128
+        padded_hidden = jnp.pad(hidden, ((0, 0), (0, lane_width - features)))
         partial_all = lax.dot_general(
             padded_hidden,
-            down_local,
+            down_local[:, :lane_width],
             (((1,), (1,)), ((), ())),
             preferred_element_type=jnp.float32,
         ).reshape(hidden.shape[0], adapter_count, -1)

time: 174 us -> 174 us (level)
  waiting for transfers between devices: 68.1 us -> 71.9 us
  matrix products: 25.9 us -> 23.5 us
    all_gather x1, waiting for transfers between devices: 33.4 us -> 36.1 us  [shards(): packed = lax.all_gather(jnp.concatenate(pieces, axis=0), 'col', axis=0)]
    unnamed x37 -> x38, local copies, waits for them, and re-layouts: 4.85 us -> 2.42 us
    dot_general x1, matrix products: 4.12 us -> 1.79 us  [shards(): lax.dot_general(padded_hidden, down_local[:, :lane_width], (((1,), (1,)),...]
    slice x0 -> x1, local copies, waits for them, and re-layouts: none -> 1.79 us  [shards(): down_local = packed[:, bounds[1]:bounds[2]].reshape(-1, weight_width)]
  transfers between devices with their start and end apart: 9 -> 9, of which waited for: 4 -> 4; matrix products, arithmetic and copies ran while one was open for 34% -> 32% of each run, Pallas kernels for 0% -> 0%
where the time goes in v10:
time: 174 us
  waiting for transfers between devices  71.9 us (41%)
  other arithmetic  34.4 us (20%)
  matrix products  23.5 us (14%)
  starting transfers between devices  17.2 us (10%)
  between operations  14.4 us (8%)
  local copies, waits for them, and re-layouts  12.2 us (7%)
    all_gather x1, waiting for transfers between devices, shards(): packed = lax.all_gather(jnp.concatenate(pieces, axis=0), 'col', axis=0)  36.1 us
    ppermute x1, waiting for transfers between devices, gather_rows(): near = lax.ppermute(own_block, 'row', ring)  26.5 us
    select_n x3, other arithmetic, gather_rows(): jnp.where(relative == 0, own_block, jnp.where(relative == 1, after, jnp.w...  12.7 us
    dot_general x1, matrix products, shards(): jnp.einsum('tci,cin->tn', full_rows.reshape(full_rows.shape[0], packed.sh...  12.5 us
    ppermute x1, waiting for transfers between devices, gather_rows(): far_half = lax.ppermute(forwarded, 'row', ring)  6.53 us
    ppermute x3, starting transfers between devices, shards(): received = lax.ppermute(partial, 'row', pairs)  5.94 us
    dot_general x1, matrix products, shards(): jnp.dot(select, value_rows, preferred_element_type=jnp.float32)  4.78 us
    ppermute x2, starting transfers between devices, gather_rows(): from_partner, far_other = lax.ppermute((near, far_half), 'row', swap)  4.55 us
  transfers between devices with their start and end apart: 9, of which 4 were waited for; matrix products, arithmetic and copies ran while one was open for 32% of the time, Pallas kernels for 0%

profile of v10, /device:TPU:1, one launch (start us, length us, event | category | flops | bytes accessed | tf_op | source)
XLA Modules:
  0.0 173.6 jit_solution(156723672470088015)
XLA Ops:
  7.2 0.7 copy.24
  8.0 0.7 copy.25
  8.8 1.8 %maximum_maximum_fusion = bf16[176,1024]{1,0:T(8,128)(2,1)} fusion(bf16[32,448]{1,0:T(8,128)(2,1)S(1)} %reshape.314, bf16[32,576]{1,0:T(8,128)(2,1)} %bitcast.82, bf16[144,256]{1,0:T(8,128)(2,1)} %param.14, bf16[144,256]{1,0:T(8,128)(2,1)} %param.13, bf16[144,512]{1,0:T(8,128)(2,1)} %param.12), kind=kLoop, calls=%fused_computation.47 | loop fusion | flops 1802240 | bytes 720896 | tf_op jit(solution)/shard_map/gathers/concatenate | solution.py:151
  10.6 3.3 %collective-permute-start = (bf16[1024,576]{0,1:T(8,128)(2,1)}, bf16[1024,576]{0,1:T(8,128)(2,1)S(1)}, u32[]{:S(2)}, u32[]{:S(2)}) collective-permute-start(bf16[1024,576]{0,1:T(8,128)(2,1)} %param.11), channel_id=1, source_target_pairs={{0,32},{32,0},{64,96},{96,64},{128,160},{160,128},{192,224},{224,1... | collective-permute-start | bytes 3538952 | tf_op jit(solution)/shard_map/gathers/ppermute | solution.py:74
  13.9 2.7 %collective-permute-done = bf16[1024,576]{0,1:T(8,128)(2,1)S(1)} collective-permute-done((bf16[1024,576]{0,1:T(8,128)(2,1)}, bf16[1024,576]{0,1:T(8,128)(2,1)S(1)}, u32[]{:S(2)}, u32[]{:S(2)}) %collective-permute-start) | collective-permute-done | bytes 1179680 | tf_op jit(solution)/shard_map/gathers/ppermute | solution.py:74
  16.6 2.3 %maximum_select_fusion = bf16[1024,1152]{0,1:T(8,128)(2,1)S(1)} fusion(bf16[1024,576]{0,1:T(8,128)(2,1)S(1)} %collective-permute-done, bf16[1024,576]{0,1:T(8,128)(2,1)} %param.11, pred[]{:T(512)S(6)} %eq.98), kind=kLoop, calls=%fused_computation.15 | loop fusion | flops 10616832 | bytes 4718593 | tf_op jit(solution)/shard_map/gathers/jit(_where)/select_n | solution.py:75
  18.9 1.1 collective-permute-start.1
  20.0 0.5 and_select_fusion.1
  20.5 26.5 %collective-permute-done.1 = bf16[1024,1152]{0,1:T(8,128)(2,1)} collective-permute-done((bf16[1024,1152]{0,1:T(8,128)(2,1)S(1)}, bf16[1024,1152]{0,1:T(8,128)(2,1)}, u32[]{:S(2)}, u32[]{:S(2)}) %collective-permute-start.1) | collective-permute-done | bytes 2359328 | tf_op jit(solution)/shard_map/gathers/ppermute | solution.py:80
  47.1 2.4 %constant_dynamic-slice_fusion = bf16[512,1152]{0,1:T(8,128)(2,1)} fusion(bf16[1024,1152]{0,1:T(8,128)(2,1)} %collective-permute-done.1, s32[]{:T(128)S(6)} %select_n.183), kind=kLoop, calls=%fused_computation.92 | loop fusion | bytes 2359300 | tf_op jit(solution)/shard_map/gathers/dynamic_slice | solution.py:82
  49.4 2.2 %collective-permute-start.3 = (bf16[512,1152]{0,1:T(8,128)(2,1)}, bf16[512,1152]{0,1:T(8,128)(2,1)S(1)}, u32[]{:S(2)}, u32[]{:S(2)}) collective-permute-start(bf16[512,1152]{0,1:T(8,128)(2,1)} %constant_dynamic-slice_fusion), channel_id=1, source_target_pairs={{0,64},{32,224},{64,128},{96,32},{128,192},{160,96},{192,0},{224,1... | collective-permute-start | bytes 3538952 | tf_op jit(solution)/shard_map/gathers/ppermute | solution.py:83
  51.7 0.5 fusion.43
  52.2 0.8 reduce-window.9
  53.0 0.7 reduce-window.6
  53.9 0.6 pad_clamp_fusion
  54.5 1.2 gather_fusion
  55.7 0.7 select_reduce_fusion.3
  56.4 0.7 fusion.46
  57.1 0.7 fusion.44
  57.7 0.8 select_reduce_fusion.1
  58.6 6.5 %collective-permute-done.3 = bf16[512,1152]{0,1:T(8,128)(2,1)S(1)} collective-permute-done((bf16[512,1152]{0,1:T(8,128)(2,1)}, bf16[512,1152]{0,1:T(8,128)(2,1)S(1)}, u32[]{:S(2)}, u32[]{:S(2)}) %collective-permute-start.3) | collective-permute-done | bytes 1179680 | tf_op jit(solution)/shard_map/gathers/ppermute | solution.py:83
  65.1 4.4 %collective-permute-start.4 = (bf16[512,1152]{0,1:T(8,128)(2,1)S(1)}, bf16[512,1152]{0,1:T(8,128)(2,1)}, u32[]{:S(2)}, u32[]{:S(2)}) collective-permute-start(bf16[512,1152]{0,1:T(8,128)(2,1)S(1)} %collective-permute-done.3), channel_id=1, source_target_pairs={{0,32},{32,0},{64,96},{96,64},{128,160},{160,128},{192,224},{224,1... | collective-permute-start | bytes 3538952 | tf_op jit(solution)/shard_map/gathers/ppermute | solution.py:84
  69.5 0.6 multiply_exponential_fusion
  70.1 0.7 fusion.42
  70.8 0.7 clamp_bitcast_fusion
  71.4 0.7 fusion.49
  72.1 2.5 %multiply_cosine_fusion = (f32[1024,64]{0,1:T(8,128)}, f32[1024,64]{0,1:T(8,128)}) fusion(f32[64]{0:T(128)} %multiply_exponential_fusion, f32[1024]{0:T(1024)S(1)} %subtract_convert_fusion.2), kind=kLoop, calls=%fused_computation.46 | loop fusion | flops 65536 | bytes 528640 | tf_op jit(solution)/shard_map/rotary/cos | solution.py:218
  74.6 4.8 %select_select_fusion.3 = (bf16[1024,1152]{0,1:T(8,128)(2,1)S(1)}, bf16[1024,1152]{0,1:T(8,128)(2,1)S(1)}, bf16[1024,1152]{0,1:T(8,128)(2,1)S(1)}) fusion(bf16[1024,1152]{0,1:T(8,128)(2,1)S(1)} %maximum_select_fusion, pred[]{:T(512)S(6)} %eq.100, pred[]{:T(512)S(6)} %eq.99, pred[]{:T(512)S(6)} %eq.97, bf16[512,1152]{0,1:T(8,128)(2,1)S(1)} %collective-permute-done.3, ...), kind=kLoop, calls=%fused_computation.20 | loop fusion | flops 16515072 | bytes 16515076 | tf_op jit(solution)/shard_map/gathers/jit(_where)/select_n | solution.py:97
  79.4 3.8 %select_select_fusion.1 = bf16[1024,1152]{0,1:T(8,128)(2,1)S(1)} fusion(bf16[1024,1152]{0,1:T(8,128)(2,1)S(1)} %maximum_select_fusion, bf16[1024,1152]{0,1:T(8,128)(2,1)S(1)} %get-tuple-element.21, bf16[1024,1152]{0,1:T(8,128)(2,1)S(1)} %get-tuple-element.20, pred[]{:T(512)S(6)} %eq.106, pred[]{:T(512)S(6)} %eq.105, pred[]{:T(512)S(6)} %eq.104, ...), kind=kLoop, calls=%fused_computation.18 | loop fusion | flops 14155776 | bytes 11796484 | tf_op jit(solution)/shard_map/gathers/jit(_where)/select_n | solution.py:97
  83.2 4.1 %select_select_fusion.2 = (bf16[1024,1152]{0,1:T(8,128)(2,1)S(1)}, bf16[1024,1152]{0,1:T(8,128)(2,1)S(1)}) fusion(bf16[1024,1152]{0,1:T(8,128)(2,1)S(1)} %maximum_select_fusion, bf16[1024,1152]{0,1:T(8,128)(2,1)S(1)} %get-tuple-element.21, bf16[1024,1152]{0,1:T(8,128)(2,1)S(1)} %get-tuple-element.20, pred[]{:T(512)S(6)} %eq.103, pred[]{:T(512)S(6)} %eq.102, ...), kind=kLoop, calls=%fused_computation.19 | loop fusion | flops 17694720 | bytes 14155783 | tf_op jit(solution)/shard_map/gathers/jit(_where)/select_n | solution.py:97
  87.3 4.3 %pad_maximum_fusion = bf16[1024,4608]{0,1:T(8,128)(2,1)} fusion(bf16[1024,1152]{0,1:T(8,128)(2,1)S(1)} %get-tuple-element.23, bf16[1024,1152]{0,1:T(8,128)(2,1)S(1)} %select_select_fusion.1, bf16[1024,1152]{0,1:T(8,128)(2,1)S(1)} %get-tuple-element.22, bf16[1024,1152]{0,1:T(8,128)(2,1)S(1)} %get-tuple-element.19), kind=kLoop, calls=%fused_computation.3 | loop fusion | flops 37748736 | bytes 18874368 | tf_op jit(solution)/shard_map/gathers/concatenate | solution.py:103
  91.6 36.1 %all-gather.3.cloned.1.call-done = bf16[5632,1024]{1,0:T(8,128)(2,1)} async-done(((bf16[176,1024]{1,0:T(8,128)(2,1)}), bf16[5632,1024]{1,0:T(8,128)(2,1)}) %all-gather.3.cloned.1.call-update) | async-done | bytes 11534352 | tf_op jit(solution)/shard_map/gathers/all_gather | solution.py:151
  127.7 1.8 %slice.62 = bf16[32,32,1024]{2,1,0:T(8,128)(2,1)S(1)} slice(bf16[32,176,1024]{2,1,0:T(8,128)(2,1)} %bitcast.76), slice={[0:32], [144:176], [0:1024]} | slice | bytes 4194304 | tf_op jit(solution)/shard_map/gathers/slice | solution.py:153
  129.5 1.8 %fusion.20 = f32[1024,1024]{0,1:T(8,128)S(1)} fusion(bf16[1024,1024]{1,0:T(8,128)(2,1)S(1)} %bitcast.73, bf16[1024,576]{0,1:T(8,128)(2,1)S(1)} %copy-done.7), kind=kOutput, calls=%fused_computation.26 | convolution fusion | flops 1342177280 | bytes 6684672 | tf_op jit(solution)/shard_map/lowrank/dot_general | solution.py:164
  131.3 0.6 select_reduce_fusion
  132.0 1.7 collective-permute-start.5
  133.7 12.5 %fusion.17 = f32[1024,1024]{0,1:T(8,128)S(1)} fusion(bf16[1024,32,144]{0,2,1:T(8,128)(2,1)S(1)} %bitcast.67, bf16[32,176,1024]{2,1,0:T(8,128)(2,1)} %bitcast.77), kind=kOutput, calls=%fused_computation.23 | convolution fusion | flops 9663676416 | bytes 23068672 | tf_op jit(solution)/shard_map/projection/tci,cin->tn/dot_general | solution.py:202
  146.4 1.3 collective-permute-start.6
  147.7 1.0 subtract_convert_fusion.1
  148.6 1.7 slice.66
  150.4 1.2 reshape.318
  151.9 0.7 copy.27
  152.7 3.0 %collective-permute-start.7 = (f32[1024,32]{0,1:T(8,128)S(1)}, f32[1024,32]{0,1:T(8,128)S(1)}, u32[]{:S(2)}, u32[]{:S(2)}) collective-permute-start(f32[1024,32]{0,1:T(8,128)S(1)} %add.130), channel_id=1, source_target_pairs={{0,128},{32,160},{64,192},{96,224},{128,0},{160,32},{192,64},{224,... | collective-permute-start | bytes 393224 | tf_op jit(solution)/shard_map/lowrank/ppermute | solution.py:175
  155.7 3.6 %fusion.11 = bf16[2304,256]{1,0:T(8,128)(2,1)} fusion(bf16[1024,256]{0,1:T(8,128)(2,1)S(1)} %bitcast.79, s32[2304]{0:T(1024)S(1)} %copy-done.13, pred[2304]{0:T(1024)(128)(4,1)S(1)} %copy-done.14), kind=kOutput, calls=%fused_computation.13 | convolution fusion | flops 1213267968 | bytes 1715456 | tf_op jit(solution)/shard_map/cache_write/dot_general | solution.py:230
  159.4 0.8 slice_add_fusion
  160.2 0.3 subtract_convert_fusion
  160.6 1.3 copy.22
  162.0 4.8 %fusion.14 = bf16[2304,256]{1,0:T(8,128)(2,1)} fusion(s32[2304]{0:T(1024)S(1)} %copy-done.13, pred[2304]{0:T(1024)(128)(4,1)S(1)} %copy-done.14, f32[1024,1024]{0,1:T(8,128)} %copy-done.5, bf16[1024,16]{0,1:T(8,128)(2,1)S(1)} %get-tuple-element.28, bf16[1024,32]{0,1:T(8,128)(2,1)S(1)} %copy-done.10, bf16[32,16,256]{2,1,0:T(8,128)(2,1)S(1)} %bitcast.80), kind=kOutput, calls=%fused_computation.14 | convolution fusion | flops 1482752000 | bytes 2600192 | tf_op jit(solution)/shard_map/cache_write/dot_general | solution.py:232
  (57 shorter events, 1.0 us)
Async XLA Ops:
  7.2 47.3 %copy-start = (s32[32]{0:T(128)S(1)}, s32[32]{0:T(128)}, u32[]{:S(2)}) copy-start(s32[32]{0:T(128)} %param.20) | copy-start | bytes 388
  7.2 120.5 %all-gather.3.cloned.1.call-start = ((), (), s32[]{:S(2)}) async-start(), calls=%async_computation | async-start | bytes 11894784 | tf_op jit(solution)/shard_map/gathers/all_gather | solution.py:151
  10.6 6.0 %collective-permute-start = (bf16[1024,576]{0,1:T(8,128)(2,1)}, bf16[1024,576]{0,1:T(8,128)(2,1)S(1)}, u32[]{:S(2)}, u32[]{:S(2)}) collective-permute-start(bf16[1024,576]{0,1:T(8,128)(2,1)} %param.11), channel_id=1, source_target_pairs={{0,32},{32,0},{64,96},{96,64},{128,160},{160,128},{192,224},{224,1... | collective-permute-start | bytes 3538952 | tf_op jit(solution)/shard_map/gathers/ppermute | solution.py:74
  13.9 6.1 %copy-start.15 = (s32[1,10]{1,0:T(1,128)S(1)}, s32[1,10]{1,0:T(1,128)}, u32[]{:S(2)}) copy-start(s32[1,10]{1,0:T(1,128)} %param.18) | copy-start | bytes 124
  18.9 32.8 %copy-start.16 = (s32[1,10]{1,0:T(1,128)S(1)}, s32[1,10]{1,0:T(1,128)}, u32[]{:S(2)}) copy-start(s32[1,10]{1,0:T(1,128)} %param.19) | copy-start | bytes 124
  18.9 28.2 %collective-permute-start.1 = (bf16[1024,1152]{0,1:T(8,128)(2,1)S(1)}, bf16[1024,1152]{0,1:T(8,128)(2,1)}, u32[]{:S(2)}, u32[]{:S(2)}) collective-permute-start(bf16[1024,1152]{0,1:T(8,128)(2,1)S(1)} %maximum_select_fusion), channel_id=1, source_target_pairs={{0,64},{32,224},{64,128},{96,32},{128,192},{160,96},{192,0},{224,1... | collective-permute-start | bytes 7077896 | tf_op jit(solution)/shard_map/gathers/ppermute | solution.py:80
  49.4 15.7 %collective-permute-start.3 = (bf16[512,1152]{0,1:T(8,128)(2,1)}, bf16[512,1152]{0,1:T(8,128)(2,1)S(1)}, u32[]{:S(2)}, u32[]{:S(2)}) collective-permute-start(bf16[512,1152]{0,1:T(8,128)(2,1)} %constant_dynamic-slice_fusion), channel_id=1, source_target_pairs={{0,64},{32,224},{64,128},{96,32},{128,192},{160,96},{192,0},{224,1... | collective-permute-start | bytes 3538952 | tf_op jit(solution)/shard_map/gathers/ppermute | solution.py:83
  53.7 20.8 %collective-permute-start.2 = (bf16[1024,1152]{0,1:T(8,128)(2,1)}, bf16[1024,1152]{0,1:T(8,128)(2,1)}, u32[]{:S(2)}, u32[]{:S(2)}) collective-permute-start(bf16[1024,1152]{0,1:T(8,128)(2,1)} %collective-permute-done.1), channel_id=1, source_target_pairs={{0,32},{32,0},{64,96},{96,64},{128,160},{160,128},{192,224},{224,1... | collective-permute-start | bytes 7077896 | tf_op jit(solution)/shard_map/gathers/ppermute | solution.py:84
  65.1 9.4 %collective-permute-start.4 = (bf16[512,1152]{0,1:T(8,128)(2,1)S(1)}, bf16[512,1152]{0,1:T(8,128)(2,1)}, u32[]{:S(2)}, u32[]{:S(2)}) collective-permute-start(bf16[512,1152]{0,1:T(8,128)(2,1)S(1)} %collective-permute-done.3), channel_id=1, source_target_pairs={{0,32},{32,0},{64,96},{96,64},{128,160},{160,128},{192,224},{224,1... | collective-permute-start | bytes 3538952 | tf_op jit(solution)/shard_map/gathers/ppermute | solution.py:84
  91.6 37.9 %copy-start.7 = (bf16[1024,576]{0,1:T(8,128)(2,1)S(1)}, bf16[1024,576]{0,1:T(8,128)(2,1)}, u32[]{:S(2)}) copy-start(bf16[1024,576]{0,1:T(8,128)(2,1)} %param.11) | copy-start | bytes 3538948
  129.5 1.8 %copy-start.12 = (pred[1024,32]{0,1:T(8,128)(4,1)S(1)}, pred[1024,32]{0,1:T(8,128)(4,1)}, u32[]{:S(2)}) copy-start(pred[1024,32]{0,1:T(8,128)(4,1)} %get-tuple-element.33) | copy-start | bytes 98308
  129.5 4.1 %copy-start.2 = (bf16[1024,4608]{0,1:T(8,128)(2,1)S(1)}, bf16[1024,4608]{0,1:T(8,128)(2,1)}, u32[]{:S(2)}) copy-start(bf16[1024,4608]{0,1:T(8,128)(2,1)} %pad_maximum_fusion) | copy-start | bytes 28311556
  132.0 14.4 %collective-permute-start.5 = (f32[1024,32]{0,1:T(8,128)S(1)}, f32[1024,32]{0,1:T(8,128)S(1)}, u32[]{:S(2)}, u32[]{:S(2)}) collective-permute-start(f32[1024,32]{0,1:T(8,128)S(1)} %select_reduce_fusion), channel_id=1, source_target_pairs={{0,32},{32,0},{64,96},{96,64},{128,160},{160,128},{192,224},{224,1... | collective-permute-start | bytes 393224 | tf_op jit(solution)/shard_map/lowrank/ppermute | solution.py:175
  146.2 2.4 %copy-start.5 = (f32[1024,1024]{0,1:T(8,128)}, f32[1024,1024]{0,1:T(8,128)S(1)}, u32[]{:S(2)}) copy-start(f32[1024,1024]{0,1:T(8,128)S(1)} %fusion.17) | copy-start | bytes 12582916
  146.2 1.5 copy-start.3
  146.2 1.5 copy-start.4
  146.4 6.3 %collective-permute-start.6 = (f32[1024,32]{0,1:T(8,128)S(1)}, f32[1024,32]{0,1:T(8,128)S(1)}, u32[]{:S(2)}, u32[]{:S(2)}) collective-permute-start(f32[1024,32]{0,1:T(8,128)S(1)} %add.129), channel_id=1, source_target_pairs={{0,64},{32,96},{64,0},{96,32},{128,192},{160,224},{192,128},{224,1... | collective-permute-start | bytes 393224 | tf_op jit(solution)/shard_map/lowrank/ppermute | solution.py:175
  151.6 1.0 copy-start.8
  151.6 1.0 copy-start.9
  151.6 4.1 %copy-start.13 = (s32[2304]{0:T(1024)S(1)}, s32[2304]{0:T(1024)}, u32[]{:S(2)}) copy-start(s32[2304]{0:T(1024)} %clamp_bitcast_fusion) | copy-start | bytes 27652
  151.6 4.1 %copy-start.14 = (pred[2304]{0:T(1024)(128)(4,1)S(1)}, pred[2304]{0:T(1024)(128)(4,1)}, u32[]{:S(2)}) copy-start(pred[2304]{0:T(1024)(128)(4,1)} %fusion.42) | copy-start | bytes 6916
  152.7 6.6 %collective-permute-start.7 = (f32[1024,32]{0,1:T(8,128)S(1)}, f32[1024,32]{0,1:T(8,128)S(1)}, u32[]{:S(2)}, u32[]{:S(2)}) collective-permute-start(f32[1024,32]{0,1:T(8,128)S(1)} %add.130), channel_id=1, source_target_pairs={{0,128},{32,160},{64,192},{96,224},{128,0},{160,32},{192,64},{224,... | collective-permute-start | bytes 393224 | tf_op jit(solution)/shard_map/lowrank/ppermute | solution.py:175
  155.7 3.7 %copy-start.6 = (f32[1024,1024]{0,1:T(8,128)S(1)}, f32[1024,1024]{0,1:T(8,128)}, u32[]{:S(2)}) copy-start(f32[1024,1024]{0,1:T(8,128)} %copy-done.5) | copy-start | bytes 12582916
  155.7 3.7 %copy-start.10 = (bf16[1024,32]{0,1:T(8,128)(2,1)S(1)}, bf16[1024,32]{0,1:T(8,128)(2,1)}, u32[]{:S(2)}) copy-start(bf16[1024,32]{0,1:T(8,128)(2,1)} %get-tuple-element.32) | copy-start | bytes 196612
  160.5 1.4 copy-start.11
  162.0 4.8 %copy-start.1 = (s32[32]{0:T(128)S(1)}, s32[32]{0:T(128)}, u32[]{:S(2)}) copy-start(s32[32]{0:T(128)} %param.20) | copy-start | bytes 388
Sparse Core Ops, SparseCore 0:
  11.1 116.5 all-gather.2

commit v11 on v9

--- a/solution.py
+++ b/solution.py
@@ -157,6 +157,13 @@
         up_value = up_all[:, query_size : query_size + rank_width * key_width]
         up_value = up_value.reshape(adapter_count, rank_width, -1)
 
+    with jax.named_scope("cache_select"):
+        rows, keep = cache_rows(lengths, starts, page_table[0])
+        select = (
+            (rows[:, None] == jnp.arange(TOK_DEV, dtype=jnp.int32)[None, :]) & keep[:, None]
+        ).astype(jnp.bfloat16)
+        select, full_rows = lax.optimization_barrier((select, full_rows))
+
     with jax.named_scope("lowrank"):
         onehot = (chosen[:, None] == jnp.arange(adapter_count, dtype=jnp.int32)[None, :])
         padded_hidden = jnp.pad(hidden, ((0, 0), (0, weight_width - features)))
@@ -222,10 +229,6 @@
 
     with jax.named_scope("cache_write"):
         pages = page_table.shape[1]
-        rows, keep = cache_rows(lengths, starts, page_table[0])
-        select = (
-            (rows[:, None] == jnp.arange(TOK_DEV, dtype=jnp.int32)[None, :]) & keep[:, None]
-        ).astype(jnp.bfloat16)
         key_cache = jnp.dot(select, key_rotated, preferred_element_type=jnp.float32)
         key_cache = key_cache.astype(jnp.bfloat16).reshape(pages, PAGE, key_width)
         value_cache = jnp.dot(select, value_rows, preferred_element_type=jnp.float32)

time: 174 us -> 176 us (1.011)
  waiting for transfers between devices: 68.1 us -> 73.6 us
  other arithmetic: 35.1 us -> 29.9 us
  matrix products: 25.9 us -> 27.9 us
    all_gather x1, waiting for transfers between devices: 33.4 us -> 38.6 us  [shards(): packed = lax.all_gather(jnp.concatenate(pieces, axis=0), 'col', axis=0)]
    convert_element_type x0 -> x1, other arithmetic: none -> 3.88 us  [shards(): select = ((rows[:, None] == jnp.arange(TOK_DEV, dtype=jnp.int32)[None, :]...]
    select_n x3, other arithmetic: 12.8 us -> 9.36 us  [gather_rows(): jnp.where(relative == 0, own_block, jnp.where(relative == 1, after, jnp.w...]
    ppermute x1, waiting for transfers between devices: 5.38 us -> 8.38 us  [gather_rows(): far_half = lax.ppermute(forwarded, 'row', ring)]
    ppermute x1, waiting for transfers between devices: 26.5 us -> 23.9 us  [gather_rows(): near = lax.ppermute(own_block, 'row', ring)]
    unnamed x37 -> x35, local copies, waits for them, and re-layouts: 4.85 us -> 4.83 us
  transfers between devices with their start and end apart: 9 -> 9, of which waited for: 4 -> 4; matrix products, arithmetic and copies ran while one was open for 34% -> 31% of each run, Pallas kernels for 0% -> 0%
where the time goes in v11:
time: 176 us; the launch traced here: 175 us
  waiting for transfers between devices  73.6 us (42%)
  other arithmetic  29.9 us (17%)
  matrix products  27.9 us (16%)
  starting transfers between devices  17.3 us (10%)
  between operations  14.4 us (8%)
  local copies, waits for them, and re-layouts  12.3 us (7%)
    all_gather x1, waiting for transfers between devices, shards(): packed = lax.all_gather(jnp.concatenate(pieces, axis=0), 'col', axis=0)  38.6 us
    ppermute x1, waiting for transfers between devices, gather_rows(): near = lax.ppermute(own_block, 'row', ring)  23.9 us
    dot_general x1, matrix products, shards(): jnp.einsum('tci,cin->tn', full_rows.reshape(full_rows.shape[0], packed.sh...  12.5 us
    select_n x3, other arithmetic, gather_rows(): jnp.where(relative == 0, own_block, jnp.where(relative == 1, after, jnp.w...  9.36 us
    ppermute x1, waiting for transfers between devices, gather_rows(): far_half = lax.ppermute(forwarded, 'row', ring)  8.38 us
    ppermute x3, starting transfers between devices, shards(): received = lax.ppermute(partial, 'row', pairs)  5.98 us
    dot_general x1, matrix products, shards(): jnp.dot(select, value_rows, preferred_element_type=jnp.float32)  5.51 us
    dot_general x1, matrix products, shards(): key_cache = jnp.dot(select, key_rotated, preferred_element_type=jnp.float32)  4.93 us
  transfers between devices with their start and end apart: 9, of which 4 were waited for; matrix products, arithmetic and copies ran while one was open for 31% of the time, Pallas kernels for 0%

profile of v11, /device:TPU:1, one launch (start us, length us, event | category | flops | bytes accessed | tf_op | source)
XLA Modules:
  0.0 175.5 jit_solution(6751839087549918985)
XLA Ops:
  7.2 0.7 copy.27
  8.0 0.7 copy.28
  8.7 0.1 reshape.312
  8.8 1.8 %maximum_maximum_fusion = bf16[176,1024]{1,0:T(8,128)(2,1)} fusion(bf16[32,448]{1,0:T(8,128)(2,1)S(1)} %reshape.312, bf16[32,576]{1,0:T(8,128)(2,1)} %bitcast.83, bf16[144,256]{1,0:T(8,128)(2,1)} %param.14, bf16[144,256]{1,0:T(8,128)(2,1)} %param.13, bf16[144,512]{1,0:T(8,128)(2,1)} %param.12), kind=kLoop, calls=%fused_computation.41 | loop fusion | flops 1802240 | bytes 720896 | tf_op jit(solution)/shard_map/gathers/concatenate | solution.py:151
  10.6 3.3 %collective-permute-start = (bf16[1024,576]{0,1:T(8,128)(2,1)}, bf16[1024,576]{0,1:T(8,128)(2,1)S(1)}, u32[]{:S(2)}, u32[]{:S(2)}) collective-permute-start(bf16[1024,576]{0,1:T(8,128)(2,1)} %param.11), channel_id=1, source_target_pairs={{0,32},{32,0},{64,96},{96,64},{128,160},{160,128},{192,224},{224,1... | collective-permute-start | bytes 3538952 | tf_op jit(solution)/shard_map/gathers/ppermute | solution.py:74
  13.9 2.7 %collective-permute-done = bf16[1024,576]{0,1:T(8,128)(2,1)S(1)} collective-permute-done((bf16[1024,576]{0,1:T(8,128)(2,1)}, bf16[1024,576]{0,1:T(8,128)(2,1)S(1)}, u32[]{:S(2)}, u32[]{:S(2)}) %collective-permute-start) | collective-permute-done | bytes 1179680 | tf_op jit(solution)/shard_map/gathers/ppermute | solution.py:74
  16.6 2.4 %maximum_select_fusion = bf16[1024,1152]{0,1:T(8,128)(2,1)S(1)} fusion(bf16[1024,576]{0,1:T(8,128)(2,1)S(1)} %collective-permute-done, bf16[1024,576]{0,1:T(8,128)(2,1)} %param.11, pred[]{:T(512)S(6)} %eq.105), kind=kLoop, calls=%fused_computation.10 | loop fusion | flops 10616832 | bytes 4718593 | tf_op jit(solution)/shard_map/gathers/jit(_where)/select_n | solution.py:75
  19.0 1.1 collective-permute-start.1
  20.2 0.2 reduce-window.9
  20.3 0.2 reduce-window.6
  20.5 0.7 gather_fusion
  21.2 0.8 select_reduce_fusion.3
  22.0 0.7 select_reduce_fusion.4
  22.6 0.7 fusion.33
  23.3 23.9 %collective-permute-done.1 = bf16[1024,1152]{0,1:T(8,128)(2,1)} collective-permute-done((bf16[1024,1152]{0,1:T(8,128)(2,1)S(1)}, bf16[1024,1152]{0,1:T(8,128)(2,1)}, u32[]{:S(2)}, u32[]{:S(2)}) %collective-permute-start.1) | collective-permute-done | bytes 2359328 | tf_op jit(solution)/shard_map/gathers/ppermute | solution.py:80
  47.2 2.4 %constant_dynamic-slice_fusion = bf16[512,1152]{0,1:T(8,128)(2,1)} fusion(bf16[1024,1152]{0,1:T(8,128)(2,1)} %collective-permute-done.1, s32[]{:T(128)S(6)} %select_n.186), kind=kLoop, calls=%fused_computation.86 | loop fusion | bytes 2359300 | tf_op jit(solution)/shard_map/gathers/dynamic_slice | solution.py:82
  49.6 2.1 %collective-permute-start.3 = (bf16[512,1152]{0,1:T(8,128)(2,1)}, bf16[512,1152]{0,1:T(8,128)(2,1)S(1)}, u32[]{:S(2)}, u32[]{:S(2)}) collective-permute-start(bf16[512,1152]{0,1:T(8,128)(2,1)} %constant_dynamic-slice_fusion), channel_id=1, source_target_pairs={{0,64},{32,224},{64,128},{96,32},{128,192},{160,96},{192,0},{224,1... | collective-permute-start | bytes 3538952 | tf_op jit(solution)/shard_map/gathers/ppermute | solution.py:83
  51.7 0.3 collective-permute-start.2
  52.0 0.8 select_reduce_fusion.1
  52.9 2.4 %copy.19 = bf16[1024,576]{1,0:T(8,128)(2,1)} copy(bf16[1024,576]{0,1:T(8,128)(2,1)} %param.11) | data formatting | bytes 2359296 | tf_op args[0]
  55.3 0.7 compare_select_fusion.2
  56.0 0.1 fusion.29
  56.1 0.7 fusion.36
  56.8 8.4 %collective-permute-done.3 = bf16[512,1152]{0,1:T(8,128)(2,1)S(1)} collective-permute-done((bf16[512,1152]{0,1:T(8,128)(2,1)}, bf16[512,1152]{0,1:T(8,128)(2,1)S(1)}, u32[]{:S(2)}, u32[]{:S(2)}) %collective-permute-start.3) | collective-permute-done | bytes 1179680 | tf_op jit(solution)/shard_map/gathers/ppermute | solution.py:83
  65.2 4.5 %collective-permute-start.4 = (bf16[512,1152]{0,1:T(8,128)(2,1)S(1)}, bf16[512,1152]{0,1:T(8,128)(2,1)S(1)}, u32[]{:S(2)}, u32[]{:S(2)}) collective-permute-start(bf16[512,1152]{0,1:T(8,128)(2,1)S(1)} %collective-permute-done.3), channel_id=1, source_target_pairs={{0,32},{32,0},{64,96},{96,64},{128,160},{160,128},{192,224},{224,1... | collective-permute-start | bytes 3538952 | tf_op jit(solution)/shard_map/gathers/ppermute | solution.py:84
  69.6 1.8 %multiply_cosine_fusion = (f32[1024,64]{0,1:T(8,128)}, f32[1024,64]{0,1:T(8,128)}) fusion(f32[64]{0:T(128)S(1)} %multiply_exponential_fusion, f32[1024]{0:T(1024)S(1)} %subtract_convert_fusion.2), kind=kLoop, calls=%fused_computation.40 | loop fusion | flops 65536 | bytes 528640 | tf_op jit(solution)/shard_map/rotary/cos | solution.py:224
  71.4 3.9 %fusion.3 = bf16[2304,1024]{1,0:T(8,128)(2,1)} fusion(s32[2304]{0:T(1024)S(1)} %clamp_bitcast_fusion, pred[2304]{0:T(1024)(128)(4,1)S(1)} %fusion.29), kind=kLoop, calls=%fused_computation.6 | loop fusion | flops 7077888 | bytes 4730112 | tf_op jit(solution)/shard_map/cache_select/convert_element_type | solution.py:164
  75.3 4.4 %select_select_fusion.3 = (bf16[1024,1152]{0,1:T(8,128)(2,1)S(1)}, bf16[1024,1152]{0,1:T(8,128)(2,1)S(1)}, bf16[1024,1152]{0,1:T(8,128)(2,1)S(1)}) fusion(bf16[1024,1152]{0,1:T(8,128)(2,1)S(1)} %maximum_select_fusion, pred[]{:T(512)S(6)} %eq.107, pred[]{:T(512)S(6)} %eq.106, pred[]{:T(512)S(6)} %eq.104, bf16[512,1152]{0,1:T(8,128)(2,1)S(1)} %collective-permute-done.3, ...), kind=kLoop, calls=%fused_computation.15 | loop fusion | flops 16515072 | bytes 16515076 | tf_op jit(solution)/shard_map/gathers/jit(_where)/select_n | solution.py:97
  79.7 2.3 %select_select_fusion.1 = bf16[1024,1152]{0,1:T(8,128)(2,1)S(1)} fusion(bf16[1024,1152]{0,1:T(8,128)(2,1)S(1)} %maximum_select_fusion, bf16[1024,1152]{0,1:T(8,128)(2,1)S(1)} %get-tuple-element.25, bf16[1024,1152]{0,1:T(8,128)(2,1)S(1)} %get-tuple-element.24, pred[]{:T(512)S(6)} %eq.113, pred[]{:T(512)S(6)} %eq.112, pred[]{:T(512)S(6)} %eq.111, ...), kind=kLoop, calls=%fused_computation.13 | loop fusion | flops 14155776 | bytes 11796484 | tf_op jit(solution)/shard_map/gathers/jit(_where)/select_n | solution.py:97
  82.1 2.6 %select_select_fusion.2 = (bf16[1024,1152]{0,1:T(8,128)(2,1)S(1)}, bf16[1024,1152]{0,1:T(8,128)(2,1)S(1)}) fusion(bf16[1024,1152]{0,1:T(8,128)(2,1)S(1)} %maximum_select_fusion, bf16[1024,1152]{0,1:T(8,128)(2,1)S(1)} %get-tuple-element.25, bf16[1024,1152]{0,1:T(8,128)(2,1)S(1)} %get-tuple-element.24, pred[]{:T(512)S(6)} %eq.110, pred[]{:T(512)S(6)} %eq.109, ...), kind=kLoop, calls=%fused_computation.14 | loop fusion | flops 17694720 | bytes 14155783 | tf_op jit(solution)/shard_map/gathers/jit(_where)/select_n | solution.py:97
  84.7 4.4 %pad_maximum_fusion = bf16[1024,4608]{0,1:T(8,128)(2,1)} fusion(bf16[1024,1152]{0,1:T(8,128)(2,1)S(1)} %get-tuple-element.27, bf16[1024,1152]{0,1:T(8,128)(2,1)S(1)} %select_select_fusion.1, bf16[1024,1152]{0,1:T(8,128)(2,1)S(1)} %get-tuple-element.26, bf16[1024,1152]{0,1:T(8,128)(2,1)S(1)} %get-tuple-element.23), kind=kLoop, calls=%fused_computation.3 | loop fusion | flops 37748736 | bytes 18874368 | tf_op jit(solution)/shard_map/gathers/concatenate | solution.py:103
  89.1 38.6 %all-gather.3.cloned.1.call-done = bf16[5632,1024]{1,0:T(8,128)(2,1)} async-done(((bf16[176,1024]{1,0:T(8,128)(2,1)}), bf16[5632,1024]{1,0:T(8,128)(2,1)}) %all-gather.3.cloned.1.call-update) | async-done | bytes 11534352 | tf_op jit(solution)/shard_map/gathers/all_gather | solution.py:151
  127.7 4.1 %select_reduce_fusion = f32[1024,32]{0,1:T(8,128)S(1)} fusion(bf16[32,176,1024]{2,1,0:T(8,128)(2,1)} %bitcast.79, bf16[1024,576]{1,0:T(8,128)(2,1)S(1)} %copy-done.7, pred[1024,32]{0,1:T(8,128)(4,1)S(1)} %copy-done.11), kind=kOutput, calls=%fused_computation.7 | convolution fusion | flops 2149548032 | bytes 3440640 | tf_op jit(solution)/shard_map/lowrank/dot_general | solution.py:170
  131.8 1.7 collective-permute-start.5
  133.5 12.5 %fusion.4 = f32[1024,1024]{0,1:T(8,128)S(1)} fusion(bf16[1024,32,144]{0,2,1:T(8,128)(2,1)S(1)} %bitcast.70, bf16[32,176,1024]{2,1,0:T(8,128)(2,1)} %bitcast.80), kind=kOutput, calls=%fused_computation.18 | convolution fusion | flops 9663676416 | bytes 23068672 | tf_op jit(solution)/shard_map/projection/tci,cin->tn/dot_general | solution.py:208
  146.2 1.3 collective-permute-start.6
  147.5 1.0 subtract_convert_fusion.1
  148.5 1.7 slice.61
  150.2 1.2 reshape.314
  151.5 0.2 copy.29
  151.7 0.6 copy-done.8
  152.4 0.1 copy-done.9
  152.5 3.0 %collective-permute-start.7 = (f32[1024,32]{0,1:T(8,128)S(1)}, f32[1024,32]{0,1:T(8,128)S(1)}, u32[]{:S(2)}, u32[]{:S(2)}) collective-permute-start(f32[1024,32]{0,1:T(8,128)S(1)} %add.136), channel_id=1, source_target_pairs={{0,128},{32,160},{64,192},{96,224},{128,0},{160,32},{192,64},{224,... | collective-permute-start | bytes 393224 | tf_op jit(solution)/shard_map/lowrank/ppermute | solution.py:181
  155.6 4.9 %convolution_convert_fusion.1 = bf16[2304,256]{1,0:T(8,128)(2,1)} fusion(bf16[2304,1024]{1,0:T(8,128)(2,1)} %fusion.3, bf16[1024,256]{0,1:T(8,128)(2,1)S(1)} %bitcast.77), kind=kOutput, calls=%fused_computation.9 | convolution fusion | flops 1208549376 | bytes 6422528 | tf_op jit(solution)/shard_map/cache_write/dot_general | solution.py:232
  160.6 0.8 slice_add_fusion
  161.4 0.3 subtract_convert_fusion
  161.8 1.3 copy.25
  163.1 5.5 %convolution_convert_fusion = bf16[2304,256]{1,0:T(8,128)(2,1)} fusion(bf16[2304,1024]{1,0:T(8,128)(2,1)} %fusion.3, f32[1024,1024]{0,1:T(8,128)} %copy-done.5, bf16[1024,16]{0,1:T(8,128)(2,1)S(1)} %get-tuple-element.32, bf16[1024,32]{0,1:T(8,128)(2,1)S(1)} %copy-done.10, bf16[32,16,256]{2,1,0:T(8,128)(2,1)S(1)} %bitcast.78), kind=kOutput, calls=%fused_computation.8 | convolution fusion | flops 1478033408 | bytes 7307264 | tf_op jit(solution)/shard_map/cache_write/dot_general | solution.py:234
  (53 shorter events, 0.6 us)
Async XLA Ops:
  7.2 13.4 %copy-start = (s32[32]{0:T(128)S(1)}, s32[32]{0:T(128)}, u32[]{:S(2)}) copy-start(s32[32]{0:T(128)} %param.20) | copy-start | bytes 388
  7.2 120.5 %all-gather.3.cloned.1.call-start = ((), (), s32[]{:S(2)}) async-start(), calls=%async_computation | async-start | bytes 11894784 | tf_op jit(solution)/shard_map/gathers/all_gather | solution.py:151
  10.6 6.0 %collective-permute-start = (bf16[1024,576]{0,1:T(8,128)(2,1)}, bf16[1024,576]{0,1:T(8,128)(2,1)S(1)}, u32[]{:S(2)}, u32[]{:S(2)}) collective-permute-start(bf16[1024,576]{0,1:T(8,128)(2,1)} %param.11), channel_id=1, source_target_pairs={{0,32},{32,0},{64,96},{96,64},{128,160},{160,128},{192,224},{224,1... | collective-permute-start | bytes 3538952 | tf_op jit(solution)/shard_map/gathers/ppermute | solution.py:74
  13.9 6.2 %copy-start.12 = (s32[1,10]{1,0:T(1,128)S(1)}, s32[1,10]{1,0:T(1,128)}, u32[]{:S(2)}) copy-start(s32[1,10]{1,0:T(1,128)} %param.18) | copy-start | bytes 124
  13.9 6.6 %copy-start.14 = (s32[1,10]{1,0:T(1,128)S(1)}, s32[1,10]{1,0:T(1,128)}, u32[]{:S(2)}) copy-start(s32[1,10]{1,0:T(1,128)} %param.19) | copy-start | bytes 124
  19.0 28.2 %collective-permute-start.1 = (bf16[1024,1152]{0,1:T(8,128)(2,1)S(1)}, bf16[1024,1152]{0,1:T(8,128)(2,1)}, u32[]{:S(2)}, u32[]{:S(2)}) collective-permute-start(bf16[1024,1152]{0,1:T(8,128)(2,1)S(1)} %maximum_select_fusion), channel_id=1, source_target_pairs={{0,64},{32,224},{64,128},{96,32},{128,192},{160,96},{192,0},{224,1... | collective-permute-start | bytes 7077896 | tf_op jit(solution)/shard_map/gathers/ppermute | solution.py:80
  20.5 31.5 %copy-start.13 = (s32[10,1]{0,1:T(1,128)}, s32[10,1]{0,1:T(1,128)S(1)}, u32[]{:S(2)}) copy-start(s32[10,1]{0,1:T(1,128)S(1)} %reduce-window.6) | copy-start | bytes 124
  49.6 15.6 %collective-permute-start.3 = (bf16[512,1152]{0,1:T(8,128)(2,1)}, bf16[512,1152]{0,1:T(8,128)(2,1)S(1)}, u32[]{:S(2)}, u32[]{:S(2)}) collective-permute-start(bf16[512,1152]{0,1:T(8,128)(2,1)} %constant_dynamic-slice_fusion), channel_id=1, source_target_pairs={{0,64},{32,224},{64,128},{96,32},{128,192},{160,96},{192,0},{224,1... | collective-permute-start | bytes 3538952 | tf_op jit(solution)/shard_map/gathers/ppermute | solution.py:83
  51.7 23.6 %collective-permute-start.2 = (bf16[1024,1152]{0,1:T(8,128)(2,1)}, bf16[1024,1152]{0,1:T(8,128)(2,1)}, u32[]{:S(2)}, u32[]{:S(2)}) collective-permute-start(bf16[1024,1152]{0,1:T(8,128)(2,1)} %collective-permute-done.1), channel_id=1, source_target_pairs={{0,32},{32,0},{64,96},{96,64},{128,160},{160,128},{192,224},{224,1... | collective-permute-start | bytes 7077896 | tf_op jit(solution)/shard_map/gathers/ppermute | solution.py:84
  65.2 10.2 %collective-permute-start.4 = (bf16[512,1152]{0,1:T(8,128)(2,1)S(1)}, bf16[512,1152]{0,1:T(8,128)(2,1)S(1)}, u32[]{:S(2)}, u32[]{:S(2)}) collective-permute-start(bf16[512,1152]{0,1:T(8,128)(2,1)S(1)} %collective-permute-done.3), channel_id=1, source_target_pairs={{0,32},{32,0},{64,96},{96,64},{128,160},{160,128},{192,224},{224,1... | collective-permute-start | bytes 3538952 | tf_op jit(solution)/shard_map/gathers/ppermute | solution.py:84
  84.7 43.0 %copy-start.7 = (bf16[1024,576]{1,0:T(8,128)(2,1)S(1)}, bf16[1024,576]{1,0:T(8,128)(2,1)}, u32[]{:S(2)}) copy-start(bf16[1024,576]{1,0:T(8,128)(2,1)} %copy.19) | copy-start | bytes 3538948
  84.7 43.0 %copy-start.11 = (pred[1024,32]{0,1:T(8,128)(4,1)S(1)}, pred[1024,32]{0,1:T(8,128)(4,1)}, u32[]{:S(2)}) copy-start(pred[1024,32]{0,1:T(8,128)(4,1)} %get-tuple-element.37) | copy-start | bytes 98308
  127.7 5.8 %copy-start.2 = (bf16[1024,4608]{0,1:T(8,128)(2,1)S(1)}, bf16[1024,4608]{0,1:T(8,128)(2,1)}, u32[]{:S(2)}) copy-start(bf16[1024,4608]{0,1:T(8,128)(2,1)} %pad_maximum_fusion) | copy-start | bytes 28311556
  131.8 14.3 %collective-permute-start.5 = (f32[1024,32]{0,1:T(8,128)S(1)}, f32[1024,32]{0,1:T(8,128)S(1)}, u32[]{:S(2)}, u32[]{:S(2)}) collective-permute-start(f32[1024,32]{0,1:T(8,128)S(1)} %select_reduce_fusion), channel_id=1, source_target_pairs={{0,32},{32,0},{64,96},{96,64},{128,160},{160,128},{192,224},{224,1... | collective-permute-start | bytes 393224 | tf_op jit(solution)/shard_map/lowrank/ppermute | solution.py:181
  146.1 2.4 %copy-start.5 = (f32[1024,1024]{0,1:T(8,128)}, f32[1024,1024]{0,1:T(8,128)S(1)}, u32[]{:S(2)}) copy-start(f32[1024,1024]{0,1:T(8,128)S(1)} %fusion.4) | copy-start | bytes 12582916
  146.1 1.4 copy-start.3
  146.1 1.4 copy-start.4
  146.2 6.3 %collective-permute-start.6 = (f32[1024,32]{0,1:T(8,128)S(1)}, f32[1024,32]{0,1:T(8,128)S(1)}, u32[]{:S(2)}, u32[]{:S(2)}) collective-permute-start(f32[1024,32]{0,1:T(8,128)S(1)} %add.135), channel_id=1, source_target_pairs={{0,64},{32,96},{64,0},{96,32},{128,192},{160,224},{192,128},{224,1... | collective-permute-start | bytes 393224 | tf_op jit(solution)/shard_map/lowrank/ppermute | solution.py:181
  151.4 1.0 copy-start.8
  151.4 1.0 copy-start.9
  152.5 8.0 %collective-permute-start.7 = (f32[1024,32]{0,1:T(8,128)S(1)}, f32[1024,32]{0,1:T(8,128)S(1)}, u32[]{:S(2)}, u32[]{:S(2)}) collective-permute-start(f32[1024,32]{0,1:T(8,128)S(1)} %add.136), channel_id=1, source_target_pairs={{0,128},{32,160},{64,192},{96,224},{128,0},{160,32},{192,64},{224,... | collective-permute-start | bytes 393224 | tf_op jit(solution)/shard_map/lowrank/ppermute | solution.py:181
  155.6 5.0 %copy-start.6 = (f32[1024,1024]{0,1:T(8,128)S(1)}, f32[1024,1024]{0,1:T(8,128)}, u32[]{:S(2)}) copy-start(f32[1024,1024]{0,1:T(8,128)} %copy-done.5) | copy-start | bytes 12582916
  155.6 5.0 %copy-start.10 = (bf16[1024,32]{0,1:T(8,128)(2,1)S(1)}, bf16[1024,32]{0,1:T(8,128)(2,1)}, u32[]{:S(2)}) copy-start(bf16[1024,32]{0,1:T(8,128)(2,1)} %get-tuple-element.36) | copy-start | bytes 196612
  163.1 5.5 %copy-start.1 = (s32[32]{0:T(128)S(1)}, s32[32]{0:T(128)}, u32[]{:S(2)}) copy-start(s32[32]{0:T(128)} %param.20) | copy-start | bytes 388
Sparse Core Ops, SparseCore 0:
  11.1 116.5 all-gather.2

commit v12 on v9

--- a/solution.py
+++ b/solution.py
@@ -219,6 +219,7 @@
         query = rotate(base_query + delta_query, cosine, sine_value).astype(jnp.bfloat16)
         key_rotated = rotate(base_key, cosine, sine_value).astype(jnp.bfloat16)
         value_rows = (base_value + delta_value).astype(jnp.bfloat16)
+        value_rows = lax.optimization_barrier(value_rows)
 
     with jax.named_scope("cache_write"):
         pages = page_table.shape[1]

time: 174 us -> 172 us (0.989)
    unnamed x37 -> x33, local copies, waits for them, and re-layouts: 4.85 us -> 4.55 us
where the time goes in v12:
time: 172 us; the launch traced here: 171 us
  waiting for transfers between devices  68 us (40%)
  other arithmetic  34.3 us (20%)
  matrix products  25.2 us (15%)
  starting transfers between devices  17 us (10%)
  between operations  14.3 us (8%)
  local copies, waits for them, and re-layouts  12.6 us (7%)
    all_gather x1, waiting for transfers between devices, shards(): packed = lax.all_gather(jnp.concatenate(pieces, axis=0), 'col', axis=0)  33.5 us
    ppermute x1, waiting for transfers between devices, gather_rows(): near = lax.ppermute(own_block, 'row', ring)  26.5 us
    select_n x3, other arithmetic, gather_rows(): jnp.where(relative == 0, own_block, jnp.where(relative == 1, after, jnp.w...  12.7 us
    dot_general x1, matrix products, shards(): jnp.einsum('tci,cin->tn', full_rows.reshape(full_rows.shape[0], packed.sh...  12.5 us
    ppermute x3, starting transfers between devices, shards(): received = lax.ppermute(partial, 'row', pairs)  5.78 us
    ppermute x1, waiting for transfers between devices, gather_rows(): far_half = lax.ppermute(forwarded, 'row', ring)  5.2 us
    ppermute x2, starting transfers between devices, gather_rows(): from_partner, far_other = lax.ppermute((near, far_half), 'row', swap)  4.55 us
    unnamed x33, local copies, waits for them, and re-layouts  4.55 us
  transfers between devices with their start and end apart: 9, of which 4 were waited for; matrix products, arithmetic and copies ran while one was open for 34% of the time, Pallas kernels for 0%

profile of v12, /device:TPU:1, one launch (start us, length us, event | category | flops | bytes accessed | tf_op | source)
XLA Modules:
  0.0 171.5 jit_solution(9137218157354865259)
XLA Ops:
  7.2 0.7 copy.27
  8.0 0.7 copy.28
  8.8 1.8 %maximum_maximum_fusion = bf16[176,1024]{1,0:T(8,128)(2,1)} fusion(bf16[32,448]{1,0:T(8,128)(2,1)S(1)} %reshape.312, bf16[32,576]{1,0:T(8,128)(2,1)} %bitcast.80, bf16[144,256]{1,0:T(8,128)(2,1)} %param.14, bf16[144,256]{1,0:T(8,128)(2,1)} %param.13, bf16[144,512]{1,0:T(8,128)(2,1)} %param.12), kind=kLoop, calls=%fused_computation.46 | loop fusion | flops 1802240 | bytes 720896 | tf_op jit(solution)/shard_map/gathers/concatenate | solution.py:151
  10.6 3.3 %collective-permute-start = (bf16[1024,576]{0,1:T(8,128)(2,1)}, bf16[1024,576]{0,1:T(8,128)(2,1)S(1)}, u32[]{:S(2)}, u32[]{:S(2)}) collective-permute-start(bf16[1024,576]{0,1:T(8,128)(2,1)} %param.11), channel_id=1, source_target_pairs={{0,32},{32,0},{64,96},{96,64},{128,160},{160,128},{192,224},{224,1... | collective-permute-start | bytes 3538952 | tf_op jit(solution)/shard_map/gathers/ppermute | solution.py:74
  13.9 2.7 %collective-permute-done = bf16[1024,576]{0,1:T(8,128)(2,1)S(1)} collective-permute-done((bf16[1024,576]{0,1:T(8,128)(2,1)}, bf16[1024,576]{0,1:T(8,128)(2,1)S(1)}, u32[]{:S(2)}, u32[]{:S(2)}) %collective-permute-start) | collective-permute-done | bytes 1179680 | tf_op jit(solution)/shard_map/gathers/ppermute | solution.py:74
  16.6 2.3 %maximum_select_fusion = bf16[1024,1152]{0,1:T(8,128)(2,1)S(1)} fusion(bf16[1024,576]{0,1:T(8,128)(2,1)S(1)} %collective-permute-done, bf16[1024,576]{0,1:T(8,128)(2,1)} %param.11, pred[]{:T(512)S(6)} %eq.98), kind=kLoop, calls=%fused_computation.15 | loop fusion | flops 10616832 | bytes 4718593 | tf_op jit(solution)/shard_map/gathers/jit(_where)/select_n | solution.py:75
  18.9 1.1 collective-permute-start.1
  20.0 0.5 and_select_fusion.1
  20.5 26.5 %collective-permute-done.1 = bf16[1024,1152]{0,1:T(8,128)(2,1)} collective-permute-done((bf16[1024,1152]{0,1:T(8,128)(2,1)S(1)}, bf16[1024,1152]{0,1:T(8,128)(2,1)}, u32[]{:S(2)}, u32[]{:S(2)}) %collective-permute-start.1) | collective-permute-done | bytes 2359328 | tf_op jit(solution)/shard_map/gathers/ppermute | solution.py:80
  47.1 2.4 %constant_dynamic-slice_fusion = bf16[512,1152]{0,1:T(8,128)(2,1)} fusion(bf16[1024,1152]{0,1:T(8,128)(2,1)} %collective-permute-done.1, s32[]{:T(128)S(6)} %select_n.183), kind=kLoop, calls=%fused_computation.91 | loop fusion | bytes 2359300 | tf_op jit(solution)/shard_map/gathers/dynamic_slice | solution.py:82
  49.4 2.2 %collective-permute-start.3 = (bf16[512,1152]{0,1:T(8,128)(2,1)}, bf16[512,1152]{0,1:T(8,128)(2,1)S(1)}, u32[]{:S(2)}, u32[]{:S(2)}) collective-permute-start(bf16[512,1152]{0,1:T(8,128)(2,1)} %constant_dynamic-slice_fusion), channel_id=1, source_target_pairs={{0,64},{32,224},{64,128},{96,32},{128,192},{160,96},{192,0},{224,1... | collective-permute-start | bytes 3538952 | tf_op jit(solution)/shard_map/gathers/ppermute | solution.py:83
  51.7 0.6 fusion.38
  52.3 0.8 reduce-window.9
  53.1 0.7 reduce-window.6
  54.0 0.7 pad_clamp_fusion
  54.6 1.2 gather_fusion
  55.9 0.7 select_reduce_fusion.3
  56.6 0.7 fusion.41
  57.3 0.7 fusion.39
  58.0 0.8 select_reduce_fusion.1
  58.7 0.7 select_reduce_fusion.4
  59.4 0.5 compare_select_fusion.2
  59.9 5.2 %collective-permute-done.3 = bf16[512,1152]{0,1:T(8,128)(2,1)S(1)} collective-permute-done((bf16[512,1152]{0,1:T(8,128)(2,1)}, bf16[512,1152]{0,1:T(8,128)(2,1)S(1)}, u32[]{:S(2)}, u32[]{:S(2)}) %collective-permute-start.3) | collective-permute-done | bytes 1179680 | tf_op jit(solution)/shard_map/gathers/ppermute | solution.py:83
  65.1 4.4 %collective-permute-start.4 = (bf16[512,1152]{0,1:T(8,128)(2,1)S(1)}, bf16[512,1152]{0,1:T(8,128)(2,1)}, u32[]{:S(2)}, u32[]{:S(2)}) collective-permute-start(bf16[512,1152]{0,1:T(8,128)(2,1)S(1)} %collective-permute-done.3), channel_id=1, source_target_pairs={{0,32},{32,0},{64,96},{96,64},{128,160},{160,128},{192,224},{224,1... | collective-permute-start | bytes 3538952 | tf_op jit(solution)/shard_map/gathers/ppermute | solution.py:84
  69.5 0.6 multiply_exponential_fusion
  70.1 2.4 %copy.19 = bf16[1024,576]{1,0:T(8,128)(2,1)} copy(bf16[1024,576]{0,1:T(8,128)(2,1)} %param.11) | data formatting | bytes 2359296 | tf_op args[0]
  72.6 1.3 clamp_bitcast_fusion
  73.9 0.7 fusion.44
  74.6 2.5 %multiply_cosine_fusion = (f32[1024,64]{0,1:T(8,128)}, f32[1024,64]{0,1:T(8,128)}) fusion(f32[64]{0:T(128)} %multiply_exponential_fusion, f32[1024]{0:T(1024)S(1)} %subtract_convert_fusion.2), kind=kLoop, calls=%fused_computation.45 | loop fusion | flops 65536 | bytes 528640 | tf_op jit(solution)/shard_map/rotary/cos | solution.py:217
  77.1 4.9 %select_select_fusion.3 = (bf16[1024,1152]{0,1:T(8,128)(2,1)S(1)}, bf16[1024,1152]{0,1:T(8,128)(2,1)S(1)}, bf16[1024,1152]{0,1:T(8,128)(2,1)S(1)}) fusion(bf16[1024,1152]{0,1:T(8,128)(2,1)S(1)} %maximum_select_fusion, pred[]{:T(512)S(6)} %eq.100, pred[]{:T(512)S(6)} %eq.99, pred[]{:T(512)S(6)} %eq.97, bf16[512,1152]{0,1:T(8,128)(2,1)S(1)} %collective-permute-done.3, ...), kind=kLoop, calls=%fused_computation.20 | loop fusion | flops 16515072 | bytes 16515076 | tf_op jit(solution)/shard_map/gathers/jit(_where)/select_n | solution.py:97
  81.9 3.8 %select_select_fusion.1 = bf16[1024,1152]{0,1:T(8,128)(2,1)S(1)} fusion(bf16[1024,1152]{0,1:T(8,128)(2,1)S(1)} %maximum_select_fusion, bf16[1024,1152]{0,1:T(8,128)(2,1)S(1)} %get-tuple-element.21, bf16[1024,1152]{0,1:T(8,128)(2,1)S(1)} %get-tuple-element.20, pred[]{:T(512)S(6)} %eq.106, pred[]{:T(512)S(6)} %eq.105, pred[]{:T(512)S(6)} %eq.104, ...), kind=kLoop, calls=%fused_computation.18 | loop fusion | flops 14155776 | bytes 11796484 | tf_op jit(solution)/shard_map/gathers/jit(_where)/select_n | solution.py:97
  85.7 4.0 %select_select_fusion.2 = (bf16[1024,1152]{0,1:T(8,128)(2,1)S(1)}, bf16[1024,1152]{0,1:T(8,128)(2,1)S(1)}) fusion(bf16[1024,1152]{0,1:T(8,128)(2,1)S(1)} %maximum_select_fusion, bf16[1024,1152]{0,1:T(8,128)(2,1)S(1)} %get-tuple-element.21, bf16[1024,1152]{0,1:T(8,128)(2,1)S(1)} %get-tuple-element.20, pred[]{:T(512)S(6)} %eq.103, pred[]{:T(512)S(6)} %eq.102, ...), kind=kLoop, calls=%fused_computation.19 | loop fusion | flops 17694720 | bytes 14155783 | tf_op jit(solution)/shard_map/gathers/jit(_where)/select_n | solution.py:97
  89.8 4.4 %pad_maximum_fusion = bf16[1024,4608]{0,1:T(8,128)(2,1)} fusion(bf16[1024,1152]{0,1:T(8,128)(2,1)S(1)} %get-tuple-element.23, bf16[1024,1152]{0,1:T(8,128)(2,1)S(1)} %select_select_fusion.1, bf16[1024,1152]{0,1:T(8,128)(2,1)S(1)} %get-tuple-element.22, bf16[1024,1152]{0,1:T(8,128)(2,1)S(1)} %get-tuple-element.19), kind=kLoop, calls=%fused_computation.3 | loop fusion | flops 37748736 | bytes 18874368 | tf_op jit(solution)/shard_map/gathers/concatenate | solution.py:103
  94.2 33.5 %all-gather.3.cloned.1.call-done = bf16[5632,1024]{1,0:T(8,128)(2,1)} async-done(((bf16[176,1024]{1,0:T(8,128)(2,1)}), bf16[5632,1024]{1,0:T(8,128)(2,1)}) %all-gather.3.cloned.1.call-update) | async-done | bytes 11534352 | tf_op jit(solution)/shard_map/gathers/all_gather | solution.py:151
  127.7 4.1 %select_reduce_fusion = f32[1024,32]{0,1:T(8,128)S(1)} fusion(bf16[32,176,1024]{2,1,0:T(8,128)(2,1)} %bitcast.76, bf16[1024,576]{1,0:T(8,128)(2,1)S(1)} %copy-done.7, pred[1024,32]{0,1:T(8,128)(4,1)S(1)} %copy-done.9), kind=kOutput, calls=%fused_computation.12 | convolution fusion | flops 2149548032 | bytes 3440640 | tf_op jit(solution)/shard_map/lowrank/dot_general | solution.py:163
  131.8 1.7 collective-permute-start.5
  133.5 12.5 %fusion.17 = f32[1024,1024]{0,1:T(8,128)S(1)} fusion(bf16[1024,32,144]{0,2,1:T(8,128)(2,1)S(1)} %bitcast.67, bf16[32,176,1024]{2,1,0:T(8,128)(2,1)} %bitcast.77), kind=kOutput, calls=%fused_computation.23 | convolution fusion | flops 9663676416 | bytes 23068672 | tf_op jit(solution)/shard_map/projection/tci,cin->tn/dot_general | solution.py:201
  146.2 1.3 collective-permute-start.6
  147.7 0.4 copy-done.5
  148.1 1.7 %slice.61 = bf16[32,32,448]{2,1,0:T(8,128)(2,1)S(1)} slice(bf16[32,176,1024]{2,1,0:T(8,128)(2,1)} %bitcast.78), slice={[0:32], [144:176], [576:1024]} | slice | bytes 1835008 | tf_op jit(solution)/shard_map/gathers/slice | solution.py:154
  149.8 1.2 reshape.314
  151.4 2.8 %collective-permute-start.7 = (f32[1024,32]{0,1:T(8,128)S(1)}, f32[1024,32]{0,1:T(8,128)S(1)}, u32[]{:S(2)}, u32[]{:S(2)}) collective-permute-start(f32[1024,32]{0,1:T(8,128)S(1)} %add.130), channel_id=1, source_target_pairs={{0,128},{32,160},{64,192},{96,224},{128,0},{160,32},{192,64},{224,... | collective-permute-start | bytes 393224 | tf_op jit(solution)/shard_map/lowrank/ppermute | solution.py:174
  154.2 3.6 %fusion.11 = bf16[2304,256]{1,0:T(8,128)(2,1)} fusion(bf16[1024,256]{0,1:T(8,128)(2,1)S(1)} %bitcast.74, s32[2304]{0:T(1024)S(1)} %copy-done.10, pred[2304]{0:T(1024)(128)(4,1)S(1)} %fusion.37), kind=kOutput, calls=%fused_computation.13 | convolution fusion | flops 1213267968 | bytes 1715456 | tf_op jit(solution)/shard_map/cache_write/dot_general | solution.py:230
  157.9 0.5 fusion.24
  158.4 3.6 %fusion.14 = bf16[2304,256]{1,0:T(8,128)(2,1)} fusion(bf16[1024,256]{0,1:T(8,128)(2,1)S(1)} %fusion.24, s32[2304]{0:T(1024)S(1)} %copy-done.10, pred[2304]{0:T(1024)(128)(4,1)S(1)} %fusion.37), kind=kOutput, calls=%fused_computation.14 | convolution fusion | flops 1213267968 | bytes 1715456 | tf_op jit(solution)/shard_map/cache_write/dot_general | solution.py:232
  162.1 0.8 slice_add_fusion
  162.9 0.4 subtract_convert_fusion
  163.3 1.3 copy.25
  (51 shorter events, 1.2 us)
Async XLA Ops:
  7.2 47.5 %copy-start = (s32[32]{0:T(128)S(1)}, s32[32]{0:T(128)}, u32[]{:S(2)}) copy-start(s32[32]{0:T(128)} %param.20) | copy-start | bytes 388
  7.2 120.5 %all-gather.3.cloned.1.call-start = ((), (), s32[]{:S(2)}) async-start(), calls=%async_computation | async-start | bytes 11894784 | tf_op jit(solution)/shard_map/gathers/all_gather | solution.py:151
  10.6 6.0 %collective-permute-start = (bf16[1024,576]{0,1:T(8,128)(2,1)}, bf16[1024,576]{0,1:T(8,128)(2,1)S(1)}, u32[]{:S(2)}, u32[]{:S(2)}) collective-permute-start(bf16[1024,576]{0,1:T(8,128)(2,1)} %param.11), channel_id=1, source_target_pairs={{0,32},{32,0},{64,96},{96,64},{128,160},{160,128},{192,224},{224,1... | collective-permute-start | bytes 3538952 | tf_op jit(solution)/shard_map/gathers/ppermute | solution.py:74
  13.9 6.1 %copy-start.11 = (s32[1,10]{1,0:T(1,128)S(1)}, s32[1,10]{1,0:T(1,128)}, u32[]{:S(2)}) copy-start(s32[1,10]{1,0:T(1,128)} %param.18) | copy-start | bytes 124
  18.9 32.8 %copy-start.13 = (s32[1,10]{1,0:T(1,128)S(1)}, s32[1,10]{1,0:T(1,128)}, u32[]{:S(2)}) copy-start(s32[1,10]{1,0:T(1,128)} %param.19) | copy-start | bytes 124
  18.9 28.2 %collective-permute-start.1 = (bf16[1024,1152]{0,1:T(8,128)(2,1)S(1)}, bf16[1024,1152]{0,1:T(8,128)(2,1)}, u32[]{:S(2)}, u32[]{:S(2)}) collective-permute-start(bf16[1024,1152]{0,1:T(8,128)(2,1)S(1)} %maximum_select_fusion), channel_id=1, source_target_pairs={{0,64},{32,224},{64,128},{96,32},{128,192},{160,96},{192,0},{224,1... | collective-permute-start | bytes 7077896 | tf_op jit(solution)/shard_map/gathers/ppermute | solution.py:80
  49.4 15.7 %collective-permute-start.3 = (bf16[512,1152]{0,1:T(8,128)(2,1)}, bf16[512,1152]{0,1:T(8,128)(2,1)S(1)}, u32[]{:S(2)}, u32[]{:S(2)}) collective-permute-start(bf16[512,1152]{0,1:T(8,128)(2,1)} %constant_dynamic-slice_fusion), channel_id=1, source_target_pairs={{0,64},{32,224},{64,128},{96,32},{128,192},{160,96},{192,0},{224,1... | collective-permute-start | bytes 3538952 | tf_op jit(solution)/shard_map/gathers/ppermute | solution.py:83
  53.1 4.9 %copy-start.12 = (s32[10,1]{0,1:T(1,128)}, s32[10,1]{0,1:T(1,128)S(1)}, u32[]{:S(2)}) copy-start(s32[10,1]{0,1:T(1,128)S(1)} %reduce-window.9) | copy-start | bytes 124
  53.8 23.3 %collective-permute-start.2 = (bf16[1024,1152]{0,1:T(8,128)(2,1)}, bf16[1024,1152]{0,1:T(8,128)(2,1)}, u32[]{:S(2)}, u32[]{:S(2)}) collective-permute-start(bf16[1024,1152]{0,1:T(8,128)(2,1)} %collective-permute-done.1), channel_id=1, source_target_pairs={{0,32},{32,0},{64,96},{96,64},{128,160},{160,128},{192,224},{224,1... | collective-permute-start | bytes 7077896 | tf_op jit(solution)/shard_map/gathers/ppermute | solution.py:84
  65.1 11.9 %collective-permute-start.4 = (bf16[512,1152]{0,1:T(8,128)(2,1)S(1)}, bf16[512,1152]{0,1:T(8,128)(2,1)}, u32[]{:S(2)}, u32[]{:S(2)}) collective-permute-start(bf16[512,1152]{0,1:T(8,128)(2,1)S(1)} %collective-permute-done.3), channel_id=1, source_target_pairs={{0,32},{32,0},{64,96},{96,64},{128,160},{160,128},{192,224},{224,1... | collective-permute-start | bytes 3538952 | tf_op jit(solution)/shard_map/gathers/ppermute | solution.py:84
  89.7 38.0 %copy-start.7 = (bf16[1024,576]{1,0:T(8,128)(2,1)S(1)}, bf16[1024,576]{1,0:T(8,128)(2,1)}, u32[]{:S(2)}) copy-start(bf16[1024,576]{1,0:T(8,128)(2,1)} %copy.19) | copy-start | bytes 3538948
  89.7 38.0 %copy-start.9 = (pred[1024,32]{0,1:T(8,128)(4,1)S(1)}, pred[1024,32]{0,1:T(8,128)(4,1)}, u32[]{:S(2)}) copy-start(pred[1024,32]{0,1:T(8,128)(4,1)} %get-tuple-element.33) | copy-start | bytes 98308
  127.7 5.8 %copy-start.2 = (bf16[1024,4608]{0,1:T(8,128)(2,1)S(1)}, bf16[1024,4608]{0,1:T(8,128)(2,1)}, u32[]{:S(2)}) copy-start(bf16[1024,4608]{0,1:T(8,128)(2,1)} %pad_maximum_fusion) | copy-start | bytes 28311556
  131.8 14.3 %collective-permute-start.5 = (f32[1024,32]{0,1:T(8,128)S(1)}, f32[1024,32]{0,1:T(8,128)S(1)}, u32[]{:S(2)}, u32[]{:S(2)}) collective-permute-start(f32[1024,32]{0,1:T(8,128)S(1)} %select_reduce_fusion), channel_id=1, source_target_pairs={{0,32},{32,0},{64,96},{96,64},{128,160},{160,128},{192,224},{224,1... | collective-permute-start | bytes 393224 | tf_op jit(solution)/shard_map/lowrank/ppermute | solution.py:174
  146.1 2.0 %copy-start.5 = (f32[1024,1024]{0,1:T(8,128)}, f32[1024,1024]{0,1:T(8,128)S(1)}, u32[]{:S(2)}) copy-start(f32[1024,1024]{0,1:T(8,128)S(1)} %fusion.17) | copy-start | bytes 12582916
  146.1 1.4 copy-start.3
  146.1 1.4 copy-start.4
  146.2 5.2 %collective-permute-start.6 = (f32[1024,32]{0,1:T(8,128)S(1)}, f32[1024,32]{0,1:T(8,128)S(1)}, u32[]{:S(2)}, u32[]{:S(2)}) collective-permute-start(f32[1024,32]{0,1:T(8,128)S(1)} %add.129), channel_id=1, source_target_pairs={{0,64},{32,96},{64,0},{96,32},{128,192},{160,224},{192,128},{224,1... | collective-permute-start | bytes 393224 | tf_op jit(solution)/shard_map/lowrank/ppermute | solution.py:174
  151.0 3.2 %copy-start.10 = (s32[2304]{0:T(1024)S(1)}, s32[2304]{0:T(1024)}, u32[]{:S(2)}) copy-start(s32[2304]{0:T(1024)} %clamp_bitcast_fusion) | copy-start | bytes 27652
  151.4 6.5 %collective-permute-start.7 = (f32[1024,32]{0,1:T(8,128)S(1)}, f32[1024,32]{0,1:T(8,128)S(1)}, u32[]{:S(2)}, u32[]{:S(2)}) collective-permute-start(f32[1024,32]{0,1:T(8,128)S(1)} %add.130), channel_id=1, source_target_pairs={{0,128},{32,160},{64,192},{96,224},{128,0},{160,32},{192,64},{224,... | collective-permute-start | bytes 393224 | tf_op jit(solution)/shard_map/lowrank/ppermute | solution.py:174
  154.2 3.7 %copy-start.6 = (f32[1024,1024]{0,1:T(8,128)S(1)}, f32[1024,1024]{0,1:T(8,128)}, u32[]{:S(2)}) copy-start(f32[1024,1024]{0,1:T(8,128)} %copy-done.5) | copy-start | bytes 12582916
  154.2 3.7 %copy-start.8 = (bf16[1024,32]{0,1:T(8,128)(2,1)S(1)}, bf16[1024,32]{0,1:T(8,128)(2,1)}, u32[]{:S(2)}) copy-start(bf16[1024,32]{0,1:T(8,128)(2,1)} %get-tuple-element.32) | copy-start | bytes 196612
  162.9 1.8 %copy-start.1 = (s32[32]{0:T(128)S(1)}, s32[32]{0:T(128)}, u32[]{:S(2)}) copy-start(s32[32]{0:T(128)} %param.20) | copy-start | bytes 388
Sparse Core Ops, SparseCore 0:
  11.1 116.5 all-gather.2

commit v13 on v12

--- a/solution.py
+++ b/solution.py
@@ -11,13 +11,9 @@
 
 
 def rotate(values, cosine, sine_value):
-    half_width = HEAD // 2
-    shaped = values.reshape(values.shape[0], -1, HEAD)
-    leading = shaped[:, :, :half_width]
-    second = shaped[:, :, half_width:]
-    rotated = jnp.concatenate(
-        [leading * cosine - second * sine_value, second * cosine + leading * sine_value], axis=2
-    )
+    shaped = values.reshape(values.shape[0], -1, 2, HEAD // 2)
+    swapped = shaped[:, :, ::-1, :]
+    rotated = shaped * cosine + swapped * sine_value
     return rotated.reshape(values.shape)
 
 
@@ -214,8 +210,9 @@
             jnp.arange(half_width, dtype=jnp.float32) * (-2.0 * math.log(10000.0) / HEAD)
         )
         angles = position.astype(jnp.float32)[:, None] * frequency[None, :]
-        cosine = jnp.cos(angles)[:, None, :]
-        sine_value = jnp.sin(angles)[:, None, :]
+        cosine = jnp.cos(angles)[:, None, None, :]
+        sine = jnp.sin(angles)
+        sine_value = jnp.stack([-sine, sine], axis=1)[:, None, :, :]
         query = rotate(base_query + delta_query, cosine, sine_value).astype(jnp.bfloat16)
         key_rotated = rotate(base_key, cosine, sine_value).astype(jnp.bfloat16)
         value_rows = (base_value + delta_value).astype(jnp.bfloat16)

time: 172 us -> 173 us (level)
    unnamed x33 -> x38, local copies, waits for them, and re-layouts: 4.55 us -> 5.71 us
where the time goes in v13:
time: 173 us; the launch traced here: 172 us
  waiting for transfers between devices  67.2 us (39%)
  other arithmetic  35.9 us (21%)
  matrix products  25.2 us (15%)
  starting transfers between devices  17 us (10%)
  between operations  14.3 us (8%)
  local copies, waits for them, and re-layouts  12.4 us (7%)
    all_gather x1, waiting for transfers between devices, shards(): packed = lax.all_gather(jnp.concatenate(pieces, axis=0), 'col', axis=0)  33 us
    ppermute x1, waiting for transfers between devices, gather_rows(): near = lax.ppermute(own_block, 'row', ring)  25.2 us
    select_n x3, other arithmetic, gather_rows(): jnp.where(relative == 0, own_block, jnp.where(relative == 1, after, jnp.w...  12.6 us
    dot_general x1, matrix products, shards(): jnp.einsum('tci,cin->tn', full_rows.reshape(full_rows.shape[0], packed.sh...  12.5 us
    ppermute x1, waiting for transfers between devices, gather_rows(): far_half = lax.ppermute(forwarded, 'row', ring)  6.21 us
    ppermute x3, starting transfers between devices, shards(): received = lax.ppermute(partial, 'row', pairs)  5.8 us
    unnamed x38, local copies, waits for them, and re-layouts  5.71 us
    ppermute x2, starting transfers between devices, gather_rows(): from_partner, far_other = lax.ppermute((near, far_half), 'row', swap)  4.55 us
  transfers between devices with their start and end apart: 9, of which 4 were waited for; matrix products, arithmetic and copies ran while one was open for 34% of the time, Pallas kernels for 0%

profile of v13, /device:TPU:1, one launch (start us, length us, event | category | flops | bytes accessed | tf_op | source)
XLA Modules:
  0.0 172.1 jit_solution(13466601277602587375)
XLA Ops:
  7.2 0.7 copy.26
  8.0 0.7 copy.27
  8.8 1.8 %maximum_maximum_fusion = bf16[176,1024]{1,0:T(8,128)(2,1)} fusion(bf16[32,448]{1,0:T(8,128)(2,1)S(1)} %reshape.371, bf16[32,576]{1,0:T(8,128)(2,1)} %bitcast.80, bf16[144,256]{1,0:T(8,128)(2,1)} %param.14, bf16[144,256]{1,0:T(8,128)(2,1)} %param.13, bf16[144,512]{1,0:T(8,128)(2,1)} %param.12), kind=kLoop, calls=%fused_computation.41 | loop fusion | flops 1802240 | bytes 720896 | tf_op jit(solution)/shard_map/gathers/concatenate | solution.py:147
  10.6 3.3 %collective-permute-start = (bf16[1024,576]{0,1:T(8,128)(2,1)}, bf16[1024,576]{0,1:T(8,128)(2,1)S(1)}, u32[]{:S(2)}, u32[]{:S(2)}) collective-permute-start(bf16[1024,576]{0,1:T(8,128)(2,1)} %param.11), channel_id=1, source_target_pairs={{0,32},{32,0},{64,96},{96,64},{128,160},{160,128},{192,224},{224,1... | collective-permute-start | bytes 3538952 | tf_op jit(solution)/shard_map/gathers/ppermute | solution.py:70
  13.9 2.7 %collective-permute-done = bf16[1024,576]{0,1:T(8,128)(2,1)S(1)} collective-permute-done((bf16[1024,576]{0,1:T(8,128)(2,1)}, bf16[1024,576]{0,1:T(8,128)(2,1)S(1)}, u32[]{:S(2)}, u32[]{:S(2)}) %collective-permute-start) | collective-permute-done | bytes 1179680 | tf_op jit(solution)/shard_map/gathers/ppermute | solution.py:70
  16.6 2.3 %maximum_select_fusion = bf16[1024,1152]{0,1:T(8,128)(2,1)S(1)} fusion(bf16[1024,576]{0,1:T(8,128)(2,1)S(1)} %collective-permute-done, bf16[1024,576]{0,1:T(8,128)(2,1)} %param.11, pred[]{:T(512)S(6)} %eq.98), kind=kLoop, calls=%fused_computation.15 | loop fusion | flops 10616832 | bytes 4718593 | tf_op jit(solution)/shard_map/gathers/jit(_where)/select_n | solution.py:71
  18.9 1.1 collective-permute-start.1
  20.0 1.3 select_reduce_fusion.3
  21.3 0.5 and_select_fusion.1
  21.8 25.2 %collective-permute-done.1 = bf16[1024,1152]{0,1:T(8,128)(2,1)} collective-permute-done((bf16[1024,1152]{0,1:T(8,128)(2,1)S(1)}, bf16[1024,1152]{0,1:T(8,128)(2,1)}, u32[]{:S(2)}, u32[]{:S(2)}) %collective-permute-start.1) | collective-permute-done | bytes 2359328 | tf_op jit(solution)/shard_map/gathers/ppermute | solution.py:76
  47.1 2.4 %constant_dynamic-slice_fusion = bf16[512,1152]{0,1:T(8,128)(2,1)} fusion(bf16[1024,1152]{0,1:T(8,128)(2,1)} %collective-permute-done.1, s32[]{:T(128)S(6)} %select_n.183), kind=kLoop, calls=%fused_computation.89 | loop fusion | bytes 2359300 | tf_op jit(solution)/shard_map/gathers/dynamic_slice | solution.py:78
  49.4 2.2 %collective-permute-start.3 = (bf16[512,1152]{0,1:T(8,128)(2,1)}, bf16[512,1152]{0,1:T(8,128)(2,1)S(1)}, u32[]{:S(2)}, u32[]{:S(2)}) collective-permute-start(bf16[512,1152]{0,1:T(8,128)(2,1)} %constant_dynamic-slice_fusion), channel_id=1, source_target_pairs={{0,64},{32,224},{64,128},{96,32},{128,192},{160,96},{192,0},{224,1... | collective-permute-start | bytes 3538952 | tf_op jit(solution)/shard_map/gathers/ppermute | solution.py:79
  51.7 1.3 reduce-window.9
  53.0 0.7 reduce-window.6
  53.7 1.2 gather_fusion
  55.0 0.7 fusion.42
  55.7 0.7 fusion.40
  56.4 0.8 select_reduce_fusion.1
  57.2 0.9 fusion.33
  58.1 0.8 pad_maximum_fusion.1
  58.9 6.2 %collective-permute-done.3 = bf16[512,1152]{0,1:T(8,128)(2,1)S(1)} collective-permute-done((bf16[512,1152]{0,1:T(8,128)(2,1)}, bf16[512,1152]{0,1:T(8,128)(2,1)S(1)}, u32[]{:S(2)}, u32[]{:S(2)}) %collective-permute-start.3) | collective-permute-done | bytes 1179680 | tf_op jit(solution)/shard_map/gathers/ppermute | solution.py:79
  65.1 4.4 %collective-permute-start.4 = (bf16[512,1152]{0,1:T(8,128)(2,1)S(1)}, bf16[512,1152]{0,1:T(8,128)(2,1)}, u32[]{:S(2)}, u32[]{:S(2)}) collective-permute-start(bf16[512,1152]{0,1:T(8,128)(2,1)S(1)} %collective-permute-done.3), channel_id=1, source_target_pairs={{0,32},{32,0},{64,96},{96,64},{128,160},{160,128},{192,224},{224,1... | collective-permute-start | bytes 3538952 | tf_op jit(solution)/shard_map/gathers/ppermute | solution.py:80
  69.5 1.3 select_reduce_fusion.4
  70.8 2.4 %copy.19 = bf16[1024,576]{1,0:T(8,128)(2,1)} copy(bf16[1024,576]{0,1:T(8,128)(2,1)} %param.11) | data formatting | bytes 2359296 | tf_op args[0]
  73.3 0.7 compare_select_fusion.2
  73.9 0.7 fusion.38
  74.6 0.7 clamp_bitcast_fusion
  75.3 0.7 fusion.45
  76.0 1.6 multiply_cosine_fusion
  77.6 4.9 %select_select_fusion.3 = (bf16[1024,1152]{0,1:T(8,128)(2,1)S(1)}, bf16[1024,1152]{0,1:T(8,128)(2,1)S(1)}, bf16[1024,1152]{0,1:T(8,128)(2,1)S(1)}) fusion(bf16[1024,1152]{0,1:T(8,128)(2,1)S(1)} %maximum_select_fusion, pred[]{:T(512)S(6)} %eq.100, pred[]{:T(512)S(6)} %eq.99, pred[]{:T(512)S(6)} %eq.97, bf16[512,1152]{0,1:T(8,128)(2,1)S(1)} %collective-permute-done.3, ...), kind=kLoop, calls=%fused_computation.20 | loop fusion | flops 16515072 | bytes 16515076 | tf_op jit(solution)/shard_map/gathers/jit(_where)/select_n | solution.py:93
  82.4 3.8 %select_select_fusion.1 = bf16[1024,1152]{0,1:T(8,128)(2,1)S(1)} fusion(bf16[1024,1152]{0,1:T(8,128)(2,1)S(1)} %maximum_select_fusion, bf16[1024,1152]{0,1:T(8,128)(2,1)S(1)} %get-tuple-element.27, bf16[1024,1152]{0,1:T(8,128)(2,1)S(1)} %get-tuple-element.26, pred[]{:T(512)S(6)} %eq.106, pred[]{:T(512)S(6)} %eq.105, pred[]{:T(512)S(6)} %eq.104, ...), kind=kLoop, calls=%fused_computation.18 | loop fusion | flops 14155776 | bytes 11796484 | tf_op jit(solution)/shard_map/gathers/jit(_where)/select_n | solution.py:93
  86.2 4.0 %select_select_fusion.2 = (bf16[1024,1152]{0,1:T(8,128)(2,1)S(1)}, bf16[1024,1152]{0,1:T(8,128)(2,1)S(1)}) fusion(bf16[1024,1152]{0,1:T(8,128)(2,1)S(1)} %maximum_select_fusion, bf16[1024,1152]{0,1:T(8,128)(2,1)S(1)} %get-tuple-element.27, bf16[1024,1152]{0,1:T(8,128)(2,1)S(1)} %get-tuple-element.26, pred[]{:T(512)S(6)} %eq.103, pred[]{:T(512)S(6)} %eq.102, ...), kind=kLoop, calls=%fused_computation.19 | loop fusion | flops 17694720 | bytes 14155783 | tf_op jit(solution)/shard_map/gathers/jit(_where)/select_n | solution.py:93
  90.3 4.4 %pad_maximum_fusion = bf16[1024,4608]{0,1:T(8,128)(2,1)} fusion(bf16[1024,1152]{0,1:T(8,128)(2,1)S(1)} %get-tuple-element.29, bf16[1024,1152]{0,1:T(8,128)(2,1)S(1)} %select_select_fusion.1, bf16[1024,1152]{0,1:T(8,128)(2,1)S(1)} %get-tuple-element.28, bf16[1024,1152]{0,1:T(8,128)(2,1)S(1)} %get-tuple-element.25), kind=kLoop, calls=%fused_computation.3 | loop fusion | flops 37748736 | bytes 18874368 | tf_op jit(solution)/shard_map/gathers/concatenate | solution.py:99
  94.7 33.0 %all-gather.3.cloned.1.call-done = bf16[5632,1024]{1,0:T(8,128)(2,1)} async-done(((bf16[176,1024]{1,0:T(8,128)(2,1)}), bf16[5632,1024]{1,0:T(8,128)(2,1)}) %all-gather.3.cloned.1.call-update) | async-done | bytes 11534352 | tf_op jit(solution)/shard_map/gathers/all_gather | solution.py:147
  127.7 4.1 %select_reduce_fusion = f32[1024,32]{0,1:T(8,128)S(1)} fusion(bf16[32,176,1024]{2,1,0:T(8,128)(2,1)} %bitcast.76, bf16[1024,576]{1,0:T(8,128)(2,1)S(1)} %copy-done.7, pred[1024,32]{0,1:T(8,128)(4,1)S(1)} %copy-done.10), kind=kOutput, calls=%fused_computation.12 | convolution fusion | flops 2149548032 | bytes 3440640 | tf_op jit(solution)/shard_map/lowrank/dot_general | solution.py:159
  131.8 1.7 collective-permute-start.5
  133.5 12.5 %fusion.17 = f32[1024,1024]{0,1:T(8,128)S(1)} fusion(bf16[1024,32,144]{0,2,1:T(8,128)(2,1)S(1)} %bitcast.67, bf16[32,176,1024]{2,1,0:T(8,128)(2,1)} %bitcast.77), kind=kOutput, calls=%fused_computation.23 | convolution fusion | flops 9663676416 | bytes 23068672 | tf_op jit(solution)/shard_map/projection/tci,cin->tn/dot_general | solution.py:197
  146.2 1.3 collective-permute-start.6
  147.7 1.0 add_convert_fusion.1
  148.7 1.7 %slice.45 = bf16[32,32,448]{2,1,0:T(8,128)(2,1)S(1)} slice(bf16[32,176,1024]{2,1,0:T(8,128)(2,1)} %bitcast.78), slice={[0:32], [144:176], [576:1024]} | slice | bytes 1835008 | tf_op jit(solution)/shard_map/gathers/slice | solution.py:150
  150.5 1.2 reshape.373
  152.0 2.8 %collective-permute-start.7 = (f32[1024,32]{0,1:T(8,128)S(1)}, f32[1024,32]{0,1:T(8,128)S(1)}, u32[]{:S(2)}, u32[]{:S(2)}) collective-permute-start(f32[1024,32]{0,1:T(8,128)S(1)} %add.130), channel_id=1, source_target_pairs={{0,128},{32,160},{64,192},{96,224},{128,0},{160,32},{192,64},{224,... | collective-permute-start | bytes 393224 | tf_op jit(solution)/shard_map/lowrank/ppermute | solution.py:170
  154.9 3.6 %fusion.11 = bf16[2304,256]{1,0:T(8,128)(2,1)} fusion(bf16[1024,256]{0,1:T(8,128)(2,1)S(1)} %bitcast.74, s32[2304]{0:T(1024)S(1)} %copy-done.11, pred[2304]{0:T(1024)(128)(4,1)S(1)} %copy-done.12), kind=kOutput, calls=%fused_computation.13 | convolution fusion | flops 1213267968 | bytes 1715456 | tf_op jit(solution)/shard_map/cache_write/dot_general | solution.py:227
  158.6 0.5 fusion.24
  159.1 3.6 %fusion.14 = bf16[2304,256]{1,0:T(8,128)(2,1)} fusion(bf16[1024,256]{0,1:T(8,128)(2,1)S(1)} %fusion.24, s32[2304]{0:T(1024)S(1)} %copy-done.11, pred[2304]{0:T(1024)(128)(4,1)S(1)} %copy-done.12), kind=kOutput, calls=%fused_computation.14 | convolution fusion | flops 1213267968 | bytes 1715456 | tf_op jit(solution)/shard_map/cache_write/dot_general | solution.py:229
  162.7 0.8 slice_add_fusion
  163.6 0.4 add_convert_fusion
  163.9 1.3 copy.23
  (55 shorter events, 1.1 us)
Async XLA Ops:
  7.2 46.5 %copy-start = (s32[32]{0:T(128)S(1)}, s32[32]{0:T(128)}, u32[]{:S(2)}) copy-start(s32[32]{0:T(128)} %param.20) | copy-start | bytes 388
  7.2 120.5 %all-gather.3.cloned.1.call-start = ((), (), s32[]{:S(2)}) async-start(), calls=%async_computation | async-start | bytes 11894784 | tf_op jit(solution)/shard_map/gathers/all_gather | solution.py:147
  10.6 6.0 %collective-permute-start = (bf16[1024,576]{0,1:T(8,128)(2,1)}, bf16[1024,576]{0,1:T(8,128)(2,1)S(1)}, u32[]{:S(2)}, u32[]{:S(2)}) collective-permute-start(bf16[1024,576]{0,1:T(8,128)(2,1)} %param.11), channel_id=1, source_target_pairs={{0,32},{32,0},{64,96},{96,64},{128,160},{160,128},{192,224},{224,1... | collective-permute-start | bytes 3538952 | tf_op jit(solution)/shard_map/gathers/ppermute | solution.py:70
  13.9 6.1 %copy-start.15 = (s32[1,10]{1,0:T(1,128)S(1)}, s32[1,10]{1,0:T(1,128)}, u32[]{:S(2)}) copy-start(s32[1,10]{1,0:T(1,128)} %param.19) | copy-start | bytes 124
  13.9 7.4 %copy-start.13 = (s32[1,10]{1,0:T(1,128)S(1)}, s32[1,10]{1,0:T(1,128)}, u32[]{:S(2)}) copy-start(s32[1,10]{1,0:T(1,128)} %param.18) | copy-start | bytes 124
  18.9 28.2 %collective-permute-start.1 = (bf16[1024,1152]{0,1:T(8,128)(2,1)S(1)}, bf16[1024,1152]{0,1:T(8,128)(2,1)}, u32[]{:S(2)}, u32[]{:S(2)}) collective-permute-start(bf16[1024,1152]{0,1:T(8,128)(2,1)S(1)} %maximum_select_fusion), channel_id=1, source_target_pairs={{0,64},{32,224},{64,128},{96,32},{128,192},{160,96},{192,0},{224,1... | collective-permute-start | bytes 7077896 | tf_op jit(solution)/shard_map/gathers/ppermute | solution.py:76
  49.4 15.7 %collective-permute-start.3 = (bf16[512,1152]{0,1:T(8,128)(2,1)}, bf16[512,1152]{0,1:T(8,128)(2,1)S(1)}, u32[]{:S(2)}, u32[]{:S(2)}) collective-permute-start(bf16[512,1152]{0,1:T(8,128)(2,1)} %constant_dynamic-slice_fusion), channel_id=1, source_target_pairs={{0,64},{32,224},{64,128},{96,32},{128,192},{160,96},{192,0},{224,1... | collective-permute-start | bytes 3538952 | tf_op jit(solution)/shard_map/gathers/ppermute | solution.py:79
  54.8 22.7 %collective-permute-start.2 = (bf16[1024,1152]{0,1:T(8,128)(2,1)}, bf16[1024,1152]{0,1:T(8,128)(2,1)}, u32[]{:S(2)}, u32[]{:S(2)}) collective-permute-start(bf16[1024,1152]{0,1:T(8,128)(2,1)} %collective-permute-done.1), channel_id=1, source_target_pairs={{0,32},{32,0},{64,96},{96,64},{128,160},{160,128},{192,224},{224,1... | collective-permute-start | bytes 7077896 | tf_op jit(solution)/shard_map/gathers/ppermute | solution.py:80
  65.1 12.4 %collective-permute-start.4 = (bf16[512,1152]{0,1:T(8,128)(2,1)S(1)}, bf16[512,1152]{0,1:T(8,128)(2,1)}, u32[]{:S(2)}, u32[]{:S(2)}) collective-permute-start(bf16[512,1152]{0,1:T(8,128)(2,1)S(1)} %collective-permute-done.3), channel_id=1, source_target_pairs={{0,32},{32,0},{64,96},{96,64},{128,160},{160,128},{192,224},{224,1... | collective-permute-start | bytes 3538952 | tf_op jit(solution)/shard_map/gathers/ppermute | solution.py:80
  70.8 2.4 %copy-start.14 = (s32[18]{0:T(128)S(1)}, s32[18]{0:T(128)}, u32[]{:S(2)}) copy-start(s32[18]{0:T(128)} %get-tuple-element.19) | copy-start | bytes 220
  90.2 37.5 %copy-start.7 = (bf16[1024,576]{1,0:T(8,128)(2,1)S(1)}, bf16[1024,576]{1,0:T(8,128)(2,1)}, u32[]{:S(2)}) copy-start(bf16[1024,576]{1,0:T(8,128)(2,1)} %copy.19) | copy-start | bytes 3538948
  90.3 37.5 %copy-start.10 = (pred[1024,32]{0,1:T(8,128)(4,1)S(1)}, pred[1024,32]{0,1:T(8,128)(4,1)}, u32[]{:S(2)}) copy-start(pred[1024,32]{0,1:T(8,128)(4,1)} %get-tuple-element.35) | copy-start | bytes 98308
  127.7 5.8 %copy-start.2 = (bf16[1024,4608]{0,1:T(8,128)(2,1)S(1)}, bf16[1024,4608]{0,1:T(8,128)(2,1)}, u32[]{:S(2)}) copy-start(bf16[1024,4608]{0,1:T(8,128)(2,1)} %pad_maximum_fusion) | copy-start | bytes 28311556
  131.8 14.3 %collective-permute-start.5 = (f32[1024,32]{0,1:T(8,128)S(1)}, f32[1024,32]{0,1:T(8,128)S(1)}, u32[]{:S(2)}, u32[]{:S(2)}) collective-permute-start(f32[1024,32]{0,1:T(8,128)S(1)} %select_reduce_fusion), channel_id=1, source_target_pairs={{0,32},{32,0},{64,96},{96,64},{128,160},{160,128},{192,224},{224,1... | collective-permute-start | bytes 393224 | tf_op jit(solution)/shard_map/lowrank/ppermute | solution.py:170
  146.1 2.7 %copy-start.4 = (f32[1024,1024]{0,1:T(8,128)}, f32[1024,1024]{0,1:T(8,128)S(1)}, u32[]{:S(2)}) copy-start(f32[1024,1024]{0,1:T(8,128)S(1)} %fusion.17) | copy-start | bytes 12582916
  146.1 1.4 copy-start.3
  146.1 1.7 copy-start.6
  146.2 5.8 %collective-permute-start.6 = (f32[1024,32]{0,1:T(8,128)S(1)}, f32[1024,32]{0,1:T(8,128)S(1)}, u32[]{:S(2)}, u32[]{:S(2)}) collective-permute-start(f32[1024,32]{0,1:T(8,128)S(1)} %add.129), channel_id=1, source_target_pairs={{0,64},{32,96},{64,0},{96,32},{128,192},{160,224},{192,128},{224,1... | collective-permute-start | bytes 393224 | tf_op jit(solution)/shard_map/lowrank/ppermute | solution.py:170
  150.5 4.4 %copy-start.11 = (s32[2304]{0:T(1024)S(1)}, s32[2304]{0:T(1024)}, u32[]{:S(2)}) copy-start(s32[2304]{0:T(1024)} %clamp_bitcast_fusion) | copy-start | bytes 27652
  150.5 4.4 %copy-start.12 = (pred[2304]{0:T(1024)(128)(4,1)S(1)}, pred[2304]{0:T(1024)(128)(4,1)}, u32[]{:S(2)}) copy-start(pred[2304]{0:T(1024)(128)(4,1)} %fusion.38) | copy-start | bytes 6916
  151.7 3.2 %copy-start.8 = (bf16[1024,2,2,64]{0,3,2,1:T(8,128)(2,1)S(1)}, bf16[1024,2,2,64]{0,3,2,1:T(8,128)(2,1)}, u32[]{:S(2)}) copy-start(bf16[1024,2,2,64]{0,3,2,1:T(8,128)(2,1)} %add_convert_fusion.1) | copy-start | bytes 1572868
  152.0 6.5 %collective-permute-start.7 = (f32[1024,32]{0,1:T(8,128)S(1)}, f32[1024,32]{0,1:T(8,128)S(1)}, u32[]{:S(2)}, u32[]{:S(2)}) collective-permute-start(f32[1024,32]{0,1:T(8,128)S(1)} %add.130), channel_id=1, source_target_pairs={{0,128},{32,160},{64,192},{96,224},{128,0},{160,32},{192,64},{224,... | collective-permute-start | bytes 393224 | tf_op jit(solution)/shard_map/lowrank/ppermute | solution.py:170
  154.9 3.7 %copy-start.5 = (f32[1024,1024]{0,1:T(8,128)S(1)}, f32[1024,1024]{0,1:T(8,128)}, u32[]{:S(2)}) copy-start(f32[1024,1024]{0,1:T(8,128)} %copy-done.4) | copy-start | bytes 12582916
  154.9 3.7 %copy-start.9 = (bf16[1024,32]{0,1:T(8,128)(2,1)S(1)}, bf16[1024,32]{0,1:T(8,128)(2,1)}, u32[]{:S(2)}) copy-start(bf16[1024,32]{0,1:T(8,128)(2,1)} %get-tuple-element.34) | copy-start | bytes 196612
  163.6 1.7 copy-start.1
Sparse Core Ops, SparseCore 0:
  11.1 116.5 all-gather.2

commit v14 on v12

--- a/solution.py
+++ b/solution.py
@@ -218,6 +218,7 @@
         sine_value = jnp.sin(angles)[:, None, :]
         query = rotate(base_query + delta_query, cosine, sine_value).astype(jnp.bfloat16)
         key_rotated = rotate(base_key, cosine, sine_value).astype(jnp.bfloat16)
+        key_rotated = lax.optimization_barrier(key_rotated)
         value_rows = (base_value + delta_value).astype(jnp.bfloat16)
         value_rows = lax.optimization_barrier(value_rows)
 

time: 172 us -> 172 us (level)
  transfers between devices with their start and end apart: 9 -> 9, of which waited for: 4 -> 4; matrix products, arithmetic and copies ran while one was open for 34% -> 33% of each run, Pallas kernels for 0% -> 0%
where the time goes in v14:
time: 172 us
  waiting for transfers between devices  68 us (40%)
  other arithmetic  34.3 us (20%)
  matrix products  25.2 us (15%)
  starting transfers between devices  17 us (10%)
  between operations  14.3 us (8%)
  local copies, waits for them, and re-layouts  12.6 us (7%)
    all_gather x1, waiting for transfers between devices, shards(): packed = lax.all_gather(jnp.concatenate(pieces, axis=0), 'col', axis=0)  33.5 us
    ppermute x1, waiting for transfers between devices, gather_rows(): near = lax.ppermute(own_block, 'row', ring)  26.5 us
    select_n x3, other arithmetic, gather_rows(): jnp.where(relative == 0, own_block, jnp.where(relative == 1, after, jnp.w...  12.7 us
    dot_general x1, matrix products, shards(): jnp.einsum('tci,cin->tn', full_rows.reshape(full_rows.shape[0], packed.sh...  12.5 us
    ppermute x3, starting transfers between devices, shards(): received = lax.ppermute(partial, 'row', pairs)  5.78 us
    ppermute x1, waiting for transfers between devices, gather_rows(): far_half = lax.ppermute(forwarded, 'row', ring)  5.2 us
    ppermute x2, starting transfers between devices, gather_rows(): from_partner, far_other = lax.ppermute((near, far_half), 'row', swap)  4.55 us
    unnamed x33, local copies, waits for them, and re-layouts  4.55 us
  transfers between devices with their start and end apart: 9, of which 4 were waited for; matrix products, arithmetic and copies ran while one was open for 33% of the time, Pallas kernels for 0%

profile of v14, /device:TPU:1, one launch (start us, length us, event | category | flops | bytes accessed | tf_op | source)
XLA Modules:
  0.0 171.5 jit_solution(17950057276320361952)
XLA Ops:
  7.2 0.7 copy.27
  8.0 0.7 copy.28
  8.8 1.8 %maximum_maximum_fusion = bf16[176,1024]{1,0:T(8,128)(2,1)} fusion(bf16[32,448]{1,0:T(8,128)(2,1)S(1)} %reshape.312, bf16[32,576]{1,0:T(8,128)(2,1)} %bitcast.80, bf16[144,256]{1,0:T(8,128)(2,1)} %param.14, bf16[144,256]{1,0:T(8,128)(2,1)} %param.13, bf16[144,512]{1,0:T(8,128)(2,1)} %param.12), kind=kLoop, calls=%fused_computation.46 | loop fusion | flops 1802240 | bytes 720896 | tf_op jit(solution)/shard_map/gathers/concatenate | solution.py:151
  10.6 3.3 %collective-permute-start = (bf16[1024,576]{0,1:T(8,128)(2,1)}, bf16[1024,576]{0,1:T(8,128)(2,1)S(1)}, u32[]{:S(2)}, u32[]{:S(2)}) collective-permute-start(bf16[1024,576]{0,1:T(8,128)(2,1)} %param.11), channel_id=1, source_target_pairs={{0,32},{32,0},{64,96},{96,64},{128,160},{160,128},{192,224},{224,1... | collective-permute-start | bytes 3538952 | tf_op jit(solution)/shard_map/gathers/ppermute | solution.py:74
  13.9 2.7 %collective-permute-done = bf16[1024,576]{0,1:T(8,128)(2,1)S(1)} collective-permute-done((bf16[1024,576]{0,1:T(8,128)(2,1)}, bf16[1024,576]{0,1:T(8,128)(2,1)S(1)}, u32[]{:S(2)}, u32[]{:S(2)}) %collective-permute-start) | collective-permute-done | bytes 1179680 | tf_op jit(solution)/shard_map/gathers/ppermute | solution.py:74
  16.6 2.3 %maximum_select_fusion = bf16[1024,1152]{0,1:T(8,128)(2,1)S(1)} fusion(bf16[1024,576]{0,1:T(8,128)(2,1)S(1)} %collective-permute-done, bf16[1024,576]{0,1:T(8,128)(2,1)} %param.11, pred[]{:T(512)S(6)} %eq.98), kind=kLoop, calls=%fused_computation.15 | loop fusion | flops 10616832 | bytes 4718593 | tf_op jit(solution)/shard_map/gathers/jit(_where)/select_n | solution.py:75
  18.9 1.1 collective-permute-start.1
  20.0 0.5 and_select_fusion.1
  20.5 26.5 %collective-permute-done.1 = bf16[1024,1152]{0,1:T(8,128)(2,1)} collective-permute-done((bf16[1024,1152]{0,1:T(8,128)(2,1)S(1)}, bf16[1024,1152]{0,1:T(8,128)(2,1)}, u32[]{:S(2)}, u32[]{:S(2)}) %collective-permute-start.1) | collective-permute-done | bytes 2359328 | tf_op jit(solution)/shard_map/gathers/ppermute | solution.py:80
  47.1 2.4 %constant_dynamic-slice_fusion = bf16[512,1152]{0,1:T(8,128)(2,1)} fusion(bf16[1024,1152]{0,1:T(8,128)(2,1)} %collective-permute-done.1, s32[]{:T(128)S(6)} %select_n.183), kind=kLoop, calls=%fused_computation.91 | loop fusion | bytes 2359300 | tf_op jit(solution)/shard_map/gathers/dynamic_slice | solution.py:82
  49.4 2.2 %collective-permute-start.3 = (bf16[512,1152]{0,1:T(8,128)(2,1)}, bf16[512,1152]{0,1:T(8,128)(2,1)S(1)}, u32[]{:S(2)}, u32[]{:S(2)}) collective-permute-start(bf16[512,1152]{0,1:T(8,128)(2,1)} %constant_dynamic-slice_fusion), channel_id=1, source_target_pairs={{0,64},{32,224},{64,128},{96,32},{128,192},{160,96},{192,0},{224,1... | collective-permute-start | bytes 3538952 | tf_op jit(solution)/shard_map/gathers/ppermute | solution.py:83
  51.7 0.6 fusion.38
  52.3 0.8 reduce-window.9
  53.1 0.7 reduce-window.6
  54.0 0.7 pad_clamp_fusion
  54.6 1.2 gather_fusion
  55.9 0.7 select_reduce_fusion.3
  56.6 0.7 fusion.41
  57.3 0.7 fusion.39
  58.0 0.8 select_reduce_fusion.1
  58.7 0.7 select_reduce_fusion.4
  59.4 0.5 compare_select_fusion.2
  59.9 5.2 %collective-permute-done.3 = bf16[512,1152]{0,1:T(8,128)(2,1)S(1)} collective-permute-done((bf16[512,1152]{0,1:T(8,128)(2,1)}, bf16[512,1152]{0,1:T(8,128)(2,1)S(1)}, u32[]{:S(2)}, u32[]{:S(2)}) %collective-permute-start.3) | collective-permute-done | bytes 1179680 | tf_op jit(solution)/shard_map/gathers/ppermute | solution.py:83
  65.1 4.4 %collective-permute-start.4 = (bf16[512,1152]{0,1:T(8,128)(2,1)S(1)}, bf16[512,1152]{0,1:T(8,128)(2,1)}, u32[]{:S(2)}, u32[]{:S(2)}) collective-permute-start(bf16[512,1152]{0,1:T(8,128)(2,1)S(1)} %collective-permute-done.3), channel_id=1, source_target_pairs={{0,32},{32,0},{64,96},{96,64},{128,160},{160,128},{192,224},{224,1... | collective-permute-start | bytes 3538952 | tf_op jit(solution)/shard_map/gathers/ppermute | solution.py:84
  69.5 0.6 multiply_exponential_fusion
  70.1 2.4 %copy.19 = bf16[1024,576]{1,0:T(8,128)(2,1)} copy(bf16[1024,576]{0,1:T(8,128)(2,1)} %param.11) | data formatting | bytes 2359296 | tf_op args[0]
  72.6 1.3 clamp_bitcast_fusion
  73.9 0.7 fusion.44
  74.6 2.5 %multiply_cosine_fusion = (f32[1024,64]{0,1:T(8,128)}, f32[1024,64]{0,1:T(8,128)}) fusion(f32[64]{0:T(128)} %multiply_exponential_fusion, f32[1024]{0:T(1024)S(1)} %subtract_convert_fusion.2), kind=kLoop, calls=%fused_computation.45 | loop fusion | flops 65536 | bytes 528640 | tf_op jit(solution)/shard_map/rotary/cos | solution.py:217
  77.1 4.9 %select_select_fusion.3 = (bf16[1024,1152]{0,1:T(8,128)(2,1)S(1)}, bf16[1024,1152]{0,1:T(8,128)(2,1)S(1)}, bf16[1024,1152]{0,1:T(8,128)(2,1)S(1)}) fusion(bf16[1024,1152]{0,1:T(8,128)(2,1)S(1)} %maximum_select_fusion, pred[]{:T(512)S(6)} %eq.100, pred[]{:T(512)S(6)} %eq.99, pred[]{:T(512)S(6)} %eq.97, bf16[512,1152]{0,1:T(8,128)(2,1)S(1)} %collective-permute-done.3, ...), kind=kLoop, calls=%fused_computation.20 | loop fusion | flops 16515072 | bytes 16515076 | tf_op jit(solution)/shard_map/gathers/jit(_where)/select_n | solution.py:97
  81.9 3.8 %select_select_fusion.1 = bf16[1024,1152]{0,1:T(8,128)(2,1)S(1)} fusion(bf16[1024,1152]{0,1:T(8,128)(2,1)S(1)} %maximum_select_fusion, bf16[1024,1152]{0,1:T(8,128)(2,1)S(1)} %get-tuple-element.21, bf16[1024,1152]{0,1:T(8,128)(2,1)S(1)} %get-tuple-element.20, pred[]{:T(512)S(6)} %eq.106, pred[]{:T(512)S(6)} %eq.105, pred[]{:T(512)S(6)} %eq.104, ...), kind=kLoop, calls=%fused_computation.18 | loop fusion | flops 14155776 | bytes 11796484 | tf_op jit(solution)/shard_map/gathers/jit(_where)/select_n | solution.py:97
  85.7 4.0 %select_select_fusion.2 = (bf16[1024,1152]{0,1:T(8,128)(2,1)S(1)}, bf16[1024,1152]{0,1:T(8,128)(2,1)S(1)}) fusion(bf16[1024,1152]{0,1:T(8,128)(2,1)S(1)} %maximum_select_fusion, bf16[1024,1152]{0,1:T(8,128)(2,1)S(1)} %get-tuple-element.21, bf16[1024,1152]{0,1:T(8,128)(2,1)S(1)} %get-tuple-element.20, pred[]{:T(512)S(6)} %eq.103, pred[]{:T(512)S(6)} %eq.102, ...), kind=kLoop, calls=%fused_computation.19 | loop fusion | flops 17694720 | bytes 14155783 | tf_op jit(solution)/shard_map/gathers/jit(_where)/select_n | solution.py:97
  89.8 4.4 %pad_maximum_fusion = bf16[1024,4608]{0,1:T(8,128)(2,1)} fusion(bf16[1024,1152]{0,1:T(8,128)(2,1)S(1)} %get-tuple-element.23, bf16[1024,1152]{0,1:T(8,128)(2,1)S(1)} %select_select_fusion.1, bf16[1024,1152]{0,1:T(8,128)(2,1)S(1)} %get-tuple-element.22, bf16[1024,1152]{0,1:T(8,128)(2,1)S(1)} %get-tuple-element.19), kind=kLoop, calls=%fused_computation.3 | loop fusion | flops 37748736 | bytes 18874368 | tf_op jit(solution)/shard_map/gathers/concatenate | solution.py:103
  94.2 33.5 %all-gather.3.cloned.1.call-done = bf16[5632,1024]{1,0:T(8,128)(2,1)} async-done(((bf16[176,1024]{1,0:T(8,128)(2,1)}), bf16[5632,1024]{1,0:T(8,128)(2,1)}) %all-gather.3.cloned.1.call-update) | async-done | bytes 11534352 | tf_op jit(solution)/shard_map/gathers/all_gather | solution.py:151
  127.7 4.1 %select_reduce_fusion = f32[1024,32]{0,1:T(8,128)S(1)} fusion(bf16[32,176,1024]{2,1,0:T(8,128)(2,1)} %bitcast.76, bf16[1024,576]{1,0:T(8,128)(2,1)S(1)} %copy-done.7, pred[1024,32]{0,1:T(8,128)(4,1)S(1)} %copy-done.9), kind=kOutput, calls=%fused_computation.12 | convolution fusion | flops 2149548032 | bytes 3440640 | tf_op jit(solution)/shard_map/lowrank/dot_general | solution.py:163
  131.8 1.7 collective-permute-start.5
  133.5 12.5 %fusion.17 = f32[1024,1024]{0,1:T(8,128)S(1)} fusion(bf16[1024,32,144]{0,2,1:T(8,128)(2,1)S(1)} %bitcast.67, bf16[32,176,1024]{2,1,0:T(8,128)(2,1)} %bitcast.77), kind=kOutput, calls=%fused_computation.23 | convolution fusion | flops 9663676416 | bytes 23068672 | tf_op jit(solution)/shard_map/projection/tci,cin->tn/dot_general | solution.py:201
  146.2 1.3 collective-permute-start.6
  147.7 0.4 copy-done.5
  148.1 1.7 %slice.61 = bf16[32,32,448]{2,1,0:T(8,128)(2,1)S(1)} slice(bf16[32,176,1024]{2,1,0:T(8,128)(2,1)} %bitcast.78), slice={[0:32], [144:176], [576:1024]} | slice | bytes 1835008 | tf_op jit(solution)/shard_map/gathers/slice | solution.py:154
  149.8 1.2 reshape.314
  151.4 2.8 %collective-permute-start.7 = (f32[1024,32]{0,1:T(8,128)S(1)}, f32[1024,32]{0,1:T(8,128)S(1)}, u32[]{:S(2)}, u32[]{:S(2)}) collective-permute-start(f32[1024,32]{0,1:T(8,128)S(1)} %add.130), channel_id=1, source_target_pairs={{0,128},{32,160},{64,192},{96,224},{128,0},{160,32},{192,64},{224,... | collective-permute-start | bytes 393224 | tf_op jit(solution)/shard_map/lowrank/ppermute | solution.py:174
  154.3 3.6 %fusion.11 = bf16[2304,256]{1,0:T(8,128)(2,1)} fusion(bf16[1024,256]{0,1:T(8,128)(2,1)S(1)} %bitcast.74, s32[2304]{0:T(1024)S(1)} %copy-done.10, pred[2304]{0:T(1024)(128)(4,1)S(1)} %fusion.37), kind=kOutput, calls=%fused_computation.13 | convolution fusion | flops 1213267968 | bytes 1715456 | tf_op jit(solution)/shard_map/cache_write/dot_general | solution.py:231
  157.9 0.5 fusion.24
  158.4 3.6 %fusion.14 = bf16[2304,256]{1,0:T(8,128)(2,1)} fusion(bf16[1024,256]{0,1:T(8,128)(2,1)S(1)} %fusion.24, s32[2304]{0:T(1024)S(1)} %copy-done.10, pred[2304]{0:T(1024)(128)(4,1)S(1)} %fusion.37), kind=kOutput, calls=%fused_computation.14 | convolution fusion | flops 1213267968 | bytes 1715456 | tf_op jit(solution)/shard_map/cache_write/dot_general | solution.py:233
  162.1 0.8 slice_add_fusion
  162.9 0.4 subtract_convert_fusion
  163.3 1.3 copy.25
  (51 shorter events, 1.2 us)
Async XLA Ops:
  7.2 47.5 %copy-start = (s32[32]{0:T(128)S(1)}, s32[32]{0:T(128)}, u32[]{:S(2)}) copy-start(s32[32]{0:T(128)} %param.20) | copy-start | bytes 388
  7.2 120.5 %all-gather.3.cloned.1.call-start = ((), (), s32[]{:S(2)}) async-start(), calls=%async_computation | async-start | bytes 11894784 | tf_op jit(solution)/shard_map/gathers/all_gather | solution.py:151
  10.6 6.0 %collective-permute-start = (bf16[1024,576]{0,1:T(8,128)(2,1)}, bf16[1024,576]{0,1:T(8,128)(2,1)S(1)}, u32[]{:S(2)}, u32[]{:S(2)}) collective-permute-start(bf16[1024,576]{0,1:T(8,128)(2,1)} %param.11), channel_id=1, source_target_pairs={{0,32},{32,0},{64,96},{96,64},{128,160},{160,128},{192,224},{224,1... | collective-permute-start | bytes 3538952 | tf_op jit(solution)/shard_map/gathers/ppermute | solution.py:74
  13.9 6.1 %copy-start.11 = (s32[1,10]{1,0:T(1,128)S(1)}, s32[1,10]{1,0:T(1,128)}, u32[]{:S(2)}) copy-start(s32[1,10]{1,0:T(1,128)} %param.18) | copy-start | bytes 124
  18.9 32.8 %copy-start.13 = (s32[1,10]{1,0:T(1,128)S(1)}, s32[1,10]{1,0:T(1,128)}, u32[]{:S(2)}) copy-start(s32[1,10]{1,0:T(1,128)} %param.19) | copy-start | bytes 124
  18.9 28.2 %collective-permute-start.1 = (bf16[1024,1152]{0,1:T(8,128)(2,1)S(1)}, bf16[1024,1152]{0,1:T(8,128)(2,1)}, u32[]{:S(2)}, u32[]{:S(2)}) collective-permute-start(bf16[1024,1152]{0,1:T(8,128)(2,1)S(1)} %maximum_select_fusion), channel_id=1, source_target_pairs={{0,64},{32,224},{64,128},{96,32},{128,192},{160,96},{192,0},{224,1... | collective-permute-start | bytes 7077896 | tf_op jit(solution)/shard_map/gathers/ppermute | solution.py:80
  49.4 15.7 %collective-permute-start.3 = (bf16[512,1152]{0,1:T(8,128)(2,1)}, bf16[512,1152]{0,1:T(8,128)(2,1)S(1)}, u32[]{:S(2)}, u32[]{:S(2)}) collective-permute-start(bf16[512,1152]{0,1:T(8,128)(2,1)} %constant_dynamic-slice_fusion), channel_id=1, source_target_pairs={{0,64},{32,224},{64,128},{96,32},{128,192},{160,96},{192,0},{224,1... | collective-permute-start | bytes 3538952 | tf_op jit(solution)/shard_map/gathers/ppermute | solution.py:83
  53.1 4.9 %copy-start.12 = (s32[10,1]{0,1:T(1,128)}, s32[10,1]{0,1:T(1,128)S(1)}, u32[]{:S(2)}) copy-start(s32[10,1]{0,1:T(1,128)S(1)} %reduce-window.9) | copy-start | bytes 124
  53.8 23.3 %collective-permute-start.2 = (bf16[1024,1152]{0,1:T(8,128)(2,1)}, bf16[1024,1152]{0,1:T(8,128)(2,1)}, u32[]{:S(2)}, u32[]{:S(2)}) collective-permute-start(bf16[1024,1152]{0,1:T(8,128)(2,1)} %collective-permute-done.1), channel_id=1, source_target_pairs={{0,32},{32,0},{64,96},{96,64},{128,160},{160,128},{192,224},{224,1... | collective-permute-start | bytes 7077896 | tf_op jit(solution)/shard_map/gathers/ppermute | solution.py:84
  65.1 11.9 %collective-permute-start.4 = (bf16[512,1152]{0,1:T(8,128)(2,1)S(1)}, bf16[512,1152]{0,1:T(8,128)(2,1)}, u32[]{:S(2)}, u32[]{:S(2)}) collective-permute-start(bf16[512,1152]{0,1:T(8,128)(2,1)S(1)} %collective-permute-done.3), channel_id=1, source_target_pairs={{0,32},{32,0},{64,96},{96,64},{128,160},{160,128},{192,224},{224,1... | collective-permute-start | bytes 3538952 | tf_op jit(solution)/shard_map/gathers/ppermute | solution.py:84
  89.7 38.0 %copy-start.7 = (bf16[1024,576]{1,0:T(8,128)(2,1)S(1)}, bf16[1024,576]{1,0:T(8,128)(2,1)}, u32[]{:S(2)}) copy-start(bf16[1024,576]{1,0:T(8,128)(2,1)} %copy.19) | copy-start | bytes 3538948
  89.7 38.0 %copy-start.9 = (pred[1024,32]{0,1:T(8,128)(4,1)S(1)}, pred[1024,32]{0,1:T(8,128)(4,1)}, u32[]{:S(2)}) copy-start(pred[1024,32]{0,1:T(8,128)(4,1)} %get-tuple-element.33) | copy-start | bytes 98308
  127.7 5.8 %copy-start.2 = (bf16[1024,4608]{0,1:T(8,128)(2,1)S(1)}, bf16[1024,4608]{0,1:T(8,128)(2,1)}, u32[]{:S(2)}) copy-start(bf16[1024,4608]{0,1:T(8,128)(2,1)} %pad_maximum_fusion) | copy-start | bytes 28311556
  131.8 14.3 %collective-permute-start.5 = (f32[1024,32]{0,1:T(8,128)S(1)}, f32[1024,32]{0,1:T(8,128)S(1)}, u32[]{:S(2)}, u32[]{:S(2)}) collective-permute-start(f32[1024,32]{0,1:T(8,128)S(1)} %select_reduce_fusion), channel_id=1, source_target_pairs={{0,32},{32,0},{64,96},{96,64},{128,160},{160,128},{192,224},{224,1... | collective-permute-start | bytes 393224 | tf_op jit(solution)/shard_map/lowrank/ppermute | solution.py:174
  146.1 2.0 %copy-start.5 = (f32[1024,1024]{0,1:T(8,128)}, f32[1024,1024]{0,1:T(8,128)S(1)}, u32[]{:S(2)}) copy-start(f32[1024,1024]{0,1:T(8,128)S(1)} %fusion.17) | copy-start | bytes 12582916
  146.1 1.4 copy-start.3
  146.1 1.4 copy-start.4
  146.2 5.2 %collective-permute-start.6 = (f32[1024,32]{0,1:T(8,128)S(1)}, f32[1024,32]{0,1:T(8,128)S(1)}, u32[]{:S(2)}, u32[]{:S(2)}) collective-permute-start(f32[1024,32]{0,1:T(8,128)S(1)} %add.129), channel_id=1, source_target_pairs={{0,64},{32,96},{64,0},{96,32},{128,192},{160,224},{192,128},{224,1... | collective-permute-start | bytes 393224 | tf_op jit(solution)/shard_map/lowrank/ppermute | solution.py:174
  151.0 3.2 %copy-start.10 = (s32[2304]{0:T(1024)S(1)}, s32[2304]{0:T(1024)}, u32[]{:S(2)}) copy-start(s32[2304]{0:T(1024)} %clamp_bitcast_fusion) | copy-start | bytes 27652
  151.4 6.5 %copy-start.6 = (f32[1024,1024]{0,1:T(8,128)S(1)}, f32[1024,1024]{0,1:T(8,128)}, u32[]{:S(2)}) copy-start(f32[1024,1024]{0,1:T(8,128)} %copy-done.5) | copy-start | bytes 12582916
  151.4 6.5 %copy-start.8 = (bf16[1024,32]{0,1:T(8,128)(2,1)S(1)}, bf16[1024,32]{0,1:T(8,128)(2,1)}, u32[]{:S(2)}) copy-start(bf16[1024,32]{0,1:T(8,128)(2,1)} %get-tuple-element.32) | copy-start | bytes 196612
  151.4 6.5 %collective-permute-start.7 = (f32[1024,32]{0,1:T(8,128)S(1)}, f32[1024,32]{0,1:T(8,128)S(1)}, u32[]{:S(2)}, u32[]{:S(2)}) collective-permute-start(f32[1024,32]{0,1:T(8,128)S(1)} %add.130), channel_id=1, source_target_pairs={{0,128},{32,160},{64,192},{96,224},{128,0},{160,32},{192,64},{224,... | collective-permute-start | bytes 393224 | tf_op jit(solution)/shard_map/lowrank/ppermute | solution.py:174
  162.9 1.8 %copy-start.1 = (s32[32]{0:T(128)S(1)}, s32[32]{0:T(128)}, u32[]{:S(2)}) copy-start(s32[32]{0:T(128)} %param.20) | copy-start | bytes 388
Sparse Core Ops, SparseCore 0:
  11.1 116.5 all-gather.2
